TPU v7x, 512 devices: a whole 4x4x16 slice. The times are simulated.
512 devices in a mesh: px: 32 (over y, x, core), py: 16 (over z).
Axes of the slice: x: 4, y: 4, z: 16, core: 2. Of those that a mesh axis runs over, the one named last changes fastest.
Arguments:
- start_vecs: float32 [8192, 64, 128], P(('px', 'py')), may hold values from -6 to 6
- local_tiles: bfloat16 [8192, 4, 128, 128], P(('px', 'py')), may hold values from -0.078125 to 0.078125
- local_cols: int32 [8192, 4], P(('px', 'py')), may hold values from 0 to 15
- halo_tiles: bfloat16 [8192, 128, 128], P(('px', 'py')), may hold values from -0.078125 to 0.078125
- halo_slot: int32 [8192], P(('px', 'py')), may hold values from 0 to 7
- boundary: int32 [2048, 2], P(('px', 'py')), may hold values from 0 to 15
Outputs:
- filtered: float32 [8192, 64, 128], P(('px', 'py'))
- gram_matrix: float32 [64, 64], replicated
Inputs may be any that keep to these rules, and one draw needn't show every extreme that they name: `local_cols`: local block indices within the partition. `boundary`: local block indices within the partition.
All inputs are finite; a program needn't handle non-finite values.
Results may differ from a plain program's by a relative error of at most 0.0055.
Values may be sent and summed in bfloat16 or wider, within the bound.
No kernel may reach another device: no remote copies, remote signals or barrier semaphores. Data moves between devices by JAX's collectives and lax.ppermute only.
A program may use at most 64 MiB of HBM per device.

v0:
```python
import jax
import jax.numpy as jnp
from jax import lax
from jax.sharding import PartitionSpec as P

DEG = 9


def from_behind(value, axis, steps):
    count = lax.axis_size(axis)
    pairs = [(source, (source + steps) % count) for source in range(count)]
    return lax.ppermute(value, axis, pairs)


def operator_apply(current, local_tiles, local_cols, halo_tiles, halo_slot, boundary):
    rounded = current.astype(jnp.bfloat16)
    outgoing = rounded[boundary]
    from_xlow = from_behind(outgoing[0], "px", 1)
    from_xhigh = from_behind(outgoing[1], "px", -1)
    from_ylow = from_behind(outgoing[2], "py", 1)
    from_yhigh = from_behind(outgoing[3], "py", -1)
    received = jnp.concatenate([from_xlow, from_xhigh, from_ylow, from_yhigh], axis=0)
    gathered = rounded[local_cols]
    product = jnp.einsum(
        "rtkj,rtij->rki", gathered, local_tiles, preferred_element_type=jnp.float32
    )
    coupled = jnp.einsum(
        "rkj,rij->rki", received[halo_slot], halo_tiles, preferred_element_type=jnp.float32
    )
    return product + coupled


def shards(start_vecs, local_tiles, local_cols, halo_tiles, halo_slot, boundary):

    def step_apply(current):
        return operator_apply(current, local_tiles, local_cols, halo_tiles, halo_slot, boundary)

    first_vecs = step_apply(start_vecs)

    def advance(step_index, state_pair):
        older_vec, newer_vec = state_pair
        return (newer_vec, 2.0 * step_apply(newer_vec) - older_vec)

    previous, current = lax.fori_loop(0, DEG - 1, advance, (start_vecs, first_vecs))
    total_rows = current.shape[0] * current.shape[2] * lax.axis_size("px") * lax.axis_size("py")
    squares = lax.psum(jnp.sum(current * current, axis=(0, 2)), ("px", "py"))
    scales = lax.rsqrt(squares / total_rows + 1e-06)
    filtered = current * scales[None, :, None]
    partial_gram = jnp.einsum("rkj,rlj->kl", filtered, filtered, precision=lax.Precision.HIGHEST)
    gram_matrix = lax.psum(partial_gram, ("px", "py")) / total_rows
    return (filtered, gram_matrix)


def solution(mesh):
    return jax.shard_map(
        shards,
        mesh=mesh,
        in_specs=(
            P(("px", "py"), None, None),
            P(("px", "py"), None, None, None),
            P(("px", "py"), None),
            P(("px", "py"), None, None),
            P(("px", "py")),
            P(("px", "py"), None),
        ),
        out_specs=(P(("px", "py"), None, None), P()),
        check_vma=False,
    )
```

profile of v0, /device:TPU:1, one launch (start us, length us, event | category | flops | bytes accessed | tf_op | source)
XLA Modules:
  0.0 419.5 jit_solution(5818227597087407548)
XLA Ops:
  3.4 4.5 %collective-permute-start.4 = (bf16[2,64,128]{2,1,0:T(8,128)(2,1)S(1)}, bf16[2,64,128]{2,1,0:T(8,128)(2,1)S(1)}, u32[]{:S(2)}, u32[]{:S(2)}) collective-permute-start(bf16[2,64,128]{2,1,0:T(8,128)(2,1)S(1)} %get-tuple-element.65), channel_id=1, source_target_pairs={{0,16},{16,32},{32,48},{48,64},{64,80},{80,96},{96,112},{112,128},... | collective-permute-start | bytes 98312 | tf_op jit(solution)/shard_map/ppermute | solution.py:12
  7.9 3.5 collective-permute-start.6
  11.4 4.5 %collective-permute-start.5 = (bf16[2,64,128]{2,1,0:T(8,128)(2,1)S(1)}, bf16[2,64,128]{2,1,0:T(8,128)(2,1)S(1)}, u32[]{:S(2)}, u32[]{:S(2)}) collective-permute-start(bf16[2,64,128]{2,1,0:T(8,128)(2,1)S(1)} %get-tuple-element.67), channel_id=1, source_target_pairs={{0,496},{16,0},{32,16},{48,32},{64,48},{80,64},{96,80},{112,96},{1... | collective-permute-start | bytes 98312 | tf_op jit(solution)/shard_map/ppermute | solution.py:12
  16.0 6.9 %collective-permute-start.7 = (bf16[2,64,128]{2,1,0:T(8,128)(2,1)S(1)}, bf16[2,64,128]{2,1,0:T(8,128)(2,1)S(1)}, u32[]{:S(2)}, u32[]{:S(2)}) collective-permute-start(bf16[2,64,128]{2,1,0:T(8,128)(2,1)S(1)} %get-tuple-element.68), channel_id=1, source_target_pairs={{0,15},{1,0},{2,1},{3,2},{4,3},{5,4},{6,5},{7,6},{8,7},{9,8},{10,9... | collective-permute-start | bytes 98312 | tf_op jit(solution)/shard_map/ppermute | solution.py:12
  24.8 2.9 convolution_bitcast_fusion.1
  29.9 184.2 %while.12 = (s32[]{:T(128)}, f32[16,64,128]{2,1,0:T(8,128)}, f32[16,64,128]{2,1,0:T(8,128)S(1)}, s32[16,4]{0,1:T(4,128)S(1)}, bf16[16,4,128,128]{3,2,1,0:T(8,128...) while((s32[]{:T(128)}, f32[16,64,128]{2,1,0:T(8,128)}, ...), condition=%wide.region_1.0_spmd, body=%wide.region_0.0_spmd.sunk | while | flops 168496400 | bytes 23345988 | solution.py:44
  30.8 3.4 collective-permute-start
  34.1 1.9 collective-permute-start.1
  36.1 6.7 %collective-permute-start.2 = (bf16[2,64,128]{2,1,0:T(8,128)(2,1)S(1)}, bf16[2,64,128]{2,1,0:T(8,128)(2,1)S(1)}, u32[]{:S(2)}, u32[]{:S(2)}) collective-permute-start(bf16[2,64,128]{2,1,0:T(8,128)(2,1)S(1)} %get-tuple-element.124), channel_id=1, source_target_pairs={{0,496},{16,0},{32,16},{48,32},{64,48},{80,64},{96,80},{112,96},{1... | collective-permute-start | bytes 98312 | tf_op jit(solution)/shard_map/while/body/eval_jaxpr/ppermute | solution.py:12
  42.8 1.9 collective-permute-start.3
  45.7 2.4 convolution_bitcast_fusion.4
  52.7 4.6 %collective-permute-start = (bf16[2,64,128]{2,1,0:T(8,128)(2,1)S(1)}, bf16[2,64,128]{2,1,0:T(8,128)(2,1)S(1)}, u32[]{:S(2)}, u32[]{:S(2)}) collective-permute-start(bf16[2,64,128]{2,1,0:T(8,128)(2,1)S(1)} %get-tuple-element.122), channel_id=1, source_target_pairs={{0,15},{1,0},{2,1},{3,2},{4,3},{5,4},{6,5},{7,6},{8,7},{9,8},{10,9... | collective-permute-start | bytes 98312 | tf_op jit(solution)/shard_map/while/body/eval_jaxpr/ppermute | solution.py:12
  57.3 1.9 collective-permute-start.1
  59.2 5.4 %collective-permute-start.2 = (bf16[2,64,128]{2,1,0:T(8,128)(2,1)S(1)}, bf16[2,64,128]{2,1,0:T(8,128)(2,1)S(1)}, u32[]{:S(2)}, u32[]{:S(2)}) collective-permute-start(bf16[2,64,128]{2,1,0:T(8,128)(2,1)S(1)} %get-tuple-element.124), channel_id=1, source_target_pairs={{0,496},{16,0},{32,16},{48,32},{64,48},{80,64},{96,80},{112,96},{1... | collective-permute-start | bytes 98312 | tf_op jit(solution)/shard_map/while/body/eval_jaxpr/ppermute | solution.py:12
  64.6 1.9 collective-permute-start.3
  67.5 2.4 convolution_bitcast_fusion.4
  74.5 4.9 %collective-permute-start = (bf16[2,64,128]{2,1,0:T(8,128)(2,1)S(1)}, bf16[2,64,128]{2,1,0:T(8,128)(2,1)S(1)}, u32[]{:S(2)}, u32[]{:S(2)}) collective-permute-start(bf16[2,64,128]{2,1,0:T(8,128)(2,1)S(1)} %get-tuple-element.122), channel_id=1, source_target_pairs={{0,15},{1,0},{2,1},{3,2},{4,3},{5,4},{6,5},{7,6},{8,7},{9,8},{10,9... | collective-permute-start | bytes 98312 | tf_op jit(solution)/shard_map/while/body/eval_jaxpr/ppermute | solution.py:12
  79.4 1.9 collective-permute-start.1
  81.3 6.7 %collective-permute-start.2 = (bf16[2,64,128]{2,1,0:T(8,128)(2,1)S(1)}, bf16[2,64,128]{2,1,0:T(8,128)(2,1)S(1)}, u32[]{:S(2)}, u32[]{:S(2)}) collective-permute-start(bf16[2,64,128]{2,1,0:T(8,128)(2,1)S(1)} %get-tuple-element.124), channel_id=1, source_target_pairs={{0,496},{16,0},{32,16},{48,32},{64,48},{80,64},{96,80},{112,96},{1... | collective-permute-start | bytes 98312 | tf_op jit(solution)/shard_map/while/body/eval_jaxpr/ppermute | solution.py:12
  88.0 1.9 collective-permute-start.3
  90.9 2.4 convolution_bitcast_fusion.4
  97.9 4.8 %collective-permute-start = (bf16[2,64,128]{2,1,0:T(8,128)(2,1)S(1)}, bf16[2,64,128]{2,1,0:T(8,128)(2,1)S(1)}, u32[]{:S(2)}, u32[]{:S(2)}) collective-permute-start(bf16[2,64,128]{2,1,0:T(8,128)(2,1)S(1)} %get-tuple-element.122), channel_id=1, source_target_pairs={{0,15},{1,0},{2,1},{3,2},{4,3},{5,4},{6,5},{7,6},{8,7},{9,8},{10,9... | collective-permute-start | bytes 98312 | tf_op jit(solution)/shard_map/while/body/eval_jaxpr/ppermute | solution.py:12
  102.8 1.9 collective-permute-start.1
  104.7 6.7 %collective-permute-start.2 = (bf16[2,64,128]{2,1,0:T(8,128)(2,1)S(1)}, bf16[2,64,128]{2,1,0:T(8,128)(2,1)S(1)}, u32[]{:S(2)}, u32[]{:S(2)}) collective-permute-start(bf16[2,64,128]{2,1,0:T(8,128)(2,1)S(1)} %get-tuple-element.124), channel_id=1, source_target_pairs={{0,496},{16,0},{32,16},{48,32},{64,48},{80,64},{96,80},{112,96},{1... | collective-permute-start | bytes 98312 | tf_op jit(solution)/shard_map/while/body/eval_jaxpr/ppermute | solution.py:12
  111.4 1.9 collective-permute-start.3
  114.3 2.4 convolution_bitcast_fusion.4
  121.3 4.9 %collective-permute-start = (bf16[2,64,128]{2,1,0:T(8,128)(2,1)S(1)}, bf16[2,64,128]{2,1,0:T(8,128)(2,1)S(1)}, u32[]{:S(2)}, u32[]{:S(2)}) collective-permute-start(bf16[2,64,128]{2,1,0:T(8,128)(2,1)S(1)} %get-tuple-element.122), channel_id=1, source_target_pairs={{0,15},{1,0},{2,1},{3,2},{4,3},{5,4},{6,5},{7,6},{8,7},{9,8},{10,9... | collective-permute-start | bytes 98312 | tf_op jit(solution)/shard_map/while/body/eval_jaxpr/ppermute | solution.py:12
  126.2 1.9 collective-permute-start.1
  128.1 6.7 %collective-permute-start.2 = (bf16[2,64,128]{2,1,0:T(8,128)(2,1)S(1)}, bf16[2,64,128]{2,1,0:T(8,128)(2,1)S(1)}, u32[]{:S(2)}, u32[]{:S(2)}) collective-permute-start(bf16[2,64,128]{2,1,0:T(8,128)(2,1)S(1)} %get-tuple-element.124), channel_id=1, source_target_pairs={{0,496},{16,0},{32,16},{48,32},{64,48},{80,64},{96,80},{112,96},{1... | collective-permute-start | bytes 98312 | tf_op jit(solution)/shard_map/while/body/eval_jaxpr/ppermute | solution.py:12
  134.8 1.9 collective-permute-start.3
  137.7 2.4 convolution_bitcast_fusion.4
  144.7 4.8 %collective-permute-start = (bf16[2,64,128]{2,1,0:T(8,128)(2,1)S(1)}, bf16[2,64,128]{2,1,0:T(8,128)(2,1)S(1)}, u32[]{:S(2)}, u32[]{:S(2)}) collective-permute-start(bf16[2,64,128]{2,1,0:T(8,128)(2,1)S(1)} %get-tuple-element.122), channel_id=1, source_target_pairs={{0,15},{1,0},{2,1},{3,2},{4,3},{5,4},{6,5},{7,6},{8,7},{9,8},{10,9... | collective-permute-start | bytes 98312 | tf_op jit(solution)/shard_map/while/body/eval_jaxpr/ppermute | solution.py:12
  149.6 1.9 collective-permute-start.1
  151.5 6.7 %collective-permute-start.2 = (bf16[2,64,128]{2,1,0:T(8,128)(2,1)S(1)}, bf16[2,64,128]{2,1,0:T(8,128)(2,1)S(1)}, u32[]{:S(2)}, u32[]{:S(2)}) collective-permute-start(bf16[2,64,128]{2,1,0:T(8,128)(2,1)S(1)} %get-tuple-element.124), channel_id=1, source_target_pairs={{0,496},{16,0},{32,16},{48,32},{64,48},{80,64},{96,80},{112,96},{1... | collective-permute-start | bytes 98312 | tf_op jit(solution)/shard_map/while/body/eval_jaxpr/ppermute | solution.py:12
  158.2 1.9 collective-permute-start.3
  161.1 2.4 convolution_bitcast_fusion.4
  168.2 4.9 %collective-permute-start = (bf16[2,64,128]{2,1,0:T(8,128)(2,1)S(1)}, bf16[2,64,128]{2,1,0:T(8,128)(2,1)S(1)}, u32[]{:S(2)}, u32[]{:S(2)}) collective-permute-start(bf16[2,64,128]{2,1,0:T(8,128)(2,1)S(1)} %get-tuple-element.122), channel_id=1, source_target_pairs={{0,15},{1,0},{2,1},{3,2},{4,3},{5,4},{6,5},{7,6},{8,7},{9,8},{10,9... | collective-permute-start | bytes 98312 | tf_op jit(solution)/shard_map/while/body/eval_jaxpr/ppermute | solution.py:12
  173.0 1.9 collective-permute-start.1
  174.9 6.7 %collective-permute-start.2 = (bf16[2,64,128]{2,1,0:T(8,128)(2,1)S(1)}, bf16[2,64,128]{2,1,0:T(8,128)(2,1)S(1)}, u32[]{:S(2)}, u32[]{:S(2)}) collective-permute-start(bf16[2,64,128]{2,1,0:T(8,128)(2,1)S(1)} %get-tuple-element.124), channel_id=1, source_target_pairs={{0,496},{16,0},{32,16},{48,32},{64,48},{80,64},{96,80},{112,96},{1... | collective-permute-start | bytes 98312 | tf_op jit(solution)/shard_map/while/body/eval_jaxpr/ppermute | solution.py:12
  181.6 1.9 collective-permute-start.3
  184.5 2.4 convolution_bitcast_fusion.4
  191.6 4.8 %collective-permute-start = (bf16[2,64,128]{2,1,0:T(8,128)(2,1)S(1)}, bf16[2,64,128]{2,1,0:T(8,128)(2,1)S(1)}, u32[]{:S(2)}, u32[]{:S(2)}) collective-permute-start(bf16[2,64,128]{2,1,0:T(8,128)(2,1)S(1)} %get-tuple-element.122), channel_id=1, source_target_pairs={{0,15},{1,0},{2,1},{3,2},{4,3},{5,4},{6,5},{7,6},{8,7},{9,8},{10,9... | collective-permute-start | bytes 98312 | tf_op jit(solution)/shard_map/while/body/eval_jaxpr/ppermute | solution.py:12
  196.4 1.9 collective-permute-start.1
  198.3 6.7 %collective-permute-start.2 = (bf16[2,64,128]{2,1,0:T(8,128)(2,1)S(1)}, bf16[2,64,128]{2,1,0:T(8,128)(2,1)S(1)}, u32[]{:S(2)}, u32[]{:S(2)}) collective-permute-start(bf16[2,64,128]{2,1,0:T(8,128)(2,1)S(1)} %get-tuple-element.124), channel_id=1, source_target_pairs={{0,496},{16,0},{32,16},{48,32},{64,48},{80,64},{96,80},{112,96},{1... | collective-permute-start | bytes 98312 | tf_op jit(solution)/shard_map/while/body/eval_jaxpr/ppermute | solution.py:12
  205.0 1.9 collective-permute-start.3
  207.9 2.4 convolution_bitcast_fusion.4
  214.3 105.2 %psum.14 = f32[64]{0:T(128)S(1)} all-reduce(f32[64]{0:T(128)S(1)} %multiply_reduce_fusion), channel_id=1, replica_groups=mesh['px'=32,'py'=16] {'px','py'}, use_global_device_ids=true, to_apply=%region_3.0 | all-reduce | flops 64 | bytes 512 | tf_op jit(solution)/shard_map/psum | solution.py:46
  320.2 98.6 %psum.15 = f32[64,64]{1,0:T(8,128)S(1)} all-reduce(f32[64,64]{1,0:T(8,128)S(1)} %convolution_bitcast_fusion.2), channel_id=1, replica_groups=mesh['px'=32,'py'=16] {'px','py'}, use_global_device_ids=true, to_apply=%region_4.0 | all-reduce | flops 4096 | bytes 32768 | tf_op jit(solution)/shard_map/psum | solution.py:50
  (257 shorter events, 51.5 us)
Async XLA Ops:
  0.6 24.1 %copy-start = (bf16[16,4,128,128]{3,2,1,0:T(8,128)(2,1)S(1)}, bf16[16,4,128,128]{3,2,1,0:T(8,128)(2,1)}, u32[]{:S(2)}) copy-start(bf16[16,4,128,128]{3,2,1,0:T(8,128)(2,1)} %param.9) | copy-start | bytes 6291460
  0.6 22.3 %copy-start.6 = (s32[16,4]{0,1:T(4,128)S(1)}, s32[16,4]{0,1:T(4,128)}, u32[]{:S(2)}) copy-start(s32[16,4]{0,1:T(4,128)} %param.10) | copy-start | bytes 772
  0.7 22.2 %copy-start.8 = (s32[16]{0:T(128)S(1)}, s32[16]{0:T(128)}, u32[]{:S(2)}) copy-start(s32[16]{0:T(128)} %param.12) | copy-start | bytes 196
  1.9 25.8 %copy-start.2 = (f32[16,64,128]{2,1,0:T(8,128)}, f32[16,64,128]{2,1,0:T(8,128)S(1)}, u32[]{:S(2)}) copy-start(f32[16,64,128]{2,1,0:T(8,128)S(1)} %copy.33) | copy-start | bytes 1572868
  3.4 24.3 %collective-permute-start.4 = (bf16[2,64,128]{2,1,0:T(8,128)(2,1)S(1)}, bf16[2,64,128]{2,1,0:T(8,128)(2,1)S(1)}, u32[]{:S(2)}, u32[]{:S(2)}) collective-permute-start(bf16[2,64,128]{2,1,0:T(8,128)(2,1)S(1)} %get-tuple-element.65), channel_id=1, source_target_pairs={{0,16},{16,32},{32,48},{48,64},{64,80},{80,96},{96,112},{112,128},... | collective-permute-start | bytes 98312 | tf_op jit(solution)/shard_map/ppermute | solution.py:12
  7.9 19.8 %collective-permute-start.6 = (bf16[2,64,128]{2,1,0:T(8,128)(2,1)S(1)}, bf16[2,64,128]{2,1,0:T(8,128)(2,1)S(1)}, u32[]{:S(2)}, u32[]{:S(2)}) collective-permute-start(bf16[2,64,128]{2,1,0:T(8,128)(2,1)S(1)} %get-tuple-element.66), channel_id=1, source_target_pairs={{0,1},{1,2},{2,3},{3,4},{4,5},{5,6},{6,7},{7,8},{8,9},{9,10},{10,1... | collective-permute-start | bytes 98312 | tf_op jit(solution)/shard_map/ppermute | solution.py:12
  11.4 16.3 %collective-permute-start.5 = (bf16[2,64,128]{2,1,0:T(8,128)(2,1)S(1)}, bf16[2,64,128]{2,1,0:T(8,128)(2,1)S(1)}, u32[]{:S(2)}, u32[]{:S(2)}) collective-permute-start(bf16[2,64,128]{2,1,0:T(8,128)(2,1)S(1)} %get-tuple-element.67), channel_id=1, source_target_pairs={{0,496},{16,0},{32,16},{48,32},{64,48},{80,64},{96,80},{112,96},{1... | collective-permute-start | bytes 98312 | tf_op jit(solution)/shard_map/ppermute | solution.py:12
  16.0 11.7 %collective-permute-start.7 = (bf16[2,64,128]{2,1,0:T(8,128)(2,1)S(1)}, bf16[2,64,128]{2,1,0:T(8,128)(2,1)S(1)}, u32[]{:S(2)}, u32[]{:S(2)}) collective-permute-start(bf16[2,64,128]{2,1,0:T(8,128)(2,1)S(1)} %get-tuple-element.68), channel_id=1, source_target_pairs={{0,15},{1,0},{2,1},{3,2},{4,3},{5,4},{6,5},{7,6},{8,7},{9,8},{10,9... | collective-permute-start | bytes 98312 | tf_op jit(solution)/shard_map/ppermute | solution.py:12
  24.8 3.6 copy-start.3
  30.8 17.3 %collective-permute-start = (bf16[2,64,128]{2,1,0:T(8,128)(2,1)S(1)}, bf16[2,64,128]{2,1,0:T(8,128)(2,1)S(1)}, u32[]{:S(2)}, u32[]{:S(2)}) collective-permute-start(bf16[2,64,128]{2,1,0:T(8,128)(2,1)S(1)} %get-tuple-element.122), channel_id=1, source_target_pairs={{0,15},{1,0},{2,1},{3,2},{4,3},{5,4},{6,5},{7,6},{8,7},{9,8},{10,9... | collective-permute-start | bytes 98312 | tf_op jit(solution)/shard_map/while/body/eval_jaxpr/ppermute | solution.py:12
  34.1 14.0 %collective-permute-start.1 = (bf16[2,64,128]{2,1,0:T(8,128)(2,1)S(1)}, bf16[2,64,128]{2,1,0:T(8,128)(2,1)S(1)}, u32[]{:S(2)}, u32[]{:S(2)}) collective-permute-start(bf16[2,64,128]{2,1,0:T(8,128)(2,1)S(1)} %get-tuple-element.123), channel_id=1, source_target_pairs={{0,1},{1,2},{2,3},{3,4},{4,5},{5,6},{6,7},{7,8},{8,9},{9,10},{10,1... | collective-permute-start | bytes 98312 | tf_op jit(solution)/shard_map/while/body/eval_jaxpr/ppermute | solution.py:12
  36.1 12.1 %collective-permute-start.2 = (bf16[2,64,128]{2,1,0:T(8,128)(2,1)S(1)}, bf16[2,64,128]{2,1,0:T(8,128)(2,1)S(1)}, u32[]{:S(2)}, u32[]{:S(2)}) collective-permute-start(bf16[2,64,128]{2,1,0:T(8,128)(2,1)S(1)} %get-tuple-element.124), channel_id=1, source_target_pairs={{0,496},{16,0},{32,16},{48,32},{64,48},{80,64},{96,80},{112,96},{1... | collective-permute-start | bytes 98312 | tf_op jit(solution)/shard_map/while/body/eval_jaxpr/ppermute | solution.py:12
  42.8 5.4 %collective-permute-start.3 = (bf16[2,64,128]{2,1,0:T(8,128)(2,1)S(1)}, bf16[2,64,128]{2,1,0:T(8,128)(2,1)S(1)}, u32[]{:S(2)}, u32[]{:S(2)}) collective-permute-start(bf16[2,64,128]{2,1,0:T(8,128)(2,1)S(1)} %get-tuple-element.125), channel_id=1, source_target_pairs={{0,16},{16,32},{32,48},{48,64},{64,80},{80,96},{96,112},{112,128},... | collective-permute-start | bytes 98312 | tf_op jit(solution)/shard_map/while/body/eval_jaxpr/ppermute | solution.py:12
  48.8 2.7 copy-start.1
  52.7 17.2 %collective-permute-start = (bf16[2,64,128]{2,1,0:T(8,128)(2,1)S(1)}, bf16[2,64,128]{2,1,0:T(8,128)(2,1)S(1)}, u32[]{:S(2)}, u32[]{:S(2)}) collective-permute-start(bf16[2,64,128]{2,1,0:T(8,128)(2,1)S(1)} %get-tuple-element.122), channel_id=1, source_target_pairs={{0,15},{1,0},{2,1},{3,2},{4,3},{5,4},{6,5},{7,6},{8,7},{9,8},{10,9... | collective-permute-start | bytes 98312 | tf_op jit(solution)/shard_map/while/body/eval_jaxpr/ppermute | solution.py:12
  57.3 12.7 %collective-permute-start.1 = (bf16[2,64,128]{2,1,0:T(8,128)(2,1)S(1)}, bf16[2,64,128]{2,1,0:T(8,128)(2,1)S(1)}, u32[]{:S(2)}, u32[]{:S(2)}) collective-permute-start(bf16[2,64,128]{2,1,0:T(8,128)(2,1)S(1)} %get-tuple-element.123), channel_id=1, source_target_pairs={{0,1},{1,2},{2,3},{3,4},{4,5},{5,6},{6,7},{7,8},{8,9},{9,10},{10,1... | collective-permute-start | bytes 98312 | tf_op jit(solution)/shard_map/while/body/eval_jaxpr/ppermute | solution.py:12
  59.2 10.7 %collective-permute-start.2 = (bf16[2,64,128]{2,1,0:T(8,128)(2,1)S(1)}, bf16[2,64,128]{2,1,0:T(8,128)(2,1)S(1)}, u32[]{:S(2)}, u32[]{:S(2)}) collective-permute-start(bf16[2,64,128]{2,1,0:T(8,128)(2,1)S(1)} %get-tuple-element.124), channel_id=1, source_target_pairs={{0,496},{16,0},{32,16},{48,32},{64,48},{80,64},{96,80},{112,96},{1... | collective-permute-start | bytes 98312 | tf_op jit(solution)/shard_map/while/body/eval_jaxpr/ppermute | solution.py:12
  64.6 5.4 %collective-permute-start.3 = (bf16[2,64,128]{2,1,0:T(8,128)(2,1)S(1)}, bf16[2,64,128]{2,1,0:T(8,128)(2,1)S(1)}, u32[]{:S(2)}, u32[]{:S(2)}) collective-permute-start(bf16[2,64,128]{2,1,0:T(8,128)(2,1)S(1)} %get-tuple-element.125), channel_id=1, source_target_pairs={{0,16},{16,32},{32,48},{48,64},{64,80},{80,96},{96,112},{112,128},... | collective-permute-start | bytes 98312 | tf_op jit(solution)/shard_map/while/body/eval_jaxpr/ppermute | solution.py:12
  70.6 2.7 copy-start.1
  74.5 18.8 %collective-permute-start = (bf16[2,64,128]{2,1,0:T(8,128)(2,1)S(1)}, bf16[2,64,128]{2,1,0:T(8,128)(2,1)S(1)}, u32[]{:S(2)}, u32[]{:S(2)}) collective-permute-start(bf16[2,64,128]{2,1,0:T(8,128)(2,1)S(1)} %get-tuple-element.122), channel_id=1, source_target_pairs={{0,15},{1,0},{2,1},{3,2},{4,3},{5,4},{6,5},{7,6},{8,7},{9,8},{10,9... | collective-permute-start | bytes 98312 | tf_op jit(solution)/shard_map/while/body/eval_jaxpr/ppermute | solution.py:12
  79.4 14.0 %collective-permute-start.1 = (bf16[2,64,128]{2,1,0:T(8,128)(2,1)S(1)}, bf16[2,64,128]{2,1,0:T(8,128)(2,1)S(1)}, u32[]{:S(2)}, u32[]{:S(2)}) collective-permute-start(bf16[2,64,128]{2,1,0:T(8,128)(2,1)S(1)} %get-tuple-element.123), channel_id=1, source_target_pairs={{0,1},{1,2},{2,3},{3,4},{4,5},{5,6},{6,7},{7,8},{8,9},{9,10},{10,1... | collective-permute-start | bytes 98312 | tf_op jit(solution)/shard_map/while/body/eval_jaxpr/ppermute | solution.py:12
  81.3 12.0 %collective-permute-start.2 = (bf16[2,64,128]{2,1,0:T(8,128)(2,1)S(1)}, bf16[2,64,128]{2,1,0:T(8,128)(2,1)S(1)}, u32[]{:S(2)}, u32[]{:S(2)}) collective-permute-start(bf16[2,64,128]{2,1,0:T(8,128)(2,1)S(1)} %get-tuple-element.124), channel_id=1, source_target_pairs={{0,496},{16,0},{32,16},{48,32},{64,48},{80,64},{96,80},{112,96},{1... | collective-permute-start | bytes 98312 | tf_op jit(solution)/shard_map/while/body/eval_jaxpr/ppermute | solution.py:12
  88.0 5.4 %collective-permute-start.3 = (bf16[2,64,128]{2,1,0:T(8,128)(2,1)S(1)}, bf16[2,64,128]{2,1,0:T(8,128)(2,1)S(1)}, u32[]{:S(2)}, u32[]{:S(2)}) collective-permute-start(bf16[2,64,128]{2,1,0:T(8,128)(2,1)S(1)} %get-tuple-element.125), channel_id=1, source_target_pairs={{0,16},{16,32},{32,48},{48,64},{64,80},{80,96},{96,112},{112,128},... | collective-permute-start | bytes 98312 | tf_op jit(solution)/shard_map/while/body/eval_jaxpr/ppermute | solution.py:12
  94.0 2.7 copy-start.1
  97.9 18.8 %collective-permute-start = (bf16[2,64,128]{2,1,0:T(8,128)(2,1)S(1)}, bf16[2,64,128]{2,1,0:T(8,128)(2,1)S(1)}, u32[]{:S(2)}, u32[]{:S(2)}) collective-permute-start(bf16[2,64,128]{2,1,0:T(8,128)(2,1)S(1)} %get-tuple-element.122), channel_id=1, source_target_pairs={{0,15},{1,0},{2,1},{3,2},{4,3},{5,4},{6,5},{7,6},{8,7},{9,8},{10,9... | collective-permute-start | bytes 98312 | tf_op jit(solution)/shard_map/while/body/eval_jaxpr/ppermute | solution.py:12
  102.8 14.0 %collective-permute-start.1 = (bf16[2,64,128]{2,1,0:T(8,128)(2,1)S(1)}, bf16[2,64,128]{2,1,0:T(8,128)(2,1)S(1)}, u32[]{:S(2)}, u32[]{:S(2)}) collective-permute-start(bf16[2,64,128]{2,1,0:T(8,128)(2,1)S(1)} %get-tuple-element.123), channel_id=1, source_target_pairs={{0,1},{1,2},{2,3},{3,4},{4,5},{5,6},{6,7},{7,8},{8,9},{9,10},{10,1... | collective-permute-start | bytes 98312 | tf_op jit(solution)/shard_map/while/body/eval_jaxpr/ppermute | solution.py:12
  104.7 12.0 %collective-permute-start.2 = (bf16[2,64,128]{2,1,0:T(8,128)(2,1)S(1)}, bf16[2,64,128]{2,1,0:T(8,128)(2,1)S(1)}, u32[]{:S(2)}, u32[]{:S(2)}) collective-permute-start(bf16[2,64,128]{2,1,0:T(8,128)(2,1)S(1)} %get-tuple-element.124), channel_id=1, source_target_pairs={{0,496},{16,0},{32,16},{48,32},{64,48},{80,64},{96,80},{112,96},{1... | collective-permute-start | bytes 98312 | tf_op jit(solution)/shard_map/while/body/eval_jaxpr/ppermute | solution.py:12
  111.4 5.4 %collective-permute-start.3 = (bf16[2,64,128]{2,1,0:T(8,128)(2,1)S(1)}, bf16[2,64,128]{2,1,0:T(8,128)(2,1)S(1)}, u32[]{:S(2)}, u32[]{:S(2)}) collective-permute-start(bf16[2,64,128]{2,1,0:T(8,128)(2,1)S(1)} %get-tuple-element.125), channel_id=1, source_target_pairs={{0,16},{16,32},{32,48},{48,64},{64,80},{80,96},{96,112},{112,128},... | collective-permute-start | bytes 98312 | tf_op jit(solution)/shard_map/while/body/eval_jaxpr/ppermute | solution.py:12
  117.4 2.7 copy-start.1
  121.3 18.8 %collective-permute-start = (bf16[2,64,128]{2,1,0:T(8,128)(2,1)S(1)}, bf16[2,64,128]{2,1,0:T(8,128)(2,1)S(1)}, u32[]{:S(2)}, u32[]{:S(2)}) collective-permute-start(bf16[2,64,128]{2,1,0:T(8,128)(2,1)S(1)} %get-tuple-element.122), channel_id=1, source_target_pairs={{0,15},{1,0},{2,1},{3,2},{4,3},{5,4},{6,5},{7,6},{8,7},{9,8},{10,9... | collective-permute-start | bytes 98312 | tf_op jit(solution)/shard_map/while/body/eval_jaxpr/ppermute | solution.py:12
  126.2 14.0 %collective-permute-start.1 = (bf16[2,64,128]{2,1,0:T(8,128)(2,1)S(1)}, bf16[2,64,128]{2,1,0:T(8,128)(2,1)S(1)}, u32[]{:S(2)}, u32[]{:S(2)}) collective-permute-start(bf16[2,64,128]{2,1,0:T(8,128)(2,1)S(1)} %get-tuple-element.123), channel_id=1, source_target_pairs={{0,1},{1,2},{2,3},{3,4},{4,5},{5,6},{6,7},{7,8},{8,9},{9,10},{10,1... | collective-permute-start | bytes 98312 | tf_op jit(solution)/shard_map/while/body/eval_jaxpr/ppermute | solution.py:12
  128.1 12.0 %collective-permute-start.2 = (bf16[2,64,128]{2,1,0:T(8,128)(2,1)S(1)}, bf16[2,64,128]{2,1,0:T(8,128)(2,1)S(1)}, u32[]{:S(2)}, u32[]{:S(2)}) collective-permute-start(bf16[2,64,128]{2,1,0:T(8,128)(2,1)S(1)} %get-tuple-element.124), channel_id=1, source_target_pairs={{0,496},{16,0},{32,16},{48,32},{64,48},{80,64},{96,80},{112,96},{1... | collective-permute-start | bytes 98312 | tf_op jit(solution)/shard_map/while/body/eval_jaxpr/ppermute | solution.py:12
  134.8 5.4 %collective-permute-start.3 = (bf16[2,64,128]{2,1,0:T(8,128)(2,1)S(1)}, bf16[2,64,128]{2,1,0:T(8,128)(2,1)S(1)}, u32[]{:S(2)}, u32[]{:S(2)}) collective-permute-start(bf16[2,64,128]{2,1,0:T(8,128)(2,1)S(1)} %get-tuple-element.125), channel_id=1, source_target_pairs={{0,16},{16,32},{32,48},{48,64},{64,80},{80,96},{96,112},{112,128},... | collective-permute-start | bytes 98312 | tf_op jit(solution)/shard_map/while/body/eval_jaxpr/ppermute | solution.py:12
  140.8 2.7 copy-start.1
  144.7 18.8 %collective-permute-start = (bf16[2,64,128]{2,1,0:T(8,128)(2,1)S(1)}, bf16[2,64,128]{2,1,0:T(8,128)(2,1)S(1)}, u32[]{:S(2)}, u32[]{:S(2)}) collective-permute-start(bf16[2,64,128]{2,1,0:T(8,128)(2,1)S(1)} %get-tuple-element.122), channel_id=1, source_target_pairs={{0,15},{1,0},{2,1},{3,2},{4,3},{5,4},{6,5},{7,6},{8,7},{9,8},{10,9... | collective-permute-start | bytes 98312 | tf_op jit(solution)/shard_map/while/body/eval_jaxpr/ppermute | solution.py:12
  149.6 14.0 %collective-permute-start.1 = (bf16[2,64,128]{2,1,0:T(8,128)(2,1)S(1)}, bf16[2,64,128]{2,1,0:T(8,128)(2,1)S(1)}, u32[]{:S(2)}, u32[]{:S(2)}) collective-permute-start(bf16[2,64,128]{2,1,0:T(8,128)(2,1)S(1)} %get-tuple-element.123), channel_id=1, source_target_pairs={{0,1},{1,2},{2,3},{3,4},{4,5},{5,6},{6,7},{7,8},{8,9},{9,10},{10,1... | collective-permute-start | bytes 98312 | tf_op jit(solution)/shard_map/while/body/eval_jaxpr/ppermute | solution.py:12
  151.5 12.0 %collective-permute-start.2 = (bf16[2,64,128]{2,1,0:T(8,128)(2,1)S(1)}, bf16[2,64,128]{2,1,0:T(8,128)(2,1)S(1)}, u32[]{:S(2)}, u32[]{:S(2)}) collective-permute-start(bf16[2,64,128]{2,1,0:T(8,128)(2,1)S(1)} %get-tuple-element.124), channel_id=1, source_target_pairs={{0,496},{16,0},{32,16},{48,32},{64,48},{80,64},{96,80},{112,96},{1... | collective-permute-start | bytes 98312 | tf_op jit(solution)/shard_map/while/body/eval_jaxpr/ppermute | solution.py:12
  158.2 5.4 %collective-permute-start.3 = (bf16[2,64,128]{2,1,0:T(8,128)(2,1)S(1)}, bf16[2,64,128]{2,1,0:T(8,128)(2,1)S(1)}, u32[]{:S(2)}, u32[]{:S(2)}) collective-permute-start(bf16[2,64,128]{2,1,0:T(8,128)(2,1)S(1)} %get-tuple-element.125), channel_id=1, source_target_pairs={{0,16},{16,32},{32,48},{48,64},{64,80},{80,96},{96,112},{112,128},... | collective-permute-start | bytes 98312 | tf_op jit(solution)/shard_map/while/body/eval_jaxpr/ppermute | solution.py:12
  168.2 18.8 %collective-permute-start = (bf16[2,64,128]{2,1,0:T(8,128)(2,1)S(1)}, bf16[2,64,128]{2,1,0:T(8,128)(2,1)S(1)}, u32[]{:S(2)}, u32[]{:S(2)}) collective-permute-start(bf16[2,64,128]{2,1,0:T(8,128)(2,1)S(1)} %get-tuple-element.122), channel_id=1, source_target_pairs={{0,15},{1,0},{2,1},{3,2},{4,3},{5,4},{6,5},{7,6},{8,7},{9,8},{10,9... | collective-permute-start | bytes 98312 | tf_op jit(solution)/shard_map/while/body/eval_jaxpr/ppermute | solution.py:12
  173.0 14.0 %collective-permute-start.1 = (bf16[2,64,128]{2,1,0:T(8,128)(2,1)S(1)}, bf16[2,64,128]{2,1,0:T(8,128)(2,1)S(1)}, u32[]{:S(2)}, u32[]{:S(2)}) collective-permute-start(bf16[2,64,128]{2,1,0:T(8,128)(2,1)S(1)} %get-tuple-element.123), channel_id=1, source_target_pairs={{0,1},{1,2},{2,3},{3,4},{4,5},{5,6},{6,7},{7,8},{8,9},{9,10},{10,1... | collective-permute-start | bytes 98312 | tf_op jit(solution)/shard_map/while/body/eval_jaxpr/ppermute | solution.py:12
  174.9 12.0 %collective-permute-start.2 = (bf16[2,64,128]{2,1,0:T(8,128)(2,1)S(1)}, bf16[2,64,128]{2,1,0:T(8,128)(2,1)S(1)}, u32[]{:S(2)}, u32[]{:S(2)}) collective-permute-start(bf16[2,64,128]{2,1,0:T(8,128)(2,1)S(1)} %get-tuple-element.124), channel_id=1, source_target_pairs={{0,496},{16,0},{32,16},{48,32},{64,48},{80,64},{96,80},{112,96},{1... | collective-permute-start | bytes 98312 | tf_op jit(solution)/shard_map/while/body/eval_jaxpr/ppermute | solution.py:12
  181.6 5.4 %collective-permute-start.3 = (bf16[2,64,128]{2,1,0:T(8,128)(2,1)S(1)}, bf16[2,64,128]{2,1,0:T(8,128)(2,1)S(1)}, u32[]{:S(2)}, u32[]{:S(2)}) collective-permute-start(bf16[2,64,128]{2,1,0:T(8,128)(2,1)S(1)} %get-tuple-element.125), channel_id=1, source_target_pairs={{0,16},{16,32},{32,48},{48,64},{64,80},{80,96},{96,112},{112,128},... | collective-permute-start | bytes 98312 | tf_op jit(solution)/shard_map/while/body/eval_jaxpr/ppermute | solution.py:12
  187.6 2.7 copy-start.1
  191.6 18.8 %collective-permute-start = (bf16[2,64,128]{2,1,0:T(8,128)(2,1)S(1)}, bf16[2,64,128]{2,1,0:T(8,128)(2,1)S(1)}, u32[]{:S(2)}, u32[]{:S(2)}) collective-permute-start(bf16[2,64,128]{2,1,0:T(8,128)(2,1)S(1)} %get-tuple-element.122), channel_id=1, source_target_pairs={{0,15},{1,0},{2,1},{3,2},{4,3},{5,4},{6,5},{7,6},{8,7},{9,8},{10,9... | collective-permute-start | bytes 98312 | tf_op jit(solution)/shard_map/while/body/eval_jaxpr/ppermute | solution.py:12
  196.4 14.0 %collective-permute-start.1 = (bf16[2,64,128]{2,1,0:T(8,128)(2,1)S(1)}, bf16[2,64,128]{2,1,0:T(8,128)(2,1)S(1)}, u32[]{:S(2)}, u32[]{:S(2)}) collective-permute-start(bf16[2,64,128]{2,1,0:T(8,128)(2,1)S(1)} %get-tuple-element.123), channel_id=1, source_target_pairs={{0,1},{1,2},{2,3},{3,4},{4,5},{5,6},{6,7},{7,8},{8,9},{9,10},{10,1... | collective-permute-start | bytes 98312 | tf_op jit(solution)/shard_map/while/body/eval_jaxpr/ppermute | solution.py:12
  198.3 12.0 %collective-permute-start.2 = (bf16[2,64,128]{2,1,0:T(8,128)(2,1)S(1)}, bf16[2,64,128]{2,1,0:T(8,128)(2,1)S(1)}, u32[]{:S(2)}, u32[]{:S(2)}) collective-permute-start(bf16[2,64,128]{2,1,0:T(8,128)(2,1)S(1)} %get-tuple-element.124), channel_id=1, source_target_pairs={{0,496},{16,0},{32,16},{48,32},{64,48},{80,64},{96,80},{112,96},{1... | collective-permute-start | bytes 98312 | tf_op jit(solution)/shard_map/while/body/eval_jaxpr/ppermute | solution.py:12
  205.0 5.4 %collective-permute-start.3 = (bf16[2,64,128]{2,1,0:T(8,128)(2,1)S(1)}, bf16[2,64,128]{2,1,0:T(8,128)(2,1)S(1)}, u32[]{:S(2)}, u32[]{:S(2)}) collective-permute-start(bf16[2,64,128]{2,1,0:T(8,128)(2,1)S(1)} %get-tuple-element.125), channel_id=1, source_target_pairs={{0,16},{16,32},{32,48},{48,64},{64,80},{80,96},{96,112},{112,128},... | collective-permute-start | bytes 98312 | tf_op jit(solution)/shard_map/while/body/eval_jaxpr/ppermute | solution.py:12
  319.6 99.8 %copy-start.5 = (f32[16,64,128]{2,1,0:T(8,128)}, f32[16,64,128]{2,1,0:T(8,128)S(1)}, u32[]{:S(2)}) copy-start(f32[16,64,128]{2,1,0:T(8,128)S(1)} %broadcast_multiply_fusion) | copy-start | bytes 1572868
  (11 other events, 17.6 us)
where the time goes:
time: 421 us; the launch traced here: 419 us
  blocking collectives  204 us (48%)
  starting transfers between devices  139 us (33%)
  matrix products  38.8 us (9%)
  local copies, waits for them, and re-layouts  32.5 us (8%)
    ppermute x36, starting transfers between devices, from_behind(): return lax.ppermute(value, axis, pairs)  139 us
    psum x1, blocking collectives, shards(): squares = lax.psum(jnp.sum(current * current, axis=(0, 2)), ('px', 'py'))  105 us
    psum x1, blocking collectives, shards(): gram_matrix = lax.psum(partial_gram, ('px', 'py')) / total_rows  98.6 us
    dot_general x9, matrix products, operator_apply(): jnp.einsum('rtkj,rtij->rki', gathered, local_tiles, preferred_element_typ...  22.3 us
    dot_general x9, matrix products, operator_apply(): jnp.einsum('rkj,rij->rki', received[halo_slot], halo_tiles, preferred_ele...  16 us
    while x48, local copies, waits for them, and re-layouts  9.86 us
  transfers between devices with their start and end apart: 36, of which 0 were waited for; matrix products, arithmetic and copies ran while one was open for 8% of the time, Pallas kernels for 0%

commit v1 on v0

--- a/solution.py
+++ b/solution.py
@@ -10,6 +10,16 @@
     count = lax.axis_size(axis)
     pairs = [(source, (source + steps) % count) for source in range(count)]
     return lax.ppermute(value, axis, pairs)
+
+
+def butterfly_sum(value, axis):
+    count = lax.axis_size(axis)
+    stride = 1
+    while stride < count:
+        pairs = [(source, source ^ stride) for source in range(count)]
+        value = value + lax.ppermute(value, axis, pairs)
+        stride *= 2
+    return value
 
 
 def operator_apply(current, local_tiles, local_cols, halo_tiles, halo_slot, boundary):
@@ -43,11 +53,12 @@
 
     previous, current = lax.fori_loop(0, DEG - 1, advance, (start_vecs, first_vecs))
     total_rows = current.shape[0] * current.shape[2] * lax.axis_size("px") * lax.axis_size("py")
-    squares = lax.psum(jnp.sum(current * current, axis=(0, 2)), ("px", "py"))
+    partial_gram = jnp.einsum("rkj,rlj->kl", current, current, precision=lax.Precision.HIGHEST)
+    raw_gram = butterfly_sum(butterfly_sum(partial_gram, "py"), "px")
+    squares = jnp.diagonal(raw_gram)
     scales = lax.rsqrt(squares / total_rows + 1e-06)
     filtered = current * scales[None, :, None]
-    partial_gram = jnp.einsum("rkj,rlj->kl", filtered, filtered, precision=lax.Precision.HIGHEST)
-    gram_matrix = lax.psum(partial_gram, ("px", "py")) / total_rows
+    gram_matrix = raw_gram * scales[:, None] * scales[None, :] / total_rows
     return (filtered, gram_matrix)
 
 

time: 421 us -> 288 us (0.68)
  blocking collectives: 204 us -> 0 us
  starting transfers between devices: 139 us -> 174 us
  waiting for transfers between devices: 0.09 us -> 31.8 us
    psum x2 -> x0, blocking collectives: 204 us -> none  [the longest x1 105 us: shards(): squares = lax.psum(jnp.sum(current * current, axis=(0, 2)), ('px', 'py'))]
    ppermute x0 -> x9, starting transfers between devices: none -> 34.5 us  [butterfly_sum(): value = value + lax.ppermute(value, axis, pairs)]
    ppermute x0 -> x9, waiting for transfers between devices: none -> 31.7 us  [butterfly_sum(): value = value + lax.ppermute(value, axis, pairs)]
  transfers between devices with their start and end apart: 36 -> 45, of which waited for: 0 -> 9; matrix products, arithmetic and copies ran while one was open for 8% -> 11% of each run, Pallas kernels for 0% -> 0%
where the time goes in v1:
time: 288 us; the launch traced here: 284 us
  starting transfers between devices  174 us (60%)
  matrix products  38.7 us (13%)
  local copies, waits for them, and re-layouts  33.3 us (12%)
  waiting for transfers between devices  31.8 us (11%)
  other arithmetic  3.23 us (1%)
    ppermute x36, starting transfers between devices, from_behind(): return lax.ppermute(value, axis, pairs)  140 us
    ppermute x9, starting transfers between devices, butterfly_sum(): value = value + lax.ppermute(value, axis, pairs)  34.5 us
    ppermute x9, waiting for transfers between devices, butterfly_sum(): value = value + lax.ppermute(value, axis, pairs)  31.7 us
    dot_general x9, matrix products, operator_apply(): jnp.einsum('rtkj,rtij->rki', gathered, local_tiles, preferred_element_typ...  22.2 us
    dot_general x9, matrix products, operator_apply(): jnp.einsum('rkj,rij->rki', received[halo_slot], halo_tiles, preferred_ele...  16 us
    while x48, local copies, waits for them, and re-layouts  9.86 us
    gather x9, local copies, waits for them, and re-layouts, operator_apply(): gathered = rounded[local_cols]  7.68 us
  transfers between devices with their start and end apart: 45, of which 9 were waited for; matrix products, arithmetic and copies ran while one was open for 11% of the time, Pallas kernels for 0%

profile of v1, /device:TPU:1, one launch (start us, length us, event | category | flops | bytes accessed | tf_op | source)
XLA Modules:
  0.0 283.9 jit_solution(10383501480777990588)
XLA Ops:
  3.4 4.5 %collective-permute-start.4 = (bf16[2,64,128]{2,1,0:T(8,128)(2,1)S(1)}, bf16[2,64,128]{2,1,0:T(8,128)(2,1)S(1)}, u32[]{:S(2)}, u32[]{:S(2)}) collective-permute-start(bf16[2,64,128]{2,1,0:T(8,128)(2,1)S(1)} %get-tuple-element.65), channel_id=1, source_target_pairs={{0,16},{16,32},{32,48},{48,64},{64,80},{80,96},{96,112},{112,128},... | collective-permute-start | bytes 98312 | tf_op jit(solution)/shard_map/ppermute | solution.py:12
  7.9 6.2 %collective-permute-start.5 = (bf16[2,64,128]{2,1,0:T(8,128)(2,1)S(1)}, bf16[2,64,128]{2,1,0:T(8,128)(2,1)S(1)}, u32[]{:S(2)}, u32[]{:S(2)}) collective-permute-start(bf16[2,64,128]{2,1,0:T(8,128)(2,1)S(1)} %get-tuple-element.67), channel_id=1, source_target_pairs={{0,496},{16,0},{32,16},{48,32},{64,48},{80,64},{96,80},{112,96},{1... | collective-permute-start | bytes 98312 | tf_op jit(solution)/shard_map/ppermute | solution.py:12
  14.1 1.9 collective-permute-start.6
  16.0 6.9 %collective-permute-start.7 = (bf16[2,64,128]{2,1,0:T(8,128)(2,1)S(1)}, bf16[2,64,128]{2,1,0:T(8,128)(2,1)S(1)}, u32[]{:S(2)}, u32[]{:S(2)}) collective-permute-start(bf16[2,64,128]{2,1,0:T(8,128)(2,1)S(1)} %get-tuple-element.68), channel_id=1, source_target_pairs={{0,15},{1,0},{2,1},{3,2},{4,3},{5,4},{6,5},{7,6},{8,7},{9,8},{10,9... | collective-permute-start | bytes 98312 | tf_op jit(solution)/shard_map/ppermute | solution.py:12
  24.8 2.9 %convolution_bitcast_fusion.1 = f32[16,64,128]{2,1,0:T(8,128)} fusion(bf16[16,4,64,128]{3,2,1,0:T(8,128)(2,1)} %bitcast.55, bf16[16,4,128,128]{3,2,1,0:T(8,128)(2,1)S(1)} %copy-done), kind=kOutput, calls=%fused_computation.19 | convolution fusion | flops 134217728 | bytes 3670016 | tf_op jit(solution)/shard_map/rtkj,rtij->rki/dot_general | solution.py:34
  30.0 184.5 %while.12 = (s32[]{:T(128)}, f32[16,64,128]{2,1,0:T(8,128)}, f32[16,64,128]{2,1,0:T(8,128)S(1)}, s32[16,4]{0,1:T(4,128)S(1)}, bf16[16,4,128,128]{3,2,1,0:T(8,128...) while((s32[]{:T(128)}, f32[16,64,128]{2,1,0:T(8,128)}, ...), condition=%wide.region_1.0_spmd, body=%wide.region_0.0_spmd.sunk | while | flops 168496400 | bytes 23345988 | solution.py:54
  30.8 3.4 %collective-permute-start = (bf16[2,64,128]{2,1,0:T(8,128)(2,1)S(1)}, bf16[2,64,128]{2,1,0:T(8,128)(2,1)S(1)}, u32[]{:S(2)}, u32[]{:S(2)}) collective-permute-start(bf16[2,64,128]{2,1,0:T(8,128)(2,1)S(1)} %get-tuple-element.122), channel_id=1, source_target_pairs={{0,15},{1,0},{2,1},{3,2},{4,3},{5,4},{6,5},{7,6},{8,7},{9,8},{10,9... | collective-permute-start | bytes 98312 | tf_op jit(solution)/shard_map/while/body/eval_jaxpr/ppermute | solution.py:12
  34.2 1.9 collective-permute-start.1
  36.1 6.7 %collective-permute-start.2 = (bf16[2,64,128]{2,1,0:T(8,128)(2,1)S(1)}, bf16[2,64,128]{2,1,0:T(8,128)(2,1)S(1)}, u32[]{:S(2)}, u32[]{:S(2)}) collective-permute-start(bf16[2,64,128]{2,1,0:T(8,128)(2,1)S(1)} %get-tuple-element.124), channel_id=1, source_target_pairs={{0,496},{16,0},{32,16},{48,32},{64,48},{80,64},{96,80},{112,96},{1... | collective-permute-start | bytes 98312 | tf_op jit(solution)/shard_map/while/body/eval_jaxpr/ppermute | solution.py:12
  45.7 2.4 convolution_bitcast_fusion.4
  52.8 4.9 %collective-permute-start = (bf16[2,64,128]{2,1,0:T(8,128)(2,1)S(1)}, bf16[2,64,128]{2,1,0:T(8,128)(2,1)S(1)}, u32[]{:S(2)}, u32[]{:S(2)}) collective-permute-start(bf16[2,64,128]{2,1,0:T(8,128)(2,1)S(1)} %get-tuple-element.122), channel_id=1, source_target_pairs={{0,15},{1,0},{2,1},{3,2},{4,3},{5,4},{6,5},{7,6},{8,7},{9,8},{10,9... | collective-permute-start | bytes 98312 | tf_op jit(solution)/shard_map/while/body/eval_jaxpr/ppermute | solution.py:12
  59.6 5.4 %collective-permute-start.2 = (bf16[2,64,128]{2,1,0:T(8,128)(2,1)S(1)}, bf16[2,64,128]{2,1,0:T(8,128)(2,1)S(1)}, u32[]{:S(2)}, u32[]{:S(2)}) collective-permute-start(bf16[2,64,128]{2,1,0:T(8,128)(2,1)S(1)} %get-tuple-element.124), channel_id=1, source_target_pairs={{0,496},{16,0},{32,16},{48,32},{64,48},{80,64},{96,80},{112,96},{1... | collective-permute-start | bytes 98312 | tf_op jit(solution)/shard_map/while/body/eval_jaxpr/ppermute | solution.py:12
  64.9 1.9 collective-permute-start.3
  67.8 2.4 convolution_bitcast_fusion.4
  74.9 4.9 %collective-permute-start = (bf16[2,64,128]{2,1,0:T(8,128)(2,1)S(1)}, bf16[2,64,128]{2,1,0:T(8,128)(2,1)S(1)}, u32[]{:S(2)}, u32[]{:S(2)}) collective-permute-start(bf16[2,64,128]{2,1,0:T(8,128)(2,1)S(1)} %get-tuple-element.122), channel_id=1, source_target_pairs={{0,15},{1,0},{2,1},{3,2},{4,3},{5,4},{6,5},{7,6},{8,7},{9,8},{10,9... | collective-permute-start | bytes 98312 | tf_op jit(solution)/shard_map/while/body/eval_jaxpr/ppermute | solution.py:12
  81.7 6.7 %collective-permute-start.2 = (bf16[2,64,128]{2,1,0:T(8,128)(2,1)S(1)}, bf16[2,64,128]{2,1,0:T(8,128)(2,1)S(1)}, u32[]{:S(2)}, u32[]{:S(2)}) collective-permute-start(bf16[2,64,128]{2,1,0:T(8,128)(2,1)S(1)} %get-tuple-element.124), channel_id=1, source_target_pairs={{0,496},{16,0},{32,16},{48,32},{64,48},{80,64},{96,80},{112,96},{1... | collective-permute-start | bytes 98312 | tf_op jit(solution)/shard_map/while/body/eval_jaxpr/ppermute | solution.py:12
  91.3 2.4 convolution_bitcast_fusion.4
  98.3 4.9 %collective-permute-start = (bf16[2,64,128]{2,1,0:T(8,128)(2,1)S(1)}, bf16[2,64,128]{2,1,0:T(8,128)(2,1)S(1)}, u32[]{:S(2)}, u32[]{:S(2)}) collective-permute-start(bf16[2,64,128]{2,1,0:T(8,128)(2,1)S(1)} %get-tuple-element.122), channel_id=1, source_target_pairs={{0,15},{1,0},{2,1},{3,2},{4,3},{5,4},{6,5},{7,6},{8,7},{9,8},{10,9... | collective-permute-start | bytes 98312 | tf_op jit(solution)/shard_map/while/body/eval_jaxpr/ppermute | solution.py:12
  105.1 6.7 %collective-permute-start.2 = (bf16[2,64,128]{2,1,0:T(8,128)(2,1)S(1)}, bf16[2,64,128]{2,1,0:T(8,128)(2,1)S(1)}, u32[]{:S(2)}, u32[]{:S(2)}) collective-permute-start(bf16[2,64,128]{2,1,0:T(8,128)(2,1)S(1)} %get-tuple-element.124), channel_id=1, source_target_pairs={{0,496},{16,0},{32,16},{48,32},{64,48},{80,64},{96,80},{112,96},{1... | collective-permute-start | bytes 98312 | tf_op jit(solution)/shard_map/while/body/eval_jaxpr/ppermute | solution.py:12
  114.7 2.4 convolution_bitcast_fusion.4
  121.7 4.9 %collective-permute-start = (bf16[2,64,128]{2,1,0:T(8,128)(2,1)S(1)}, bf16[2,64,128]{2,1,0:T(8,128)(2,1)S(1)}, u32[]{:S(2)}, u32[]{:S(2)}) collective-permute-start(bf16[2,64,128]{2,1,0:T(8,128)(2,1)S(1)} %get-tuple-element.122), channel_id=1, source_target_pairs={{0,15},{1,0},{2,1},{3,2},{4,3},{5,4},{6,5},{7,6},{8,7},{9,8},{10,9... | collective-permute-start | bytes 98312 | tf_op jit(solution)/shard_map/while/body/eval_jaxpr/ppermute | solution.py:12
  126.6 1.9 collective-permute-start.1
  128.5 6.7 %collective-permute-start.2 = (bf16[2,64,128]{2,1,0:T(8,128)(2,1)S(1)}, bf16[2,64,128]{2,1,0:T(8,128)(2,1)S(1)}, u32[]{:S(2)}, u32[]{:S(2)}) collective-permute-start(bf16[2,64,128]{2,1,0:T(8,128)(2,1)S(1)} %get-tuple-element.124), channel_id=1, source_target_pairs={{0,496},{16,0},{32,16},{48,32},{64,48},{80,64},{96,80},{112,96},{1... | collective-permute-start | bytes 98312 | tf_op jit(solution)/shard_map/while/body/eval_jaxpr/ppermute | solution.py:12
  135.2 1.9 collective-permute-start.3
  138.1 2.4 convolution_bitcast_fusion.4
  145.1 4.9 %collective-permute-start = (bf16[2,64,128]{2,1,0:T(8,128)(2,1)S(1)}, bf16[2,64,128]{2,1,0:T(8,128)(2,1)S(1)}, u32[]{:S(2)}, u32[]{:S(2)}) collective-permute-start(bf16[2,64,128]{2,1,0:T(8,128)(2,1)S(1)} %get-tuple-element.122), channel_id=1, source_target_pairs={{0,15},{1,0},{2,1},{3,2},{4,3},{5,4},{6,5},{7,6},{8,7},{9,8},{10,9... | collective-permute-start | bytes 98312 | tf_op jit(solution)/shard_map/while/body/eval_jaxpr/ppermute | solution.py:12
  151.9 6.7 %collective-permute-start.2 = (bf16[2,64,128]{2,1,0:T(8,128)(2,1)S(1)}, bf16[2,64,128]{2,1,0:T(8,128)(2,1)S(1)}, u32[]{:S(2)}, u32[]{:S(2)}) collective-permute-start(bf16[2,64,128]{2,1,0:T(8,128)(2,1)S(1)} %get-tuple-element.124), channel_id=1, source_target_pairs={{0,496},{16,0},{32,16},{48,32},{64,48},{80,64},{96,80},{112,96},{1... | collective-permute-start | bytes 98312 | tf_op jit(solution)/shard_map/while/body/eval_jaxpr/ppermute | solution.py:12
  161.5 2.4 convolution_bitcast_fusion.4
  168.5 4.9 %collective-permute-start = (bf16[2,64,128]{2,1,0:T(8,128)(2,1)S(1)}, bf16[2,64,128]{2,1,0:T(8,128)(2,1)S(1)}, u32[]{:S(2)}, u32[]{:S(2)}) collective-permute-start(bf16[2,64,128]{2,1,0:T(8,128)(2,1)S(1)} %get-tuple-element.122), channel_id=1, source_target_pairs={{0,15},{1,0},{2,1},{3,2},{4,3},{5,4},{6,5},{7,6},{8,7},{9,8},{10,9... | collective-permute-start | bytes 98312 | tf_op jit(solution)/shard_map/while/body/eval_jaxpr/ppermute | solution.py:12
  175.3 6.7 %collective-permute-start.2 = (bf16[2,64,128]{2,1,0:T(8,128)(2,1)S(1)}, bf16[2,64,128]{2,1,0:T(8,128)(2,1)S(1)}, u32[]{:S(2)}, u32[]{:S(2)}) collective-permute-start(bf16[2,64,128]{2,1,0:T(8,128)(2,1)S(1)} %get-tuple-element.124), channel_id=1, source_target_pairs={{0,496},{16,0},{32,16},{48,32},{64,48},{80,64},{96,80},{112,96},{1... | collective-permute-start | bytes 98312 | tf_op jit(solution)/shard_map/while/body/eval_jaxpr/ppermute | solution.py:12
  184.9 2.4 convolution_bitcast_fusion.4
  191.9 4.9 %collective-permute-start = (bf16[2,64,128]{2,1,0:T(8,128)(2,1)S(1)}, bf16[2,64,128]{2,1,0:T(8,128)(2,1)S(1)}, u32[]{:S(2)}, u32[]{:S(2)}) collective-permute-start(bf16[2,64,128]{2,1,0:T(8,128)(2,1)S(1)} %get-tuple-element.122), channel_id=1, source_target_pairs={{0,15},{1,0},{2,1},{3,2},{4,3},{5,4},{6,5},{7,6},{8,7},{9,8},{10,9... | collective-permute-start | bytes 98312 | tf_op jit(solution)/shard_map/while/body/eval_jaxpr/ppermute | solution.py:12
  196.8 1.9 collective-permute-start.1
  198.7 6.7 %collective-permute-start.2 = (bf16[2,64,128]{2,1,0:T(8,128)(2,1)S(1)}, bf16[2,64,128]{2,1,0:T(8,128)(2,1)S(1)}, u32[]{:S(2)}, u32[]{:S(2)}) collective-permute-start(bf16[2,64,128]{2,1,0:T(8,128)(2,1)S(1)} %get-tuple-element.124), channel_id=1, source_target_pairs={{0,496},{16,0},{32,16},{48,32},{64,48},{80,64},{96,80},{112,96},{1... | collective-permute-start | bytes 98312 | tf_op jit(solution)/shard_map/while/body/eval_jaxpr/ppermute | solution.py:12
  205.4 1.9 collective-permute-start.3
  208.3 2.4 convolution_bitcast_fusion.4
  215.1 1.9 collective-permute-start.8
  217.0 2.7 collective-permute-done.8
  221.6 3.7 %collective-permute-done.9 = f32[64,64]{1,0:T(8,128)S(1)} collective-permute-done((f32[64,64]{1,0:T(8,128)S(1)}, f32[64,64]{1,0:T(8,128)S(1)}, u32[]{:S(2)}, u32[]{:S(2)}) %collective-permute-start.9) | collective-permute-done | bytes 16416 | tf_op jit(solution)/shard_map/ppermute | solution.py:20
  225.4 4.6 %collective-permute-start.10 = (f32[64,64]{1,0:T(8,128)S(1)}, f32[64,64]{1,0:T(8,128)S(1)}, u32[]{:S(2)}, u32[]{:S(2)}) collective-permute-start(f32[64,64]{1,0:T(8,128)S(1)} %add.102), channel_id=1, source_target_pairs={{0,4},{1,5},{2,6},{3,7},{4,0},{5,1},{6,2},{7,3},{8,12},{9,13},{10,... | collective-permute-start | bytes 49160 | tf_op jit(solution)/shard_map/ppermute | solution.py:20
  229.9 4.2 %collective-permute-done.10 = f32[64,64]{1,0:T(8,128)S(1)} collective-permute-done((f32[64,64]{1,0:T(8,128)S(1)}, f32[64,64]{1,0:T(8,128)S(1)}, u32[]{:S(2)}, u32[]{:S(2)}) %collective-permute-start.10) | collective-permute-done | bytes 16416 | tf_op jit(solution)/shard_map/ppermute | solution.py:20
  234.2 7.0 %collective-permute-start.11 = (f32[64,64]{1,0:T(8,128)S(1)}, f32[64,64]{1,0:T(8,128)S(1)}, u32[]{:S(2)}, u32[]{:S(2)}) collective-permute-start(f32[64,64]{1,0:T(8,128)S(1)} %add.103), channel_id=1, source_target_pairs={{0,8},{1,9},{2,10},{3,11},{4,12},{5,13},{6,14},{7,15},{8,0},{9,1},... | collective-permute-start | bytes 49160 | tf_op jit(solution)/shard_map/ppermute | solution.py:20
  241.2 6.3 %collective-permute-done.11 = f32[64,64]{1,0:T(8,128)S(1)} collective-permute-done((f32[64,64]{1,0:T(8,128)S(1)}, f32[64,64]{1,0:T(8,128)S(1)}, u32[]{:S(2)}, u32[]{:S(2)}) %collective-permute-start.11) | collective-permute-done | bytes 16416 | tf_op jit(solution)/shard_map/ppermute | solution.py:20
  247.5 11.4 %collective-permute-start.12 = (f32[64,64]{1,0:T(8,128)S(1)}, f32[64,64]{1,0:T(8,128)S(1)}, u32[]{:S(2)}, u32[]{:S(2)}) collective-permute-start(f32[64,64]{1,0:T(8,128)S(1)} %add.104), channel_id=1, source_target_pairs={{0,16},{16,0},{32,48},{48,32},{64,80},{80,64},{96,112},{112,96},{1... | collective-permute-start | bytes 49160 | tf_op jit(solution)/shard_map/ppermute | solution.py:20
  261.8 2.7 collective-permute-done.13
  266.4 4.2 %collective-permute-done.14 = f32[64,64]{1,0:T(8,128)S(1)} collective-permute-done((f32[64,64]{1,0:T(8,128)S(1)}, f32[64,64]{1,0:T(8,128)S(1)}, u32[]{:S(2)}, u32[]{:S(2)}) %collective-permute-start.14) | collective-permute-done | bytes 16416 | tf_op jit(solution)/shard_map/ppermute | solution.py:20
  272.6 2.7 collective-permute-done.15
  277.2 4.2 %collective-permute-done.16 = f32[64,64]{1,0:T(8,128)S(1)} collective-permute-done((f32[64,64]{1,0:T(8,128)S(1)}, f32[64,64]{1,0:T(8,128)S(1)}, u32[]{:S(2)}, u32[]{:S(2)}) %collective-permute-start.16) | collective-permute-done | bytes 16416 | tf_op jit(solution)/shard_map/ppermute | solution.py:20
  (281 shorter events, 82.8 us)
Async XLA Ops:
  0.6 24.2 %copy-start = (bf16[16,4,128,128]{3,2,1,0:T(8,128)(2,1)S(1)}, bf16[16,4,128,128]{3,2,1,0:T(8,128)(2,1)}, u32[]{:S(2)}) copy-start(bf16[16,4,128,128]{3,2,1,0:T(8,128)(2,1)} %param.9) | copy-start | bytes 6291460
  0.6 22.3 %copy-start.5 = (s32[16,4]{0,1:T(4,128)S(1)}, s32[16,4]{0,1:T(4,128)}, u32[]{:S(2)}) copy-start(s32[16,4]{0,1:T(4,128)} %param.10) | copy-start | bytes 772
  1.9 25.9 %copy-start.2 = (f32[16,64,128]{2,1,0:T(8,128)}, f32[16,64,128]{2,1,0:T(8,128)S(1)}, u32[]{:S(2)}) copy-start(f32[16,64,128]{2,1,0:T(8,128)S(1)} %copy.33) | copy-start | bytes 1572868
  3.4 24.4 %collective-permute-start.4 = (bf16[2,64,128]{2,1,0:T(8,128)(2,1)S(1)}, bf16[2,64,128]{2,1,0:T(8,128)(2,1)S(1)}, u32[]{:S(2)}, u32[]{:S(2)}) collective-permute-start(bf16[2,64,128]{2,1,0:T(8,128)(2,1)S(1)} %get-tuple-element.65), channel_id=1, source_target_pairs={{0,16},{16,32},{32,48},{48,64},{64,80},{80,96},{96,112},{112,128},... | collective-permute-start | bytes 98312 | tf_op jit(solution)/shard_map/ppermute | solution.py:12
  7.9 19.9 %collective-permute-start.5 = (bf16[2,64,128]{2,1,0:T(8,128)(2,1)S(1)}, bf16[2,64,128]{2,1,0:T(8,128)(2,1)S(1)}, u32[]{:S(2)}, u32[]{:S(2)}) collective-permute-start(bf16[2,64,128]{2,1,0:T(8,128)(2,1)S(1)} %get-tuple-element.67), channel_id=1, source_target_pairs={{0,496},{16,0},{32,16},{48,32},{64,48},{80,64},{96,80},{112,96},{1... | collective-permute-start | bytes 98312 | tf_op jit(solution)/shard_map/ppermute | solution.py:12
  14.1 13.7 %collective-permute-start.6 = (bf16[2,64,128]{2,1,0:T(8,128)(2,1)S(1)}, bf16[2,64,128]{2,1,0:T(8,128)(2,1)S(1)}, u32[]{:S(2)}, u32[]{:S(2)}) collective-permute-start(bf16[2,64,128]{2,1,0:T(8,128)(2,1)S(1)} %get-tuple-element.66), channel_id=1, source_target_pairs={{0,1},{1,2},{2,3},{3,4},{4,5},{5,6},{6,7},{7,8},{8,9},{9,10},{10,1... | collective-permute-start | bytes 98312 | tf_op jit(solution)/shard_map/ppermute | solution.py:12
  16.0 11.8 %collective-permute-start.7 = (bf16[2,64,128]{2,1,0:T(8,128)(2,1)S(1)}, bf16[2,64,128]{2,1,0:T(8,128)(2,1)S(1)}, u32[]{:S(2)}, u32[]{:S(2)}) collective-permute-start(bf16[2,64,128]{2,1,0:T(8,128)(2,1)S(1)} %get-tuple-element.68), channel_id=1, source_target_pairs={{0,15},{1,0},{2,1},{3,2},{4,3},{5,4},{6,5},{7,6},{8,7},{9,8},{10,9... | collective-permute-start | bytes 98312 | tf_op jit(solution)/shard_map/ppermute | solution.py:12
  30.8 17.3 %collective-permute-start = (bf16[2,64,128]{2,1,0:T(8,128)(2,1)S(1)}, bf16[2,64,128]{2,1,0:T(8,128)(2,1)S(1)}, u32[]{:S(2)}, u32[]{:S(2)}) collective-permute-start(bf16[2,64,128]{2,1,0:T(8,128)(2,1)S(1)} %get-tuple-element.122), channel_id=1, source_target_pairs={{0,15},{1,0},{2,1},{3,2},{4,3},{5,4},{6,5},{7,6},{8,7},{9,8},{10,9... | collective-permute-start | bytes 98312 | tf_op jit(solution)/shard_map/while/body/eval_jaxpr/ppermute | solution.py:12
  34.2 14.0 %collective-permute-start.1 = (bf16[2,64,128]{2,1,0:T(8,128)(2,1)S(1)}, bf16[2,64,128]{2,1,0:T(8,128)(2,1)S(1)}, u32[]{:S(2)}, u32[]{:S(2)}) collective-permute-start(bf16[2,64,128]{2,1,0:T(8,128)(2,1)S(1)} %get-tuple-element.123), channel_id=1, source_target_pairs={{0,1},{1,2},{2,3},{3,4},{4,5},{5,6},{6,7},{7,8},{8,9},{9,10},{10,1... | collective-permute-start | bytes 98312 | tf_op jit(solution)/shard_map/while/body/eval_jaxpr/ppermute | solution.py:12
  36.1 12.1 %collective-permute-start.2 = (bf16[2,64,128]{2,1,0:T(8,128)(2,1)S(1)}, bf16[2,64,128]{2,1,0:T(8,128)(2,1)S(1)}, u32[]{:S(2)}, u32[]{:S(2)}) collective-permute-start(bf16[2,64,128]{2,1,0:T(8,128)(2,1)S(1)} %get-tuple-element.124), channel_id=1, source_target_pairs={{0,496},{16,0},{32,16},{48,32},{64,48},{80,64},{96,80},{112,96},{1... | collective-permute-start | bytes 98312 | tf_op jit(solution)/shard_map/while/body/eval_jaxpr/ppermute | solution.py:12
  42.8 5.4 %collective-permute-start.3 = (bf16[2,64,128]{2,1,0:T(8,128)(2,1)S(1)}, bf16[2,64,128]{2,1,0:T(8,128)(2,1)S(1)}, u32[]{:S(2)}, u32[]{:S(2)}) collective-permute-start(bf16[2,64,128]{2,1,0:T(8,128)(2,1)S(1)} %get-tuple-element.125), channel_id=1, source_target_pairs={{0,16},{16,32},{32,48},{48,64},{64,80},{80,96},{96,112},{112,128},... | collective-permute-start | bytes 98312 | tf_op jit(solution)/shard_map/while/body/eval_jaxpr/ppermute | solution.py:12
  52.8 17.5 %collective-permute-start = (bf16[2,64,128]{2,1,0:T(8,128)(2,1)S(1)}, bf16[2,64,128]{2,1,0:T(8,128)(2,1)S(1)}, u32[]{:S(2)}, u32[]{:S(2)}) collective-permute-start(bf16[2,64,128]{2,1,0:T(8,128)(2,1)S(1)} %get-tuple-element.122), channel_id=1, source_target_pairs={{0,15},{1,0},{2,1},{3,2},{4,3},{5,4},{6,5},{7,6},{8,7},{9,8},{10,9... | collective-permute-start | bytes 98312 | tf_op jit(solution)/shard_map/while/body/eval_jaxpr/ppermute | solution.py:12
  57.6 12.7 %collective-permute-start.1 = (bf16[2,64,128]{2,1,0:T(8,128)(2,1)S(1)}, bf16[2,64,128]{2,1,0:T(8,128)(2,1)S(1)}, u32[]{:S(2)}, u32[]{:S(2)}) collective-permute-start(bf16[2,64,128]{2,1,0:T(8,128)(2,1)S(1)} %get-tuple-element.123), channel_id=1, source_target_pairs={{0,1},{1,2},{2,3},{3,4},{4,5},{5,6},{6,7},{7,8},{8,9},{9,10},{10,1... | collective-permute-start | bytes 98312 | tf_op jit(solution)/shard_map/while/body/eval_jaxpr/ppermute | solution.py:12
  59.6 10.7 %collective-permute-start.2 = (bf16[2,64,128]{2,1,0:T(8,128)(2,1)S(1)}, bf16[2,64,128]{2,1,0:T(8,128)(2,1)S(1)}, u32[]{:S(2)}, u32[]{:S(2)}) collective-permute-start(bf16[2,64,128]{2,1,0:T(8,128)(2,1)S(1)} %get-tuple-element.124), channel_id=1, source_target_pairs={{0,496},{16,0},{32,16},{48,32},{64,48},{80,64},{96,80},{112,96},{1... | collective-permute-start | bytes 98312 | tf_op jit(solution)/shard_map/while/body/eval_jaxpr/ppermute | solution.py:12
  64.9 5.4 %collective-permute-start.3 = (bf16[2,64,128]{2,1,0:T(8,128)(2,1)S(1)}, bf16[2,64,128]{2,1,0:T(8,128)(2,1)S(1)}, u32[]{:S(2)}, u32[]{:S(2)}) collective-permute-start(bf16[2,64,128]{2,1,0:T(8,128)(2,1)S(1)} %get-tuple-element.125), channel_id=1, source_target_pairs={{0,16},{16,32},{32,48},{48,64},{64,80},{80,96},{96,112},{112,128},... | collective-permute-start | bytes 98312 | tf_op jit(solution)/shard_map/while/body/eval_jaxpr/ppermute | solution.py:12
  74.9 18.8 %collective-permute-start = (bf16[2,64,128]{2,1,0:T(8,128)(2,1)S(1)}, bf16[2,64,128]{2,1,0:T(8,128)(2,1)S(1)}, u32[]{:S(2)}, u32[]{:S(2)}) collective-permute-start(bf16[2,64,128]{2,1,0:T(8,128)(2,1)S(1)} %get-tuple-element.122), channel_id=1, source_target_pairs={{0,15},{1,0},{2,1},{3,2},{4,3},{5,4},{6,5},{7,6},{8,7},{9,8},{10,9... | collective-permute-start | bytes 98312 | tf_op jit(solution)/shard_map/while/body/eval_jaxpr/ppermute | solution.py:12
  79.7 14.0 %collective-permute-start.1 = (bf16[2,64,128]{2,1,0:T(8,128)(2,1)S(1)}, bf16[2,64,128]{2,1,0:T(8,128)(2,1)S(1)}, u32[]{:S(2)}, u32[]{:S(2)}) collective-permute-start(bf16[2,64,128]{2,1,0:T(8,128)(2,1)S(1)} %get-tuple-element.123), channel_id=1, source_target_pairs={{0,1},{1,2},{2,3},{3,4},{4,5},{5,6},{6,7},{7,8},{8,9},{9,10},{10,1... | collective-permute-start | bytes 98312 | tf_op jit(solution)/shard_map/while/body/eval_jaxpr/ppermute | solution.py:12
  81.7 12.0 %collective-permute-start.2 = (bf16[2,64,128]{2,1,0:T(8,128)(2,1)S(1)}, bf16[2,64,128]{2,1,0:T(8,128)(2,1)S(1)}, u32[]{:S(2)}, u32[]{:S(2)}) collective-permute-start(bf16[2,64,128]{2,1,0:T(8,128)(2,1)S(1)} %get-tuple-element.124), channel_id=1, source_target_pairs={{0,496},{16,0},{32,16},{48,32},{64,48},{80,64},{96,80},{112,96},{1... | collective-permute-start | bytes 98312 | tf_op jit(solution)/shard_map/while/body/eval_jaxpr/ppermute | solution.py:12
  88.4 5.4 %collective-permute-start.3 = (bf16[2,64,128]{2,1,0:T(8,128)(2,1)S(1)}, bf16[2,64,128]{2,1,0:T(8,128)(2,1)S(1)}, u32[]{:S(2)}, u32[]{:S(2)}) collective-permute-start(bf16[2,64,128]{2,1,0:T(8,128)(2,1)S(1)} %get-tuple-element.125), channel_id=1, source_target_pairs={{0,16},{16,32},{32,48},{48,64},{64,80},{80,96},{96,112},{112,128},... | collective-permute-start | bytes 98312 | tf_op jit(solution)/shard_map/while/body/eval_jaxpr/ppermute | solution.py:12
  98.3 18.8 %collective-permute-start = (bf16[2,64,128]{2,1,0:T(8,128)(2,1)S(1)}, bf16[2,64,128]{2,1,0:T(8,128)(2,1)S(1)}, u32[]{:S(2)}, u32[]{:S(2)}) collective-permute-start(bf16[2,64,128]{2,1,0:T(8,128)(2,1)S(1)} %get-tuple-element.122), channel_id=1, source_target_pairs={{0,15},{1,0},{2,1},{3,2},{4,3},{5,4},{6,5},{7,6},{8,7},{9,8},{10,9... | collective-permute-start | bytes 98312 | tf_op jit(solution)/shard_map/while/body/eval_jaxpr/ppermute | solution.py:12
  103.1 14.0 %collective-permute-start.1 = (bf16[2,64,128]{2,1,0:T(8,128)(2,1)S(1)}, bf16[2,64,128]{2,1,0:T(8,128)(2,1)S(1)}, u32[]{:S(2)}, u32[]{:S(2)}) collective-permute-start(bf16[2,64,128]{2,1,0:T(8,128)(2,1)S(1)} %get-tuple-element.123), channel_id=1, source_target_pairs={{0,1},{1,2},{2,3},{3,4},{4,5},{5,6},{6,7},{7,8},{8,9},{9,10},{10,1... | collective-permute-start | bytes 98312 | tf_op jit(solution)/shard_map/while/body/eval_jaxpr/ppermute | solution.py:12
  105.1 12.0 %collective-permute-start.2 = (bf16[2,64,128]{2,1,0:T(8,128)(2,1)S(1)}, bf16[2,64,128]{2,1,0:T(8,128)(2,1)S(1)}, u32[]{:S(2)}, u32[]{:S(2)}) collective-permute-start(bf16[2,64,128]{2,1,0:T(8,128)(2,1)S(1)} %get-tuple-element.124), channel_id=1, source_target_pairs={{0,496},{16,0},{32,16},{48,32},{64,48},{80,64},{96,80},{112,96},{1... | collective-permute-start | bytes 98312 | tf_op jit(solution)/shard_map/while/body/eval_jaxpr/ppermute | solution.py:12
  111.8 5.4 %collective-permute-start.3 = (bf16[2,64,128]{2,1,0:T(8,128)(2,1)S(1)}, bf16[2,64,128]{2,1,0:T(8,128)(2,1)S(1)}, u32[]{:S(2)}, u32[]{:S(2)}) collective-permute-start(bf16[2,64,128]{2,1,0:T(8,128)(2,1)S(1)} %get-tuple-element.125), channel_id=1, source_target_pairs={{0,16},{16,32},{32,48},{48,64},{64,80},{80,96},{96,112},{112,128},... | collective-permute-start | bytes 98312 | tf_op jit(solution)/shard_map/while/body/eval_jaxpr/ppermute | solution.py:12
  121.7 18.8 %collective-permute-start = (bf16[2,64,128]{2,1,0:T(8,128)(2,1)S(1)}, bf16[2,64,128]{2,1,0:T(8,128)(2,1)S(1)}, u32[]{:S(2)}, u32[]{:S(2)}) collective-permute-start(bf16[2,64,128]{2,1,0:T(8,128)(2,1)S(1)} %get-tuple-element.122), channel_id=1, source_target_pairs={{0,15},{1,0},{2,1},{3,2},{4,3},{5,4},{6,5},{7,6},{8,7},{9,8},{10,9... | collective-permute-start | bytes 98312 | tf_op jit(solution)/shard_map/while/body/eval_jaxpr/ppermute | solution.py:12
  126.6 14.0 %collective-permute-start.1 = (bf16[2,64,128]{2,1,0:T(8,128)(2,1)S(1)}, bf16[2,64,128]{2,1,0:T(8,128)(2,1)S(1)}, u32[]{:S(2)}, u32[]{:S(2)}) collective-permute-start(bf16[2,64,128]{2,1,0:T(8,128)(2,1)S(1)} %get-tuple-element.123), channel_id=1, source_target_pairs={{0,1},{1,2},{2,3},{3,4},{4,5},{5,6},{6,7},{7,8},{8,9},{9,10},{10,1... | collective-permute-start | bytes 98312 | tf_op jit(solution)/shard_map/while/body/eval_jaxpr/ppermute | solution.py:12
  128.5 12.0 %collective-permute-start.2 = (bf16[2,64,128]{2,1,0:T(8,128)(2,1)S(1)}, bf16[2,64,128]{2,1,0:T(8,128)(2,1)S(1)}, u32[]{:S(2)}, u32[]{:S(2)}) collective-permute-start(bf16[2,64,128]{2,1,0:T(8,128)(2,1)S(1)} %get-tuple-element.124), channel_id=1, source_target_pairs={{0,496},{16,0},{32,16},{48,32},{64,48},{80,64},{96,80},{112,96},{1... | collective-permute-start | bytes 98312 | tf_op jit(solution)/shard_map/while/body/eval_jaxpr/ppermute | solution.py:12
  135.2 5.4 %collective-permute-start.3 = (bf16[2,64,128]{2,1,0:T(8,128)(2,1)S(1)}, bf16[2,64,128]{2,1,0:T(8,128)(2,1)S(1)}, u32[]{:S(2)}, u32[]{:S(2)}) collective-permute-start(bf16[2,64,128]{2,1,0:T(8,128)(2,1)S(1)} %get-tuple-element.125), channel_id=1, source_target_pairs={{0,16},{16,32},{32,48},{48,64},{64,80},{80,96},{96,112},{112,128},... | collective-permute-start | bytes 98312 | tf_op jit(solution)/shard_map/while/body/eval_jaxpr/ppermute | solution.py:12
  145.1 18.8 %collective-permute-start = (bf16[2,64,128]{2,1,0:T(8,128)(2,1)S(1)}, bf16[2,64,128]{2,1,0:T(8,128)(2,1)S(1)}, u32[]{:S(2)}, u32[]{:S(2)}) collective-permute-start(bf16[2,64,128]{2,1,0:T(8,128)(2,1)S(1)} %get-tuple-element.122), channel_id=1, source_target_pairs={{0,15},{1,0},{2,1},{3,2},{4,3},{5,4},{6,5},{7,6},{8,7},{9,8},{10,9... | collective-permute-start | bytes 98312 | tf_op jit(solution)/shard_map/while/body/eval_jaxpr/ppermute | solution.py:12
  150.0 14.0 %collective-permute-start.1 = (bf16[2,64,128]{2,1,0:T(8,128)(2,1)S(1)}, bf16[2,64,128]{2,1,0:T(8,128)(2,1)S(1)}, u32[]{:S(2)}, u32[]{:S(2)}) collective-permute-start(bf16[2,64,128]{2,1,0:T(8,128)(2,1)S(1)} %get-tuple-element.123), channel_id=1, source_target_pairs={{0,1},{1,2},{2,3},{3,4},{4,5},{5,6},{6,7},{7,8},{8,9},{9,10},{10,1... | collective-permute-start | bytes 98312 | tf_op jit(solution)/shard_map/while/body/eval_jaxpr/ppermute | solution.py:12
  151.9 12.0 %collective-permute-start.2 = (bf16[2,64,128]{2,1,0:T(8,128)(2,1)S(1)}, bf16[2,64,128]{2,1,0:T(8,128)(2,1)S(1)}, u32[]{:S(2)}, u32[]{:S(2)}) collective-permute-start(bf16[2,64,128]{2,1,0:T(8,128)(2,1)S(1)} %get-tuple-element.124), channel_id=1, source_target_pairs={{0,496},{16,0},{32,16},{48,32},{64,48},{80,64},{96,80},{112,96},{1... | collective-permute-start | bytes 98312 | tf_op jit(solution)/shard_map/while/body/eval_jaxpr/ppermute | solution.py:12
  158.6 5.4 %collective-permute-start.3 = (bf16[2,64,128]{2,1,0:T(8,128)(2,1)S(1)}, bf16[2,64,128]{2,1,0:T(8,128)(2,1)S(1)}, u32[]{:S(2)}, u32[]{:S(2)}) collective-permute-start(bf16[2,64,128]{2,1,0:T(8,128)(2,1)S(1)} %get-tuple-element.125), channel_id=1, source_target_pairs={{0,16},{16,32},{32,48},{48,64},{64,80},{80,96},{96,112},{112,128},... | collective-permute-start | bytes 98312 | tf_op jit(solution)/shard_map/while/body/eval_jaxpr/ppermute | solution.py:12
  168.5 18.8 %collective-permute-start = (bf16[2,64,128]{2,1,0:T(8,128)(2,1)S(1)}, bf16[2,64,128]{2,1,0:T(8,128)(2,1)S(1)}, u32[]{:S(2)}, u32[]{:S(2)}) collective-permute-start(bf16[2,64,128]{2,1,0:T(8,128)(2,1)S(1)} %get-tuple-element.122), channel_id=1, source_target_pairs={{0,15},{1,0},{2,1},{3,2},{4,3},{5,4},{6,5},{7,6},{8,7},{9,8},{10,9... | collective-permute-start | bytes 98312 | tf_op jit(solution)/shard_map/while/body/eval_jaxpr/ppermute | solution.py:12
  173.4 14.0 %collective-permute-start.1 = (bf16[2,64,128]{2,1,0:T(8,128)(2,1)S(1)}, bf16[2,64,128]{2,1,0:T(8,128)(2,1)S(1)}, u32[]{:S(2)}, u32[]{:S(2)}) collective-permute-start(bf16[2,64,128]{2,1,0:T(8,128)(2,1)S(1)} %get-tuple-element.123), channel_id=1, source_target_pairs={{0,1},{1,2},{2,3},{3,4},{4,5},{5,6},{6,7},{7,8},{8,9},{9,10},{10,1... | collective-permute-start | bytes 98312 | tf_op jit(solution)/shard_map/while/body/eval_jaxpr/ppermute | solution.py:12
  175.3 12.0 %collective-permute-start.2 = (bf16[2,64,128]{2,1,0:T(8,128)(2,1)S(1)}, bf16[2,64,128]{2,1,0:T(8,128)(2,1)S(1)}, u32[]{:S(2)}, u32[]{:S(2)}) collective-permute-start(bf16[2,64,128]{2,1,0:T(8,128)(2,1)S(1)} %get-tuple-element.124), channel_id=1, source_target_pairs={{0,496},{16,0},{32,16},{48,32},{64,48},{80,64},{96,80},{112,96},{1... | collective-permute-start | bytes 98312 | tf_op jit(solution)/shard_map/while/body/eval_jaxpr/ppermute | solution.py:12
  182.0 5.4 %collective-permute-start.3 = (bf16[2,64,128]{2,1,0:T(8,128)(2,1)S(1)}, bf16[2,64,128]{2,1,0:T(8,128)(2,1)S(1)}, u32[]{:S(2)}, u32[]{:S(2)}) collective-permute-start(bf16[2,64,128]{2,1,0:T(8,128)(2,1)S(1)} %get-tuple-element.125), channel_id=1, source_target_pairs={{0,16},{16,32},{32,48},{48,64},{64,80},{80,96},{96,112},{112,128},... | collective-permute-start | bytes 98312 | tf_op jit(solution)/shard_map/while/body/eval_jaxpr/ppermute | solution.py:12
  191.9 18.8 %collective-permute-start = (bf16[2,64,128]{2,1,0:T(8,128)(2,1)S(1)}, bf16[2,64,128]{2,1,0:T(8,128)(2,1)S(1)}, u32[]{:S(2)}, u32[]{:S(2)}) collective-permute-start(bf16[2,64,128]{2,1,0:T(8,128)(2,1)S(1)} %get-tuple-element.122), channel_id=1, source_target_pairs={{0,15},{1,0},{2,1},{3,2},{4,3},{5,4},{6,5},{7,6},{8,7},{9,8},{10,9... | collective-permute-start | bytes 98312 | tf_op jit(solution)/shard_map/while/body/eval_jaxpr/ppermute | solution.py:12
  196.8 14.0 %collective-permute-start.1 = (bf16[2,64,128]{2,1,0:T(8,128)(2,1)S(1)}, bf16[2,64,128]{2,1,0:T(8,128)(2,1)S(1)}, u32[]{:S(2)}, u32[]{:S(2)}) collective-permute-start(bf16[2,64,128]{2,1,0:T(8,128)(2,1)S(1)} %get-tuple-element.123), channel_id=1, source_target_pairs={{0,1},{1,2},{2,3},{3,4},{4,5},{5,6},{6,7},{7,8},{8,9},{9,10},{10,1... | collective-permute-start | bytes 98312 | tf_op jit(solution)/shard_map/while/body/eval_jaxpr/ppermute | solution.py:12
  198.7 12.0 %collective-permute-start.2 = (bf16[2,64,128]{2,1,0:T(8,128)(2,1)S(1)}, bf16[2,64,128]{2,1,0:T(8,128)(2,1)S(1)}, u32[]{:S(2)}, u32[]{:S(2)}) collective-permute-start(bf16[2,64,128]{2,1,0:T(8,128)(2,1)S(1)} %get-tuple-element.124), channel_id=1, source_target_pairs={{0,496},{16,0},{32,16},{48,32},{64,48},{80,64},{96,80},{112,96},{1... | collective-permute-start | bytes 98312 | tf_op jit(solution)/shard_map/while/body/eval_jaxpr/ppermute | solution.py:12
  205.4 5.4 %collective-permute-start.3 = (bf16[2,64,128]{2,1,0:T(8,128)(2,1)S(1)}, bf16[2,64,128]{2,1,0:T(8,128)(2,1)S(1)}, u32[]{:S(2)}, u32[]{:S(2)}) collective-permute-start(bf16[2,64,128]{2,1,0:T(8,128)(2,1)S(1)} %get-tuple-element.125), channel_id=1, source_target_pairs={{0,16},{16,32},{32,48},{48,64},{64,80},{80,96},{96,112},{112,128},... | collective-permute-start | bytes 98312 | tf_op jit(solution)/shard_map/while/body/eval_jaxpr/ppermute | solution.py:12
  215.1 4.7 %collective-permute-start.8 = (f32[64,64]{1,0:T(8,128)S(1)}, f32[64,64]{1,0:T(8,128)S(1)}, u32[]{:S(2)}, u32[]{:S(2)}) collective-permute-start(f32[64,64]{1,0:T(8,128)S(1)} %convolution_bitcast_fusion.2), channel_id=1, source_target_pairs={{0,1},{1,0},{2,3},{3,2},{4,5},{5,4},{6,7},{7,6},{8,9},{9,8},{10,11... | collective-permute-start | bytes 49160 | tf_op jit(solution)/shard_map/ppermute | solution.py:20
  219.7 5.6 %collective-permute-start.9 = (f32[64,64]{1,0:T(8,128)S(1)}, f32[64,64]{1,0:T(8,128)S(1)}, u32[]{:S(2)}, u32[]{:S(2)}) collective-permute-start(f32[64,64]{1,0:T(8,128)S(1)} %add.101), channel_id=1, source_target_pairs={{0,2},{1,3},{2,0},{3,1},{4,6},{5,7},{6,4},{7,5},{8,10},{9,11},{10,... | collective-permute-start | bytes 49160 | tf_op jit(solution)/shard_map/ppermute | solution.py:20
  225.4 8.8 %collective-permute-start.10 = (f32[64,64]{1,0:T(8,128)S(1)}, f32[64,64]{1,0:T(8,128)S(1)}, u32[]{:S(2)}, u32[]{:S(2)}) collective-permute-start(f32[64,64]{1,0:T(8,128)S(1)} %add.102), channel_id=1, source_target_pairs={{0,4},{1,5},{2,6},{3,7},{4,0},{5,1},{6,2},{7,3},{8,12},{9,13},{10,... | collective-permute-start | bytes 49160 | tf_op jit(solution)/shard_map/ppermute | solution.py:20
  234.2 13.4 %collective-permute-start.11 = (f32[64,64]{1,0:T(8,128)S(1)}, f32[64,64]{1,0:T(8,128)S(1)}, u32[]{:S(2)}, u32[]{:S(2)}) collective-permute-start(f32[64,64]{1,0:T(8,128)S(1)} %add.103), channel_id=1, source_target_pairs={{0,8},{1,9},{2,10},{3,11},{4,12},{5,13},{6,14},{7,15},{8,0},{9,1},... | collective-permute-start | bytes 49160 | tf_op jit(solution)/shard_map/ppermute | solution.py:20
  247.5 12.3 %collective-permute-start.12 = (f32[64,64]{1,0:T(8,128)S(1)}, f32[64,64]{1,0:T(8,128)S(1)}, u32[]{:S(2)}, u32[]{:S(2)}) collective-permute-start(f32[64,64]{1,0:T(8,128)S(1)} %add.104), channel_id=1, source_target_pairs={{0,16},{16,0},{32,48},{48,32},{64,80},{80,64},{96,112},{112,96},{1... | collective-permute-start | bytes 49160 | tf_op jit(solution)/shard_map/ppermute | solution.py:20
  259.8 4.6 %collective-permute-start.13 = (f32[64,64]{1,0:T(8,128)S(1)}, f32[64,64]{1,0:T(8,128)S(1)}, u32[]{:S(2)}, u32[]{:S(2)}) collective-permute-start(f32[64,64]{1,0:T(8,128)S(1)} %add.105), channel_id=1, source_target_pairs={{0,32},{16,48},{32,0},{48,16},{64,96},{80,112},{96,64},{112,80},{1... | collective-permute-start | bytes 49160 | tf_op jit(solution)/shard_map/ppermute | solution.py:20
  264.5 6.2 %collective-permute-start.14 = (f32[64,64]{1,0:T(8,128)S(1)}, f32[64,64]{1,0:T(8,128)S(1)}, u32[]{:S(2)}, u32[]{:S(2)}) collective-permute-start(f32[64,64]{1,0:T(8,128)S(1)} %add.106), channel_id=1, source_target_pairs={{0,64},{16,80},{32,96},{48,112},{64,0},{80,16},{96,32},{112,48},{1... | collective-permute-start | bytes 49160 | tf_op jit(solution)/shard_map/ppermute | solution.py:20
  270.6 4.6 %collective-permute-start.15 = (f32[64,64]{1,0:T(8,128)S(1)}, f32[64,64]{1,0:T(8,128)S(1)}, u32[]{:S(2)}, u32[]{:S(2)}) collective-permute-start(f32[64,64]{1,0:T(8,128)S(1)} %add.107), channel_id=1, source_target_pairs={{0,128},{16,144},{32,160},{48,176},{64,192},{80,208},{96,224},{112... | collective-permute-start | bytes 49160 | tf_op jit(solution)/shard_map/ppermute | solution.py:20
  275.3 6.2 %collective-permute-start.16 = (f32[64,64]{1,0:T(8,128)S(1)}, f32[64,64]{1,0:T(8,128)S(1)}, u32[]{:S(2)}, u32[]{:S(2)}) collective-permute-start(f32[64,64]{1,0:T(8,128)S(1)} %add.108), channel_id=1, source_target_pairs={{0,256},{16,272},{32,288},{48,304},{64,320},{80,336},{96,352},{112... | collective-permute-start | bytes 49160 | tf_op jit(solution)/shard_map/ppermute | solution.py:20
  (19 other events, 59.6 us)

commit v2 on v1

--- a/solution.py
+++ b/solution.py
@@ -22,36 +22,49 @@
     return value
 
 
-def operator_apply(current, local_tiles, local_cols, halo_tiles, halo_slot, boundary):
-    rounded = current.astype(jnp.bfloat16)
-    outgoing = rounded[boundary]
-    from_xlow = from_behind(outgoing[0], "px", 1)
-    from_xhigh = from_behind(outgoing[1], "px", -1)
-    from_ylow = from_behind(outgoing[2], "py", 1)
-    from_yhigh = from_behind(outgoing[3], "py", -1)
-    received = jnp.concatenate([from_xlow, from_xhigh, from_ylow, from_yhigh], axis=0)
-    gathered = rounded[local_cols]
+def exchange(outgoing, per_list):
+    pieces = [outgoing[d * per_list:(d + 1) * per_list] for d in range(4)]
+    from_xlow = from_behind(pieces[0], "px", 1)
+    from_xhigh = from_behind(pieces[1], "px", -1)
+    from_ylow = from_behind(pieces[2], "py", 1)
+    from_yhigh = from_behind(pieces[3], "py", -1)
+    return jnp.concatenate([from_xlow, from_xhigh, from_ylow, from_yhigh], axis=0)
+
+
+def rows_apply(rounded, received, tiles, cols, halo, slot):
+    gathered = rounded[cols]
     product = jnp.einsum(
-        "rtkj,rtij->rki", gathered, local_tiles, preferred_element_type=jnp.float32
+        "rtkj,rtij->rki", gathered, tiles, preferred_element_type=jnp.float32
     )
     coupled = jnp.einsum(
-        "rkj,rij->rki", received[halo_slot], halo_tiles, preferred_element_type=jnp.float32
+        "rkj,rij->rki", received[slot], halo, preferred_element_type=jnp.float32
     )
     return product + coupled
 
 
 def shards(start_vecs, local_tiles, local_cols, halo_tiles, halo_slot, boundary):
+    per_list = boundary.shape[1]
+    picks = boundary.reshape(-1)
+    edge = (local_tiles[picks], local_cols[picks], halo_tiles[picks], halo_slot[picks])
+    whole = (local_tiles, local_cols, halo_tiles, halo_slot)
 
-    def step_apply(current):
-        return operator_apply(current, local_tiles, local_cols, halo_tiles, halo_slot, boundary)
+    older = start_vecs
+    rounded = start_vecs.astype(jnp.bfloat16)
+    received = exchange(rounded[picks], per_list)
+    edge_next = rows_apply(rounded, received, *edge)
+    received_next = exchange(edge_next.astype(jnp.bfloat16), per_list)
+    current = rows_apply(rounded, received, *whole)
+    received = received_next
+    for step in range(1, DEG):
+        rounded = current.astype(jnp.bfloat16)
+        if step < DEG - 1:
+            edge_next = 2.0 * rows_apply(rounded, received, *edge) - older[picks]
+            received_next = exchange(edge_next.astype(jnp.bfloat16), per_list)
+        newer = 2.0 * rows_apply(rounded, received, *whole) - older
+        older, current = current, newer
+        if step < DEG - 1:
+            received = received_next
 
-    first_vecs = step_apply(start_vecs)
-
-    def advance(step_index, state_pair):
-        older_vec, newer_vec = state_pair
-        return (newer_vec, 2.0 * step_apply(newer_vec) - older_vec)
-
-    previous, current = lax.fori_loop(0, DEG - 1, advance, (start_vecs, first_vecs))
     total_rows = current.shape[0] * current.shape[2] * lax.axis_size("px") * lax.axis_size("py")
     partial_gram = jnp.einsum("rkj,rlj->kl", current, current, precision=lax.Precision.HIGHEST)
     raw_gram = butterfly_sum(butterfly_sum(partial_gram, "py"), "px")

time: 288 us -> 409 us (1.42)
  local copies, waits for them, and re-layouts: 33.3 us -> 113 us
  matrix products: 38.7 us -> 69.2 us
  starting transfers between devices: 174 us -> 181 us
    gather x27 -> x47, local copies, waits for them, and re-layouts: 18.2 us -> 83.3 us  [the longest x17 39.9 us: rows_apply(): gathered = rounded[cols]]
    dot_general x18 -> x34, matrix products: 38.2 us -> 68.6 us  [the longest x17 35.4 us: rows_apply(): jnp.einsum('rtkj,rtij->rki', gathered, tiles, preferred_element_type=jnp....]
    unnamed x13 -> x60, local copies, waits for them, and re-layouts: 1.23 us -> 17.8 us
    while x48 -> x0, local copies, waits for them, and re-layouts: 9.86 us -> none
    ppermute x36, starting transfers between devices: 140 us -> 146 us  [from_behind(): return lax.ppermute(value, axis, pairs)]
    concatenate x0 -> x8, local copies, waits for them, and re-layouts: none -> 5.38 us  [exchange(): jnp.concatenate([from_xlow, from_xhigh, from_ylow, from_yhigh], axis=0)]
    slice x9, local copies, waits for them, and re-layouts: 0.1 us -> 5.07 us  [exchange(): pieces = [outgoing[d * per_list:(d + 1) * per_list] for d in range(4)]]
  transfers between devices with their start and end apart: 45 -> 45, of which waited for: 9 -> 9; matrix products, arithmetic and copies ran while one was open for 11% -> 20% of each run, Pallas kernels for 0% -> 0%
where the time goes in v2:
time: 409 us; the launch traced here: 402 us
  starting transfers between devices  181 us (44%)
  local copies, waits for them, and re-layouts  113 us (28%)
  matrix products  69.2 us (17%)
  waiting for transfers between devices  31.3 us (8%)
  other arithmetic  5.54 us (1%)
    ppermute x36, starting transfers between devices, from_behind(): return lax.ppermute(value, axis, pairs)  146 us
    gather x17, local copies, waits for them, and re-layouts, rows_apply(): gathered = rounded[cols]  39.9 us
    ppermute x9, starting transfers between devices, butterfly_sum(): value = value + lax.ppermute(value, axis, pairs)  35.6 us
    dot_general x17, matrix products, rows_apply(): jnp.einsum('rtkj,rtij->rki', gathered, tiles, preferred_element_type=jnp....  35.4 us
    dot_general x17, matrix products, rows_apply(): jnp.einsum('rkj,rij->rki', received[slot], halo, preferred_element_type=j...  33.2 us
    ppermute x9, waiting for transfers between devices, butterfly_sum(): value = value + lax.ppermute(value, axis, pairs)  31.2 us
    gather x17, local copies, waits for them, and re-layouts, rows_apply(): received[slot]  22.3 us
    unnamed x60, local copies, waits for them, and re-layouts  17.8 us
  transfers between devices with their start and end apart: 45, of which 9 were waited for; matrix products, arithmetic and copies ran while one was open for 20% of the time, Pallas kernels for 0%

profile of v2, /device:TPU:1, one launch (start us, length us, event | category | flops | bytes accessed | tf_op | source)
XLA Modules:
  0.0 401.6 jit_solution(2551259366924176893)
XLA Ops:
  4.0 4.5 %collective-permute-start = (bf16[2,64,128]{2,1,0:T(8,128)(2,1)S(1)}, bf16[2,64,128]{2,1,0:T(8,128)(2,1)}, u32[]{:S(2)}, u32[]{:S(2)}) collective-permute-start(bf16[2,64,128]{2,1,0:T(8,128)(2,1)S(1)} %get-tuple-element.37), channel_id=1, source_target_pairs={{0,16},{16,32},{32,48},{48,64},{64,80},{80,96},{96,112},{112,128},... | collective-permute-start | bytes 98312 | tf_op jit(solution)/shard_map/ppermute | solution.py:12
  8.5 6.2 %collective-permute-start.1 = (bf16[2,64,128]{2,1,0:T(8,128)(2,1)}, bf16[2,64,128]{2,1,0:T(8,128)(2,1)}, u32[]{:S(2)}, u32[]{:S(2)}) collective-permute-start(bf16[2,64,128]{2,1,0:T(8,128)(2,1)} %get-tuple-element.36), channel_id=1, source_target_pairs={{0,496},{16,0},{32,16},{48,32},{64,48},{80,64},{96,80},{112,96},{1... | collective-permute-start | bytes 98312 | tf_op jit(solution)/shard_map/ppermute | solution.py:12
  16.6 6.9 %collective-permute-start.3 = (bf16[2,64,128]{2,1,0:T(8,128)(2,1)}, bf16[2,64,128]{2,1,0:T(8,128)(2,1)}, u32[]{:S(2)}, u32[]{:S(2)}) collective-permute-start(bf16[2,64,128]{2,1,0:T(8,128)(2,1)} %get-tuple-element.34), channel_id=1, source_target_pairs={{0,15},{1,0},{2,1},{3,2},{4,3},{5,4},{6,5},{7,6},{8,7},{9,8},{10,9... | collective-permute-start | bytes 98312 | tf_op jit(solution)/shard_map/ppermute | solution.py:12
  32.3 2.9 convolution_bitcast_fusion.8
  55.6 3.9 collective-permute-start.4
  59.5 4.1 %collective-permute-start.5 = (bf16[2,64,128]{2,1,0:T(8,128)(2,1)}, bf16[2,64,128]{2,1,0:T(8,128)(2,1)}, u32[]{:S(2)}, u32[]{:S(2)}) collective-permute-start(bf16[2,64,128]{2,1,0:T(8,128)(2,1)} %get-tuple-element.32), channel_id=1, source_target_pairs={{0,496},{16,0},{32,16},{48,32},{64,48},{80,64},{96,80},{112,96},{1... | collective-permute-start | bytes 98312 | tf_op jit(solution)/shard_map/ppermute | solution.py:12
  65.6 4.6 %collective-permute-start.7 = (bf16[2,64,128]{2,1,0:T(8,128)(2,1)}, bf16[2,64,128]{2,1,0:T(8,128)(2,1)}, u32[]{:S(2)}, u32[]{:S(2)}) collective-permute-start(bf16[2,64,128]{2,1,0:T(8,128)(2,1)} %get-tuple-element.30), channel_id=1, source_target_pairs={{0,15},{1,0},{2,1},{3,2},{4,3},{5,4},{6,5},{7,6},{8,7},{9,8},{10,9... | collective-permute-start | bytes 98312 | tf_op jit(solution)/shard_map/ppermute | solution.py:12
  70.2 2.9 convolution_bitcast_fusion.7
  82.3 2.8 fusion.51
  94.0 7.5 %collective-permute-start.9 = (bf16[2,64,128]{2,1,0:T(8,128)(2,1)}, bf16[2,64,128]{2,1,0:T(8,128)(2,1)}, u32[]{:S(2)}, u32[]{:S(2)}) collective-permute-start(bf16[2,64,128]{2,1,0:T(8,128)(2,1)} %get-tuple-element.28), channel_id=1, source_target_pairs={{0,496},{16,0},{32,16},{48,32},{64,48},{80,64},{96,80},{112,96},{1... | collective-permute-start | bytes 98312 | tf_op jit(solution)/shard_map/ppermute | solution.py:12
  103.4 4.6 %collective-permute-start.11 = (bf16[2,64,128]{2,1,0:T(8,128)(2,1)}, bf16[2,64,128]{2,1,0:T(8,128)(2,1)}, u32[]{:S(2)}, u32[]{:S(2)}) collective-permute-start(bf16[2,64,128]{2,1,0:T(8,128)(2,1)} %get-tuple-element.26), channel_id=1, source_target_pairs={{0,15},{1,0},{2,1},{3,2},{4,3},{5,4},{6,5},{7,6},{8,7},{9,8},{10,9... | collective-permute-start | bytes 98312 | tf_op jit(solution)/shard_map/ppermute | solution.py:12
  108.0 2.9 convolution_bitcast_fusion.6
  120.0 2.8 fusion.52
  131.7 7.5 %collective-permute-start.13 = (bf16[2,64,128]{2,1,0:T(8,128)(2,1)}, bf16[2,64,128]{2,1,0:T(8,128)(2,1)}, u32[]{:S(2)}, u32[]{:S(2)}) collective-permute-start(bf16[2,64,128]{2,1,0:T(8,128)(2,1)} %get-tuple-element.24), channel_id=1, source_target_pairs={{0,496},{16,0},{32,16},{48,32},{64,48},{80,64},{96,80},{112,96},{1... | collective-permute-start | bytes 98312 | tf_op jit(solution)/shard_map/ppermute | solution.py:12
  141.1 4.6 %collective-permute-start.15 = (bf16[2,64,128]{2,1,0:T(8,128)(2,1)}, bf16[2,64,128]{2,1,0:T(8,128)(2,1)}, u32[]{:S(2)}, u32[]{:S(2)}) collective-permute-start(bf16[2,64,128]{2,1,0:T(8,128)(2,1)} %get-tuple-element.22), channel_id=1, source_target_pairs={{0,15},{1,0},{2,1},{3,2},{4,3},{5,4},{6,5},{7,6},{8,7},{9,8},{10,9... | collective-permute-start | bytes 98312 | tf_op jit(solution)/shard_map/ppermute | solution.py:12
  145.7 2.9 convolution_bitcast_fusion.5
  157.8 2.8 fusion.53
  163.0 2.6 gather_fusion.21
  169.6 7.5 %collective-permute-start.17 = (bf16[2,64,128]{2,1,0:T(8,128)(2,1)}, bf16[2,64,128]{2,1,0:T(8,128)(2,1)}, u32[]{:S(2)}, u32[]{:S(2)}) collective-permute-start(bf16[2,64,128]{2,1,0:T(8,128)(2,1)} %get-tuple-element.20), channel_id=1, source_target_pairs={{0,496},{16,0},{32,16},{48,32},{64,48},{80,64},{96,80},{112,96},{1... | collective-permute-start | bytes 98312 | tf_op jit(solution)/shard_map/ppermute | solution.py:12
  179.0 4.6 %collective-permute-start.19 = (bf16[2,64,128]{2,1,0:T(8,128)(2,1)}, bf16[2,64,128]{2,1,0:T(8,128)(2,1)}, u32[]{:S(2)}, u32[]{:S(2)}) collective-permute-start(bf16[2,64,128]{2,1,0:T(8,128)(2,1)} %get-tuple-element.18), channel_id=1, source_target_pairs={{0,15},{1,0},{2,1},{3,2},{4,3},{5,4},{6,5},{7,6},{8,7},{9,8},{10,9... | collective-permute-start | bytes 98312 | tf_op jit(solution)/shard_map/ppermute | solution.py:12
  183.6 2.9 convolution_bitcast_fusion.4
  195.7 2.8 fusion.54
  200.9 2.6 gather_fusion.26
  207.4 7.5 %collective-permute-start.21 = (bf16[2,64,128]{2,1,0:T(8,128)(2,1)}, bf16[2,64,128]{2,1,0:T(8,128)(2,1)}, u32[]{:S(2)}, u32[]{:S(2)}) collective-permute-start(bf16[2,64,128]{2,1,0:T(8,128)(2,1)} %get-tuple-element.16), channel_id=1, source_target_pairs={{0,496},{16,0},{32,16},{48,32},{64,48},{80,64},{96,80},{112,96},{1... | collective-permute-start | bytes 98312 | tf_op jit(solution)/shard_map/ppermute | solution.py:12
  216.8 4.6 %collective-permute-start.23 = (bf16[2,64,128]{2,1,0:T(8,128)(2,1)}, bf16[2,64,128]{2,1,0:T(8,128)(2,1)}, u32[]{:S(2)}, u32[]{:S(2)}) collective-permute-start(bf16[2,64,128]{2,1,0:T(8,128)(2,1)} %get-tuple-element.14), channel_id=1, source_target_pairs={{0,15},{1,0},{2,1},{3,2},{4,3},{5,4},{6,5},{7,6},{8,7},{9,8},{10,9... | collective-permute-start | bytes 98312 | tf_op jit(solution)/shard_map/ppermute | solution.py:12
  221.4 2.9 convolution_bitcast_fusion.3
  233.5 2.8 fusion.55
  245.2 7.5 %collective-permute-start.25 = (bf16[2,64,128]{2,1,0:T(8,128)(2,1)}, bf16[2,64,128]{2,1,0:T(8,128)(2,1)}, u32[]{:S(2)}, u32[]{:S(2)}) collective-permute-start(bf16[2,64,128]{2,1,0:T(8,128)(2,1)} %get-tuple-element.12), channel_id=1, source_target_pairs={{0,496},{16,0},{32,16},{48,32},{64,48},{80,64},{96,80},{112,96},{1... | collective-permute-start | bytes 98312 | tf_op jit(solution)/shard_map/ppermute | solution.py:12
  254.7 4.8 %collective-permute-start.27 = (bf16[2,64,128]{2,1,0:T(8,128)(2,1)}, bf16[2,64,128]{2,1,0:T(8,128)(2,1)}, u32[]{:S(2)}, u32[]{:S(2)}) collective-permute-start(bf16[2,64,128]{2,1,0:T(8,128)(2,1)} %get-tuple-element.10), channel_id=1, source_target_pairs={{0,15},{1,0},{2,1},{3,2},{4,3},{5,4},{6,5},{7,6},{8,7},{9,8},{10,9... | collective-permute-start | bytes 98312 | tf_op jit(solution)/shard_map/ppermute | solution.py:12
  259.5 2.9 convolution_bitcast_fusion.2
  271.5 2.8 fusion.56
  282.7 7.5 %collective-permute-start.29 = (bf16[2,64,128]{2,1,0:T(8,128)(2,1)S(1)}, bf16[2,64,128]{2,1,0:T(8,128)(2,1)S(1)}, u32[]{:S(2)}, u32[]{:S(2)}) collective-permute-start(bf16[2,64,128]{2,1,0:T(8,128)(2,1)S(1)} %get-tuple-element.8), channel_id=1, source_target_pairs={{0,496},{16,0},{32,16},{48,32},{64,48},{80,64},{96,80},{112,96},{1... | collective-permute-start | bytes 98312 | tf_op jit(solution)/shard_map/ppermute | solution.py:12
  292.2 4.6 %collective-permute-start.31 = (bf16[2,64,128]{2,1,0:T(8,128)(2,1)S(1)}, bf16[2,64,128]{2,1,0:T(8,128)(2,1)S(1)}, u32[]{:S(2)}, u32[]{:S(2)}) collective-permute-start(bf16[2,64,128]{2,1,0:T(8,128)(2,1)S(1)} %get-tuple-element.6), channel_id=1, source_target_pairs={{0,15},{1,0},{2,1},{3,2},{4,3},{5,4},{6,5},{7,6},{8,7},{9,8},{10,9... | collective-permute-start | bytes 98312 | tf_op jit(solution)/shard_map/ppermute | solution.py:12
  296.8 2.9 convolution_bitcast_fusion.1
  307.6 7.5 %collective-permute-start.33 = (bf16[2,64,128]{2,1,0:T(8,128)(2,1)}, bf16[2,64,128]{2,1,0:T(8,128)(2,1)S(1)}, u32[]{:S(2)}, u32[]{:S(2)}) collective-permute-start(bf16[2,64,128]{2,1,0:T(8,128)(2,1)} %get-tuple-element.5), channel_id=1, source_target_pairs={{0,496},{16,0},{32,16},{48,32},{64,48},{80,64},{96,80},{112,96},{1... | collective-permute-start | bytes 98312 | tf_op jit(solution)/shard_map/ppermute | solution.py:12
  317.1 4.6 %collective-permute-start.35 = (bf16[2,64,128]{2,1,0:T(8,128)(2,1)S(1)}, bf16[2,64,128]{2,1,0:T(8,128)(2,1)}, u32[]{:S(2)}, u32[]{:S(2)}) collective-permute-start(bf16[2,64,128]{2,1,0:T(8,128)(2,1)S(1)} %get-tuple-element.3), channel_id=1, source_target_pairs={{0,15},{1,0},{2,1},{3,2},{4,3},{5,4},{6,5},{7,6},{8,7},{9,8},{10,9... | collective-permute-start | bytes 98312 | tf_op jit(solution)/shard_map/ppermute | solution.py:12
  324.9 2.9 convolution_bitcast_fusion
  334.2 2.7 collective-permute-done.36
  338.8 3.7 collective-permute-done.37
  342.5 3.5 collective-permute-start.38
  346.0 5.7 %collective-permute-done.38 = f32[64,64]{1,0:T(8,128)S(1)} collective-permute-done((f32[64,64]{1,0:T(8,128)S(1)}, f32[64,64]{1,0:T(8,128)S(1)}, u32[]{:S(2)}, u32[]{:S(2)}) %collective-permute-start.38) | collective-permute-done | bytes 16416 | tf_op jit(solution)/shard_map/ppermute | solution.py:20
  351.7 9.0 %collective-permute-start.39 = (f32[64,64]{1,0:T(8,128)S(1)}, f32[64,64]{1,0:T(8,128)S(1)}, u32[]{:S(2)}, u32[]{:S(2)}) collective-permute-start(f32[64,64]{1,0:T(8,128)S(1)} %add.201), channel_id=1, source_target_pairs={{0,8},{1,9},{2,10},{3,11},{4,12},{5,13},{6,14},{7,15},{8,0},{9,1},... | collective-permute-start | bytes 49160 | tf_op jit(solution)/shard_map/ppermute | solution.py:20
  360.7 4.3 %collective-permute-done.39 = f32[64,64]{1,0:T(8,128)S(1)} collective-permute-done((f32[64,64]{1,0:T(8,128)S(1)}, f32[64,64]{1,0:T(8,128)S(1)}, u32[]{:S(2)}, u32[]{:S(2)}) %collective-permute-start.39) | collective-permute-done | bytes 16416 | tf_op jit(solution)/shard_map/ppermute | solution.py:20
  365.1 11.6 %collective-permute-start.40 = (f32[64,64]{1,0:T(8,128)S(1)}, f32[64,64]{1,0:T(8,128)S(1)}, u32[]{:S(2)}, u32[]{:S(2)}) collective-permute-start(f32[64,64]{1,0:T(8,128)S(1)} %add.202), channel_id=1, source_target_pairs={{0,16},{16,0},{32,48},{48,32},{64,80},{80,64},{96,112},{112,96},{1... | collective-permute-start | bytes 49160 | tf_op jit(solution)/shard_map/ppermute | solution.py:20
  379.5 2.7 collective-permute-done.41
  384.1 4.2 %collective-permute-done.42 = f32[64,64]{1,0:T(8,128)S(1)} collective-permute-done((f32[64,64]{1,0:T(8,128)S(1)}, f32[64,64]{1,0:T(8,128)S(1)}, u32[]{:S(2)}, u32[]{:S(2)}) %collective-permute-start.42) | collective-permute-done | bytes 16416 | tf_op jit(solution)/shard_map/ppermute | solution.py:20
  390.3 2.7 collective-permute-done.43
  394.9 4.2 %collective-permute-done.44 = f32[64,64]{1,0:T(8,128)S(1)} collective-permute-done((f32[64,64]{1,0:T(8,128)S(1)}, f32[64,64]{1,0:T(8,128)S(1)}, u32[]{:S(2)}, u32[]{:S(2)}) %collective-permute-start.44) | collective-permute-done | bytes 16416 | tf_op jit(solution)/shard_map/ppermute | solution.py:20
  (231 shorter events, 182.9 us)
Async XLA Ops:
  0.6 29.3 %copy-start = (bf16[16,4,128,128]{3,2,1,0:T(8,128)(2,1)S(1)}, bf16[16,4,128,128]{3,2,1,0:T(8,128)(2,1)}, u32[]{:S(2)}) copy-start(bf16[16,4,128,128]{3,2,1,0:T(8,128)(2,1)} %param.7) | copy-start | bytes 6291460
  4.0 36.4 %collective-permute-start = (bf16[2,64,128]{2,1,0:T(8,128)(2,1)S(1)}, bf16[2,64,128]{2,1,0:T(8,128)(2,1)}, u32[]{:S(2)}, u32[]{:S(2)}) collective-permute-start(bf16[2,64,128]{2,1,0:T(8,128)(2,1)S(1)} %get-tuple-element.37), channel_id=1, source_target_pairs={{0,16},{16,32},{32,48},{48,64},{64,80},{80,96},{96,112},{112,128},... | collective-permute-start | bytes 98312 | tf_op jit(solution)/shard_map/ppermute | solution.py:12
  8.5 32.7 %collective-permute-start.1 = (bf16[2,64,128]{2,1,0:T(8,128)(2,1)}, bf16[2,64,128]{2,1,0:T(8,128)(2,1)}, u32[]{:S(2)}, u32[]{:S(2)}) collective-permute-start(bf16[2,64,128]{2,1,0:T(8,128)(2,1)} %get-tuple-element.36), channel_id=1, source_target_pairs={{0,496},{16,0},{32,16},{48,32},{64,48},{80,64},{96,80},{112,96},{1... | collective-permute-start | bytes 98312 | tf_op jit(solution)/shard_map/ppermute | solution.py:12
  14.6 27.3 %collective-permute-start.2 = (bf16[2,64,128]{2,1,0:T(8,128)(2,1)}, bf16[2,64,128]{2,1,0:T(8,128)(2,1)}, u32[]{:S(2)}, u32[]{:S(2)}) collective-permute-start(bf16[2,64,128]{2,1,0:T(8,128)(2,1)} %get-tuple-element.35), channel_id=1, source_target_pairs={{0,1},{1,2},{2,3},{3,4},{4,5},{5,6},{6,7},{7,8},{8,9},{9,10},{10,1... | collective-permute-start | bytes 98312 | tf_op jit(solution)/shard_map/ppermute | solution.py:12
  16.6 26.1 %collective-permute-start.3 = (bf16[2,64,128]{2,1,0:T(8,128)(2,1)}, bf16[2,64,128]{2,1,0:T(8,128)(2,1)}, u32[]{:S(2)}, u32[]{:S(2)}) collective-permute-start(bf16[2,64,128]{2,1,0:T(8,128)(2,1)} %get-tuple-element.34), channel_id=1, source_target_pairs={{0,15},{1,0},{2,1},{3,2},{4,3},{5,4},{6,5},{7,6},{8,7},{9,8},{10,9... | collective-permute-start | bytes 98312 | tf_op jit(solution)/shard_map/ppermute | solution.py:12
  55.6 21.0 %collective-permute-start.4 = (bf16[2,64,128]{2,1,0:T(8,128)(2,1)S(1)}, bf16[2,64,128]{2,1,0:T(8,128)(2,1)}, u32[]{:S(2)}, u32[]{:S(2)}) collective-permute-start(bf16[2,64,128]{2,1,0:T(8,128)(2,1)S(1)} %get-tuple-element.33), channel_id=1, source_target_pairs={{0,16},{16,32},{32,48},{48,64},{64,80},{80,96},{96,112},{112,128},... | collective-permute-start | bytes 98312 | tf_op jit(solution)/shard_map/ppermute | solution.py:12
  59.5 17.8 %collective-permute-start.5 = (bf16[2,64,128]{2,1,0:T(8,128)(2,1)}, bf16[2,64,128]{2,1,0:T(8,128)(2,1)}, u32[]{:S(2)}, u32[]{:S(2)}) collective-permute-start(bf16[2,64,128]{2,1,0:T(8,128)(2,1)} %get-tuple-element.32), channel_id=1, source_target_pairs={{0,496},{16,0},{32,16},{48,32},{64,48},{80,64},{96,80},{112,96},{1... | collective-permute-start | bytes 98312 | tf_op jit(solution)/shard_map/ppermute | solution.py:12
  63.7 14.4 %collective-permute-start.6 = (bf16[2,64,128]{2,1,0:T(8,128)(2,1)}, bf16[2,64,128]{2,1,0:T(8,128)(2,1)}, u32[]{:S(2)}, u32[]{:S(2)}) collective-permute-start(bf16[2,64,128]{2,1,0:T(8,128)(2,1)} %get-tuple-element.31), channel_id=1, source_target_pairs={{0,1},{1,2},{2,3},{3,4},{4,5},{5,6},{6,7},{7,8},{8,9},{9,10},{10,1... | collective-permute-start | bytes 98312 | tf_op jit(solution)/shard_map/ppermute | solution.py:12
  65.6 13.3 %collective-permute-start.7 = (bf16[2,64,128]{2,1,0:T(8,128)(2,1)}, bf16[2,64,128]{2,1,0:T(8,128)(2,1)}, u32[]{:S(2)}, u32[]{:S(2)}) collective-permute-start(bf16[2,64,128]{2,1,0:T(8,128)(2,1)} %get-tuple-element.30), channel_id=1, source_target_pairs={{0,15},{1,0},{2,1},{3,2},{4,3},{5,4},{6,5},{7,6},{8,7},{9,8},{10,9... | collective-permute-start | bytes 98312 | tf_op jit(solution)/shard_map/ppermute | solution.py:12
  92.0 22.3 %collective-permute-start.8 = (bf16[2,64,128]{2,1,0:T(8,128)(2,1)S(1)}, bf16[2,64,128]{2,1,0:T(8,128)(2,1)}, u32[]{:S(2)}, u32[]{:S(2)}) collective-permute-start(bf16[2,64,128]{2,1,0:T(8,128)(2,1)S(1)} %get-tuple-element.29), channel_id=1, source_target_pairs={{0,16},{16,32},{32,48},{48,64},{64,80},{80,96},{96,112},{112,128},... | collective-permute-start | bytes 98312 | tf_op jit(solution)/shard_map/ppermute | solution.py:12
  94.0 21.1 %collective-permute-start.9 = (bf16[2,64,128]{2,1,0:T(8,128)(2,1)}, bf16[2,64,128]{2,1,0:T(8,128)(2,1)}, u32[]{:S(2)}, u32[]{:S(2)}) collective-permute-start(bf16[2,64,128]{2,1,0:T(8,128)(2,1)} %get-tuple-element.28), channel_id=1, source_target_pairs={{0,496},{16,0},{32,16},{48,32},{64,48},{80,64},{96,80},{112,96},{1... | collective-permute-start | bytes 98312 | tf_op jit(solution)/shard_map/ppermute | solution.py:12
  101.5 14.4 %collective-permute-start.10 = (bf16[2,64,128]{2,1,0:T(8,128)(2,1)}, bf16[2,64,128]{2,1,0:T(8,128)(2,1)}, u32[]{:S(2)}, u32[]{:S(2)}) collective-permute-start(bf16[2,64,128]{2,1,0:T(8,128)(2,1)} %get-tuple-element.27), channel_id=1, source_target_pairs={{0,1},{1,2},{2,3},{3,4},{4,5},{5,6},{6,7},{7,8},{8,9},{9,10},{10,1... | collective-permute-start | bytes 98312 | tf_op jit(solution)/shard_map/ppermute | solution.py:12
  103.4 13.2 %collective-permute-start.11 = (bf16[2,64,128]{2,1,0:T(8,128)(2,1)}, bf16[2,64,128]{2,1,0:T(8,128)(2,1)}, u32[]{:S(2)}, u32[]{:S(2)}) collective-permute-start(bf16[2,64,128]{2,1,0:T(8,128)(2,1)} %get-tuple-element.26), channel_id=1, source_target_pairs={{0,15},{1,0},{2,1},{3,2},{4,3},{5,4},{6,5},{7,6},{8,7},{9,8},{10,9... | collective-permute-start | bytes 98312 | tf_op jit(solution)/shard_map/ppermute | solution.py:12
  129.8 22.3 %collective-permute-start.12 = (bf16[2,64,128]{2,1,0:T(8,128)(2,1)S(1)}, bf16[2,64,128]{2,1,0:T(8,128)(2,1)}, u32[]{:S(2)}, u32[]{:S(2)}) collective-permute-start(bf16[2,64,128]{2,1,0:T(8,128)(2,1)S(1)} %get-tuple-element.25), channel_id=1, source_target_pairs={{0,16},{16,32},{32,48},{48,64},{64,80},{80,96},{96,112},{112,128},... | collective-permute-start | bytes 98312 | tf_op jit(solution)/shard_map/ppermute | solution.py:12
  131.7 21.2 %collective-permute-start.13 = (bf16[2,64,128]{2,1,0:T(8,128)(2,1)}, bf16[2,64,128]{2,1,0:T(8,128)(2,1)}, u32[]{:S(2)}, u32[]{:S(2)}) collective-permute-start(bf16[2,64,128]{2,1,0:T(8,128)(2,1)} %get-tuple-element.24), channel_id=1, source_target_pairs={{0,496},{16,0},{32,16},{48,32},{64,48},{80,64},{96,80},{112,96},{1... | collective-permute-start | bytes 98312 | tf_op jit(solution)/shard_map/ppermute | solution.py:12
  139.2 14.4 %collective-permute-start.14 = (bf16[2,64,128]{2,1,0:T(8,128)(2,1)}, bf16[2,64,128]{2,1,0:T(8,128)(2,1)}, u32[]{:S(2)}, u32[]{:S(2)}) collective-permute-start(bf16[2,64,128]{2,1,0:T(8,128)(2,1)} %get-tuple-element.23), channel_id=1, source_target_pairs={{0,1},{1,2},{2,3},{3,4},{4,5},{5,6},{6,7},{7,8},{8,9},{9,10},{10,1... | collective-permute-start | bytes 98312 | tf_op jit(solution)/shard_map/ppermute | solution.py:12
  141.1 13.3 %collective-permute-start.15 = (bf16[2,64,128]{2,1,0:T(8,128)(2,1)}, bf16[2,64,128]{2,1,0:T(8,128)(2,1)}, u32[]{:S(2)}, u32[]{:S(2)}) collective-permute-start(bf16[2,64,128]{2,1,0:T(8,128)(2,1)} %get-tuple-element.22), channel_id=1, source_target_pairs={{0,15},{1,0},{2,1},{3,2},{4,3},{5,4},{6,5},{7,6},{8,7},{9,8},{10,9... | collective-permute-start | bytes 98312 | tf_op jit(solution)/shard_map/ppermute | solution.py:12
  167.6 22.3 %collective-permute-start.16 = (bf16[2,64,128]{2,1,0:T(8,128)(2,1)S(1)}, bf16[2,64,128]{2,1,0:T(8,128)(2,1)}, u32[]{:S(2)}, u32[]{:S(2)}) collective-permute-start(bf16[2,64,128]{2,1,0:T(8,128)(2,1)S(1)} %get-tuple-element.21), channel_id=1, source_target_pairs={{0,16},{16,32},{32,48},{48,64},{64,80},{80,96},{96,112},{112,128},... | collective-permute-start | bytes 98312 | tf_op jit(solution)/shard_map/ppermute | solution.py:12
  169.6 21.2 %collective-permute-start.17 = (bf16[2,64,128]{2,1,0:T(8,128)(2,1)}, bf16[2,64,128]{2,1,0:T(8,128)(2,1)}, u32[]{:S(2)}, u32[]{:S(2)}) collective-permute-start(bf16[2,64,128]{2,1,0:T(8,128)(2,1)} %get-tuple-element.20), channel_id=1, source_target_pairs={{0,496},{16,0},{32,16},{48,32},{64,48},{80,64},{96,80},{112,96},{1... | collective-permute-start | bytes 98312 | tf_op jit(solution)/shard_map/ppermute | solution.py:12
  177.1 14.4 %collective-permute-start.18 = (bf16[2,64,128]{2,1,0:T(8,128)(2,1)}, bf16[2,64,128]{2,1,0:T(8,128)(2,1)}, u32[]{:S(2)}, u32[]{:S(2)}) collective-permute-start(bf16[2,64,128]{2,1,0:T(8,128)(2,1)} %get-tuple-element.19), channel_id=1, source_target_pairs={{0,1},{1,2},{2,3},{3,4},{4,5},{5,6},{6,7},{7,8},{8,9},{9,10},{10,1... | collective-permute-start | bytes 98312 | tf_op jit(solution)/shard_map/ppermute | solution.py:12
  179.0 13.3 %collective-permute-start.19 = (bf16[2,64,128]{2,1,0:T(8,128)(2,1)}, bf16[2,64,128]{2,1,0:T(8,128)(2,1)}, u32[]{:S(2)}, u32[]{:S(2)}) collective-permute-start(bf16[2,64,128]{2,1,0:T(8,128)(2,1)} %get-tuple-element.18), channel_id=1, source_target_pairs={{0,15},{1,0},{2,1},{3,2},{4,3},{5,4},{6,5},{7,6},{8,7},{9,8},{10,9... | collective-permute-start | bytes 98312 | tf_op jit(solution)/shard_map/ppermute | solution.py:12
  205.5 22.3 %collective-permute-start.20 = (bf16[2,64,128]{2,1,0:T(8,128)(2,1)S(1)}, bf16[2,64,128]{2,1,0:T(8,128)(2,1)}, u32[]{:S(2)}, u32[]{:S(2)}) collective-permute-start(bf16[2,64,128]{2,1,0:T(8,128)(2,1)S(1)} %get-tuple-element.17), channel_id=1, source_target_pairs={{0,16},{16,32},{32,48},{48,64},{64,80},{80,96},{96,112},{112,128},... | collective-permute-start | bytes 98312 | tf_op jit(solution)/shard_map/ppermute | solution.py:12
  207.4 21.2 %collective-permute-start.21 = (bf16[2,64,128]{2,1,0:T(8,128)(2,1)}, bf16[2,64,128]{2,1,0:T(8,128)(2,1)}, u32[]{:S(2)}, u32[]{:S(2)}) collective-permute-start(bf16[2,64,128]{2,1,0:T(8,128)(2,1)} %get-tuple-element.16), channel_id=1, source_target_pairs={{0,496},{16,0},{32,16},{48,32},{64,48},{80,64},{96,80},{112,96},{1... | collective-permute-start | bytes 98312 | tf_op jit(solution)/shard_map/ppermute | solution.py:12
  214.9 14.4 %collective-permute-start.22 = (bf16[2,64,128]{2,1,0:T(8,128)(2,1)}, bf16[2,64,128]{2,1,0:T(8,128)(2,1)}, u32[]{:S(2)}, u32[]{:S(2)}) collective-permute-start(bf16[2,64,128]{2,1,0:T(8,128)(2,1)} %get-tuple-element.15), channel_id=1, source_target_pairs={{0,1},{1,2},{2,3},{3,4},{4,5},{5,6},{6,7},{7,8},{8,9},{9,10},{10,1... | collective-permute-start | bytes 98312 | tf_op jit(solution)/shard_map/ppermute | solution.py:12
  216.8 13.3 %collective-permute-start.23 = (bf16[2,64,128]{2,1,0:T(8,128)(2,1)}, bf16[2,64,128]{2,1,0:T(8,128)(2,1)}, u32[]{:S(2)}, u32[]{:S(2)}) collective-permute-start(bf16[2,64,128]{2,1,0:T(8,128)(2,1)} %get-tuple-element.14), channel_id=1, source_target_pairs={{0,15},{1,0},{2,1},{3,2},{4,3},{5,4},{6,5},{7,6},{8,7},{9,8},{10,9... | collective-permute-start | bytes 98312 | tf_op jit(solution)/shard_map/ppermute | solution.py:12
  243.3 22.5 %collective-permute-start.24 = (bf16[2,64,128]{2,1,0:T(8,128)(2,1)S(1)}, bf16[2,64,128]{2,1,0:T(8,128)(2,1)}, u32[]{:S(2)}, u32[]{:S(2)}) collective-permute-start(bf16[2,64,128]{2,1,0:T(8,128)(2,1)S(1)} %get-tuple-element.13), channel_id=1, source_target_pairs={{0,16},{16,32},{32,48},{48,64},{64,80},{80,96},{96,112},{112,128},... | collective-permute-start | bytes 98312 | tf_op jit(solution)/shard_map/ppermute | solution.py:12
  245.2 21.4 %collective-permute-start.25 = (bf16[2,64,128]{2,1,0:T(8,128)(2,1)}, bf16[2,64,128]{2,1,0:T(8,128)(2,1)}, u32[]{:S(2)}, u32[]{:S(2)}) collective-permute-start(bf16[2,64,128]{2,1,0:T(8,128)(2,1)} %get-tuple-element.12), channel_id=1, source_target_pairs={{0,496},{16,0},{32,16},{48,32},{64,48},{80,64},{96,80},{112,96},{1... | collective-permute-start | bytes 98312 | tf_op jit(solution)/shard_map/ppermute | solution.py:12
  252.8 14.6 %collective-permute-start.26 = (bf16[2,64,128]{2,1,0:T(8,128)(2,1)}, bf16[2,64,128]{2,1,0:T(8,128)(2,1)}, u32[]{:S(2)}, u32[]{:S(2)}) collective-permute-start(bf16[2,64,128]{2,1,0:T(8,128)(2,1)} %get-tuple-element.11), channel_id=1, source_target_pairs={{0,1},{1,2},{2,3},{3,4},{4,5},{5,6},{6,7},{7,8},{8,9},{9,10},{10,1... | collective-permute-start | bytes 98312 | tf_op jit(solution)/shard_map/ppermute | solution.py:12
  254.7 13.4 %collective-permute-start.27 = (bf16[2,64,128]{2,1,0:T(8,128)(2,1)}, bf16[2,64,128]{2,1,0:T(8,128)(2,1)}, u32[]{:S(2)}, u32[]{:S(2)}) collective-permute-start(bf16[2,64,128]{2,1,0:T(8,128)(2,1)} %get-tuple-element.10), channel_id=1, source_target_pairs={{0,15},{1,0},{2,1},{3,2},{4,3},{5,4},{6,5},{7,6},{8,7},{9,8},{10,9... | collective-permute-start | bytes 98312 | tf_op jit(solution)/shard_map/ppermute | solution.py:12
  280.7 20.2 %collective-permute-start.28 = (bf16[2,64,128]{2,1,0:T(8,128)(2,1)S(1)}, bf16[2,64,128]{2,1,0:T(8,128)(2,1)S(1)}, u32[]{:S(2)}, u32[]{:S(2)}) collective-permute-start(bf16[2,64,128]{2,1,0:T(8,128)(2,1)S(1)} %get-tuple-element.9), channel_id=1, source_target_pairs={{0,16},{16,32},{32,48},{48,64},{64,80},{80,96},{96,112},{112,128},... | collective-permute-start | bytes 98312 | tf_op jit(solution)/shard_map/ppermute | solution.py:12
  282.7 18.1 %collective-permute-start.29 = (bf16[2,64,128]{2,1,0:T(8,128)(2,1)S(1)}, bf16[2,64,128]{2,1,0:T(8,128)(2,1)S(1)}, u32[]{:S(2)}, u32[]{:S(2)}) collective-permute-start(bf16[2,64,128]{2,1,0:T(8,128)(2,1)S(1)} %get-tuple-element.8), channel_id=1, source_target_pairs={{0,496},{16,0},{32,16},{48,32},{64,48},{80,64},{96,80},{112,96},{1... | collective-permute-start | bytes 98312 | tf_op jit(solution)/shard_map/ppermute | solution.py:12
  290.3 10.6 %collective-permute-start.30 = (bf16[2,64,128]{2,1,0:T(8,128)(2,1)S(1)}, bf16[2,64,128]{2,1,0:T(8,128)(2,1)S(1)}, u32[]{:S(2)}, u32[]{:S(2)}) collective-permute-start(bf16[2,64,128]{2,1,0:T(8,128)(2,1)S(1)} %get-tuple-element.7), channel_id=1, source_target_pairs={{0,1},{1,2},{2,3},{3,4},{4,5},{5,6},{6,7},{7,8},{8,9},{9,10},{10,1... | collective-permute-start | bytes 98312 | tf_op jit(solution)/shard_map/ppermute | solution.py:12
  292.2 8.7 %collective-permute-start.31 = (bf16[2,64,128]{2,1,0:T(8,128)(2,1)S(1)}, bf16[2,64,128]{2,1,0:T(8,128)(2,1)S(1)}, u32[]{:S(2)}, u32[]{:S(2)}) collective-permute-start(bf16[2,64,128]{2,1,0:T(8,128)(2,1)S(1)} %get-tuple-element.6), channel_id=1, source_target_pairs={{0,15},{1,0},{2,1},{3,2},{4,3},{5,4},{6,5},{7,6},{8,7},{9,8},{10,9... | collective-permute-start | bytes 98312 | tf_op jit(solution)/shard_map/ppermute | solution.py:12
  300.9 20.8 %copy-start.1 = (bf16[16,128,128]{2,1,0:T(8,128)(2,1)S(1)}, bf16[16,128,128]{2,1,0:T(8,128)(2,1)}, u32[]{:S(2)}) copy-start(bf16[16,128,128]{2,1,0:T(8,128)(2,1)} %param.9) | copy-start | bytes 1572868
  300.9 20.8 %copy-start.2 = (f32[16,64,128]{2,1,0:T(8,128)S(1)}, f32[16,64,128]{2,1,0:T(8,128)}, u32[]{:S(2)}) copy-start(f32[16,64,128]{2,1,0:T(8,128)} %get-tuple-element.49) | copy-start | bytes 1572868
  305.7 22.1 %collective-permute-start.32 = (bf16[2,64,128]{2,1,0:T(8,128)(2,1)}, bf16[2,64,128]{2,1,0:T(8,128)(2,1)S(1)}, u32[]{:S(2)}, u32[]{:S(2)}) collective-permute-start(bf16[2,64,128]{2,1,0:T(8,128)(2,1)} %get-tuple-element.2), channel_id=1, source_target_pairs={{0,16},{16,32},{32,48},{48,64},{64,80},{80,96},{96,112},{112,128},... | collective-permute-start | bytes 98312 | tf_op jit(solution)/shard_map/ppermute | solution.py:12
  307.6 20.2 %collective-permute-start.33 = (bf16[2,64,128]{2,1,0:T(8,128)(2,1)}, bf16[2,64,128]{2,1,0:T(8,128)(2,1)S(1)}, u32[]{:S(2)}, u32[]{:S(2)}) collective-permute-start(bf16[2,64,128]{2,1,0:T(8,128)(2,1)} %get-tuple-element.5), channel_id=1, source_target_pairs={{0,496},{16,0},{32,16},{48,32},{64,48},{80,64},{96,80},{112,96},{1... | collective-permute-start | bytes 98312 | tf_op jit(solution)/shard_map/ppermute | solution.py:12
  315.1 12.7 %collective-permute-start.34 = (bf16[2,64,128]{2,1,0:T(8,128)(2,1)S(1)}, bf16[2,64,128]{2,1,0:T(8,128)(2,1)}, u32[]{:S(2)}, u32[]{:S(2)}) collective-permute-start(bf16[2,64,128]{2,1,0:T(8,128)(2,1)S(1)} %get-tuple-element.4), channel_id=1, source_target_pairs={{0,1},{1,2},{2,3},{3,4},{4,5},{5,6},{6,7},{7,8},{8,9},{9,10},{10,1... | collective-permute-start | bytes 98312 | tf_op jit(solution)/shard_map/ppermute | solution.py:12
  317.1 10.8 %collective-permute-start.35 = (bf16[2,64,128]{2,1,0:T(8,128)(2,1)S(1)}, bf16[2,64,128]{2,1,0:T(8,128)(2,1)}, u32[]{:S(2)}, u32[]{:S(2)}) collective-permute-start(bf16[2,64,128]{2,1,0:T(8,128)(2,1)S(1)} %get-tuple-element.3), channel_id=1, source_target_pairs={{0,15},{1,0},{2,1},{3,2},{4,3},{5,4},{6,5},{7,6},{8,7},{9,8},{10,9... | collective-permute-start | bytes 98312 | tf_op jit(solution)/shard_map/ppermute | solution.py:12
  332.2 4.7 %collective-permute-start.36 = (f32[64,64]{1,0:T(8,128)S(1)}, f32[64,64]{1,0:T(8,128)S(1)}, u32[]{:S(2)}, u32[]{:S(2)}) collective-permute-start(f32[64,64]{1,0:T(8,128)S(1)} %convolution_bitcast_fusion.17), channel_id=1, source_target_pairs={{0,1},{1,0},{2,3},{3,2},{4,5},{5,4},{6,7},{7,6},{8,9},{9,8},{10,11... | collective-permute-start | bytes 49160 | tf_op jit(solution)/shard_map/ppermute | solution.py:20
  336.9 5.6 %collective-permute-start.37 = (f32[64,64]{1,0:T(8,128)S(1)}, f32[64,64]{1,0:T(8,128)S(1)}, u32[]{:S(2)}, u32[]{:S(2)}) collective-permute-start(f32[64,64]{1,0:T(8,128)S(1)} %add.199), channel_id=1, source_target_pairs={{0,2},{1,3},{2,0},{3,1},{4,6},{5,7},{6,4},{7,5},{8,10},{9,11},{10,... | collective-permute-start | bytes 49160 | tf_op jit(solution)/shard_map/ppermute | solution.py:20
  342.5 9.1 %collective-permute-start.38 = (f32[64,64]{1,0:T(8,128)S(1)}, f32[64,64]{1,0:T(8,128)S(1)}, u32[]{:S(2)}, u32[]{:S(2)}) collective-permute-start(f32[64,64]{1,0:T(8,128)S(1)} %add.200), channel_id=1, source_target_pairs={{0,4},{1,5},{2,6},{3,7},{4,0},{5,1},{6,2},{7,3},{8,12},{9,13},{10,... | collective-permute-start | bytes 49160 | tf_op jit(solution)/shard_map/ppermute | solution.py:20
  351.7 13.4 %collective-permute-start.39 = (f32[64,64]{1,0:T(8,128)S(1)}, f32[64,64]{1,0:T(8,128)S(1)}, u32[]{:S(2)}, u32[]{:S(2)}) collective-permute-start(f32[64,64]{1,0:T(8,128)S(1)} %add.201), channel_id=1, source_target_pairs={{0,8},{1,9},{2,10},{3,11},{4,12},{5,13},{6,14},{7,15},{8,0},{9,1},... | collective-permute-start | bytes 49160 | tf_op jit(solution)/shard_map/ppermute | solution.py:20
  365.1 12.5 %collective-permute-start.40 = (f32[64,64]{1,0:T(8,128)S(1)}, f32[64,64]{1,0:T(8,128)S(1)}, u32[]{:S(2)}, u32[]{:S(2)}) collective-permute-start(f32[64,64]{1,0:T(8,128)S(1)} %add.202), channel_id=1, source_target_pairs={{0,16},{16,0},{32,48},{48,32},{64,80},{80,64},{96,112},{112,96},{1... | collective-permute-start | bytes 49160 | tf_op jit(solution)/shard_map/ppermute | solution.py:20
  377.6 4.6 %collective-permute-start.41 = (f32[64,64]{1,0:T(8,128)S(1)}, f32[64,64]{1,0:T(8,128)S(1)}, u32[]{:S(2)}, u32[]{:S(2)}) collective-permute-start(f32[64,64]{1,0:T(8,128)S(1)} %add.203), channel_id=1, source_target_pairs={{0,32},{16,48},{32,0},{48,16},{64,96},{80,112},{96,64},{112,80},{1... | collective-permute-start | bytes 49160 | tf_op jit(solution)/shard_map/ppermute | solution.py:20
  382.2 6.2 %collective-permute-start.42 = (f32[64,64]{1,0:T(8,128)S(1)}, f32[64,64]{1,0:T(8,128)S(1)}, u32[]{:S(2)}, u32[]{:S(2)}) collective-permute-start(f32[64,64]{1,0:T(8,128)S(1)} %add.204), channel_id=1, source_target_pairs={{0,64},{16,80},{32,96},{48,112},{64,0},{80,16},{96,32},{112,48},{1... | collective-permute-start | bytes 49160 | tf_op jit(solution)/shard_map/ppermute | solution.py:20
  388.4 4.6 %collective-permute-start.43 = (f32[64,64]{1,0:T(8,128)S(1)}, f32[64,64]{1,0:T(8,128)S(1)}, u32[]{:S(2)}, u32[]{:S(2)}) collective-permute-start(f32[64,64]{1,0:T(8,128)S(1)} %add.205), channel_id=1, source_target_pairs={{0,128},{16,144},{32,160},{48,176},{64,192},{80,208},{96,224},{112... | collective-permute-start | bytes 49160 | tf_op jit(solution)/shard_map/ppermute | solution.py:20
  393.0 6.2 %collective-permute-start.44 = (f32[64,64]{1,0:T(8,128)S(1)}, f32[64,64]{1,0:T(8,128)S(1)}, u32[]{:S(2)}, u32[]{:S(2)}) collective-permute-start(f32[64,64]{1,0:T(8,128)S(1)} %add.206), channel_id=1, source_target_pairs={{0,256},{16,272},{32,288},{48,304},{64,320},{80,336},{96,352},{112... | collective-permute-start | bytes 49160 | tf_op jit(solution)/shard_map/ppermute | solution.py:20
  (14 other events, 167.8 us)

commit v3 on v2

--- a/solution.py
+++ b/solution.py
@@ -24,43 +24,51 @@
 
 def exchange(outgoing, per_list):
     pieces = [outgoing[d * per_list:(d + 1) * per_list] for d in range(4)]
-    from_xlow = from_behind(pieces[0], "px", 1)
-    from_xhigh = from_behind(pieces[1], "px", -1)
-    from_ylow = from_behind(pieces[2], "py", 1)
-    from_yhigh = from_behind(pieces[3], "py", -1)
-    return jnp.concatenate([from_xlow, from_xhigh, from_ylow, from_yhigh], axis=0)
+    return [
+        from_behind(pieces[0], "px", 1),
+        from_behind(pieces[1], "px", -1),
+        from_behind(pieces[2], "py", 1),
+        from_behind(pieces[3], "py", -1),
+    ]
 
 
-def rows_apply(rounded, received, tiles, cols, halo, slot):
-    gathered = rounded[cols]
-    product = jnp.einsum(
-        "rtkj,rtij->rki", gathered, tiles, preferred_element_type=jnp.float32
+def halo_term(pieces, chooser, halo):
+    received = jnp.concatenate(pieces, axis=0)
+    chosen = jnp.einsum("rs,skj->rkj", chooser, received, preferred_element_type=jnp.float32)
+    return jnp.einsum(
+        "rkj,rij->rki", chosen.astype(jnp.bfloat16), halo, preferred_element_type=jnp.float32
     )
-    coupled = jnp.einsum(
-        "rkj,rij->rki", received[slot], halo, preferred_element_type=jnp.float32
+
+
+def local_term(rounded, tiles, cols):
+    return jnp.einsum(
+        "rtkj,rtij->rki", rounded[cols], tiles, preferred_element_type=jnp.float32
     )
-    return product + coupled
 
 
 def shards(start_vecs, local_tiles, local_cols, halo_tiles, halo_slot, boundary):
     per_list = boundary.shape[1]
+    slots = 4 * per_list
     picks = boundary.reshape(-1)
-    edge = (local_tiles[picks], local_cols[picks], halo_tiles[picks], halo_slot[picks])
-    whole = (local_tiles, local_cols, halo_tiles, halo_slot)
+    edge_halo = halo_tiles[picks]
+    edge_chooser = jax.nn.one_hot(halo_slot[picks], slots, dtype=jnp.bfloat16)
+    whole_chooser = jax.nn.one_hot(halo_slot, slots, dtype=jnp.bfloat16)
 
-    older = start_vecs
     rounded = start_vecs.astype(jnp.bfloat16)
     received = exchange(rounded[picks], per_list)
-    edge_next = rows_apply(rounded, received, *edge)
+    local_part = local_term(rounded, local_tiles, local_cols)
+    edge_next = local_part[picks] + halo_term(received, edge_chooser, edge_halo)
     received_next = exchange(edge_next.astype(jnp.bfloat16), per_list)
-    current = rows_apply(rounded, received, *whole)
+    older = start_vecs
+    current = local_part + halo_term(received, whole_chooser, halo_tiles)
     received = received_next
     for step in range(1, DEG):
         rounded = current.astype(jnp.bfloat16)
+        local_part = 2.0 * local_term(rounded, local_tiles, local_cols) - older
         if step < DEG - 1:
-            edge_next = 2.0 * rows_apply(rounded, received, *edge) - older[picks]
+            edge_next = local_part[picks] + 2.0 * halo_term(received, edge_chooser, edge_halo)
             received_next = exchange(edge_next.astype(jnp.bfloat16), per_list)
-        newer = 2.0 * rows_apply(rounded, received, *whole) - older
+        newer = local_part + 2.0 * halo_term(received, whole_chooser, halo_tiles)
         older, current = current, newer
         if step < DEG - 1:
             received = received_next

time: 409 us -> 315 us (0.77)
  local copies, waits for them, and re-layouts: 113 us -> 35.1 us
  matrix products: 69.2 us -> 50.1 us
  other arithmetic: 5.54 us -> 10.7 us
    gather x46 -> x19, local copies, waits for them, and re-layouts: 82.7 us -> 26.8 us  [the longest x9 15.4 us: local_term(): rounded[cols]]
    dot_general x34 -> x43, matrix products: 68.6 us -> 49.5 us  [the longest x17 26.9 us: halo_term(): jnp.einsum('rkj,rij->rki', chosen.astype(jnp.bfloat16), halo, preferred_e...]
    unnamed x60 -> x25, local copies, waits for them, and re-layouts: 17.8 us -> 0.98 us
    concatenate x1 -> x9, other arithmetic: 0.8 us -> 7.24 us  [halo_term(): received = jnp.concatenate(pieces, axis=0)]
    concatenate x8 -> x0, local copies, waits for them, and re-layouts: 5.38 us -> none  [exchange(): jnp.concatenate([from_xlow, from_xhigh, from_ylow, from_yhigh], axis=0)]
where the time goes in v3:
time: 315 us; the launch traced here: 310 us
  starting transfers between devices  182 us (58%)
  matrix products  50.1 us (16%)
  local copies, waits for them, and re-layouts  35.1 us (11%)
  waiting for transfers between devices  30.1 us (10%)
  other arithmetic  10.7 us (3%)
    ppermute x36, starting transfers between devices, from_behind(): return lax.ppermute(value, axis, pairs)  146 us
    ppermute x9, starting transfers between devices, butterfly_sum(): value = value + lax.ppermute(value, axis, pairs)  36.7 us
    ppermute x9, waiting for transfers between devices, butterfly_sum(): value = value + lax.ppermute(value, axis, pairs)  30 us
    dot_general x17, matrix products, halo_term(): jnp.einsum('rkj,rij->rki', chosen.astype(jnp.bfloat16), halo, preferred_e...  26.9 us
    dot_general x9, matrix products, local_term(): jnp.einsum('rtkj,rtij->rki', rounded[cols], tiles, preferred_element_type...  18.3 us
    gather x9, local copies, waits for them, and re-layouts, local_term(): rounded[cols]  15.4 us
    gather x7, local copies, waits for them, and re-layouts, shards(): local_part[picks] + 2.0 * halo_term(received, edge_chooser, edge_halo)  8.88 us
    concatenate x9, other arithmetic, halo_term(): received = jnp.concatenate(pieces, axis=0)  7.24 us
  transfers between devices with their start and end apart: 45, of which 9 were waited for; matrix products, arithmetic and copies ran while one was open for 20% of the time, Pallas kernels for 0%

profile of v3, /device:TPU:1, one launch (start us, length us, event | category | flops | bytes accessed | tf_op | source)
XLA Modules:
  0.0 309.9 jit_solution(18423333375354633304)
XLA Ops:
  4.0 4.5 %collective-permute-start = (bf16[2,64,128]{2,1,0:T(8,128)(2,1)}, bf16[2,64,128]{2,1,0:T(8,128)(2,1)S(1)}, u32[]{:S(2)}, u32[]{:S(2)}) collective-permute-start(bf16[2,64,128]{2,1,0:T(8,128)(2,1)} %get-tuple-element.34), channel_id=1, source_target_pairs={{0,16},{16,32},{32,48},{48,64},{64,80},{80,96},{96,112},{112,128},... | collective-permute-start | bytes 98312 | tf_op jit(solution)/shard_map/ppermute | solution.py:12
  8.5 6.2 %collective-permute-start.1 = (bf16[2,64,128]{2,1,0:T(8,128)(2,1)}, bf16[2,64,128]{2,1,0:T(8,128)(2,1)S(1)}, u32[]{:S(2)}, u32[]{:S(2)}) collective-permute-start(bf16[2,64,128]{2,1,0:T(8,128)(2,1)} %get-tuple-element.36), channel_id=1, source_target_pairs={{0,496},{16,0},{32,16},{48,32},{64,48},{80,64},{96,80},{112,96},{1... | collective-permute-start | bytes 98312 | tf_op jit(solution)/shard_map/ppermute | solution.py:12
  14.6 1.9 collective-permute-start.2
  16.6 6.9 %collective-permute-start.3 = (bf16[2,64,128]{2,1,0:T(8,128)(2,1)S(1)}, bf16[2,64,128]{2,1,0:T(8,128)(2,1)}, u32[]{:S(2)}, u32[]{:S(2)}) collective-permute-start(bf16[2,64,128]{2,1,0:T(8,128)(2,1)S(1)} %get-tuple-element.37), channel_id=1, source_target_pairs={{0,15},{1,0},{2,1},{3,2},{4,3},{5,4},{6,5},{7,6},{8,7},{9,8},{10,9... | collective-permute-start | bytes 98312 | tf_op jit(solution)/shard_map/ppermute | solution.py:12
  26.0 2.1 convolution_bitcast_fusion.8
  33.9 3.9 %collective-permute-start.4 = (bf16[2,64,128]{2,1,0:T(8,128)(2,1)}, bf16[2,64,128]{2,1,0:T(8,128)(2,1)S(1)}, u32[]{:S(2)}, u32[]{:S(2)}) collective-permute-start(bf16[2,64,128]{2,1,0:T(8,128)(2,1)} %get-tuple-element.30), channel_id=1, source_target_pairs={{0,16},{16,32},{32,48},{48,64},{64,80},{80,96},{96,112},{112,128},... | collective-permute-start | bytes 98312 | tf_op jit(solution)/shard_map/ppermute | solution.py:12
  37.8 4.1 %collective-permute-start.5 = (bf16[2,64,128]{2,1,0:T(8,128)(2,1)}, bf16[2,64,128]{2,1,0:T(8,128)(2,1)S(1)}, u32[]{:S(2)}, u32[]{:S(2)}) collective-permute-start(bf16[2,64,128]{2,1,0:T(8,128)(2,1)} %get-tuple-element.33), channel_id=1, source_target_pairs={{0,496},{16,0},{32,16},{48,32},{64,48},{80,64},{96,80},{112,96},{1... | collective-permute-start | bytes 98312 | tf_op jit(solution)/shard_map/ppermute | solution.py:12
  43.9 4.6 %collective-permute-start.7 = (bf16[2,64,128]{2,1,0:T(8,128)(2,1)S(1)}, bf16[2,64,128]{2,1,0:T(8,128)(2,1)}, u32[]{:S(2)}, u32[]{:S(2)}) collective-permute-start(bf16[2,64,128]{2,1,0:T(8,128)(2,1)S(1)} %get-tuple-element.31), channel_id=1, source_target_pairs={{0,15},{1,0},{2,1},{3,2},{4,3},{5,4},{6,5},{7,6},{8,7},{9,8},{10,9... | collective-permute-start | bytes 98312 | tf_op jit(solution)/shard_map/ppermute | solution.py:12
  48.5 2.3 fusion.120
  52.5 2.2 fusion.1
  61.1 4.6 %collective-permute-start.11 = (bf16[2,64,128]{2,1,0:T(8,128)(2,1)}, bf16[2,64,128]{2,1,0:T(8,128)(2,1)S(1)}, u32[]{:S(2)}, u32[]{:S(2)}) collective-permute-start(bf16[2,64,128]{2,1,0:T(8,128)(2,1)} %get-tuple-element.27), channel_id=1, source_target_pairs={{0,15},{1,0},{2,1},{3,2},{4,3},{5,4},{6,5},{7,6},{8,7},{9,8},{10,9... | collective-permute-start | bytes 98312 | tf_op jit(solution)/shard_map/ppermute | solution.py:12
  65.7 2.5 collective-permute-start.8
  68.2 7.5 %collective-permute-start.9 = (bf16[2,64,128]{2,1,0:T(8,128)(2,1)S(1)}, bf16[2,64,128]{2,1,0:T(8,128)(2,1)}, u32[]{:S(2)}, u32[]{:S(2)}) collective-permute-start(bf16[2,64,128]{2,1,0:T(8,128)(2,1)S(1)} %get-tuple-element.29), channel_id=1, source_target_pairs={{0,496},{16,0},{32,16},{48,32},{64,48},{80,64},{96,80},{112,96},{1... | collective-permute-start | bytes 98312 | tf_op jit(solution)/shard_map/ppermute | solution.py:12
  75.7 2.3 fusion.121
  79.7 2.2 fusion.3
  88.4 7.0 %collective-permute-start.13 = (bf16[2,64,128]{2,1,0:T(8,128)(2,1)}, bf16[2,64,128]{2,1,0:T(8,128)(2,1)S(1)}, u32[]{:S(2)}, u32[]{:S(2)}) collective-permute-start(bf16[2,64,128]{2,1,0:T(8,128)(2,1)} %get-tuple-element.25), channel_id=1, source_target_pairs={{0,496},{16,0},{32,16},{48,32},{64,48},{80,64},{96,80},{112,96},{1... | collective-permute-start | bytes 98312 | tf_op jit(solution)/shard_map/ppermute | solution.py:12
  97.3 4.6 %collective-permute-start.15 = (bf16[2,64,128]{2,1,0:T(8,128)(2,1)S(1)}, bf16[2,64,128]{2,1,0:T(8,128)(2,1)}, u32[]{:S(2)}, u32[]{:S(2)}) collective-permute-start(bf16[2,64,128]{2,1,0:T(8,128)(2,1)S(1)} %get-tuple-element.23), channel_id=1, source_target_pairs={{0,15},{1,0},{2,1},{3,2},{4,3},{5,4},{6,5},{7,6},{8,7},{9,8},{10,9... | collective-permute-start | bytes 98312 | tf_op jit(solution)/shard_map/ppermute | solution.py:12
  101.8 2.3 fusion.122
  105.9 2.2 fusion.5
  114.4 7.5 %collective-permute-start.17 = (bf16[2,64,128]{2,1,0:T(8,128)(2,1)}, bf16[2,64,128]{2,1,0:T(8,128)(2,1)S(1)}, u32[]{:S(2)}, u32[]{:S(2)}) collective-permute-start(bf16[2,64,128]{2,1,0:T(8,128)(2,1)} %get-tuple-element.21), channel_id=1, source_target_pairs={{0,496},{16,0},{32,16},{48,32},{64,48},{80,64},{96,80},{112,96},{1... | collective-permute-start | bytes 98312 | tf_op jit(solution)/shard_map/ppermute | solution.py:12
  123.9 4.6 %collective-permute-start.19 = (bf16[2,64,128]{2,1,0:T(8,128)(2,1)S(1)}, bf16[2,64,128]{2,1,0:T(8,128)(2,1)}, u32[]{:S(2)}, u32[]{:S(2)}) collective-permute-start(bf16[2,64,128]{2,1,0:T(8,128)(2,1)S(1)} %get-tuple-element.19), channel_id=1, source_target_pairs={{0,15},{1,0},{2,1},{3,2},{4,3},{5,4},{6,5},{7,6},{8,7},{9,8},{10,9... | collective-permute-start | bytes 98312 | tf_op jit(solution)/shard_map/ppermute | solution.py:12
  128.5 2.3 fusion.123
  132.5 2.2 fusion.7
  141.1 7.5 %collective-permute-start.21 = (bf16[2,64,128]{2,1,0:T(8,128)(2,1)}, bf16[2,64,128]{2,1,0:T(8,128)(2,1)S(1)}, u32[]{:S(2)}, u32[]{:S(2)}) collective-permute-start(bf16[2,64,128]{2,1,0:T(8,128)(2,1)} %get-tuple-element.17), channel_id=1, source_target_pairs={{0,496},{16,0},{32,16},{48,32},{64,48},{80,64},{96,80},{112,96},{1... | collective-permute-start | bytes 98312 | tf_op jit(solution)/shard_map/ppermute | solution.py:12
  150.6 4.6 %collective-permute-start.23 = (bf16[2,64,128]{2,1,0:T(8,128)(2,1)S(1)}, bf16[2,64,128]{2,1,0:T(8,128)(2,1)}, u32[]{:S(2)}, u32[]{:S(2)}) collective-permute-start(bf16[2,64,128]{2,1,0:T(8,128)(2,1)S(1)} %get-tuple-element.15), channel_id=1, source_target_pairs={{0,15},{1,0},{2,1},{3,2},{4,3},{5,4},{6,5},{7,6},{8,7},{9,8},{10,9... | collective-permute-start | bytes 98312 | tf_op jit(solution)/shard_map/ppermute | solution.py:12
  155.2 2.3 fusion.124
  159.2 2.2 fusion.9
  167.8 7.5 %collective-permute-start.25 = (bf16[2,64,128]{2,1,0:T(8,128)(2,1)}, bf16[2,64,128]{2,1,0:T(8,128)(2,1)S(1)}, u32[]{:S(2)}, u32[]{:S(2)}) collective-permute-start(bf16[2,64,128]{2,1,0:T(8,128)(2,1)} %get-tuple-element.13), channel_id=1, source_target_pairs={{0,496},{16,0},{32,16},{48,32},{64,48},{80,64},{96,80},{112,96},{1... | collective-permute-start | bytes 98312 | tf_op jit(solution)/shard_map/ppermute | solution.py:12
  177.2 4.6 %collective-permute-start.27 = (bf16[2,64,128]{2,1,0:T(8,128)(2,1)S(1)}, bf16[2,64,128]{2,1,0:T(8,128)(2,1)}, u32[]{:S(2)}, u32[]{:S(2)}) collective-permute-start(bf16[2,64,128]{2,1,0:T(8,128)(2,1)S(1)} %get-tuple-element.11), channel_id=1, source_target_pairs={{0,15},{1,0},{2,1},{3,2},{4,3},{5,4},{6,5},{7,6},{8,7},{9,8},{10,9... | collective-permute-start | bytes 98312 | tf_op jit(solution)/shard_map/ppermute | solution.py:12
  181.8 2.3 fusion.125
  185.8 2.2 fusion.11
  194.5 7.5 %collective-permute-start.29 = (bf16[2,64,128]{2,1,0:T(8,128)(2,1)}, bf16[2,64,128]{2,1,0:T(8,128)(2,1)S(1)}, u32[]{:S(2)}, u32[]{:S(2)}) collective-permute-start(bf16[2,64,128]{2,1,0:T(8,128)(2,1)} %get-tuple-element.9), channel_id=1, source_target_pairs={{0,496},{16,0},{32,16},{48,32},{64,48},{80,64},{96,80},{112,96},{1... | collective-permute-start | bytes 98312 | tf_op jit(solution)/shard_map/ppermute | solution.py:12
  203.9 4.8 %collective-permute-start.31 = (bf16[2,64,128]{2,1,0:T(8,128)(2,1)S(1)}, bf16[2,64,128]{2,1,0:T(8,128)(2,1)}, u32[]{:S(2)}, u32[]{:S(2)}) collective-permute-start(bf16[2,64,128]{2,1,0:T(8,128)(2,1)S(1)} %get-tuple-element.7), channel_id=1, source_target_pairs={{0,15},{1,0},{2,1},{3,2},{4,3},{5,4},{6,5},{7,6},{8,7},{9,8},{10,9... | collective-permute-start | bytes 98312 | tf_op jit(solution)/shard_map/ppermute | solution.py:12
  208.7 2.3 fusion.126
  212.7 2.2 fusion.13
  221.3 7.5 %collective-permute-start.33 = (bf16[2,64,128]{2,1,0:T(8,128)(2,1)}, bf16[2,64,128]{2,1,0:T(8,128)(2,1)S(1)}, u32[]{:S(2)}, u32[]{:S(2)}) collective-permute-start(bf16[2,64,128]{2,1,0:T(8,128)(2,1)} %get-tuple-element.5), channel_id=1, source_target_pairs={{0,496},{16,0},{32,16},{48,32},{64,48},{80,64},{96,80},{112,96},{1... | collective-permute-start | bytes 98312 | tf_op jit(solution)/shard_map/ppermute | solution.py:12
  230.8 4.6 %collective-permute-start.35 = (bf16[2,64,128]{2,1,0:T(8,128)(2,1)S(1)}, bf16[2,64,128]{2,1,0:T(8,128)(2,1)}, u32[]{:S(2)}, u32[]{:S(2)}) collective-permute-start(bf16[2,64,128]{2,1,0:T(8,128)(2,1)S(1)} %get-tuple-element.3), channel_id=1, source_target_pairs={{0,15},{1,0},{2,1},{3,2},{4,3},{5,4},{6,5},{7,6},{8,7},{9,8},{10,9... | collective-permute-start | bytes 98312 | tf_op jit(solution)/shard_map/ppermute | solution.py:12
  242.6 2.7 collective-permute-done.36
  247.2 3.8 %collective-permute-done.37 = f32[64,64]{1,0:T(8,128)S(1)} collective-permute-done((f32[64,64]{1,0:T(8,128)S(1)}, f32[64,64]{1,0:T(8,128)S(1)}, u32[]{:S(2)}, u32[]{:S(2)}) %collective-permute-start.37) | collective-permute-done | bytes 16416 | tf_op jit(solution)/shard_map/ppermute | solution.py:20
  251.1 5.0 %collective-permute-start.38 = (f32[64,64]{1,0:T(8,128)S(1)}, f32[64,64]{1,0:T(8,128)S(1)}, u32[]{:S(2)}, u32[]{:S(2)}) collective-permute-start(f32[64,64]{1,0:T(8,128)S(1)} %add.151), channel_id=1, source_target_pairs={{0,4},{1,5},{2,6},{3,7},{4,0},{5,1},{6,2},{7,3},{8,12},{9,13},{10,... | collective-permute-start | bytes 49160 | tf_op jit(solution)/shard_map/ppermute | solution.py:20
  256.1 4.1 %collective-permute-done.38 = f32[64,64]{1,0:T(8,128)S(1)} collective-permute-done((f32[64,64]{1,0:T(8,128)S(1)}, f32[64,64]{1,0:T(8,128)S(1)}, u32[]{:S(2)}, u32[]{:S(2)}) %collective-permute-start.38) | collective-permute-done | bytes 16416 | tf_op jit(solution)/shard_map/ppermute | solution.py:20
  260.2 8.8 %collective-permute-start.39 = (f32[64,64]{1,0:T(8,128)S(1)}, f32[64,64]{1,0:T(8,128)S(1)}, u32[]{:S(2)}, u32[]{:S(2)}) collective-permute-start(f32[64,64]{1,0:T(8,128)S(1)} %add.152), channel_id=1, source_target_pairs={{0,8},{1,9},{2,10},{3,11},{4,12},{5,13},{6,14},{7,15},{8,0},{9,1},... | collective-permute-start | bytes 49160 | tf_op jit(solution)/shard_map/ppermute | solution.py:20
  269.0 4.6 %collective-permute-done.39 = f32[64,64]{1,0:T(8,128)S(1)} collective-permute-done((f32[64,64]{1,0:T(8,128)S(1)}, f32[64,64]{1,0:T(8,128)S(1)}, u32[]{:S(2)}, u32[]{:S(2)}) %collective-permute-start.39) | collective-permute-done | bytes 16416 | tf_op jit(solution)/shard_map/ppermute | solution.py:20
  273.6 11.4 %collective-permute-start.40 = (f32[64,64]{1,0:T(8,128)S(1)}, f32[64,64]{1,0:T(8,128)S(1)}, u32[]{:S(2)}, u32[]{:S(2)}) collective-permute-start(f32[64,64]{1,0:T(8,128)S(1)} %add.153), channel_id=1, source_target_pairs={{0,16},{16,0},{32,48},{48,32},{64,80},{80,64},{96,112},{112,96},{1... | collective-permute-start | bytes 49160 | tf_op jit(solution)/shard_map/ppermute | solution.py:20
  287.7 2.7 collective-permute-done.41
  292.4 4.2 %collective-permute-done.42 = f32[64,64]{1,0:T(8,128)S(1)} collective-permute-done((f32[64,64]{1,0:T(8,128)S(1)}, f32[64,64]{1,0:T(8,128)S(1)}, u32[]{:S(2)}, u32[]{:S(2)}) %collective-permute-start.42) | collective-permute-done | bytes 16416 | tf_op jit(solution)/shard_map/ppermute | solution.py:20
  298.5 2.7 collective-permute-done.43
  303.2 4.2 %collective-permute-done.44 = f32[64,64]{1,0:T(8,128)S(1)} collective-permute-done((f32[64,64]{1,0:T(8,128)S(1)}, f32[64,64]{1,0:T(8,128)S(1)}, u32[]{:S(2)}, u32[]{:S(2)}) %collective-permute-start.44) | collective-permute-done | bytes 16416 | tf_op jit(solution)/shard_map/ppermute | solution.py:20
  (171 shorter events, 101.5 us)
Async XLA Ops:
  0.6 25.4 %copy-start = (bf16[16,4,128,128]{3,2,1,0:T(8,128)(2,1)S(1)}, bf16[16,4,128,128]{3,2,1,0:T(8,128)(2,1)}, u32[]{:S(2)}) copy-start(bf16[16,4,128,128]{3,2,1,0:T(8,128)(2,1)} %param.7) | copy-start | bytes 6291460
  4.0 26.7 %collective-permute-start = (bf16[2,64,128]{2,1,0:T(8,128)(2,1)}, bf16[2,64,128]{2,1,0:T(8,128)(2,1)S(1)}, u32[]{:S(2)}, u32[]{:S(2)}) collective-permute-start(bf16[2,64,128]{2,1,0:T(8,128)(2,1)} %get-tuple-element.34), channel_id=1, source_target_pairs={{0,16},{16,32},{32,48},{48,64},{64,80},{80,96},{96,112},{112,128},... | collective-permute-start | bytes 98312 | tf_op jit(solution)/shard_map/ppermute | solution.py:12
  8.5 22.3 %collective-permute-start.1 = (bf16[2,64,128]{2,1,0:T(8,128)(2,1)}, bf16[2,64,128]{2,1,0:T(8,128)(2,1)S(1)}, u32[]{:S(2)}, u32[]{:S(2)}) collective-permute-start(bf16[2,64,128]{2,1,0:T(8,128)(2,1)} %get-tuple-element.36), channel_id=1, source_target_pairs={{0,496},{16,0},{32,16},{48,32},{64,48},{80,64},{96,80},{112,96},{1... | collective-permute-start | bytes 98312 | tf_op jit(solution)/shard_map/ppermute | solution.py:12
  14.6 16.1 %collective-permute-start.2 = (bf16[2,64,128]{2,1,0:T(8,128)(2,1)S(1)}, bf16[2,64,128]{2,1,0:T(8,128)(2,1)}, u32[]{:S(2)}, u32[]{:S(2)}) collective-permute-start(bf16[2,64,128]{2,1,0:T(8,128)(2,1)S(1)} %get-tuple-element.35), channel_id=1, source_target_pairs={{0,1},{1,2},{2,3},{3,4},{4,5},{5,6},{6,7},{7,8},{8,9},{9,10},{10,1... | collective-permute-start | bytes 98312 | tf_op jit(solution)/shard_map/ppermute | solution.py:12
  16.6 14.2 %collective-permute-start.3 = (bf16[2,64,128]{2,1,0:T(8,128)(2,1)S(1)}, bf16[2,64,128]{2,1,0:T(8,128)(2,1)}, u32[]{:S(2)}, u32[]{:S(2)}) collective-permute-start(bf16[2,64,128]{2,1,0:T(8,128)(2,1)S(1)} %get-tuple-element.37), channel_id=1, source_target_pairs={{0,15},{1,0},{2,1},{3,2},{4,3},{5,4},{6,5},{7,6},{8,7},{9,8},{10,9... | collective-permute-start | bytes 98312 | tf_op jit(solution)/shard_map/ppermute | solution.py:12
  33.9 22.1 %collective-permute-start.4 = (bf16[2,64,128]{2,1,0:T(8,128)(2,1)}, bf16[2,64,128]{2,1,0:T(8,128)(2,1)S(1)}, u32[]{:S(2)}, u32[]{:S(2)}) collective-permute-start(bf16[2,64,128]{2,1,0:T(8,128)(2,1)} %get-tuple-element.30), channel_id=1, source_target_pairs={{0,16},{16,32},{32,48},{48,64},{64,80},{80,96},{96,112},{112,128},... | collective-permute-start | bytes 98312 | tf_op jit(solution)/shard_map/ppermute | solution.py:12
  37.8 18.1 %collective-permute-start.5 = (bf16[2,64,128]{2,1,0:T(8,128)(2,1)}, bf16[2,64,128]{2,1,0:T(8,128)(2,1)S(1)}, u32[]{:S(2)}, u32[]{:S(2)}) collective-permute-start(bf16[2,64,128]{2,1,0:T(8,128)(2,1)} %get-tuple-element.33), channel_id=1, source_target_pairs={{0,496},{16,0},{32,16},{48,32},{64,48},{80,64},{96,80},{112,96},{1... | collective-permute-start | bytes 98312 | tf_op jit(solution)/shard_map/ppermute | solution.py:12
  42.0 14.0 %collective-permute-start.6 = (bf16[2,64,128]{2,1,0:T(8,128)(2,1)S(1)}, bf16[2,64,128]{2,1,0:T(8,128)(2,1)}, u32[]{:S(2)}, u32[]{:S(2)}) collective-permute-start(bf16[2,64,128]{2,1,0:T(8,128)(2,1)S(1)} %get-tuple-element.32), channel_id=1, source_target_pairs={{0,1},{1,2},{2,3},{3,4},{4,5},{5,6},{6,7},{7,8},{8,9},{9,10},{10,1... | collective-permute-start | bytes 98312 | tf_op jit(solution)/shard_map/ppermute | solution.py:12
  43.9 12.1 %collective-permute-start.7 = (bf16[2,64,128]{2,1,0:T(8,128)(2,1)S(1)}, bf16[2,64,128]{2,1,0:T(8,128)(2,1)}, u32[]{:S(2)}, u32[]{:S(2)}) collective-permute-start(bf16[2,64,128]{2,1,0:T(8,128)(2,1)S(1)} %get-tuple-element.31), channel_id=1, source_target_pairs={{0,15},{1,0},{2,1},{3,2},{4,3},{5,4},{6,5},{7,6},{8,7},{9,8},{10,9... | collective-permute-start | bytes 98312 | tf_op jit(solution)/shard_map/ppermute | solution.py:12
  59.2 24.0 %collective-permute-start.10 = (bf16[2,64,128]{2,1,0:T(8,128)(2,1)}, bf16[2,64,128]{2,1,0:T(8,128)(2,1)S(1)}, u32[]{:S(2)}, u32[]{:S(2)}) collective-permute-start(bf16[2,64,128]{2,1,0:T(8,128)(2,1)} %get-tuple-element.28), channel_id=1, source_target_pairs={{0,1},{1,2},{2,3},{3,4},{4,5},{5,6},{6,7},{7,8},{8,9},{9,10},{10,1... | collective-permute-start | bytes 98312 | tf_op jit(solution)/shard_map/ppermute | solution.py:12
  61.1 22.1 %collective-permute-start.11 = (bf16[2,64,128]{2,1,0:T(8,128)(2,1)}, bf16[2,64,128]{2,1,0:T(8,128)(2,1)S(1)}, u32[]{:S(2)}, u32[]{:S(2)}) collective-permute-start(bf16[2,64,128]{2,1,0:T(8,128)(2,1)} %get-tuple-element.27), channel_id=1, source_target_pairs={{0,15},{1,0},{2,1},{3,2},{4,3},{5,4},{6,5},{7,6},{8,7},{9,8},{10,9... | collective-permute-start | bytes 98312 | tf_op jit(solution)/shard_map/ppermute | solution.py:12
  65.7 17.6 %collective-permute-start.8 = (bf16[2,64,128]{2,1,0:T(8,128)(2,1)S(1)}, bf16[2,64,128]{2,1,0:T(8,128)(2,1)}, u32[]{:S(2)}, u32[]{:S(2)}) collective-permute-start(bf16[2,64,128]{2,1,0:T(8,128)(2,1)S(1)} %get-tuple-element.26), channel_id=1, source_target_pairs={{0,16},{16,32},{32,48},{48,64},{64,80},{80,96},{96,112},{112,128},... | collective-permute-start | bytes 98312 | tf_op jit(solution)/shard_map/ppermute | solution.py:12
  68.2 15.0 %collective-permute-start.9 = (bf16[2,64,128]{2,1,0:T(8,128)(2,1)S(1)}, bf16[2,64,128]{2,1,0:T(8,128)(2,1)}, u32[]{:S(2)}, u32[]{:S(2)}) collective-permute-start(bf16[2,64,128]{2,1,0:T(8,128)(2,1)S(1)} %get-tuple-element.29), channel_id=1, source_target_pairs={{0,496},{16,0},{32,16},{48,32},{64,48},{80,64},{96,80},{112,96},{1... | collective-permute-start | bytes 98312 | tf_op jit(solution)/shard_map/ppermute | solution.py:12
  86.4 22.9 %collective-permute-start.12 = (bf16[2,64,128]{2,1,0:T(8,128)(2,1)}, bf16[2,64,128]{2,1,0:T(8,128)(2,1)S(1)}, u32[]{:S(2)}, u32[]{:S(2)}) collective-permute-start(bf16[2,64,128]{2,1,0:T(8,128)(2,1)} %get-tuple-element.22), channel_id=1, source_target_pairs={{0,16},{16,32},{32,48},{48,64},{64,80},{80,96},{96,112},{112,128},... | collective-permute-start | bytes 98312 | tf_op jit(solution)/shard_map/ppermute | solution.py:12
  88.4 21.0 %collective-permute-start.13 = (bf16[2,64,128]{2,1,0:T(8,128)(2,1)}, bf16[2,64,128]{2,1,0:T(8,128)(2,1)S(1)}, u32[]{:S(2)}, u32[]{:S(2)}) collective-permute-start(bf16[2,64,128]{2,1,0:T(8,128)(2,1)} %get-tuple-element.25), channel_id=1, source_target_pairs={{0,496},{16,0},{32,16},{48,32},{64,48},{80,64},{96,80},{112,96},{1... | collective-permute-start | bytes 98312 | tf_op jit(solution)/shard_map/ppermute | solution.py:12
  95.3 14.0 %collective-permute-start.14 = (bf16[2,64,128]{2,1,0:T(8,128)(2,1)S(1)}, bf16[2,64,128]{2,1,0:T(8,128)(2,1)}, u32[]{:S(2)}, u32[]{:S(2)}) collective-permute-start(bf16[2,64,128]{2,1,0:T(8,128)(2,1)S(1)} %get-tuple-element.24), channel_id=1, source_target_pairs={{0,1},{1,2},{2,3},{3,4},{4,5},{5,6},{6,7},{7,8},{8,9},{9,10},{10,1... | collective-permute-start | bytes 98312 | tf_op jit(solution)/shard_map/ppermute | solution.py:12
  97.3 12.1 %collective-permute-start.15 = (bf16[2,64,128]{2,1,0:T(8,128)(2,1)S(1)}, bf16[2,64,128]{2,1,0:T(8,128)(2,1)}, u32[]{:S(2)}, u32[]{:S(2)}) collective-permute-start(bf16[2,64,128]{2,1,0:T(8,128)(2,1)S(1)} %get-tuple-element.23), channel_id=1, source_target_pairs={{0,15},{1,0},{2,1},{3,2},{4,3},{5,4},{6,5},{7,6},{8,7},{9,8},{10,9... | collective-permute-start | bytes 98312 | tf_op jit(solution)/shard_map/ppermute | solution.py:12
  112.5 23.5 %collective-permute-start.16 = (bf16[2,64,128]{2,1,0:T(8,128)(2,1)}, bf16[2,64,128]{2,1,0:T(8,128)(2,1)S(1)}, u32[]{:S(2)}, u32[]{:S(2)}) collective-permute-start(bf16[2,64,128]{2,1,0:T(8,128)(2,1)} %get-tuple-element.18), channel_id=1, source_target_pairs={{0,16},{16,32},{32,48},{48,64},{64,80},{80,96},{96,112},{112,128},... | collective-permute-start | bytes 98312 | tf_op jit(solution)/shard_map/ppermute | solution.py:12
  114.4 21.6 %collective-permute-start.17 = (bf16[2,64,128]{2,1,0:T(8,128)(2,1)}, bf16[2,64,128]{2,1,0:T(8,128)(2,1)S(1)}, u32[]{:S(2)}, u32[]{:S(2)}) collective-permute-start(bf16[2,64,128]{2,1,0:T(8,128)(2,1)} %get-tuple-element.21), channel_id=1, source_target_pairs={{0,496},{16,0},{32,16},{48,32},{64,48},{80,64},{96,80},{112,96},{1... | collective-permute-start | bytes 98312 | tf_op jit(solution)/shard_map/ppermute | solution.py:12
  122.0 14.0 %collective-permute-start.18 = (bf16[2,64,128]{2,1,0:T(8,128)(2,1)S(1)}, bf16[2,64,128]{2,1,0:T(8,128)(2,1)}, u32[]{:S(2)}, u32[]{:S(2)}) collective-permute-start(bf16[2,64,128]{2,1,0:T(8,128)(2,1)S(1)} %get-tuple-element.20), channel_id=1, source_target_pairs={{0,1},{1,2},{2,3},{3,4},{4,5},{5,6},{6,7},{7,8},{8,9},{9,10},{10,1... | collective-permute-start | bytes 98312 | tf_op jit(solution)/shard_map/ppermute | solution.py:12
  123.9 12.1 %collective-permute-start.19 = (bf16[2,64,128]{2,1,0:T(8,128)(2,1)S(1)}, bf16[2,64,128]{2,1,0:T(8,128)(2,1)}, u32[]{:S(2)}, u32[]{:S(2)}) collective-permute-start(bf16[2,64,128]{2,1,0:T(8,128)(2,1)S(1)} %get-tuple-element.19), channel_id=1, source_target_pairs={{0,15},{1,0},{2,1},{3,2},{4,3},{5,4},{6,5},{7,6},{8,7},{9,8},{10,9... | collective-permute-start | bytes 98312 | tf_op jit(solution)/shard_map/ppermute | solution.py:12
  134.7 15.9 %copy-start.7 = (f32[16,64,128]{2,1,0:T(8,128)}, f32[16,64,128]{2,1,0:T(8,128)S(1)}, u32[]{:S(2)}) copy-start(f32[16,64,128]{2,1,0:T(8,128)S(1)} %fusion.7) | copy-start | bytes 1572868
  139.2 23.4 %collective-permute-start.20 = (bf16[2,64,128]{2,1,0:T(8,128)(2,1)}, bf16[2,64,128]{2,1,0:T(8,128)(2,1)S(1)}, u32[]{:S(2)}, u32[]{:S(2)}) collective-permute-start(bf16[2,64,128]{2,1,0:T(8,128)(2,1)} %get-tuple-element.14), channel_id=1, source_target_pairs={{0,16},{16,32},{32,48},{48,64},{64,80},{80,96},{96,112},{112,128},... | collective-permute-start | bytes 98312 | tf_op jit(solution)/shard_map/ppermute | solution.py:12
  141.1 21.5 %collective-permute-start.21 = (bf16[2,64,128]{2,1,0:T(8,128)(2,1)}, bf16[2,64,128]{2,1,0:T(8,128)(2,1)S(1)}, u32[]{:S(2)}, u32[]{:S(2)}) collective-permute-start(bf16[2,64,128]{2,1,0:T(8,128)(2,1)} %get-tuple-element.17), channel_id=1, source_target_pairs={{0,496},{16,0},{32,16},{48,32},{64,48},{80,64},{96,80},{112,96},{1... | collective-permute-start | bytes 98312 | tf_op jit(solution)/shard_map/ppermute | solution.py:12
  148.7 14.0 %collective-permute-start.22 = (bf16[2,64,128]{2,1,0:T(8,128)(2,1)S(1)}, bf16[2,64,128]{2,1,0:T(8,128)(2,1)}, u32[]{:S(2)}, u32[]{:S(2)}) collective-permute-start(bf16[2,64,128]{2,1,0:T(8,128)(2,1)S(1)} %get-tuple-element.16), channel_id=1, source_target_pairs={{0,1},{1,2},{2,3},{3,4},{4,5},{5,6},{6,7},{7,8},{8,9},{9,10},{10,1... | collective-permute-start | bytes 98312 | tf_op jit(solution)/shard_map/ppermute | solution.py:12
  150.6 12.1 %collective-permute-start.23 = (bf16[2,64,128]{2,1,0:T(8,128)(2,1)S(1)}, bf16[2,64,128]{2,1,0:T(8,128)(2,1)}, u32[]{:S(2)}, u32[]{:S(2)}) collective-permute-start(bf16[2,64,128]{2,1,0:T(8,128)(2,1)S(1)} %get-tuple-element.15), channel_id=1, source_target_pairs={{0,15},{1,0},{2,1},{3,2},{4,3},{5,4},{6,5},{7,6},{8,7},{9,8},{10,9... | collective-permute-start | bytes 98312 | tf_op jit(solution)/shard_map/ppermute | solution.py:12
  165.9 23.5 %collective-permute-start.24 = (bf16[2,64,128]{2,1,0:T(8,128)(2,1)}, bf16[2,64,128]{2,1,0:T(8,128)(2,1)S(1)}, u32[]{:S(2)}, u32[]{:S(2)}) collective-permute-start(bf16[2,64,128]{2,1,0:T(8,128)(2,1)} %get-tuple-element.10), channel_id=1, source_target_pairs={{0,16},{16,32},{32,48},{48,64},{64,80},{80,96},{96,112},{112,128},... | collective-permute-start | bytes 98312 | tf_op jit(solution)/shard_map/ppermute | solution.py:12
  167.8 21.6 %collective-permute-start.25 = (bf16[2,64,128]{2,1,0:T(8,128)(2,1)}, bf16[2,64,128]{2,1,0:T(8,128)(2,1)S(1)}, u32[]{:S(2)}, u32[]{:S(2)}) collective-permute-start(bf16[2,64,128]{2,1,0:T(8,128)(2,1)} %get-tuple-element.13), channel_id=1, source_target_pairs={{0,496},{16,0},{32,16},{48,32},{64,48},{80,64},{96,80},{112,96},{1... | collective-permute-start | bytes 98312 | tf_op jit(solution)/shard_map/ppermute | solution.py:12
  175.3 14.0 %collective-permute-start.26 = (bf16[2,64,128]{2,1,0:T(8,128)(2,1)S(1)}, bf16[2,64,128]{2,1,0:T(8,128)(2,1)}, u32[]{:S(2)}, u32[]{:S(2)}) collective-permute-start(bf16[2,64,128]{2,1,0:T(8,128)(2,1)S(1)} %get-tuple-element.12), channel_id=1, source_target_pairs={{0,1},{1,2},{2,3},{3,4},{4,5},{5,6},{6,7},{7,8},{8,9},{9,10},{10,1... | collective-permute-start | bytes 98312 | tf_op jit(solution)/shard_map/ppermute | solution.py:12
  177.2 12.1 %collective-permute-start.27 = (bf16[2,64,128]{2,1,0:T(8,128)(2,1)S(1)}, bf16[2,64,128]{2,1,0:T(8,128)(2,1)}, u32[]{:S(2)}, u32[]{:S(2)}) collective-permute-start(bf16[2,64,128]{2,1,0:T(8,128)(2,1)S(1)} %get-tuple-element.11), channel_id=1, source_target_pairs={{0,15},{1,0},{2,1},{3,2},{4,3},{5,4},{6,5},{7,6},{8,7},{9,8},{10,9... | collective-permute-start | bytes 98312 | tf_op jit(solution)/shard_map/ppermute | solution.py:12
  188.0 15.9 %copy-start.9 = (f32[16,64,128]{2,1,0:T(8,128)}, f32[16,64,128]{2,1,0:T(8,128)S(1)}, u32[]{:S(2)}) copy-start(f32[16,64,128]{2,1,0:T(8,128)S(1)} %fusion.11) | copy-start | bytes 1572868
  192.5 23.6 %collective-permute-start.28 = (bf16[2,64,128]{2,1,0:T(8,128)(2,1)}, bf16[2,64,128]{2,1,0:T(8,128)(2,1)S(1)}, u32[]{:S(2)}, u32[]{:S(2)}) collective-permute-start(bf16[2,64,128]{2,1,0:T(8,128)(2,1)} %get-tuple-element.6), channel_id=1, source_target_pairs={{0,16},{16,32},{32,48},{48,64},{64,80},{80,96},{96,112},{112,128},... | collective-permute-start | bytes 98312 | tf_op jit(solution)/shard_map/ppermute | solution.py:12
  194.5 21.7 %collective-permute-start.29 = (bf16[2,64,128]{2,1,0:T(8,128)(2,1)}, bf16[2,64,128]{2,1,0:T(8,128)(2,1)S(1)}, u32[]{:S(2)}, u32[]{:S(2)}) collective-permute-start(bf16[2,64,128]{2,1,0:T(8,128)(2,1)} %get-tuple-element.9), channel_id=1, source_target_pairs={{0,496},{16,0},{32,16},{48,32},{64,48},{80,64},{96,80},{112,96},{1... | collective-permute-start | bytes 98312 | tf_op jit(solution)/shard_map/ppermute | solution.py:12
  202.0 14.2 %collective-permute-start.30 = (bf16[2,64,128]{2,1,0:T(8,128)(2,1)S(1)}, bf16[2,64,128]{2,1,0:T(8,128)(2,1)}, u32[]{:S(2)}, u32[]{:S(2)}) collective-permute-start(bf16[2,64,128]{2,1,0:T(8,128)(2,1)S(1)} %get-tuple-element.8), channel_id=1, source_target_pairs={{0,1},{1,2},{2,3},{3,4},{4,5},{5,6},{6,7},{7,8},{8,9},{9,10},{10,1... | collective-permute-start | bytes 98312 | tf_op jit(solution)/shard_map/ppermute | solution.py:12
  203.9 12.3 %collective-permute-start.31 = (bf16[2,64,128]{2,1,0:T(8,128)(2,1)S(1)}, bf16[2,64,128]{2,1,0:T(8,128)(2,1)}, u32[]{:S(2)}, u32[]{:S(2)}) collective-permute-start(bf16[2,64,128]{2,1,0:T(8,128)(2,1)S(1)} %get-tuple-element.7), channel_id=1, source_target_pairs={{0,15},{1,0},{2,1},{3,2},{4,3},{5,4},{6,5},{7,6},{8,7},{9,8},{10,9... | collective-permute-start | bytes 98312 | tf_op jit(solution)/shard_map/ppermute | solution.py:12
  219.4 18.2 %collective-permute-start.32 = (bf16[2,64,128]{2,1,0:T(8,128)(2,1)}, bf16[2,64,128]{2,1,0:T(8,128)(2,1)S(1)}, u32[]{:S(2)}, u32[]{:S(2)}) collective-permute-start(bf16[2,64,128]{2,1,0:T(8,128)(2,1)} %get-tuple-element.2), channel_id=1, source_target_pairs={{0,16},{16,32},{32,48},{48,64},{64,80},{80,96},{96,112},{112,128},... | collective-permute-start | bytes 98312 | tf_op jit(solution)/shard_map/ppermute | solution.py:12
  221.3 16.2 %collective-permute-start.33 = (bf16[2,64,128]{2,1,0:T(8,128)(2,1)}, bf16[2,64,128]{2,1,0:T(8,128)(2,1)S(1)}, u32[]{:S(2)}, u32[]{:S(2)}) collective-permute-start(bf16[2,64,128]{2,1,0:T(8,128)(2,1)} %get-tuple-element.5), channel_id=1, source_target_pairs={{0,496},{16,0},{32,16},{48,32},{64,48},{80,64},{96,80},{112,96},{1... | collective-permute-start | bytes 98312 | tf_op jit(solution)/shard_map/ppermute | solution.py:12
  228.8 8.7 %collective-permute-start.34 = (bf16[2,64,128]{2,1,0:T(8,128)(2,1)S(1)}, bf16[2,64,128]{2,1,0:T(8,128)(2,1)}, u32[]{:S(2)}, u32[]{:S(2)}) collective-permute-start(bf16[2,64,128]{2,1,0:T(8,128)(2,1)S(1)} %get-tuple-element.4), channel_id=1, source_target_pairs={{0,1},{1,2},{2,3},{3,4},{4,5},{5,6},{6,7},{7,8},{8,9},{9,10},{10,1... | collective-permute-start | bytes 98312 | tf_op jit(solution)/shard_map/ppermute | solution.py:12
  230.8 6.8 %collective-permute-start.35 = (bf16[2,64,128]{2,1,0:T(8,128)(2,1)S(1)}, bf16[2,64,128]{2,1,0:T(8,128)(2,1)}, u32[]{:S(2)}, u32[]{:S(2)}) collective-permute-start(bf16[2,64,128]{2,1,0:T(8,128)(2,1)S(1)} %get-tuple-element.3), channel_id=1, source_target_pairs={{0,15},{1,0},{2,1},{3,2},{4,3},{5,4},{6,5},{7,6},{8,7},{9,8},{10,9... | collective-permute-start | bytes 98312 | tf_op jit(solution)/shard_map/ppermute | solution.py:12
  240.7 4.7 %collective-permute-start.36 = (f32[64,64]{1,0:T(8,128)S(1)}, f32[64,64]{1,0:T(8,128)S(1)}, u32[]{:S(2)}, u32[]{:S(2)}) collective-permute-start(f32[64,64]{1,0:T(8,128)S(1)} %convolution_bitcast_fusion.9), channel_id=1, source_target_pairs={{0,1},{1,0},{2,3},{3,2},{4,5},{5,4},{6,7},{7,6},{8,9},{9,8},{10,11... | collective-permute-start | bytes 49160 | tf_op jit(solution)/shard_map/ppermute | solution.py:20
  245.3 5.8 %collective-permute-start.37 = (f32[64,64]{1,0:T(8,128)S(1)}, f32[64,64]{1,0:T(8,128)S(1)}, u32[]{:S(2)}, u32[]{:S(2)}) collective-permute-start(f32[64,64]{1,0:T(8,128)S(1)} %add.150), channel_id=1, source_target_pairs={{0,2},{1,3},{2,0},{3,1},{4,6},{5,7},{6,4},{7,5},{8,10},{9,11},{10,... | collective-permute-start | bytes 49160 | tf_op jit(solution)/shard_map/ppermute | solution.py:20
  251.1 9.1 %collective-permute-start.38 = (f32[64,64]{1,0:T(8,128)S(1)}, f32[64,64]{1,0:T(8,128)S(1)}, u32[]{:S(2)}, u32[]{:S(2)}) collective-permute-start(f32[64,64]{1,0:T(8,128)S(1)} %add.151), channel_id=1, source_target_pairs={{0,4},{1,5},{2,6},{3,7},{4,0},{5,1},{6,2},{7,3},{8,12},{9,13},{10,... | collective-permute-start | bytes 49160 | tf_op jit(solution)/shard_map/ppermute | solution.py:20
  260.2 13.4 %collective-permute-start.39 = (f32[64,64]{1,0:T(8,128)S(1)}, f32[64,64]{1,0:T(8,128)S(1)}, u32[]{:S(2)}, u32[]{:S(2)}) collective-permute-start(f32[64,64]{1,0:T(8,128)S(1)} %add.152), channel_id=1, source_target_pairs={{0,8},{1,9},{2,10},{3,11},{4,12},{5,13},{6,14},{7,15},{8,0},{9,1},... | collective-permute-start | bytes 49160 | tf_op jit(solution)/shard_map/ppermute | solution.py:20
  273.6 12.2 %collective-permute-start.40 = (f32[64,64]{1,0:T(8,128)S(1)}, f32[64,64]{1,0:T(8,128)S(1)}, u32[]{:S(2)}, u32[]{:S(2)}) collective-permute-start(f32[64,64]{1,0:T(8,128)S(1)} %add.153), channel_id=1, source_target_pairs={{0,16},{16,0},{32,48},{48,32},{64,80},{80,64},{96,112},{112,96},{1... | collective-permute-start | bytes 49160 | tf_op jit(solution)/shard_map/ppermute | solution.py:20
  285.8 4.6 %collective-permute-start.41 = (f32[64,64]{1,0:T(8,128)S(1)}, f32[64,64]{1,0:T(8,128)S(1)}, u32[]{:S(2)}, u32[]{:S(2)}) collective-permute-start(f32[64,64]{1,0:T(8,128)S(1)} %add.154), channel_id=1, source_target_pairs={{0,32},{16,48},{32,0},{48,16},{64,96},{80,112},{96,64},{112,80},{1... | collective-permute-start | bytes 49160 | tf_op jit(solution)/shard_map/ppermute | solution.py:20
  290.5 6.2 %collective-permute-start.42 = (f32[64,64]{1,0:T(8,128)S(1)}, f32[64,64]{1,0:T(8,128)S(1)}, u32[]{:S(2)}, u32[]{:S(2)}) collective-permute-start(f32[64,64]{1,0:T(8,128)S(1)} %add.155), channel_id=1, source_target_pairs={{0,64},{16,80},{32,96},{48,112},{64,0},{80,16},{96,32},{112,48},{1... | collective-permute-start | bytes 49160 | tf_op jit(solution)/shard_map/ppermute | solution.py:20
  296.6 4.6 %collective-permute-start.43 = (f32[64,64]{1,0:T(8,128)S(1)}, f32[64,64]{1,0:T(8,128)S(1)}, u32[]{:S(2)}, u32[]{:S(2)}) collective-permute-start(f32[64,64]{1,0:T(8,128)S(1)} %add.156), channel_id=1, source_target_pairs={{0,128},{16,144},{32,160},{48,176},{64,192},{80,208},{96,224},{112... | collective-permute-start | bytes 49160 | tf_op jit(solution)/shard_map/ppermute | solution.py:20
  301.3 6.2 %collective-permute-start.44 = (f32[64,64]{1,0:T(8,128)S(1)}, f32[64,64]{1,0:T(8,128)S(1)}, u32[]{:S(2)}, u32[]{:S(2)}) collective-permute-start(f32[64,64]{1,0:T(8,128)S(1)} %add.157), channel_id=1, source_target_pairs={{0,256},{16,272},{32,288},{48,304},{64,320},{80,336},{96,352},{112... | collective-permute-start | bytes 49160 | tf_op jit(solution)/shard_map/ppermute | solution.py:20
  (9 other events, 87.5 us)

commit v4 on v3

--- a/solution.py
+++ b/solution.py
@@ -2,6 +2,7 @@
 import jax.numpy as jnp
 from jax import lax
 from jax.sharding import PartitionSpec as P
+
 
 DEG = 9
 
@@ -22,14 +23,20 @@
     return value
 
 
-def exchange(outgoing, per_list):
+def exchange(outgoing, per_list, fillers=()):
     pieces = [outgoing[d * per_list:(d + 1) * per_list] for d in range(4)]
-    return [
-        from_behind(pieces[0], "px", 1),
-        from_behind(pieces[1], "px", -1),
-        from_behind(pieces[2], "py", 1),
-        from_behind(pieces[3], "py", -1),
-    ]
+    routes = [("px", 1), ("px", -1), ("py", 1), ("py", -1)]
+    received = []
+    carried = None
+    for d, (axis, steps) in enumerate(routes):
+        piece = pieces[d]
+        if d > 0 and d - 1 < len(fillers):
+            carried = fillers[d - 1](carried)
+            piece, carried = lax.optimization_barrier((piece, carried))
+        received.append(from_behind(piece, axis, steps))
+    for filler in fillers[3:]:
+        carried = filler(carried)
+    return received, carried
 
 
 def halo_term(pieces, chooser, halo):
@@ -55,23 +62,40 @@
     whole_chooser = jax.nn.one_hot(halo_slot, slots, dtype=jnp.bfloat16)
 
     rounded = start_vecs.astype(jnp.bfloat16)
-    received = exchange(rounded[picks], per_list)
+    received, _ = exchange(rounded[picks], per_list)
     local_part = local_term(rounded, local_tiles, local_cols)
     edge_next = local_part[picks] + halo_term(received, edge_chooser, edge_halo)
-    received_next = exchange(edge_next.astype(jnp.bfloat16), per_list)
     older = start_vecs
-    current = local_part + halo_term(received, whole_chooser, halo_tiles)
-    received = received_next
     for step in range(1, DEG):
-        rounded = current.astype(jnp.bfloat16)
-        local_part = 2.0 * local_term(rounded, local_tiles, local_cols) - older
-        if step < DEG - 1:
-            edge_next = local_part[picks] + 2.0 * halo_term(received, edge_chooser, edge_halo)
-            received_next = exchange(edge_next.astype(jnp.bfloat16), per_list)
-        newer = local_part + 2.0 * halo_term(received, whole_chooser, halo_tiles)
-        older, current = current, newer
-        if step < DEG - 1:
-            received = received_next
+      halo_scale = 1.0 if step == 1 else 2.0
+      state = (older, local_part, received)
+
+      def whole_vector(carried, state=state, halo_scale=halo_scale):
+          _, local_vec, blocks = state
+          return local_vec + halo_scale * halo_term(blocks, whole_chooser, halo_tiles)
+
+      def gathered_blocks(carried):
+          return carried, carried.astype(jnp.bfloat16)[local_cols]
+
+      def next_local(carried, older_vec=older):
+          current_vec, gathered = carried
+          product = jnp.einsum(
+              "rtkj,rtij->rki", gathered, local_tiles, preferred_element_type=jnp.float32
+          )
+          return current_vec, 2.0 * product - older_vec
+
+      def next_edge(carried):
+          current_vec, local_vec = carried
+          return current_vec, local_vec, local_vec[picks]
+
+      received_next, (current, local_part, edge_local) = exchange(
+          edge_next.astype(jnp.bfloat16), per_list,
+          (whole_vector, gathered_blocks, next_local, next_edge),
+      )
+      older = current
+      received = received_next
+      edge_next = edge_local + 2.0 * halo_term(received, edge_chooser, edge_halo)
+    current = local_part + 2.0 * halo_term(received, whole_chooser, halo_tiles)
 
     total_rows = current.shape[0] * current.shape[2] * lax.axis_size("px") * lax.axis_size("py")
     partial_gram = jnp.einsum("rkj,rlj->kl", current, current, precision=lax.Precision.HIGHEST)

time: 315 us -> 300 us (0.952)
  matrix products: 50.1 us -> 32.9 us
    dot_general x17, matrix products: 26.9 us -> 8.37 us  [halo_term(): jnp.einsum('rkj,rij->rki', chosen.astype(jnp.bfloat16), halo, preferred_e...]
    dot_general x0 -> x8, matrix products: none -> 17.6 us  [next_local(): jnp.einsum('rtkj,rtij->rki', gathered, local_tiles, preferred_element_typ...]
    dot_general x9 -> x1, matrix products: 18.3 us -> 2.1 us  [local_term(): jnp.einsum('rtkj,rtij->rki', rounded[cols], tiles, preferred_element_type...]
    gather x8 -> x16, local copies, waits for them, and re-layouts: 9.45 us -> 23.1 us  [the longest x8 13.7 us: gathered_blocks(): return (carried, carried.astype(jnp.bfloat16)[local_cols])]
    gather x9 -> x1, local copies, waits for them, and re-layouts: 15.4 us -> 1.71 us  [local_term(): rounded[cols]]
  transfers between devices with their start and end apart: 45 -> 45, of which waited for: 9 -> 10; matrix products, arithmetic and copies ran while one was open for 20% -> 5% of each run, Pallas kernels for 0% -> 0%
where the time goes in v4:
time: 300 us; the launch traced here: 296 us
  starting transfers between devices  182 us (61%)
  local copies, waits for them, and re-layouts  35.2 us (12%)
  waiting for transfers between devices  33.2 us (11%)
  matrix products  32.9 us (11%)
  other arithmetic  10.5 us (4%)
    ppermute x36, starting transfers between devices, from_behind(): return lax.ppermute(value, axis, pairs)  147 us
    ppermute x9, starting transfers between devices, butterfly_sum(): value = value + lax.ppermute(value, axis, pairs)  35.1 us
    ppermute x9, waiting for transfers between devices, butterfly_sum(): value = value + lax.ppermute(value, axis, pairs)  31.8 us
    dot_general x8, matrix products, next_local(): jnp.einsum('rtkj,rtij->rki', gathered, local_tiles, preferred_element_typ...  17.6 us
    gather x8, local copies, waits for them, and re-layouts, gathered_blocks(): return (carried, carried.astype(jnp.bfloat16)[local_cols])  13.7 us
    gather x7, local copies, waits for them, and re-layouts, next_edge(): return (current_vec, local_vec, local_vec[picks])  8.84 us
    dot_general x17, matrix products, halo_term(): jnp.einsum('rkj,rij->rki', chosen.astype(jnp.bfloat16), halo, preferred_e...  8.37 us
    concatenate x9, other arithmetic, halo_term(): received = jnp.concatenate(pieces, axis=0)  6.74 us
  transfers between devices with their start and end apart: 45, of which 10 were waited for; matrix products, arithmetic and copies ran while one was open for 5% of the time, Pallas kernels for 0%

profile of v4, /device:TPU:1, one launch (start us, length us, event | category | flops | bytes accessed | tf_op | source)
XLA Modules:
  0.0 295.8 jit_solution(12107861910513717481)
XLA Ops:
  4.0 4.5 %collective-permute-start = (bf16[2,64,128]{2,1,0:T(8,128)(2,1)}, bf16[2,64,128]{2,1,0:T(8,128)(2,1)S(1)}, u32[]{:S(2)}, u32[]{:S(2)}) collective-permute-start(bf16[2,64,128]{2,1,0:T(8,128)(2,1)} %get-tuple-element.158), channel_id=1, source_target_pairs={{0,16},{16,32},{32,48},{48,64},{64,80},{80,96},{96,112},{112,128},... | collective-permute-start | bytes 98312 | tf_op jit(solution)/shard_map/ppermute | solution.py:13
  8.4 6.2 %collective-permute-start.1 = (bf16[2,64,128]{2,1,0:T(8,128)(2,1)}, bf16[2,64,128]{2,1,0:T(8,128)(2,1)S(1)}, u32[]{:S(2)}, u32[]{:S(2)}) collective-permute-start(bf16[2,64,128]{2,1,0:T(8,128)(2,1)} %get-tuple-element.160), channel_id=1, source_target_pairs={{0,496},{16,0},{32,16},{48,32},{64,48},{80,64},{96,80},{112,96},{1... | collective-permute-start | bytes 98312 | tf_op jit(solution)/shard_map/ppermute | solution.py:13
  14.6 1.9 collective-permute-start.2
  16.6 6.9 %collective-permute-start.3 = (bf16[2,64,128]{2,1,0:T(8,128)(2,1)S(1)}, bf16[2,64,128]{2,1,0:T(8,128)(2,1)}, u32[]{:S(2)}, u32[]{:S(2)}) collective-permute-start(bf16[2,64,128]{2,1,0:T(8,128)(2,1)S(1)} %get-tuple-element.161), channel_id=1, source_target_pairs={{0,15},{1,0},{2,1},{3,2},{4,3},{5,4},{6,5},{7,6},{8,7},{9,8},{10,9... | collective-permute-start | bytes 98312 | tf_op jit(solution)/shard_map/ppermute | solution.py:13
  26.0 2.1 convolution_bitcast_fusion.8
  36.9 2.2 fusion.1
  39.1 3.4 %collective-permute-start.7 = (bf16[2,64,128]{2,1,0:T(8,128)(2,1)}, bf16[2,64,128]{2,1,0:T(8,128)(2,1)S(1)}, u32[]{:S(2)}, u32[]{:S(2)}) collective-permute-start(bf16[2,64,128]{2,1,0:T(8,128)(2,1)} %get-tuple-element.70), channel_id=1, source_target_pairs={{0,15},{1,0},{2,1},{3,2},{4,3},{5,4},{6,5},{7,6},{8,7},{9,8},{10,9... | collective-permute-start | bytes 98312 | tf_op jit(solution)/shard_map/ppermute | solution.py:13
  42.5 1.9 collective-permute-start.6
  44.4 6.7 %collective-permute-start.5 = (bf16[2,64,128]{2,1,0:T(8,128)(2,1)S(1)}, bf16[2,64,128]{2,1,0:T(8,128)(2,1)}, u32[]{:S(2)}, u32[]{:S(2)}) collective-permute-start(bf16[2,64,128]{2,1,0:T(8,128)(2,1)S(1)} %get-tuple-element.68), channel_id=1, source_target_pairs={{0,496},{16,0},{32,16},{48,32},{64,48},{80,64},{96,80},{112,96},{1... | collective-permute-start | bytes 98312 | tf_op jit(solution)/shard_map/ppermute | solution.py:13
  58.9 2.2 fusion.3
  61.1 4.8 %collective-permute-start.11 = (bf16[2,64,128]{2,1,0:T(8,128)(2,1)}, bf16[2,64,128]{2,1,0:T(8,128)(2,1)S(1)}, u32[]{:S(2)}, u32[]{:S(2)}) collective-permute-start(bf16[2,64,128]{2,1,0:T(8,128)(2,1)} %get-tuple-element.78), channel_id=1, source_target_pairs={{0,15},{1,0},{2,1},{3,2},{4,3},{5,4},{6,5},{7,6},{8,7},{9,8},{10,9... | collective-permute-start | bytes 98312 | tf_op jit(solution)/shard_map/ppermute | solution.py:13
  65.9 1.9 collective-permute-start.10
  67.8 7.6 %collective-permute-start.9 = (bf16[2,64,128]{2,1,0:T(8,128)(2,1)S(1)}, bf16[2,64,128]{2,1,0:T(8,128)(2,1)}, u32[]{:S(2)}, u32[]{:S(2)}) collective-permute-start(bf16[2,64,128]{2,1,0:T(8,128)(2,1)S(1)} %get-tuple-element.76), channel_id=1, source_target_pairs={{0,496},{16,0},{32,16},{48,32},{64,48},{80,64},{96,80},{112,96},{1... | collective-permute-start | bytes 98312 | tf_op jit(solution)/shard_map/ppermute | solution.py:13
  75.5 1.9 collective-permute-start.8
  83.2 2.2 fusion.5
  85.4 4.8 %collective-permute-start.15 = (bf16[2,64,128]{2,1,0:T(8,128)(2,1)}, bf16[2,64,128]{2,1,0:T(8,128)(2,1)S(1)}, u32[]{:S(2)}, u32[]{:S(2)}) collective-permute-start(bf16[2,64,128]{2,1,0:T(8,128)(2,1)} %get-tuple-element.86), channel_id=1, source_target_pairs={{0,15},{1,0},{2,1},{3,2},{4,3},{5,4},{6,5},{7,6},{8,7},{9,8},{10,9... | collective-permute-start | bytes 98312 | tf_op jit(solution)/shard_map/ppermute | solution.py:13
  90.3 1.9 collective-permute-start.14
  92.2 7.6 %collective-permute-start.13 = (bf16[2,64,128]{2,1,0:T(8,128)(2,1)S(1)}, bf16[2,64,128]{2,1,0:T(8,128)(2,1)}, u32[]{:S(2)}, u32[]{:S(2)}) collective-permute-start(bf16[2,64,128]{2,1,0:T(8,128)(2,1)S(1)} %get-tuple-element.84), channel_id=1, source_target_pairs={{0,496},{16,0},{32,16},{48,32},{64,48},{80,64},{96,80},{112,96},{1... | collective-permute-start | bytes 98312 | tf_op jit(solution)/shard_map/ppermute | solution.py:13
  99.8 1.9 collective-permute-start.12
  107.5 2.2 fusion.7
  109.7 4.9 %collective-permute-start.19 = (bf16[2,64,128]{2,1,0:T(8,128)(2,1)}, bf16[2,64,128]{2,1,0:T(8,128)(2,1)S(1)}, u32[]{:S(2)}, u32[]{:S(2)}) collective-permute-start(bf16[2,64,128]{2,1,0:T(8,128)(2,1)} %get-tuple-element.94), channel_id=1, source_target_pairs={{0,15},{1,0},{2,1},{3,2},{4,3},{5,4},{6,5},{7,6},{8,7},{9,8},{10,9... | collective-permute-start | bytes 98312 | tf_op jit(solution)/shard_map/ppermute | solution.py:13
  114.6 1.9 collective-permute-start.18
  116.5 7.6 %collective-permute-start.17 = (bf16[2,64,128]{2,1,0:T(8,128)(2,1)S(1)}, bf16[2,64,128]{2,1,0:T(8,128)(2,1)}, u32[]{:S(2)}, u32[]{:S(2)}) collective-permute-start(bf16[2,64,128]{2,1,0:T(8,128)(2,1)S(1)} %get-tuple-element.92), channel_id=1, source_target_pairs={{0,496},{16,0},{32,16},{48,32},{64,48},{80,64},{96,80},{112,96},{1... | collective-permute-start | bytes 98312 | tf_op jit(solution)/shard_map/ppermute | solution.py:13
  124.1 1.9 collective-permute-start.16
  131.9 2.2 fusion.9
  134.1 4.8 %collective-permute-start.23 = (bf16[2,64,128]{2,1,0:T(8,128)(2,1)}, bf16[2,64,128]{2,1,0:T(8,128)(2,1)S(1)}, u32[]{:S(2)}, u32[]{:S(2)}) collective-permute-start(bf16[2,64,128]{2,1,0:T(8,128)(2,1)} %get-tuple-element.102), channel_id=1, source_target_pairs={{0,15},{1,0},{2,1},{3,2},{4,3},{5,4},{6,5},{7,6},{8,7},{9,8},{10,9... | collective-permute-start | bytes 98312 | tf_op jit(solution)/shard_map/ppermute | solution.py:13
  140.9 7.6 %collective-permute-start.21 = (bf16[2,64,128]{2,1,0:T(8,128)(2,1)S(1)}, bf16[2,64,128]{2,1,0:T(8,128)(2,1)}, u32[]{:S(2)}, u32[]{:S(2)}) collective-permute-start(bf16[2,64,128]{2,1,0:T(8,128)(2,1)S(1)} %get-tuple-element.100), channel_id=1, source_target_pairs={{0,496},{16,0},{32,16},{48,32},{64,48},{80,64},{96,80},{112,96},{1... | collective-permute-start | bytes 98312 | tf_op jit(solution)/shard_map/ppermute | solution.py:13
  156.2 2.2 fusion.11
  158.4 4.9 %collective-permute-start.27 = (bf16[2,64,128]{2,1,0:T(8,128)(2,1)}, bf16[2,64,128]{2,1,0:T(8,128)(2,1)S(1)}, u32[]{:S(2)}, u32[]{:S(2)}) collective-permute-start(bf16[2,64,128]{2,1,0:T(8,128)(2,1)} %get-tuple-element.110), channel_id=1, source_target_pairs={{0,15},{1,0},{2,1},{3,2},{4,3},{5,4},{6,5},{7,6},{8,7},{9,8},{10,9... | collective-permute-start | bytes 98312 | tf_op jit(solution)/shard_map/ppermute | solution.py:13
  165.2 7.6 %collective-permute-start.25 = (bf16[2,64,128]{2,1,0:T(8,128)(2,1)S(1)}, bf16[2,64,128]{2,1,0:T(8,128)(2,1)}, u32[]{:S(2)}, u32[]{:S(2)}) collective-permute-start(bf16[2,64,128]{2,1,0:T(8,128)(2,1)S(1)} %get-tuple-element.108), channel_id=1, source_target_pairs={{0,496},{16,0},{32,16},{48,32},{64,48},{80,64},{96,80},{112,96},{1... | collective-permute-start | bytes 98312 | tf_op jit(solution)/shard_map/ppermute | solution.py:13
  172.8 2.1 collective-permute-start.24
  180.7 2.2 fusion.13
  182.9 4.8 %collective-permute-start.31 = (bf16[2,64,128]{2,1,0:T(8,128)(2,1)}, bf16[2,64,128]{2,1,0:T(8,128)(2,1)S(1)}, u32[]{:S(2)}, u32[]{:S(2)}) collective-permute-start(bf16[2,64,128]{2,1,0:T(8,128)(2,1)} %get-tuple-element.118), channel_id=1, source_target_pairs={{0,15},{1,0},{2,1},{3,2},{4,3},{5,4},{6,5},{7,6},{8,7},{9,8},{10,9... | collective-permute-start | bytes 98312 | tf_op jit(solution)/shard_map/ppermute | solution.py:13
  189.7 7.4 %collective-permute-start.29 = (bf16[2,64,128]{2,1,0:T(8,128)(2,1)S(1)}, bf16[2,64,128]{2,1,0:T(8,128)(2,1)}, u32[]{:S(2)}, u32[]{:S(2)}) collective-permute-start(bf16[2,64,128]{2,1,0:T(8,128)(2,1)S(1)} %get-tuple-element.116), channel_id=1, source_target_pairs={{0,496},{16,0},{32,16},{48,32},{64,48},{80,64},{96,80},{112,96},{1... | collective-permute-start | bytes 98312 | tf_op jit(solution)/shard_map/ppermute | solution.py:13
  205.3 2.2 fusion.15
  207.5 4.9 %collective-permute-start.35 = (bf16[2,64,128]{2,1,0:T(8,128)(2,1)S(1)}, bf16[2,64,128]{2,1,0:T(8,128)(2,1)S(1)}, u32[]{:S(2)}, u32[]{:S(2)}) collective-permute-start(bf16[2,64,128]{2,1,0:T(8,128)(2,1)S(1)} %get-tuple-element.125), channel_id=1, source_target_pairs={{0,15},{1,0},{2,1},{3,2},{4,3},{5,4},{6,5},{7,6},{8,7},{9,8},{10,9... | collective-permute-start | bytes 98312 | tf_op jit(solution)/shard_map/ppermute | solution.py:13
  214.3 7.6 %collective-permute-start.33 = (bf16[2,64,128]{2,1,0:T(8,128)(2,1)S(1)}, bf16[2,64,128]{2,1,0:T(8,128)(2,1)S(1)}, u32[]{:S(2)}, u32[]{:S(2)}) collective-permute-start(bf16[2,64,128]{2,1,0:T(8,128)(2,1)S(1)} %get-tuple-element.123), channel_id=1, source_target_pairs={{0,496},{16,0},{32,16},{48,32},{64,48},{80,64},{96,80},{112,96},{1... | collective-permute-start | bytes 98312 | tf_op jit(solution)/shard_map/ppermute | solution.py:13
  228.2 2.7 collective-permute-done.36
  232.9 3.7 %collective-permute-done.37 = f32[64,64]{1,0:T(8,128)S(1)} collective-permute-done((f32[64,64]{1,0:T(8,128)S(1)}, f32[64,64]{1,0:T(8,128)S(1)}, u32[]{:S(2)}, u32[]{:S(2)}) %collective-permute-start.37) | collective-permute-done | bytes 16416 | tf_op jit(solution)/shard_map/ppermute | solution.py:21
  236.6 4.4 %collective-permute-start.38 = (f32[64,64]{1,0:T(8,128)S(1)}, f32[64,64]{1,0:T(8,128)S(1)}, u32[]{:S(2)}, u32[]{:S(2)}) collective-permute-start(f32[64,64]{1,0:T(8,128)S(1)} %add.151), channel_id=1, source_target_pairs={{0,4},{1,5},{2,6},{3,7},{4,0},{5,1},{6,2},{7,3},{8,12},{9,13},{10,... | collective-permute-start | bytes 49160 | tf_op jit(solution)/shard_map/ppermute | solution.py:21
  241.0 4.3 %collective-permute-done.38 = f32[64,64]{1,0:T(8,128)S(1)} collective-permute-done((f32[64,64]{1,0:T(8,128)S(1)}, f32[64,64]{1,0:T(8,128)S(1)}, u32[]{:S(2)}, u32[]{:S(2)}) %collective-permute-start.38) | collective-permute-done | bytes 16416 | tf_op jit(solution)/shard_map/ppermute | solution.py:21
  245.4 7.0 %collective-permute-start.39 = (f32[64,64]{1,0:T(8,128)S(1)}, f32[64,64]{1,0:T(8,128)S(1)}, u32[]{:S(2)}, u32[]{:S(2)}) collective-permute-start(f32[64,64]{1,0:T(8,128)S(1)} %add.152), channel_id=1, source_target_pairs={{0,8},{1,9},{2,10},{3,11},{4,12},{5,13},{6,14},{7,15},{8,0},{9,1},... | collective-permute-start | bytes 49160 | tf_op jit(solution)/shard_map/ppermute | solution.py:21
  252.4 6.3 %collective-permute-done.39 = f32[64,64]{1,0:T(8,128)S(1)} collective-permute-done((f32[64,64]{1,0:T(8,128)S(1)}, f32[64,64]{1,0:T(8,128)S(1)}, u32[]{:S(2)}, u32[]{:S(2)}) %collective-permute-start.39) | collective-permute-done | bytes 16416 | tf_op jit(solution)/shard_map/ppermute | solution.py:21
  258.7 12.2 %collective-permute-start.40 = (f32[64,64]{1,0:T(8,128)S(1)}, f32[64,64]{1,0:T(8,128)S(1)}, u32[]{:S(2)}, u32[]{:S(2)}) collective-permute-start(f32[64,64]{1,0:T(8,128)S(1)} %add.153), channel_id=1, source_target_pairs={{0,16},{16,0},{32,48},{48,32},{64,80},{80,64},{96,112},{112,96},{1... | collective-permute-start | bytes 49160 | tf_op jit(solution)/shard_map/ppermute | solution.py:21
  273.7 2.7 collective-permute-done.41
  278.3 4.2 %collective-permute-done.42 = f32[64,64]{1,0:T(8,128)S(1)} collective-permute-done((f32[64,64]{1,0:T(8,128)S(1)}, f32[64,64]{1,0:T(8,128)S(1)}, u32[]{:S(2)}, u32[]{:S(2)}) %collective-permute-start.42) | collective-permute-done | bytes 16416 | tf_op jit(solution)/shard_map/ppermute | solution.py:21
  284.5 2.7 collective-permute-done.43
  289.2 4.2 %collective-permute-done.44 = f32[64,64]{1,0:T(8,128)S(1)} collective-permute-done((f32[64,64]{1,0:T(8,128)S(1)}, f32[64,64]{1,0:T(8,128)S(1)}, u32[]{:S(2)}, u32[]{:S(2)}) %collective-permute-start.44) | collective-permute-done | bytes 16416 | tf_op jit(solution)/shard_map/ppermute | solution.py:21
  (190 shorter events, 87.9 us)
Async XLA Ops:
  0.6 25.4 %copy-start = (bf16[16,4,128,128]{3,2,1,0:T(8,128)(2,1)S(1)}, bf16[16,4,128,128]{3,2,1,0:T(8,128)(2,1)}, u32[]{:S(2)}) copy-start(bf16[16,4,128,128]{3,2,1,0:T(8,128)(2,1)} %param.7) | copy-start | bytes 6291460
  4.0 26.7 %collective-permute-start = (bf16[2,64,128]{2,1,0:T(8,128)(2,1)}, bf16[2,64,128]{2,1,0:T(8,128)(2,1)S(1)}, u32[]{:S(2)}, u32[]{:S(2)}) collective-permute-start(bf16[2,64,128]{2,1,0:T(8,128)(2,1)} %get-tuple-element.158), channel_id=1, source_target_pairs={{0,16},{16,32},{32,48},{48,64},{64,80},{80,96},{96,112},{112,128},... | collective-permute-start | bytes 98312 | tf_op jit(solution)/shard_map/ppermute | solution.py:13
  8.4 22.2 %collective-permute-start.1 = (bf16[2,64,128]{2,1,0:T(8,128)(2,1)}, bf16[2,64,128]{2,1,0:T(8,128)(2,1)S(1)}, u32[]{:S(2)}, u32[]{:S(2)}) collective-permute-start(bf16[2,64,128]{2,1,0:T(8,128)(2,1)} %get-tuple-element.160), channel_id=1, source_target_pairs={{0,496},{16,0},{32,16},{48,32},{64,48},{80,64},{96,80},{112,96},{1... | collective-permute-start | bytes 98312 | tf_op jit(solution)/shard_map/ppermute | solution.py:13
  14.6 16.1 %collective-permute-start.2 = (bf16[2,64,128]{2,1,0:T(8,128)(2,1)S(1)}, bf16[2,64,128]{2,1,0:T(8,128)(2,1)}, u32[]{:S(2)}, u32[]{:S(2)}) collective-permute-start(bf16[2,64,128]{2,1,0:T(8,128)(2,1)S(1)} %get-tuple-element.159), channel_id=1, source_target_pairs={{0,1},{1,2},{2,3},{3,4},{4,5},{5,6},{6,7},{7,8},{8,9},{9,10},{10,1... | collective-permute-start | bytes 98312 | tf_op jit(solution)/shard_map/ppermute | solution.py:13
  16.6 14.2 %collective-permute-start.3 = (bf16[2,64,128]{2,1,0:T(8,128)(2,1)S(1)}, bf16[2,64,128]{2,1,0:T(8,128)(2,1)}, u32[]{:S(2)}, u32[]{:S(2)}) collective-permute-start(bf16[2,64,128]{2,1,0:T(8,128)(2,1)S(1)} %get-tuple-element.161), channel_id=1, source_target_pairs={{0,15},{1,0},{2,1},{3,2},{4,3},{5,4},{6,5},{7,6},{8,7},{9,8},{10,9... | collective-permute-start | bytes 98312 | tf_op jit(solution)/shard_map/ppermute | solution.py:13
  26.0 4.0 %copy-start.2 = (bf16[16,128,128]{2,1,0:T(8,128)(2,1)S(1)}, bf16[16,128,128]{2,1,0:T(8,128)(2,1)}, u32[]{:S(2)}) copy-start(bf16[16,128,128]{2,1,0:T(8,128)(2,1)} %param.9) | copy-start | bytes 1572868
  39.1 15.2 %collective-permute-start.7 = (bf16[2,64,128]{2,1,0:T(8,128)(2,1)}, bf16[2,64,128]{2,1,0:T(8,128)(2,1)S(1)}, u32[]{:S(2)}, u32[]{:S(2)}) collective-permute-start(bf16[2,64,128]{2,1,0:T(8,128)(2,1)} %get-tuple-element.70), channel_id=1, source_target_pairs={{0,15},{1,0},{2,1},{3,2},{4,3},{5,4},{6,5},{7,6},{8,7},{9,8},{10,9... | collective-permute-start | bytes 98312 | tf_op jit(solution)/shard_map/ppermute | solution.py:13
  42.5 11.8 %collective-permute-start.6 = (bf16[2,64,128]{2,1,0:T(8,128)(2,1)S(1)}, bf16[2,64,128]{2,1,0:T(8,128)(2,1)}, u32[]{:S(2)}, u32[]{:S(2)}) collective-permute-start(bf16[2,64,128]{2,1,0:T(8,128)(2,1)S(1)} %get-tuple-element.69), channel_id=1, source_target_pairs={{0,1},{1,2},{2,3},{3,4},{4,5},{5,6},{6,7},{7,8},{8,9},{9,10},{10,1... | collective-permute-start | bytes 98312 | tf_op jit(solution)/shard_map/ppermute | solution.py:13
  44.4 9.9 %collective-permute-start.5 = (bf16[2,64,128]{2,1,0:T(8,128)(2,1)S(1)}, bf16[2,64,128]{2,1,0:T(8,128)(2,1)}, u32[]{:S(2)}, u32[]{:S(2)}) collective-permute-start(bf16[2,64,128]{2,1,0:T(8,128)(2,1)S(1)} %get-tuple-element.68), channel_id=1, source_target_pairs={{0,496},{16,0},{32,16},{48,32},{64,48},{80,64},{96,80},{112,96},{1... | collective-permute-start | bytes 98312 | tf_op jit(solution)/shard_map/ppermute | solution.py:13
  51.1 3.2 %collective-permute-start.4 = (bf16[2,64,128]{2,1,0:T(8,128)(2,1)S(1)}, bf16[2,64,128]{2,1,0:T(8,128)(2,1)}, u32[]{:S(2)}, u32[]{:S(2)}) collective-permute-start(bf16[2,64,128]{2,1,0:T(8,128)(2,1)S(1)} %get-tuple-element.154), channel_id=1, source_target_pairs={{0,16},{16,32},{32,48},{48,64},{64,80},{80,96},{96,112},{112,128},... | collective-permute-start | bytes 98312 | tf_op jit(solution)/shard_map/ppermute | solution.py:13
  61.1 17.6 %collective-permute-start.11 = (bf16[2,64,128]{2,1,0:T(8,128)(2,1)}, bf16[2,64,128]{2,1,0:T(8,128)(2,1)S(1)}, u32[]{:S(2)}, u32[]{:S(2)}) collective-permute-start(bf16[2,64,128]{2,1,0:T(8,128)(2,1)} %get-tuple-element.78), channel_id=1, source_target_pairs={{0,15},{1,0},{2,1},{3,2},{4,3},{5,4},{6,5},{7,6},{8,7},{9,8},{10,9... | collective-permute-start | bytes 98312 | tf_op jit(solution)/shard_map/ppermute | solution.py:13
  65.9 12.7 %collective-permute-start.10 = (bf16[2,64,128]{2,1,0:T(8,128)(2,1)S(1)}, bf16[2,64,128]{2,1,0:T(8,128)(2,1)}, u32[]{:S(2)}, u32[]{:S(2)}) collective-permute-start(bf16[2,64,128]{2,1,0:T(8,128)(2,1)S(1)} %get-tuple-element.77), channel_id=1, source_target_pairs={{0,1},{1,2},{2,3},{3,4},{4,5},{5,6},{6,7},{7,8},{8,9},{9,10},{10,1... | collective-permute-start | bytes 98312 | tf_op jit(solution)/shard_map/ppermute | solution.py:13
  67.8 10.8 %collective-permute-start.9 = (bf16[2,64,128]{2,1,0:T(8,128)(2,1)S(1)}, bf16[2,64,128]{2,1,0:T(8,128)(2,1)}, u32[]{:S(2)}, u32[]{:S(2)}) collective-permute-start(bf16[2,64,128]{2,1,0:T(8,128)(2,1)S(1)} %get-tuple-element.76), channel_id=1, source_target_pairs={{0,496},{16,0},{32,16},{48,32},{64,48},{80,64},{96,80},{112,96},{1... | collective-permute-start | bytes 98312 | tf_op jit(solution)/shard_map/ppermute | solution.py:13
  75.5 3.2 %collective-permute-start.8 = (bf16[2,64,128]{2,1,0:T(8,128)(2,1)S(1)}, bf16[2,64,128]{2,1,0:T(8,128)(2,1)}, u32[]{:S(2)}, u32[]{:S(2)}) collective-permute-start(bf16[2,64,128]{2,1,0:T(8,128)(2,1)S(1)} %get-tuple-element.150), channel_id=1, source_target_pairs={{0,16},{16,32},{32,48},{48,64},{64,80},{80,96},{96,112},{112,128},... | collective-permute-start | bytes 98312 | tf_op jit(solution)/shard_map/ppermute | solution.py:13
  85.4 17.6 %collective-permute-start.15 = (bf16[2,64,128]{2,1,0:T(8,128)(2,1)}, bf16[2,64,128]{2,1,0:T(8,128)(2,1)S(1)}, u32[]{:S(2)}, u32[]{:S(2)}) collective-permute-start(bf16[2,64,128]{2,1,0:T(8,128)(2,1)} %get-tuple-element.86), channel_id=1, source_target_pairs={{0,15},{1,0},{2,1},{3,2},{4,3},{5,4},{6,5},{7,6},{8,7},{9,8},{10,9... | collective-permute-start | bytes 98312 | tf_op jit(solution)/shard_map/ppermute | solution.py:13
  90.3 12.7 %collective-permute-start.14 = (bf16[2,64,128]{2,1,0:T(8,128)(2,1)S(1)}, bf16[2,64,128]{2,1,0:T(8,128)(2,1)}, u32[]{:S(2)}, u32[]{:S(2)}) collective-permute-start(bf16[2,64,128]{2,1,0:T(8,128)(2,1)S(1)} %get-tuple-element.85), channel_id=1, source_target_pairs={{0,1},{1,2},{2,3},{3,4},{4,5},{5,6},{6,7},{7,8},{8,9},{9,10},{10,1... | collective-permute-start | bytes 98312 | tf_op jit(solution)/shard_map/ppermute | solution.py:13
  92.2 10.8 %collective-permute-start.13 = (bf16[2,64,128]{2,1,0:T(8,128)(2,1)S(1)}, bf16[2,64,128]{2,1,0:T(8,128)(2,1)}, u32[]{:S(2)}, u32[]{:S(2)}) collective-permute-start(bf16[2,64,128]{2,1,0:T(8,128)(2,1)S(1)} %get-tuple-element.84), channel_id=1, source_target_pairs={{0,496},{16,0},{32,16},{48,32},{64,48},{80,64},{96,80},{112,96},{1... | collective-permute-start | bytes 98312 | tf_op jit(solution)/shard_map/ppermute | solution.py:13
  99.8 3.2 %collective-permute-start.12 = (bf16[2,64,128]{2,1,0:T(8,128)(2,1)S(1)}, bf16[2,64,128]{2,1,0:T(8,128)(2,1)}, u32[]{:S(2)}, u32[]{:S(2)}) collective-permute-start(bf16[2,64,128]{2,1,0:T(8,128)(2,1)S(1)} %get-tuple-element.146), channel_id=1, source_target_pairs={{0,16},{16,32},{32,48},{48,64},{64,80},{80,96},{96,112},{112,128},... | collective-permute-start | bytes 98312 | tf_op jit(solution)/shard_map/ppermute | solution.py:13
  109.7 17.6 %collective-permute-start.19 = (bf16[2,64,128]{2,1,0:T(8,128)(2,1)}, bf16[2,64,128]{2,1,0:T(8,128)(2,1)S(1)}, u32[]{:S(2)}, u32[]{:S(2)}) collective-permute-start(bf16[2,64,128]{2,1,0:T(8,128)(2,1)} %get-tuple-element.94), channel_id=1, source_target_pairs={{0,15},{1,0},{2,1},{3,2},{4,3},{5,4},{6,5},{7,6},{8,7},{9,8},{10,9... | collective-permute-start | bytes 98312 | tf_op jit(solution)/shard_map/ppermute | solution.py:13
  114.6 12.7 %collective-permute-start.18 = (bf16[2,64,128]{2,1,0:T(8,128)(2,1)S(1)}, bf16[2,64,128]{2,1,0:T(8,128)(2,1)}, u32[]{:S(2)}, u32[]{:S(2)}) collective-permute-start(bf16[2,64,128]{2,1,0:T(8,128)(2,1)S(1)} %get-tuple-element.93), channel_id=1, source_target_pairs={{0,1},{1,2},{2,3},{3,4},{4,5},{5,6},{6,7},{7,8},{8,9},{9,10},{10,1... | collective-permute-start | bytes 98312 | tf_op jit(solution)/shard_map/ppermute | solution.py:13
  116.5 10.8 %collective-permute-start.17 = (bf16[2,64,128]{2,1,0:T(8,128)(2,1)S(1)}, bf16[2,64,128]{2,1,0:T(8,128)(2,1)}, u32[]{:S(2)}, u32[]{:S(2)}) collective-permute-start(bf16[2,64,128]{2,1,0:T(8,128)(2,1)S(1)} %get-tuple-element.92), channel_id=1, source_target_pairs={{0,496},{16,0},{32,16},{48,32},{64,48},{80,64},{96,80},{112,96},{1... | collective-permute-start | bytes 98312 | tf_op jit(solution)/shard_map/ppermute | solution.py:13
  124.1 3.2 %collective-permute-start.16 = (bf16[2,64,128]{2,1,0:T(8,128)(2,1)S(1)}, bf16[2,64,128]{2,1,0:T(8,128)(2,1)}, u32[]{:S(2)}, u32[]{:S(2)}) collective-permute-start(bf16[2,64,128]{2,1,0:T(8,128)(2,1)S(1)} %get-tuple-element.142), channel_id=1, source_target_pairs={{0,16},{16,32},{32,48},{48,64},{64,80},{80,96},{96,112},{112,128},... | collective-permute-start | bytes 98312 | tf_op jit(solution)/shard_map/ppermute | solution.py:13
  134.1 17.6 %collective-permute-start.23 = (bf16[2,64,128]{2,1,0:T(8,128)(2,1)}, bf16[2,64,128]{2,1,0:T(8,128)(2,1)S(1)}, u32[]{:S(2)}, u32[]{:S(2)}) collective-permute-start(bf16[2,64,128]{2,1,0:T(8,128)(2,1)} %get-tuple-element.102), channel_id=1, source_target_pairs={{0,15},{1,0},{2,1},{3,2},{4,3},{5,4},{6,5},{7,6},{8,7},{9,8},{10,9... | collective-permute-start | bytes 98312 | tf_op jit(solution)/shard_map/ppermute | solution.py:13
  138.9 12.7 %collective-permute-start.22 = (bf16[2,64,128]{2,1,0:T(8,128)(2,1)S(1)}, bf16[2,64,128]{2,1,0:T(8,128)(2,1)}, u32[]{:S(2)}, u32[]{:S(2)}) collective-permute-start(bf16[2,64,128]{2,1,0:T(8,128)(2,1)S(1)} %get-tuple-element.101), channel_id=1, source_target_pairs={{0,1},{1,2},{2,3},{3,4},{4,5},{5,6},{6,7},{7,8},{8,9},{9,10},{10,1... | collective-permute-start | bytes 98312 | tf_op jit(solution)/shard_map/ppermute | solution.py:13
  140.9 10.8 %collective-permute-start.21 = (bf16[2,64,128]{2,1,0:T(8,128)(2,1)S(1)}, bf16[2,64,128]{2,1,0:T(8,128)(2,1)}, u32[]{:S(2)}, u32[]{:S(2)}) collective-permute-start(bf16[2,64,128]{2,1,0:T(8,128)(2,1)S(1)} %get-tuple-element.100), channel_id=1, source_target_pairs={{0,496},{16,0},{32,16},{48,32},{64,48},{80,64},{96,80},{112,96},{1... | collective-permute-start | bytes 98312 | tf_op jit(solution)/shard_map/ppermute | solution.py:13
  148.5 3.2 %collective-permute-start.20 = (bf16[2,64,128]{2,1,0:T(8,128)(2,1)S(1)}, bf16[2,64,128]{2,1,0:T(8,128)(2,1)}, u32[]{:S(2)}, u32[]{:S(2)}) collective-permute-start(bf16[2,64,128]{2,1,0:T(8,128)(2,1)S(1)} %get-tuple-element.138), channel_id=1, source_target_pairs={{0,16},{16,32},{32,48},{48,64},{64,80},{80,96},{96,112},{112,128},... | collective-permute-start | bytes 98312 | tf_op jit(solution)/shard_map/ppermute | solution.py:13
  158.4 17.8 %collective-permute-start.27 = (bf16[2,64,128]{2,1,0:T(8,128)(2,1)}, bf16[2,64,128]{2,1,0:T(8,128)(2,1)S(1)}, u32[]{:S(2)}, u32[]{:S(2)}) collective-permute-start(bf16[2,64,128]{2,1,0:T(8,128)(2,1)} %get-tuple-element.110), channel_id=1, source_target_pairs={{0,15},{1,0},{2,1},{3,2},{4,3},{5,4},{6,5},{7,6},{8,7},{9,8},{10,9... | collective-permute-start | bytes 98312 | tf_op jit(solution)/shard_map/ppermute | solution.py:13
  163.3 12.9 %collective-permute-start.26 = (bf16[2,64,128]{2,1,0:T(8,128)(2,1)S(1)}, bf16[2,64,128]{2,1,0:T(8,128)(2,1)}, u32[]{:S(2)}, u32[]{:S(2)}) collective-permute-start(bf16[2,64,128]{2,1,0:T(8,128)(2,1)S(1)} %get-tuple-element.109), channel_id=1, source_target_pairs={{0,1},{1,2},{2,3},{3,4},{4,5},{5,6},{6,7},{7,8},{8,9},{9,10},{10,1... | collective-permute-start | bytes 98312 | tf_op jit(solution)/shard_map/ppermute | solution.py:13
  165.2 11.0 %collective-permute-start.25 = (bf16[2,64,128]{2,1,0:T(8,128)(2,1)S(1)}, bf16[2,64,128]{2,1,0:T(8,128)(2,1)}, u32[]{:S(2)}, u32[]{:S(2)}) collective-permute-start(bf16[2,64,128]{2,1,0:T(8,128)(2,1)S(1)} %get-tuple-element.108), channel_id=1, source_target_pairs={{0,496},{16,0},{32,16},{48,32},{64,48},{80,64},{96,80},{112,96},{1... | collective-permute-start | bytes 98312 | tf_op jit(solution)/shard_map/ppermute | solution.py:13
  172.8 3.4 %collective-permute-start.24 = (bf16[2,64,128]{2,1,0:T(8,128)(2,1)S(1)}, bf16[2,64,128]{2,1,0:T(8,128)(2,1)}, u32[]{:S(2)}, u32[]{:S(2)}) collective-permute-start(bf16[2,64,128]{2,1,0:T(8,128)(2,1)S(1)} %get-tuple-element.134), channel_id=1, source_target_pairs={{0,16},{16,32},{32,48},{48,64},{64,80},{80,96},{96,112},{112,128},... | collective-permute-start | bytes 98312 | tf_op jit(solution)/shard_map/ppermute | solution.py:13
  182.9 18.6 %copy-start.10 = (f32[16,64,128]{2,1,0:T(8,128)}, f32[16,64,128]{2,1,0:T(8,128)S(1)}, u32[]{:S(2)}) copy-start(f32[16,64,128]{2,1,0:T(8,128)S(1)} %fusion.13) | copy-start | bytes 1572868
  182.9 17.4 %collective-permute-start.31 = (bf16[2,64,128]{2,1,0:T(8,128)(2,1)}, bf16[2,64,128]{2,1,0:T(8,128)(2,1)S(1)}, u32[]{:S(2)}, u32[]{:S(2)}) collective-permute-start(bf16[2,64,128]{2,1,0:T(8,128)(2,1)} %get-tuple-element.118), channel_id=1, source_target_pairs={{0,15},{1,0},{2,1},{3,2},{4,3},{5,4},{6,5},{7,6},{8,7},{9,8},{10,9... | collective-permute-start | bytes 98312 | tf_op jit(solution)/shard_map/ppermute | solution.py:13
  187.8 12.5 %collective-permute-start.30 = (bf16[2,64,128]{2,1,0:T(8,128)(2,1)S(1)}, bf16[2,64,128]{2,1,0:T(8,128)(2,1)}, u32[]{:S(2)}, u32[]{:S(2)}) collective-permute-start(bf16[2,64,128]{2,1,0:T(8,128)(2,1)S(1)} %get-tuple-element.117), channel_id=1, source_target_pairs={{0,1},{1,2},{2,3},{3,4},{4,5},{5,6},{6,7},{7,8},{8,9},{9,10},{10,1... | collective-permute-start | bytes 98312 | tf_op jit(solution)/shard_map/ppermute | solution.py:13
  189.7 10.6 %collective-permute-start.29 = (bf16[2,64,128]{2,1,0:T(8,128)(2,1)S(1)}, bf16[2,64,128]{2,1,0:T(8,128)(2,1)}, u32[]{:S(2)}, u32[]{:S(2)}) collective-permute-start(bf16[2,64,128]{2,1,0:T(8,128)(2,1)S(1)} %get-tuple-element.116), channel_id=1, source_target_pairs={{0,496},{16,0},{32,16},{48,32},{64,48},{80,64},{96,80},{112,96},{1... | collective-permute-start | bytes 98312 | tf_op jit(solution)/shard_map/ppermute | solution.py:13
  197.1 3.2 %collective-permute-start.28 = (bf16[2,64,128]{2,1,0:T(8,128)(2,1)S(1)}, bf16[2,64,128]{2,1,0:T(8,128)(2,1)}, u32[]{:S(2)}, u32[]{:S(2)}) collective-permute-start(bf16[2,64,128]{2,1,0:T(8,128)(2,1)S(1)} %get-tuple-element.130), channel_id=1, source_target_pairs={{0,16},{16,32},{32,48},{48,64},{64,80},{80,96},{96,112},{112,128},... | collective-permute-start | bytes 98312 | tf_op jit(solution)/shard_map/ppermute | solution.py:13
  207.5 16.3 %collective-permute-start.35 = (bf16[2,64,128]{2,1,0:T(8,128)(2,1)S(1)}, bf16[2,64,128]{2,1,0:T(8,128)(2,1)S(1)}, u32[]{:S(2)}, u32[]{:S(2)}) collective-permute-start(bf16[2,64,128]{2,1,0:T(8,128)(2,1)S(1)} %get-tuple-element.125), channel_id=1, source_target_pairs={{0,15},{1,0},{2,1},{3,2},{4,3},{5,4},{6,5},{7,6},{8,7},{9,8},{10,9... | collective-permute-start | bytes 98312 | tf_op jit(solution)/shard_map/ppermute | solution.py:13
  212.3 11.5 %collective-permute-start.34 = (bf16[2,64,128]{2,1,0:T(8,128)(2,1)S(1)}, bf16[2,64,128]{2,1,0:T(8,128)(2,1)S(1)}, u32[]{:S(2)}, u32[]{:S(2)}) collective-permute-start(bf16[2,64,128]{2,1,0:T(8,128)(2,1)S(1)} %get-tuple-element.124), channel_id=1, source_target_pairs={{0,1},{1,2},{2,3},{3,4},{4,5},{5,6},{6,7},{7,8},{8,9},{9,10},{10,1... | collective-permute-start | bytes 98312 | tf_op jit(solution)/shard_map/ppermute | solution.py:13
  214.3 9.6 %collective-permute-start.33 = (bf16[2,64,128]{2,1,0:T(8,128)(2,1)S(1)}, bf16[2,64,128]{2,1,0:T(8,128)(2,1)S(1)}, u32[]{:S(2)}, u32[]{:S(2)}) collective-permute-start(bf16[2,64,128]{2,1,0:T(8,128)(2,1)S(1)} %get-tuple-element.123), channel_id=1, source_target_pairs={{0,496},{16,0},{32,16},{48,32},{64,48},{80,64},{96,80},{112,96},{1... | collective-permute-start | bytes 98312 | tf_op jit(solution)/shard_map/ppermute | solution.py:13
  221.9 3.1 %collective-permute-start.32 = (bf16[2,64,128]{2,1,0:T(8,128)(2,1)S(1)}, bf16[2,64,128]{2,1,0:T(8,128)(2,1)S(1)}, u32[]{:S(2)}, u32[]{:S(2)}) collective-permute-start(bf16[2,64,128]{2,1,0:T(8,128)(2,1)S(1)} %get-tuple-element.126), channel_id=1, source_target_pairs={{0,16},{16,32},{32,48},{48,64},{64,80},{80,96},{96,112},{112,128},... | collective-permute-start | bytes 98312 | tf_op jit(solution)/shard_map/ppermute | solution.py:13
  226.3 4.7 %collective-permute-start.36 = (f32[64,64]{1,0:T(8,128)S(1)}, f32[64,64]{1,0:T(8,128)S(1)}, u32[]{:S(2)}, u32[]{:S(2)}) collective-permute-start(f32[64,64]{1,0:T(8,128)S(1)} %convolution_bitcast_fusion.9), channel_id=1, source_target_pairs={{0,1},{1,0},{2,3},{3,2},{4,5},{5,4},{6,7},{7,6},{8,9},{9,8},{10,11... | collective-permute-start | bytes 49160 | tf_op jit(solution)/shard_map/ppermute | solution.py:21
  231.0 5.6 %collective-permute-start.37 = (f32[64,64]{1,0:T(8,128)S(1)}, f32[64,64]{1,0:T(8,128)S(1)}, u32[]{:S(2)}, u32[]{:S(2)}) collective-permute-start(f32[64,64]{1,0:T(8,128)S(1)} %add.150), channel_id=1, source_target_pairs={{0,2},{1,3},{2,0},{3,1},{4,6},{5,7},{6,4},{7,5},{8,10},{9,11},{10,... | collective-permute-start | bytes 49160 | tf_op jit(solution)/shard_map/ppermute | solution.py:21
  236.6 8.7 %collective-permute-start.38 = (f32[64,64]{1,0:T(8,128)S(1)}, f32[64,64]{1,0:T(8,128)S(1)}, u32[]{:S(2)}, u32[]{:S(2)}) collective-permute-start(f32[64,64]{1,0:T(8,128)S(1)} %add.151), channel_id=1, source_target_pairs={{0,4},{1,5},{2,6},{3,7},{4,0},{5,1},{6,2},{7,3},{8,12},{9,13},{10,... | collective-permute-start | bytes 49160 | tf_op jit(solution)/shard_map/ppermute | solution.py:21
  245.4 13.4 %collective-permute-start.39 = (f32[64,64]{1,0:T(8,128)S(1)}, f32[64,64]{1,0:T(8,128)S(1)}, u32[]{:S(2)}, u32[]{:S(2)}) collective-permute-start(f32[64,64]{1,0:T(8,128)S(1)} %add.152), channel_id=1, source_target_pairs={{0,8},{1,9},{2,10},{3,11},{4,12},{5,13},{6,14},{7,15},{8,0},{9,1},... | collective-permute-start | bytes 49160 | tf_op jit(solution)/shard_map/ppermute | solution.py:21
  258.7 13.0 %collective-permute-start.40 = (f32[64,64]{1,0:T(8,128)S(1)}, f32[64,64]{1,0:T(8,128)S(1)}, u32[]{:S(2)}, u32[]{:S(2)}) collective-permute-start(f32[64,64]{1,0:T(8,128)S(1)} %add.153), channel_id=1, source_target_pairs={{0,16},{16,0},{32,48},{48,32},{64,80},{80,64},{96,112},{112,96},{1... | collective-permute-start | bytes 49160 | tf_op jit(solution)/shard_map/ppermute | solution.py:21
  271.8 4.6 %collective-permute-start.41 = (f32[64,64]{1,0:T(8,128)S(1)}, f32[64,64]{1,0:T(8,128)S(1)}, u32[]{:S(2)}, u32[]{:S(2)}) collective-permute-start(f32[64,64]{1,0:T(8,128)S(1)} %add.154), channel_id=1, source_target_pairs={{0,32},{16,48},{32,0},{48,16},{64,96},{80,112},{96,64},{112,80},{1... | collective-permute-start | bytes 49160 | tf_op jit(solution)/shard_map/ppermute | solution.py:21
  276.4 6.2 %collective-permute-start.42 = (f32[64,64]{1,0:T(8,128)S(1)}, f32[64,64]{1,0:T(8,128)S(1)}, u32[]{:S(2)}, u32[]{:S(2)}) collective-permute-start(f32[64,64]{1,0:T(8,128)S(1)} %add.155), channel_id=1, source_target_pairs={{0,64},{16,80},{32,96},{48,112},{64,0},{80,16},{96,32},{112,48},{1... | collective-permute-start | bytes 49160 | tf_op jit(solution)/shard_map/ppermute | solution.py:21
  282.6 4.6 %collective-permute-start.43 = (f32[64,64]{1,0:T(8,128)S(1)}, f32[64,64]{1,0:T(8,128)S(1)}, u32[]{:S(2)}, u32[]{:S(2)}) collective-permute-start(f32[64,64]{1,0:T(8,128)S(1)} %add.156), channel_id=1, source_target_pairs={{0,128},{16,144},{32,160},{48,176},{64,192},{80,208},{96,224},{112... | collective-permute-start | bytes 49160 | tf_op jit(solution)/shard_map/ppermute | solution.py:21
  287.2 6.2 %collective-permute-start.44 = (f32[64,64]{1,0:T(8,128)S(1)}, f32[64,64]{1,0:T(8,128)S(1)}, u32[]{:S(2)}, u32[]{:S(2)}) collective-permute-start(f32[64,64]{1,0:T(8,128)S(1)} %add.157), channel_id=1, source_target_pairs={{0,256},{16,272},{32,288},{48,304},{64,320},{80,336},{96,352},{112... | collective-permute-start | bytes 49160 | tf_op jit(solution)/shard_map/ppermute | solution.py:21
  (15 other events, 22.6 us)

commit v5 on v3

v5 whole, which is shorter than its diff:
```python
import functools

import jax
import jax.numpy as jnp
from jax import lax
from jax.experimental import pallas as pl
from jax.experimental.pallas import tpu as pltpu
from jax.sharding import PartitionSpec as P

DEG = 9
INTERPRET = False
CONTRACT_LAST = (((1,), (1,)), ((), ()))


def from_behind(value, axis, steps):
    count = lax.axis_size(axis)
    pairs = [(source, (source + steps) % count) for source in range(count)]
    return lax.ppermute(value, axis, pairs)


def butterfly_sum(value, axis):
    count = lax.axis_size(axis)
    stride = 1
    while stride < count:
        pairs = [(source, source ^ stride) for source in range(count)]
        value = value + lax.ppermute(value, axis, pairs)
        stride *= 2
    return value


def _local_kernel(cols_ref, rounded_ref, tiles_ref, out_ref):
    rows, per_row = tiles_ref.shape[0], tiles_ref.shape[1]
    for r in range(rows):
        acc = None
        for t in range(per_row):
            block = rounded_ref[cols_ref[r * per_row + t]]
            part = lax.dot_general(
                block, tiles_ref[r, t], CONTRACT_LAST, preferred_element_type=jnp.float32
            )
            acc = part if acc is None else acc + part
        out_ref[r] = acc


def local_product(rounded, tiles, cols):
    vmem = pl.BlockSpec(memory_space=pltpu.VMEM)
    return pl.pallas_call(
        _local_kernel,
        out_shape=jax.ShapeDtypeStruct((tiles.shape[0],) + rounded.shape[1:], jnp.float32),
        in_specs=[pl.BlockSpec(memory_space=pltpu.SMEM), vmem, vmem],
        out_specs=vmem,
        interpret=INTERPRET,
    )(cols.reshape(-1), rounded, tiles)


def _combine_kernel(slot_ref, picks_ref, local_ref, older_ref, halo_ref, *refs, scale, with_older):
    pieces, (vec_ref, rounded_ref), edge_refs, (received_ref,) = refs[:4], refs[4:6], refs[6:10], refs[10:]
    per_list = pieces[0].shape[0]
    for d in range(4):
        for i in range(per_list):
            received_ref[d * per_list + i] = pieces[d][i]
    for r in range(local_ref.shape[0]):
        block = received_ref[slot_ref[r]]
        coupled = lax.dot_general(
            block, halo_ref[r], CONTRACT_LAST, preferred_element_type=jnp.float32
        )
        value = local_ref[r] + coupled
        if with_older:
            value = scale * value - older_ref[r]
        vec_ref[r] = value
        rounded_ref[r] = value.astype(jnp.bfloat16)
    for d in range(4):
        for i in range(per_list):
            edge_refs[d][i] = rounded_ref[picks_ref[d * per_list + i]]


def combine(local, older, pieces, halo, slot, picks, scale, with_older):
    vmem = pl.BlockSpec(memory_space=pltpu.VMEM)
    smem = pl.BlockSpec(memory_space=pltpu.SMEM)
    per_list = pieces[0].shape[0]
    piece_shape = jax.ShapeDtypeStruct(pieces[0].shape, jnp.bfloat16)
    kernel = functools.partial(_combine_kernel, scale=scale, with_older=with_older)
    outs = pl.pallas_call(
        kernel,
        out_shape=(
            jax.ShapeDtypeStruct(local.shape, jnp.float32),
            jax.ShapeDtypeStruct(local.shape, jnp.bfloat16),
        ) + (piece_shape,) * 4,
        in_specs=[smem, smem] + [vmem] * 7,
        out_specs=(vmem,) * 6,
        scratch_shapes=[pltpu.VMEM((4 * per_list,) + pieces[0].shape[1:], jnp.bfloat16)],
        interpret=INTERPRET,
    )(slot, picks, local, older, halo, *pieces)
    return outs[0], outs[1], list(outs[2:])


def exchange(pieces):
    return [
        from_behind(pieces[0], "px", 1),
        from_behind(pieces[1], "px", -1),
        from_behind(pieces[2], "py", 1),
        from_behind(pieces[3], "py", -1),
    ]


def shards(start_vecs, local_tiles, local_cols, halo_tiles, halo_slot, boundary):
    per_list = boundary.shape[1]
    picks = boundary.reshape(-1)
    rounded = start_vecs.astype(jnp.bfloat16)
    outgoing = [rounded[boundary[d]] for d in range(4)]
    older = start_vecs
    current = start_vecs
    for step in range(DEG):
        received = exchange(outgoing)
        local = local_product(rounded, local_tiles, local_cols)
        newer, rounded, outgoing = combine(
            local, older, received, halo_tiles, halo_slot, picks, 2.0, step > 0
        )
        older, current = current, newer

    total_rows = current.shape[0] * current.shape[2] * lax.axis_size("px") * lax.axis_size("py")
    partial_gram = jnp.einsum("rkj,rlj->kl", current, current, precision=lax.Precision.HIGHEST)
    raw_gram = butterfly_sum(butterfly_sum(partial_gram, "py"), "px")
    squares = jnp.diagonal(raw_gram)
    scales = lax.rsqrt(squares / total_rows + 1e-06)
    filtered = current * scales[None, :, None]
    gram_matrix = raw_gram * scales[:, None] * scales[None, :] / total_rows
    return (filtered, gram_matrix)


def solution(mesh):
    return jax.shard_map(
        shards,
        mesh=mesh,
        in_specs=(
            P(("px", "py"), None, None),
            P(("px", "py"), None, None, None),
            P(("px", "py"), None),
            P(("px", "py"), None, None),
            P(("px", "py")),
            P(("px", "py"), None),
        ),
        out_specs=(P(("px", "py"), None, None), P()),
        check_vma=False,
    )
```

time: 315 us -> 297 us (0.943)
  Pallas kernels: 0 us -> 61 us
  matrix products: 50.1 us -> 1.82 us
  local copies, waits for them, and re-layouts: 35.1 us -> 13.5 us
  other arithmetic: 10.7 us -> 2.8 us
    pallas_call x0 -> x18, Pallas kernels: none -> 61 us  [the longest x9 35.6 us: local_product(): pl.pallas_call(_local_kernel, out_shape=jax.ShapeDtypeStruct((tiles.shape...]
    dot_general x43 -> x0, matrix products: 49.5 us -> none  [the longest x17 26.9 us: halo_term(): jnp.einsum('rkj,rij->rki', chosen.astype(jnp.bfloat16), halo, preferred_e...]
    gather x20 -> x4, local copies, waits for them, and re-layouts: 27.3 us -> 2.24 us  [shards(): outgoing = [rounded[boundary[d]] for d in range(4)]]
    concatenate x9 -> x0, other arithmetic: 7.24 us -> none  [halo_term(): received = jnp.concatenate(pieces, axis=0)]
    unnamed x25 -> x78, local copies, waits for them, and re-layouts: 0.98 us -> 8.09 us
    slice x9 -> x1, local copies, waits for them, and re-layouts: 5.7 us -> 1.04 us  [shards(): outgoing = [rounded[boundary[d]] for d in range(4)]]
  transfers between devices with their start and end apart: 45 -> 45, of which waited for: 9 -> 9; matrix products, arithmetic and copies ran while one was open for 20% -> 2% of each run, Pallas kernels for 0% -> 12%
where the time goes in v5:
time: 297 us; the launch traced here: 293 us
  starting transfers between devices  182 us (61%)
  Pallas kernels  61 us (21%)
  waiting for transfers between devices  30.7 us (10%)
  local copies, waits for them, and re-layouts  13.5 us (5%)
    ppermute x36, starting transfers between devices, from_behind(): return lax.ppermute(value, axis, pairs)  145 us
    ppermute x9, starting transfers between devices, butterfly_sum(): value = value + lax.ppermute(value, axis, pairs)  36.5 us
    pallas_call x9, Pallas kernels, local_product(): pl.pallas_call(_local_kernel, out_shape=jax.ShapeDtypeStruct((tiles.shape...  35.6 us
    ppermute x9, waiting for transfers between devices, butterfly_sum(): value = value + lax.ppermute(value, axis, pairs)  30.6 us
    pallas_call x9, Pallas kernels, combine(): pl.pallas_call(kernel, out_shape=(jax.ShapeDtypeStruct(local.shape, jnp.f...  25.4 us
    unnamed x78, local copies, waits for them, and re-layouts  8.09 us
  transfers between devices with their start and end apart: 45, of which 9 were waited for; matrix products, arithmetic and copies ran while one was open for 2% of the time, Pallas kernels for 12%

profile of v5, /device:TPU:1, one launch (start us, length us, event | category | flops | bytes accessed | tf_op | source)
XLA Modules:
  0.0 293.2 jit_solution(2751175380512313412)
XLA Ops:
  3.4 4.5 %collective-permute-start = (bf16[2,64,128]{2,1,0:T(8,128)(2,1)S(1)}, bf16[2,64,128]{2,1,0:T(8,128)(2,1)S(1)}, u32[]{:S(2)}, u32[]{:S(2)}) collective-permute-start(bf16[2,64,128]{2,1,0:T(8,128)(2,1)S(1)} %gather_fusion), channel_id=1, source_target_pairs={{0,16},{16,32},{32,48},{48,64},{64,80},{80,96},{96,112},{112,128},... | collective-permute-start | bytes 98312 | tf_op jit(solution)/shard_map/ppermute | solution.py:18
  8.4 6.2 %collective-permute-start.1 = (bf16[2,64,128]{2,1,0:T(8,128)(2,1)S(1)}, bf16[2,64,128]{2,1,0:T(8,128)(2,1)S(1)}, u32[]{:S(2)}, u32[]{:S(2)}) collective-permute-start(bf16[2,64,128]{2,1,0:T(8,128)(2,1)S(1)} %gather_fusion.1), channel_id=1, source_target_pairs={{0,496},{16,0},{32,16},{48,32},{64,48},{80,64},{96,80},{112,96},{1... | collective-permute-start | bytes 98312 | tf_op jit(solution)/shard_map/ppermute | solution.py:18
  17.7 6.9 %collective-permute-start.3 = (bf16[2,64,128]{2,1,0:T(8,128)(2,1)S(1)}, bf16[2,64,128]{2,1,0:T(8,128)(2,1)S(1)}, u32[]{:S(2)}, u32[]{:S(2)}) collective-permute-start(bf16[2,64,128]{2,1,0:T(8,128)(2,1)S(1)} %gather_fusion.3), channel_id=1, source_target_pairs={{0,15},{1,0},{2,1},{3,2},{4,3},{5,4},{6,5},{7,6},{8,7},{9,8},{10,9... | collective-permute-start | bytes 98312 | tf_op jit(solution)/shard_map/ppermute | solution.py:18
  27.4 4.0 %shard_map.77.local_ref = f32[16,64,128]{2,1,0:T(8,128)} custom-call(s32[64]{0:T(128)} %reshape.146.cols_ref, bf16[16,64,128]{2,1,0:T(8,128)(2,1)} %copy-done.1, bf16[16,4,128,128]{3,2,1,0:T(8,128)(2,1)} %tiles_ref.17), custom_call_target="tpu_custom_call" | custom-call | tf_op jit(solution)/shard_map/pallas_call | solution.py:46
  32.6 2.9 shard_map.78
  35.4 3.9 %collective-permute-start.4 = (bf16[2,64,128]{2,1,0:T(8,128)(2,1)}, bf16[2,64,128]{2,1,0:T(8,128)(2,1)S(1)}, u32[]{:S(2)}, u32[]{:S(2)}) collective-permute-start(bf16[2,64,128]{2,1,0:T(8,128)(2,1)} %get-tuple-element.51), channel_id=1, source_target_pairs={{0,16},{16,32},{32,48},{48,64},{64,80},{80,96},{96,112},{112,128},... | collective-permute-start | bytes 98312 | tf_op jit(solution)/shard_map/ppermute | solution.py:18
  39.4 4.1 %collective-permute-start.5 = (bf16[2,64,128]{2,1,0:T(8,128)(2,1)}, bf16[2,64,128]{2,1,0:T(8,128)(2,1)S(1)}, u32[]{:S(2)}, u32[]{:S(2)}) collective-permute-start(bf16[2,64,128]{2,1,0:T(8,128)(2,1)} %get-tuple-element.52), channel_id=1, source_target_pairs={{0,496},{16,0},{32,16},{48,32},{64,48},{80,64},{96,80},{112,96},{1... | collective-permute-start | bytes 98312 | tf_op jit(solution)/shard_map/ppermute | solution.py:18
  45.4 4.6 %collective-permute-start.7 = (bf16[2,64,128]{2,1,0:T(8,128)(2,1)}, bf16[2,64,128]{2,1,0:T(8,128)(2,1)S(1)}, u32[]{:S(2)}, u32[]{:S(2)}) collective-permute-start(bf16[2,64,128]{2,1,0:T(8,128)(2,1)} %get-tuple-element.54), channel_id=1, source_target_pairs={{0,15},{1,0},{2,1},{3,2},{4,3},{5,4},{6,5},{7,6},{8,7},{9,8},{10,9... | collective-permute-start | bytes 98312 | tf_op jit(solution)/shard_map/ppermute | solution.py:18
  50.0 4.0 %shard_map.79.local_ref = f32[16,64,128]{2,1,0:T(8,128)} custom-call(s32[64]{0:T(128)} %reshape.146.cols_ref, bf16[16,64,128]{2,1,0:T(8,128)(2,1)} %get-tuple-element.50.rounded_ref, bf16[16,4,128,128]{3,2,1,0:T(8,128)(2,1)} %tiles_ref.17), custom_call_target="tpu_custom_call" | custom-call | tf_op jit(solution)/shard_map/pallas_call | solution.py:46
  55.2 2.8 shard_map.80
  59.9 4.6 %collective-permute-start.11 = (bf16[2,64,128]{2,1,0:T(8,128)(2,1)}, bf16[2,64,128]{2,1,0:T(8,128)(2,1)S(1)}, u32[]{:S(2)}, u32[]{:S(2)}) collective-permute-start(bf16[2,64,128]{2,1,0:T(8,128)(2,1)} %get-tuple-element.60), channel_id=1, source_target_pairs={{0,15},{1,0},{2,1},{3,2},{4,3},{5,4},{6,5},{7,6},{8,7},{9,8},{10,9... | collective-permute-start | bytes 98312 | tf_op jit(solution)/shard_map/ppermute | solution.py:18
  67.1 7.5 %collective-permute-start.9 = (bf16[2,64,128]{2,1,0:T(8,128)(2,1)}, bf16[2,64,128]{2,1,0:T(8,128)(2,1)S(1)}, u32[]{:S(2)}, u32[]{:S(2)}) collective-permute-start(bf16[2,64,128]{2,1,0:T(8,128)(2,1)} %get-tuple-element.58), channel_id=1, source_target_pairs={{0,496},{16,0},{32,16},{48,32},{64,48},{80,64},{96,80},{112,96},{1... | collective-permute-start | bytes 98312 | tf_op jit(solution)/shard_map/ppermute | solution.py:18
  74.5 4.0 %shard_map.81.local_ref = f32[16,64,128]{2,1,0:T(8,128)} custom-call(s32[64]{0:T(128)} %reshape.146.cols_ref, bf16[16,64,128]{2,1,0:T(8,128)(2,1)} %get-tuple-element.55.rounded_ref, bf16[16,4,128,128]{3,2,1,0:T(8,128)(2,1)} %tiles_ref.17), custom_call_target="tpu_custom_call" | custom-call | tf_op jit(solution)/shard_map/pallas_call | solution.py:46
  79.1 2.8 shard_map.82
  83.9 7.0 %collective-permute-start.13 = (bf16[2,64,128]{2,1,0:T(8,128)(2,1)}, bf16[2,64,128]{2,1,0:T(8,128)(2,1)S(1)}, u32[]{:S(2)}, u32[]{:S(2)}) collective-permute-start(bf16[2,64,128]{2,1,0:T(8,128)(2,1)} %get-tuple-element.64), channel_id=1, source_target_pairs={{0,496},{16,0},{32,16},{48,32},{64,48},{80,64},{96,80},{112,96},{1... | collective-permute-start | bytes 98312 | tf_op jit(solution)/shard_map/ppermute | solution.py:18
  92.8 4.6 %collective-permute-start.15 = (bf16[2,64,128]{2,1,0:T(8,128)(2,1)}, bf16[2,64,128]{2,1,0:T(8,128)(2,1)S(1)}, u32[]{:S(2)}, u32[]{:S(2)}) collective-permute-start(bf16[2,64,128]{2,1,0:T(8,128)(2,1)} %get-tuple-element.66), channel_id=1, source_target_pairs={{0,15},{1,0},{2,1},{3,2},{4,3},{5,4},{6,5},{7,6},{8,7},{9,8},{10,9... | collective-permute-start | bytes 98312 | tf_op jit(solution)/shard_map/ppermute | solution.py:18
  97.4 4.0 %shard_map.83.local_ref = f32[16,64,128]{2,1,0:T(8,128)} custom-call(s32[64]{0:T(128)} %reshape.146.cols_ref, bf16[16,64,128]{2,1,0:T(8,128)(2,1)} %get-tuple-element.61.rounded_ref, bf16[16,4,128,128]{3,2,1,0:T(8,128)(2,1)} %tiles_ref.17), custom_call_target="tpu_custom_call" | custom-call | tf_op jit(solution)/shard_map/pallas_call | solution.py:46
  102.0 2.8 shard_map.84
  106.7 7.5 %collective-permute-start.17 = (bf16[2,64,128]{2,1,0:T(8,128)(2,1)}, bf16[2,64,128]{2,1,0:T(8,128)(2,1)S(1)}, u32[]{:S(2)}, u32[]{:S(2)}) collective-permute-start(bf16[2,64,128]{2,1,0:T(8,128)(2,1)} %get-tuple-element.70), channel_id=1, source_target_pairs={{0,496},{16,0},{32,16},{48,32},{64,48},{80,64},{96,80},{112,96},{1... | collective-permute-start | bytes 98312 | tf_op jit(solution)/shard_map/ppermute | solution.py:18
  116.2 4.6 %collective-permute-start.19 = (bf16[2,64,128]{2,1,0:T(8,128)(2,1)}, bf16[2,64,128]{2,1,0:T(8,128)(2,1)S(1)}, u32[]{:S(2)}, u32[]{:S(2)}) collective-permute-start(bf16[2,64,128]{2,1,0:T(8,128)(2,1)} %get-tuple-element.72), channel_id=1, source_target_pairs={{0,15},{1,0},{2,1},{3,2},{4,3},{5,4},{6,5},{7,6},{8,7},{9,8},{10,9... | collective-permute-start | bytes 98312 | tf_op jit(solution)/shard_map/ppermute | solution.py:18
  120.8 4.0 %shard_map.85.local_ref = f32[16,64,128]{2,1,0:T(8,128)} custom-call(s32[64]{0:T(128)} %reshape.146.cols_ref, bf16[16,64,128]{2,1,0:T(8,128)(2,1)} %get-tuple-element.67.rounded_ref, bf16[16,4,128,128]{3,2,1,0:T(8,128)(2,1)} %tiles_ref.17), custom_call_target="tpu_custom_call" | custom-call | tf_op jit(solution)/shard_map/pallas_call | solution.py:46
  125.4 2.8 shard_map.86
  130.1 7.5 %collective-permute-start.21 = (bf16[2,64,128]{2,1,0:T(8,128)(2,1)}, bf16[2,64,128]{2,1,0:T(8,128)(2,1)S(1)}, u32[]{:S(2)}, u32[]{:S(2)}) collective-permute-start(bf16[2,64,128]{2,1,0:T(8,128)(2,1)} %get-tuple-element.76), channel_id=1, source_target_pairs={{0,496},{16,0},{32,16},{48,32},{64,48},{80,64},{96,80},{112,96},{1... | collective-permute-start | bytes 98312 | tf_op jit(solution)/shard_map/ppermute | solution.py:18
  139.5 4.6 %collective-permute-start.23 = (bf16[2,64,128]{2,1,0:T(8,128)(2,1)}, bf16[2,64,128]{2,1,0:T(8,128)(2,1)S(1)}, u32[]{:S(2)}, u32[]{:S(2)}) collective-permute-start(bf16[2,64,128]{2,1,0:T(8,128)(2,1)} %get-tuple-element.78), channel_id=1, source_target_pairs={{0,15},{1,0},{2,1},{3,2},{4,3},{5,4},{6,5},{7,6},{8,7},{9,8},{10,9... | collective-permute-start | bytes 98312 | tf_op jit(solution)/shard_map/ppermute | solution.py:18
  144.1 4.0 %shard_map.87.local_ref = f32[16,64,128]{2,1,0:T(8,128)} custom-call(s32[64]{0:T(128)} %reshape.146.cols_ref, bf16[16,64,128]{2,1,0:T(8,128)(2,1)} %get-tuple-element.73.rounded_ref, bf16[16,4,128,128]{3,2,1,0:T(8,128)(2,1)} %tiles_ref.17), custom_call_target="tpu_custom_call" | custom-call | tf_op jit(solution)/shard_map/pallas_call | solution.py:46
  148.7 2.9 shard_map.88
  153.5 7.5 %collective-permute-start.25 = (bf16[2,64,128]{2,1,0:T(8,128)(2,1)}, bf16[2,64,128]{2,1,0:T(8,128)(2,1)S(1)}, u32[]{:S(2)}, u32[]{:S(2)}) collective-permute-start(bf16[2,64,128]{2,1,0:T(8,128)(2,1)} %get-tuple-element.82), channel_id=1, source_target_pairs={{0,496},{16,0},{32,16},{48,32},{64,48},{80,64},{96,80},{112,96},{1... | collective-permute-start | bytes 98312 | tf_op jit(solution)/shard_map/ppermute | solution.py:18
  163.0 4.6 %collective-permute-start.27 = (bf16[2,64,128]{2,1,0:T(8,128)(2,1)}, bf16[2,64,128]{2,1,0:T(8,128)(2,1)S(1)}, u32[]{:S(2)}, u32[]{:S(2)}) collective-permute-start(bf16[2,64,128]{2,1,0:T(8,128)(2,1)} %get-tuple-element.84), channel_id=1, source_target_pairs={{0,15},{1,0},{2,1},{3,2},{4,3},{5,4},{6,5},{7,6},{8,7},{9,8},{10,9... | collective-permute-start | bytes 98312 | tf_op jit(solution)/shard_map/ppermute | solution.py:18
  167.5 4.0 %shard_map.89.local_ref = f32[16,64,128]{2,1,0:T(8,128)} custom-call(s32[64]{0:T(128)} %reshape.146.cols_ref, bf16[16,64,128]{2,1,0:T(8,128)(2,1)} %get-tuple-element.79.rounded_ref, bf16[16,4,128,128]{3,2,1,0:T(8,128)(2,1)} %tiles_ref.17), custom_call_target="tpu_custom_call" | custom-call | tf_op jit(solution)/shard_map/pallas_call | solution.py:46
  172.1 2.8 shard_map.90
  176.9 7.5 %collective-permute-start.29 = (bf16[2,64,128]{2,1,0:T(8,128)(2,1)}, bf16[2,64,128]{2,1,0:T(8,128)(2,1)S(1)}, u32[]{:S(2)}, u32[]{:S(2)}) collective-permute-start(bf16[2,64,128]{2,1,0:T(8,128)(2,1)} %get-tuple-element.88), channel_id=1, source_target_pairs={{0,496},{16,0},{32,16},{48,32},{64,48},{80,64},{96,80},{112,96},{1... | collective-permute-start | bytes 98312 | tf_op jit(solution)/shard_map/ppermute | solution.py:18
  186.4 4.6 %collective-permute-start.31 = (bf16[2,64,128]{2,1,0:T(8,128)(2,1)}, bf16[2,64,128]{2,1,0:T(8,128)(2,1)S(1)}, u32[]{:S(2)}, u32[]{:S(2)}) collective-permute-start(bf16[2,64,128]{2,1,0:T(8,128)(2,1)} %get-tuple-element.90), channel_id=1, source_target_pairs={{0,15},{1,0},{2,1},{3,2},{4,3},{5,4},{6,5},{7,6},{8,7},{9,8},{10,9... | collective-permute-start | bytes 98312 | tf_op jit(solution)/shard_map/ppermute | solution.py:18
  190.9 4.0 %shard_map.91.local_ref = f32[16,64,128]{2,1,0:T(8,128)} custom-call(s32[64]{0:T(128)} %reshape.146.cols_ref, bf16[16,64,128]{2,1,0:T(8,128)(2,1)} %get-tuple-element.85.rounded_ref, bf16[16,4,128,128]{3,2,1,0:T(8,128)(2,1)} %tiles_ref.17), custom_call_target="tpu_custom_call" | custom-call | tf_op jit(solution)/shard_map/pallas_call | solution.py:46
  195.5 2.8 shard_map.92
  200.3 7.5 %collective-permute-start.33 = (bf16[2,64,128]{2,1,0:T(8,128)(2,1)}, bf16[2,64,128]{2,1,0:T(8,128)(2,1)S(1)}, u32[]{:S(2)}, u32[]{:S(2)}) collective-permute-start(bf16[2,64,128]{2,1,0:T(8,128)(2,1)} %get-tuple-element.94), channel_id=1, source_target_pairs={{0,496},{16,0},{32,16},{48,32},{64,48},{80,64},{96,80},{112,96},{1... | collective-permute-start | bytes 98312 | tf_op jit(solution)/shard_map/ppermute | solution.py:18
  209.7 4.6 %collective-permute-start.35 = (bf16[2,64,128]{2,1,0:T(8,128)(2,1)}, bf16[2,64,128]{2,1,0:T(8,128)(2,1)S(1)}, u32[]{:S(2)}, u32[]{:S(2)}) collective-permute-start(bf16[2,64,128]{2,1,0:T(8,128)(2,1)} %get-tuple-element.96), channel_id=1, source_target_pairs={{0,15},{1,0},{2,1},{3,2},{4,3},{5,4},{6,5},{7,6},{8,7},{9,8},{10,9... | collective-permute-start | bytes 98312 | tf_op jit(solution)/shard_map/ppermute | solution.py:18
  214.3 4.0 %shard_map.93.local_ref = f32[16,64,128]{2,1,0:T(8,128)} custom-call(s32[64]{0:T(128)} %reshape.146.cols_ref, bf16[16,64,128]{2,1,0:T(8,128)(2,1)} %get-tuple-element.91.rounded_ref, bf16[16,4,128,128]{3,2,1,0:T(8,128)(2,1)} %tiles_ref.17), custom_call_target="tpu_custom_call" | custom-call | tf_op jit(solution)/shard_map/pallas_call | solution.py:46
  218.9 2.8 shard_map.94
  225.5 2.7 collective-permute-done.36
  230.1 3.7 %collective-permute-done.37 = f32[64,64]{1,0:T(8,128)S(1)} collective-permute-done((f32[64,64]{1,0:T(8,128)S(1)}, f32[64,64]{1,0:T(8,128)S(1)}, u32[]{:S(2)}, u32[]{:S(2)}) %collective-permute-start.37) | collective-permute-done | bytes 16416 | tf_op jit(solution)/shard_map/ppermute | solution.py:26
  233.8 3.6 %collective-permute-start.38 = (f32[64,64]{1,0:T(8,128)S(1)}, f32[64,64]{1,0:T(8,128)S(1)}, u32[]{:S(2)}, u32[]{:S(2)}) collective-permute-start(f32[64,64]{1,0:T(8,128)S(1)} %add.94), channel_id=1, source_target_pairs={{0,4},{1,5},{2,6},{3,7},{4,0},{5,1},{6,2},{7,3},{8,12},{9,13},{10,... | collective-permute-start | bytes 49160 | tf_op jit(solution)/shard_map/ppermute | solution.py:26
  237.5 5.4 %collective-permute-done.38 = f32[64,64]{1,0:T(8,128)S(1)} collective-permute-done((f32[64,64]{1,0:T(8,128)S(1)}, f32[64,64]{1,0:T(8,128)S(1)}, u32[]{:S(2)}, u32[]{:S(2)}) %collective-permute-start.38) | collective-permute-done | bytes 16416 | tf_op jit(solution)/shard_map/ppermute | solution.py:26
  242.9 9.3 %collective-permute-start.39 = (f32[64,64]{1,0:T(8,128)S(1)}, f32[64,64]{1,0:T(8,128)S(1)}, u32[]{:S(2)}, u32[]{:S(2)}) collective-permute-start(f32[64,64]{1,0:T(8,128)S(1)} %add.95), channel_id=1, source_target_pairs={{0,8},{1,9},{2,10},{3,11},{4,12},{5,13},{6,14},{7,15},{8,0},{9,1},... | collective-permute-start | bytes 49160 | tf_op jit(solution)/shard_map/ppermute | solution.py:26
  252.2 4.1 %collective-permute-done.39 = f32[64,64]{1,0:T(8,128)S(1)} collective-permute-done((f32[64,64]{1,0:T(8,128)S(1)}, f32[64,64]{1,0:T(8,128)S(1)}, u32[]{:S(2)}, u32[]{:S(2)}) %collective-permute-start.39) | collective-permute-done | bytes 16416 | tf_op jit(solution)/shard_map/ppermute | solution.py:26
  256.2 12.1 %collective-permute-start.40 = (f32[64,64]{1,0:T(8,128)S(1)}, f32[64,64]{1,0:T(8,128)S(1)}, u32[]{:S(2)}, u32[]{:S(2)}) collective-permute-start(f32[64,64]{1,0:T(8,128)S(1)} %add.96), channel_id=1, source_target_pairs={{0,16},{16,0},{32,48},{48,32},{64,80},{80,64},{96,112},{112,96},{1... | collective-permute-start | bytes 49160 | tf_op jit(solution)/shard_map/ppermute | solution.py:26
  271.1 2.7 collective-permute-done.41
  275.7 4.2 %collective-permute-done.42 = f32[64,64]{1,0:T(8,128)S(1)} collective-permute-done((f32[64,64]{1,0:T(8,128)S(1)}, f32[64,64]{1,0:T(8,128)S(1)}, u32[]{:S(2)}, u32[]{:S(2)}) %collective-permute-start.42) | collective-permute-done | bytes 16416 | tf_op jit(solution)/shard_map/ppermute | solution.py:26
  286.6 4.2 %collective-permute-done.44 = f32[64,64]{1,0:T(8,128)S(1)} collective-permute-done((f32[64,64]{1,0:T(8,128)S(1)}, f32[64,64]{1,0:T(8,128)S(1)}, u32[]{:S(2)}, u32[]{:S(2)}) %collective-permute-start.44) | collective-permute-done | bytes 16416 | tf_op jit(solution)/shard_map/ppermute | solution.py:26
  (167 shorter events, 64.4 us)
Async XLA Ops:
  1.7 25.7 %copy-start.1 = (bf16[16,64,128]{2,1,0:T(8,128)(2,1)}, bf16[16,64,128]{2,1,0:T(8,128)(2,1)S(1)}, u32[]{:S(2)}) copy-start(bf16[16,64,128]{2,1,0:T(8,128)(2,1)S(1)} %convert_element_type.3.rounded_ref) | copy-start | bytes 786436
  3.4 28.0 %collective-permute-start = (bf16[2,64,128]{2,1,0:T(8,128)(2,1)S(1)}, bf16[2,64,128]{2,1,0:T(8,128)(2,1)S(1)}, u32[]{:S(2)}, u32[]{:S(2)}) collective-permute-start(bf16[2,64,128]{2,1,0:T(8,128)(2,1)S(1)} %gather_fusion), channel_id=1, source_target_pairs={{0,16},{16,32},{32,48},{48,64},{64,80},{80,96},{96,112},{112,128},... | collective-permute-start | bytes 98312 | tf_op jit(solution)/shard_map/ppermute | solution.py:18
  8.4 22.9 %collective-permute-start.1 = (bf16[2,64,128]{2,1,0:T(8,128)(2,1)S(1)}, bf16[2,64,128]{2,1,0:T(8,128)(2,1)S(1)}, u32[]{:S(2)}, u32[]{:S(2)}) collective-permute-start(bf16[2,64,128]{2,1,0:T(8,128)(2,1)S(1)} %gather_fusion.1), channel_id=1, source_target_pairs={{0,496},{16,0},{32,16},{48,32},{64,48},{80,64},{96,80},{112,96},{1... | collective-permute-start | bytes 98312 | tf_op jit(solution)/shard_map/ppermute | solution.py:18
  15.2 16.2 %collective-permute-start.2 = (bf16[2,64,128]{2,1,0:T(8,128)(2,1)S(1)}, bf16[2,64,128]{2,1,0:T(8,128)(2,1)S(1)}, u32[]{:S(2)}, u32[]{:S(2)}) collective-permute-start(bf16[2,64,128]{2,1,0:T(8,128)(2,1)S(1)} %gather_fusion.2), channel_id=1, source_target_pairs={{0,1},{1,2},{2,3},{3,4},{4,5},{5,6},{6,7},{7,8},{8,9},{9,10},{10,1... | collective-permute-start | bytes 98312 | tf_op jit(solution)/shard_map/ppermute | solution.py:18
  17.7 13.7 %collective-permute-start.3 = (bf16[2,64,128]{2,1,0:T(8,128)(2,1)S(1)}, bf16[2,64,128]{2,1,0:T(8,128)(2,1)S(1)}, u32[]{:S(2)}, u32[]{:S(2)}) collective-permute-start(bf16[2,64,128]{2,1,0:T(8,128)(2,1)S(1)} %gather_fusion.3), channel_id=1, source_target_pairs={{0,15},{1,0},{2,1},{3,2},{4,3},{5,4},{6,5},{7,6},{8,7},{9,8},{10,9... | collective-permute-start | bytes 98312 | tf_op jit(solution)/shard_map/ppermute | solution.py:18
  35.4 18.5 %collective-permute-start.4 = (bf16[2,64,128]{2,1,0:T(8,128)(2,1)}, bf16[2,64,128]{2,1,0:T(8,128)(2,1)S(1)}, u32[]{:S(2)}, u32[]{:S(2)}) collective-permute-start(bf16[2,64,128]{2,1,0:T(8,128)(2,1)} %get-tuple-element.51), channel_id=1, source_target_pairs={{0,16},{16,32},{32,48},{48,64},{64,80},{80,96},{96,112},{112,128},... | collective-permute-start | bytes 98312 | tf_op jit(solution)/shard_map/ppermute | solution.py:18
  39.4 14.6 %collective-permute-start.5 = (bf16[2,64,128]{2,1,0:T(8,128)(2,1)}, bf16[2,64,128]{2,1,0:T(8,128)(2,1)S(1)}, u32[]{:S(2)}, u32[]{:S(2)}) collective-permute-start(bf16[2,64,128]{2,1,0:T(8,128)(2,1)} %get-tuple-element.52), channel_id=1, source_target_pairs={{0,496},{16,0},{32,16},{48,32},{64,48},{80,64},{96,80},{112,96},{1... | collective-permute-start | bytes 98312 | tf_op jit(solution)/shard_map/ppermute | solution.py:18
  43.5 10.5 %collective-permute-start.6 = (bf16[2,64,128]{2,1,0:T(8,128)(2,1)}, bf16[2,64,128]{2,1,0:T(8,128)(2,1)S(1)}, u32[]{:S(2)}, u32[]{:S(2)}) collective-permute-start(bf16[2,64,128]{2,1,0:T(8,128)(2,1)} %get-tuple-element.53), channel_id=1, source_target_pairs={{0,1},{1,2},{2,3},{3,4},{4,5},{5,6},{6,7},{7,8},{8,9},{9,10},{10,1... | collective-permute-start | bytes 98312 | tf_op jit(solution)/shard_map/ppermute | solution.py:18
  45.4 8.6 %collective-permute-start.7 = (bf16[2,64,128]{2,1,0:T(8,128)(2,1)}, bf16[2,64,128]{2,1,0:T(8,128)(2,1)S(1)}, u32[]{:S(2)}, u32[]{:S(2)}) collective-permute-start(bf16[2,64,128]{2,1,0:T(8,128)(2,1)} %get-tuple-element.54), channel_id=1, source_target_pairs={{0,15},{1,0},{2,1},{3,2},{4,3},{5,4},{6,5},{7,6},{8,7},{9,8},{10,9... | collective-permute-start | bytes 98312 | tf_op jit(solution)/shard_map/ppermute | solution.py:18
  58.0 20.5 %collective-permute-start.10 = (bf16[2,64,128]{2,1,0:T(8,128)(2,1)}, bf16[2,64,128]{2,1,0:T(8,128)(2,1)S(1)}, u32[]{:S(2)}, u32[]{:S(2)}) collective-permute-start(bf16[2,64,128]{2,1,0:T(8,128)(2,1)} %get-tuple-element.59), channel_id=1, source_target_pairs={{0,1},{1,2},{2,3},{3,4},{4,5},{5,6},{6,7},{7,8},{8,9},{9,10},{10,1... | collective-permute-start | bytes 98312 | tf_op jit(solution)/shard_map/ppermute | solution.py:18
  59.9 18.6 %collective-permute-start.11 = (bf16[2,64,128]{2,1,0:T(8,128)(2,1)}, bf16[2,64,128]{2,1,0:T(8,128)(2,1)S(1)}, u32[]{:S(2)}, u32[]{:S(2)}) collective-permute-start(bf16[2,64,128]{2,1,0:T(8,128)(2,1)} %get-tuple-element.60), channel_id=1, source_target_pairs={{0,15},{1,0},{2,1},{3,2},{4,3},{5,4},{6,5},{7,6},{8,7},{9,8},{10,9... | collective-permute-start | bytes 98312 | tf_op jit(solution)/shard_map/ppermute | solution.py:18
  64.5 14.0 %collective-permute-start.8 = (bf16[2,64,128]{2,1,0:T(8,128)(2,1)}, bf16[2,64,128]{2,1,0:T(8,128)(2,1)S(1)}, u32[]{:S(2)}, u32[]{:S(2)}) collective-permute-start(bf16[2,64,128]{2,1,0:T(8,128)(2,1)} %get-tuple-element.57), channel_id=1, source_target_pairs={{0,16},{16,32},{32,48},{48,64},{64,80},{80,96},{96,112},{112,128},... | collective-permute-start | bytes 98312 | tf_op jit(solution)/shard_map/ppermute | solution.py:18
  67.1 11.5 %collective-permute-start.9 = (bf16[2,64,128]{2,1,0:T(8,128)(2,1)}, bf16[2,64,128]{2,1,0:T(8,128)(2,1)S(1)}, u32[]{:S(2)}, u32[]{:S(2)}) collective-permute-start(bf16[2,64,128]{2,1,0:T(8,128)(2,1)} %get-tuple-element.58), channel_id=1, source_target_pairs={{0,496},{16,0},{32,16},{48,32},{64,48},{80,64},{96,80},{112,96},{1... | collective-permute-start | bytes 98312 | tf_op jit(solution)/shard_map/ppermute | solution.py:18
  78.5 0.6 copy-start.23
  82.0 19.4 %collective-permute-start.12 = (bf16[2,64,128]{2,1,0:T(8,128)(2,1)}, bf16[2,64,128]{2,1,0:T(8,128)(2,1)S(1)}, u32[]{:S(2)}, u32[]{:S(2)}) collective-permute-start(bf16[2,64,128]{2,1,0:T(8,128)(2,1)} %get-tuple-element.63), channel_id=1, source_target_pairs={{0,16},{16,32},{32,48},{48,64},{64,80},{80,96},{96,112},{112,128},... | collective-permute-start | bytes 98312 | tf_op jit(solution)/shard_map/ppermute | solution.py:18
  83.9 17.4 %collective-permute-start.13 = (bf16[2,64,128]{2,1,0:T(8,128)(2,1)}, bf16[2,64,128]{2,1,0:T(8,128)(2,1)S(1)}, u32[]{:S(2)}, u32[]{:S(2)}) collective-permute-start(bf16[2,64,128]{2,1,0:T(8,128)(2,1)} %get-tuple-element.64), channel_id=1, source_target_pairs={{0,496},{16,0},{32,16},{48,32},{64,48},{80,64},{96,80},{112,96},{1... | collective-permute-start | bytes 98312 | tf_op jit(solution)/shard_map/ppermute | solution.py:18
  90.9 10.5 %collective-permute-start.14 = (bf16[2,64,128]{2,1,0:T(8,128)(2,1)}, bf16[2,64,128]{2,1,0:T(8,128)(2,1)S(1)}, u32[]{:S(2)}, u32[]{:S(2)}) collective-permute-start(bf16[2,64,128]{2,1,0:T(8,128)(2,1)} %get-tuple-element.65), channel_id=1, source_target_pairs={{0,1},{1,2},{2,3},{3,4},{4,5},{5,6},{6,7},{7,8},{8,9},{9,10},{10,1... | collective-permute-start | bytes 98312 | tf_op jit(solution)/shard_map/ppermute | solution.py:18
  92.8 8.6 %collective-permute-start.15 = (bf16[2,64,128]{2,1,0:T(8,128)(2,1)}, bf16[2,64,128]{2,1,0:T(8,128)(2,1)S(1)}, u32[]{:S(2)}, u32[]{:S(2)}) collective-permute-start(bf16[2,64,128]{2,1,0:T(8,128)(2,1)} %get-tuple-element.66), channel_id=1, source_target_pairs={{0,15},{1,0},{2,1},{3,2},{4,3},{5,4},{6,5},{7,6},{8,7},{9,8},{10,9... | collective-permute-start | bytes 98312 | tf_op jit(solution)/shard_map/ppermute | solution.py:18
  104.8 19.9 %collective-permute-start.16 = (bf16[2,64,128]{2,1,0:T(8,128)(2,1)}, bf16[2,64,128]{2,1,0:T(8,128)(2,1)S(1)}, u32[]{:S(2)}, u32[]{:S(2)}) collective-permute-start(bf16[2,64,128]{2,1,0:T(8,128)(2,1)} %get-tuple-element.69), channel_id=1, source_target_pairs={{0,16},{16,32},{32,48},{48,64},{64,80},{80,96},{96,112},{112,128},... | collective-permute-start | bytes 98312 | tf_op jit(solution)/shard_map/ppermute | solution.py:18
  106.7 18.0 %collective-permute-start.17 = (bf16[2,64,128]{2,1,0:T(8,128)(2,1)}, bf16[2,64,128]{2,1,0:T(8,128)(2,1)S(1)}, u32[]{:S(2)}, u32[]{:S(2)}) collective-permute-start(bf16[2,64,128]{2,1,0:T(8,128)(2,1)} %get-tuple-element.70), channel_id=1, source_target_pairs={{0,496},{16,0},{32,16},{48,32},{64,48},{80,64},{96,80},{112,96},{1... | collective-permute-start | bytes 98312 | tf_op jit(solution)/shard_map/ppermute | solution.py:18
  114.2 10.5 %collective-permute-start.18 = (bf16[2,64,128]{2,1,0:T(8,128)(2,1)}, bf16[2,64,128]{2,1,0:T(8,128)(2,1)S(1)}, u32[]{:S(2)}, u32[]{:S(2)}) collective-permute-start(bf16[2,64,128]{2,1,0:T(8,128)(2,1)} %get-tuple-element.71), channel_id=1, source_target_pairs={{0,1},{1,2},{2,3},{3,4},{4,5},{5,6},{6,7},{7,8},{8,9},{9,10},{10,1... | collective-permute-start | bytes 98312 | tf_op jit(solution)/shard_map/ppermute | solution.py:18
  116.2 8.6 %collective-permute-start.19 = (bf16[2,64,128]{2,1,0:T(8,128)(2,1)}, bf16[2,64,128]{2,1,0:T(8,128)(2,1)S(1)}, u32[]{:S(2)}, u32[]{:S(2)}) collective-permute-start(bf16[2,64,128]{2,1,0:T(8,128)(2,1)} %get-tuple-element.72), channel_id=1, source_target_pairs={{0,15},{1,0},{2,1},{3,2},{4,3},{5,4},{6,5},{7,6},{8,7},{9,8},{10,9... | collective-permute-start | bytes 98312 | tf_op jit(solution)/shard_map/ppermute | solution.py:18
  128.2 19.9 %collective-permute-start.20 = (bf16[2,64,128]{2,1,0:T(8,128)(2,1)}, bf16[2,64,128]{2,1,0:T(8,128)(2,1)S(1)}, u32[]{:S(2)}, u32[]{:S(2)}) collective-permute-start(bf16[2,64,128]{2,1,0:T(8,128)(2,1)} %get-tuple-element.75), channel_id=1, source_target_pairs={{0,16},{16,32},{32,48},{48,64},{64,80},{80,96},{96,112},{112,128},... | collective-permute-start | bytes 98312 | tf_op jit(solution)/shard_map/ppermute | solution.py:18
  130.1 18.0 %collective-permute-start.21 = (bf16[2,64,128]{2,1,0:T(8,128)(2,1)}, bf16[2,64,128]{2,1,0:T(8,128)(2,1)S(1)}, u32[]{:S(2)}, u32[]{:S(2)}) collective-permute-start(bf16[2,64,128]{2,1,0:T(8,128)(2,1)} %get-tuple-element.76), channel_id=1, source_target_pairs={{0,496},{16,0},{32,16},{48,32},{64,48},{80,64},{96,80},{112,96},{1... | collective-permute-start | bytes 98312 | tf_op jit(solution)/shard_map/ppermute | solution.py:18
  137.6 10.5 %collective-permute-start.22 = (bf16[2,64,128]{2,1,0:T(8,128)(2,1)}, bf16[2,64,128]{2,1,0:T(8,128)(2,1)S(1)}, u32[]{:S(2)}, u32[]{:S(2)}) collective-permute-start(bf16[2,64,128]{2,1,0:T(8,128)(2,1)} %get-tuple-element.77), channel_id=1, source_target_pairs={{0,1},{1,2},{2,3},{3,4},{4,5},{5,6},{6,7},{7,8},{8,9},{9,10},{10,1... | collective-permute-start | bytes 98312 | tf_op jit(solution)/shard_map/ppermute | solution.py:18
  139.5 8.6 %collective-permute-start.23 = (bf16[2,64,128]{2,1,0:T(8,128)(2,1)}, bf16[2,64,128]{2,1,0:T(8,128)(2,1)S(1)}, u32[]{:S(2)}, u32[]{:S(2)}) collective-permute-start(bf16[2,64,128]{2,1,0:T(8,128)(2,1)} %get-tuple-element.78), channel_id=1, source_target_pairs={{0,15},{1,0},{2,1},{3,2},{4,3},{5,4},{6,5},{7,6},{8,7},{9,8},{10,9... | collective-permute-start | bytes 98312 | tf_op jit(solution)/shard_map/ppermute | solution.py:18
  151.6 19.9 %collective-permute-start.24 = (bf16[2,64,128]{2,1,0:T(8,128)(2,1)}, bf16[2,64,128]{2,1,0:T(8,128)(2,1)S(1)}, u32[]{:S(2)}, u32[]{:S(2)}) collective-permute-start(bf16[2,64,128]{2,1,0:T(8,128)(2,1)} %get-tuple-element.81), channel_id=1, source_target_pairs={{0,16},{16,32},{32,48},{48,64},{64,80},{80,96},{96,112},{112,128},... | collective-permute-start | bytes 98312 | tf_op jit(solution)/shard_map/ppermute | solution.py:18
  153.5 18.0 %collective-permute-start.25 = (bf16[2,64,128]{2,1,0:T(8,128)(2,1)}, bf16[2,64,128]{2,1,0:T(8,128)(2,1)S(1)}, u32[]{:S(2)}, u32[]{:S(2)}) collective-permute-start(bf16[2,64,128]{2,1,0:T(8,128)(2,1)} %get-tuple-element.82), channel_id=1, source_target_pairs={{0,496},{16,0},{32,16},{48,32},{64,48},{80,64},{96,80},{112,96},{1... | collective-permute-start | bytes 98312 | tf_op jit(solution)/shard_map/ppermute | solution.py:18
  161.0 10.5 %collective-permute-start.26 = (bf16[2,64,128]{2,1,0:T(8,128)(2,1)}, bf16[2,64,128]{2,1,0:T(8,128)(2,1)S(1)}, u32[]{:S(2)}, u32[]{:S(2)}) collective-permute-start(bf16[2,64,128]{2,1,0:T(8,128)(2,1)} %get-tuple-element.83), channel_id=1, source_target_pairs={{0,1},{1,2},{2,3},{3,4},{4,5},{5,6},{6,7},{7,8},{8,9},{9,10},{10,1... | collective-permute-start | bytes 98312 | tf_op jit(solution)/shard_map/ppermute | solution.py:18
  163.0 8.6 %collective-permute-start.27 = (bf16[2,64,128]{2,1,0:T(8,128)(2,1)}, bf16[2,64,128]{2,1,0:T(8,128)(2,1)S(1)}, u32[]{:S(2)}, u32[]{:S(2)}) collective-permute-start(bf16[2,64,128]{2,1,0:T(8,128)(2,1)} %get-tuple-element.84), channel_id=1, source_target_pairs={{0,15},{1,0},{2,1},{3,2},{4,3},{5,4},{6,5},{7,6},{8,7},{9,8},{10,9... | collective-permute-start | bytes 98312 | tf_op jit(solution)/shard_map/ppermute | solution.py:18
  175.0 19.9 %collective-permute-start.28 = (bf16[2,64,128]{2,1,0:T(8,128)(2,1)}, bf16[2,64,128]{2,1,0:T(8,128)(2,1)S(1)}, u32[]{:S(2)}, u32[]{:S(2)}) collective-permute-start(bf16[2,64,128]{2,1,0:T(8,128)(2,1)} %get-tuple-element.87), channel_id=1, source_target_pairs={{0,16},{16,32},{32,48},{48,64},{64,80},{80,96},{96,112},{112,128},... | collective-permute-start | bytes 98312 | tf_op jit(solution)/shard_map/ppermute | solution.py:18
  176.9 18.0 %collective-permute-start.29 = (bf16[2,64,128]{2,1,0:T(8,128)(2,1)}, bf16[2,64,128]{2,1,0:T(8,128)(2,1)S(1)}, u32[]{:S(2)}, u32[]{:S(2)}) collective-permute-start(bf16[2,64,128]{2,1,0:T(8,128)(2,1)} %get-tuple-element.88), channel_id=1, source_target_pairs={{0,496},{16,0},{32,16},{48,32},{64,48},{80,64},{96,80},{112,96},{1... | collective-permute-start | bytes 98312 | tf_op jit(solution)/shard_map/ppermute | solution.py:18
  184.4 10.5 %collective-permute-start.30 = (bf16[2,64,128]{2,1,0:T(8,128)(2,1)}, bf16[2,64,128]{2,1,0:T(8,128)(2,1)S(1)}, u32[]{:S(2)}, u32[]{:S(2)}) collective-permute-start(bf16[2,64,128]{2,1,0:T(8,128)(2,1)} %get-tuple-element.89), channel_id=1, source_target_pairs={{0,1},{1,2},{2,3},{3,4},{4,5},{5,6},{6,7},{7,8},{8,9},{9,10},{10,1... | collective-permute-start | bytes 98312 | tf_op jit(solution)/shard_map/ppermute | solution.py:18
  186.4 8.6 %collective-permute-start.31 = (bf16[2,64,128]{2,1,0:T(8,128)(2,1)}, bf16[2,64,128]{2,1,0:T(8,128)(2,1)S(1)}, u32[]{:S(2)}, u32[]{:S(2)}) collective-permute-start(bf16[2,64,128]{2,1,0:T(8,128)(2,1)} %get-tuple-element.90), channel_id=1, source_target_pairs={{0,15},{1,0},{2,1},{3,2},{4,3},{5,4},{6,5},{7,6},{8,7},{9,8},{10,9... | collective-permute-start | bytes 98312 | tf_op jit(solution)/shard_map/ppermute | solution.py:18
  198.4 19.9 %collective-permute-start.32 = (bf16[2,64,128]{2,1,0:T(8,128)(2,1)}, bf16[2,64,128]{2,1,0:T(8,128)(2,1)S(1)}, u32[]{:S(2)}, u32[]{:S(2)}) collective-permute-start(bf16[2,64,128]{2,1,0:T(8,128)(2,1)} %get-tuple-element.93), channel_id=1, source_target_pairs={{0,16},{16,32},{32,48},{48,64},{64,80},{80,96},{96,112},{112,128},... | collective-permute-start | bytes 98312 | tf_op jit(solution)/shard_map/ppermute | solution.py:18
  200.3 18.0 %collective-permute-start.33 = (bf16[2,64,128]{2,1,0:T(8,128)(2,1)}, bf16[2,64,128]{2,1,0:T(8,128)(2,1)S(1)}, u32[]{:S(2)}, u32[]{:S(2)}) collective-permute-start(bf16[2,64,128]{2,1,0:T(8,128)(2,1)} %get-tuple-element.94), channel_id=1, source_target_pairs={{0,496},{16,0},{32,16},{48,32},{64,48},{80,64},{96,80},{112,96},{1... | collective-permute-start | bytes 98312 | tf_op jit(solution)/shard_map/ppermute | solution.py:18
  207.8 10.5 %collective-permute-start.34 = (bf16[2,64,128]{2,1,0:T(8,128)(2,1)}, bf16[2,64,128]{2,1,0:T(8,128)(2,1)S(1)}, u32[]{:S(2)}, u32[]{:S(2)}) collective-permute-start(bf16[2,64,128]{2,1,0:T(8,128)(2,1)} %get-tuple-element.95), channel_id=1, source_target_pairs={{0,1},{1,2},{2,3},{3,4},{4,5},{5,6},{6,7},{7,8},{8,9},{9,10},{10,1... | collective-permute-start | bytes 98312 | tf_op jit(solution)/shard_map/ppermute | solution.py:18
  209.7 8.6 %collective-permute-start.35 = (bf16[2,64,128]{2,1,0:T(8,128)(2,1)}, bf16[2,64,128]{2,1,0:T(8,128)(2,1)S(1)}, u32[]{:S(2)}, u32[]{:S(2)}) collective-permute-start(bf16[2,64,128]{2,1,0:T(8,128)(2,1)} %get-tuple-element.96), channel_id=1, source_target_pairs={{0,15},{1,0},{2,1},{3,2},{4,3},{5,4},{6,5},{7,6},{8,7},{9,8},{10,9... | collective-permute-start | bytes 98312 | tf_op jit(solution)/shard_map/ppermute | solution.py:18
  221.7 70.6 %copy-start = (f32[16,64,128]{2,1,0:T(8,128)S(1)}, f32[16,64,128]{2,1,0:T(8,128)}, u32[]{:S(2)}) copy-start(f32[16,64,128]{2,1,0:T(8,128)} %get-tuple-element.97) | copy-start | bytes 1572868
  223.5 4.7 %collective-permute-start.36 = (f32[64,64]{1,0:T(8,128)S(1)}, f32[64,64]{1,0:T(8,128)S(1)}, u32[]{:S(2)}, u32[]{:S(2)}) collective-permute-start(f32[64,64]{1,0:T(8,128)S(1)} %convolution_bitcast_fusion), channel_id=1, source_target_pairs={{0,1},{1,0},{2,3},{3,2},{4,5},{5,4},{6,7},{7,6},{8,9},{9,8},{10,11... | collective-permute-start | bytes 49160 | tf_op jit(solution)/shard_map/ppermute | solution.py:26
  228.2 5.6 %collective-permute-start.37 = (f32[64,64]{1,0:T(8,128)S(1)}, f32[64,64]{1,0:T(8,128)S(1)}, u32[]{:S(2)}, u32[]{:S(2)}) collective-permute-start(f32[64,64]{1,0:T(8,128)S(1)} %add.93), channel_id=1, source_target_pairs={{0,2},{1,3},{2,0},{3,1},{4,6},{5,7},{6,4},{7,5},{8,10},{9,11},{10,... | collective-permute-start | bytes 49160 | tf_op jit(solution)/shard_map/ppermute | solution.py:26
  233.8 9.0 %collective-permute-start.38 = (f32[64,64]{1,0:T(8,128)S(1)}, f32[64,64]{1,0:T(8,128)S(1)}, u32[]{:S(2)}, u32[]{:S(2)}) collective-permute-start(f32[64,64]{1,0:T(8,128)S(1)} %add.94), channel_id=1, source_target_pairs={{0,4},{1,5},{2,6},{3,7},{4,0},{5,1},{6,2},{7,3},{8,12},{9,13},{10,... | collective-permute-start | bytes 49160 | tf_op jit(solution)/shard_map/ppermute | solution.py:26
  242.9 13.4 %collective-permute-start.39 = (f32[64,64]{1,0:T(8,128)S(1)}, f32[64,64]{1,0:T(8,128)S(1)}, u32[]{:S(2)}, u32[]{:S(2)}) collective-permute-start(f32[64,64]{1,0:T(8,128)S(1)} %add.95), channel_id=1, source_target_pairs={{0,8},{1,9},{2,10},{3,11},{4,12},{5,13},{6,14},{7,15},{8,0},{9,1},... | collective-permute-start | bytes 49160 | tf_op jit(solution)/shard_map/ppermute | solution.py:26
  256.2 12.9 %collective-permute-start.40 = (f32[64,64]{1,0:T(8,128)S(1)}, f32[64,64]{1,0:T(8,128)S(1)}, u32[]{:S(2)}, u32[]{:S(2)}) collective-permute-start(f32[64,64]{1,0:T(8,128)S(1)} %add.96), channel_id=1, source_target_pairs={{0,16},{16,0},{32,48},{48,32},{64,80},{80,64},{96,112},{112,96},{1... | collective-permute-start | bytes 49160 | tf_op jit(solution)/shard_map/ppermute | solution.py:26
  269.2 4.6 %collective-permute-start.41 = (f32[64,64]{1,0:T(8,128)S(1)}, f32[64,64]{1,0:T(8,128)S(1)}, u32[]{:S(2)}, u32[]{:S(2)}) collective-permute-start(f32[64,64]{1,0:T(8,128)S(1)} %add.97), channel_id=1, source_target_pairs={{0,32},{16,48},{32,0},{48,16},{64,96},{80,112},{96,64},{112,80},{1... | collective-permute-start | bytes 49160 | tf_op jit(solution)/shard_map/ppermute | solution.py:26
  273.8 6.2 %collective-permute-start.42 = (f32[64,64]{1,0:T(8,128)S(1)}, f32[64,64]{1,0:T(8,128)S(1)}, u32[]{:S(2)}, u32[]{:S(2)}) collective-permute-start(f32[64,64]{1,0:T(8,128)S(1)} %add.98), channel_id=1, source_target_pairs={{0,64},{16,80},{32,96},{48,112},{64,0},{80,16},{96,32},{112,48},{1... | collective-permute-start | bytes 49160 | tf_op jit(solution)/shard_map/ppermute | solution.py:26
  280.0 4.6 %collective-permute-start.43 = (f32[64,64]{1,0:T(8,128)S(1)}, f32[64,64]{1,0:T(8,128)S(1)}, u32[]{:S(2)}, u32[]{:S(2)}) collective-permute-start(f32[64,64]{1,0:T(8,128)S(1)} %add.99), channel_id=1, source_target_pairs={{0,128},{16,144},{32,160},{48,176},{64,192},{80,208},{96,224},{112... | collective-permute-start | bytes 49160 | tf_op jit(solution)/shard_map/ppermute | solution.py:26
  284.6 6.2 %collective-permute-start.44 = (f32[64,64]{1,0:T(8,128)S(1)}, f32[64,64]{1,0:T(8,128)S(1)}, u32[]{:S(2)}, u32[]{:S(2)}) collective-permute-start(f32[64,64]{1,0:T(8,128)S(1)} %add.100), channel_id=1, source_target_pairs={{0,256},{16,272},{32,288},{48,304},{64,320},{80,336},{96,352},{112... | collective-permute-start | bytes 49160 | tf_op jit(solution)/shard_map/ppermute | solution.py:26
  (35 other events, 21.2 us)

commit v6 on v5

--- a/solution.py
+++ b/solution.py
@@ -7,9 +7,9 @@
 from jax.experimental.pallas import tpu as pltpu
 from jax.sharding import PartitionSpec as P
 
+
 DEG = 9
 INTERPRET = False
-CONTRACT_LAST = (((1,), (1,)), ((), ()))
 
 
 def from_behind(value, axis, steps):
@@ -28,28 +28,25 @@
     return value
 
 
-def _local_kernel(cols_ref, rounded_ref, tiles_ref, out_ref):
-    rows, per_row = tiles_ref.shape[0], tiles_ref.shape[1]
+def _local_kernel(cols_ref, rounded_ref, stacked_ref, out_ref):
+    rows = stacked_ref.shape[0]
+    per_row = stacked_ref.shape[1] // rounded_ref.shape[2]
     for r in range(rows):
-        acc = None
-        for t in range(per_row):
-            block = rounded_ref[cols_ref[r * per_row + t]]
-            part = lax.dot_general(
-                block, tiles_ref[r, t], CONTRACT_LAST, preferred_element_type=jnp.float32
-            )
-            acc = part if acc is None else acc + part
-        out_ref[r] = acc
+        blocks = [rounded_ref[cols_ref[r * per_row + t]] for t in range(per_row)]
+        out_ref[r] = jnp.dot(
+            jnp.concatenate(blocks, axis=1), stacked_ref[r], preferred_element_type=jnp.float32
+        )
 
 
-def local_product(rounded, tiles, cols):
+def local_product(rounded, stacked, cols):
     vmem = pl.BlockSpec(memory_space=pltpu.VMEM)
     return pl.pallas_call(
         _local_kernel,
-        out_shape=jax.ShapeDtypeStruct((tiles.shape[0],) + rounded.shape[1:], jnp.float32),
+        out_shape=jax.ShapeDtypeStruct((stacked.shape[0],) + rounded.shape[1:], jnp.float32),
         in_specs=[pl.BlockSpec(memory_space=pltpu.SMEM), vmem, vmem],
         out_specs=vmem,
         interpret=INTERPRET,
-    )(cols.reshape(-1), rounded, tiles)
+    )(cols.reshape(-1), rounded, stacked)
 
 
 def _combine_kernel(slot_ref, picks_ref, local_ref, older_ref, halo_ref, *refs, scale, with_older):
@@ -60,9 +57,7 @@
             received_ref[d * per_list + i] = pieces[d][i]
     for r in range(local_ref.shape[0]):
         block = received_ref[slot_ref[r]]
-        coupled = lax.dot_general(
-            block, halo_ref[r], CONTRACT_LAST, preferred_element_type=jnp.float32
-        )
+        coupled = jnp.dot(block, halo_ref[r], preferred_element_type=jnp.float32)
         value = local_ref[r] + coupled
         if with_older:
             value = scale * value - older_ref[r]
@@ -94,26 +89,27 @@
 
 
 def exchange(pieces):
-    return [
-        from_behind(pieces[0], "px", 1),
-        from_behind(pieces[1], "px", -1),
-        from_behind(pieces[2], "py", 1),
-        from_behind(pieces[3], "py", -1),
-    ]
+    from_yhigh = from_behind(pieces[3], "py", -1)
+    from_ylow = from_behind(pieces[2], "py", 1)
+    from_xhigh = from_behind(pieces[1], "px", -1)
+    from_xlow = from_behind(pieces[0], "px", 1)
+    return [from_xlow, from_xhigh, from_ylow, from_yhigh]
 
 
 def shards(start_vecs, local_tiles, local_cols, halo_tiles, halo_slot, boundary):
-    per_list = boundary.shape[1]
     picks = boundary.reshape(-1)
     rounded = start_vecs.astype(jnp.bfloat16)
     outgoing = [rounded[boundary[d]] for d in range(4)]
+    rows, per_row, size = local_tiles.shape[0], local_tiles.shape[1], local_tiles.shape[3]
+    stacked = jnp.swapaxes(local_tiles, 2, 3).reshape(rows, per_row * size, size)
+    halo_t = jnp.swapaxes(halo_tiles, 1, 2)
     older = start_vecs
     current = start_vecs
     for step in range(DEG):
         received = exchange(outgoing)
-        local = local_product(rounded, local_tiles, local_cols)
+        local = local_product(rounded, stacked, local_cols)
         newer, rounded, outgoing = combine(
-            local, older, received, halo_tiles, halo_slot, picks, 2.0, step > 0
+            local, older, received, halo_t, halo_slot, picks, 2.0, step > 0
         )
         older, current = current, newer
 

time: 297 us -> 290 us (0.976)
  Pallas kernels: 61 us -> 50.7 us
  local copies, waits for them, and re-layouts: 13.5 us -> 17.2 us
    pallas_call x9, Pallas kernels: 35.6 us -> 27 us  [local_product(): pl.pallas_call(_local_kernel, out_shape=jax.ShapeDtypeStruct((stacked.sha...]
    transpose x0 -> x1, local copies, waits for them, and re-layouts: none -> 3.97 us  [shards(): jnp.swapaxes(local_tiles, 2, 3).reshape(rows, per_row * size, size)]
    unnamed x78 -> x83, local copies, waits for them, and re-layouts: 8.09 us -> 7.85 us
  transfers between devices with their start and end apart: 45 -> 45, of which waited for: 9 -> 9; matrix products, arithmetic and copies ran while one was open for 2% -> 3% of each run, Pallas kernels for 12% -> 9%
where the time goes in v6:
time: 290 us; the launch traced here: 286 us
  starting transfers between devices  183 us (63%)
  Pallas kernels  50.7 us (17%)
  waiting for transfers between devices  29.8 us (10%)
  local copies, waits for them, and re-layouts  17.2 us (6%)
    ppermute x36, starting transfers between devices, from_behind(): return lax.ppermute(value, axis, pairs)  145 us
    ppermute x9, starting transfers between devices, butterfly_sum(): value = value + lax.ppermute(value, axis, pairs)  37.2 us
    ppermute x9, waiting for transfers between devices, butterfly_sum(): value = value + lax.ppermute(value, axis, pairs)  29.7 us
    pallas_call x9, Pallas kernels, local_product(): pl.pallas_call(_local_kernel, out_shape=jax.ShapeDtypeStruct((stacked.sha...  27 us
    pallas_call x9, Pallas kernels, combine(): pl.pallas_call(kernel, out_shape=(jax.ShapeDtypeStruct(local.shape, jnp.f...  23.6 us
    unnamed x83, local copies, waits for them, and re-layouts  7.85 us
  transfers between devices with their start and end apart: 45, of which 9 were waited for; matrix products, arithmetic and copies ran while one was open for 3% of the time, Pallas kernels for 9%

profile of v6, /device:TPU:1, one launch (start us, length us, event | category | flops | bytes accessed | tf_op | source)
XLA Modules:
  0.0 286.4 jit_solution(14651677753575155070)
XLA Ops:
  3.4 4.5 %collective-permute-start = (bf16[2,64,128]{2,1,0:T(8,128)(2,1)S(1)}, bf16[2,64,128]{2,1,0:T(8,128)(2,1)S(1)}, u32[]{:S(2)}, u32[]{:S(2)}) collective-permute-start(bf16[2,64,128]{2,1,0:T(8,128)(2,1)S(1)} %gather_fusion), channel_id=1, source_target_pairs={{0,16},{16,32},{32,48},{48,64},{64,80},{80,96},{96,112},{112,128},... | collective-permute-start | bytes 98312 | tf_op jit(solution)/shard_map/ppermute | solution.py:18
  8.4 6.2 %collective-permute-start.1 = (bf16[2,64,128]{2,1,0:T(8,128)(2,1)S(1)}, bf16[2,64,128]{2,1,0:T(8,128)(2,1)S(1)}, u32[]{:S(2)}, u32[]{:S(2)}) collective-permute-start(bf16[2,64,128]{2,1,0:T(8,128)(2,1)S(1)} %gather_fusion.1), channel_id=1, source_target_pairs={{0,496},{16,0},{32,16},{48,32},{64,48},{80,64},{96,80},{112,96},{1... | collective-permute-start | bytes 98312 | tf_op jit(solution)/shard_map/ppermute | solution.py:18
  17.7 6.9 %collective-permute-start.3 = (bf16[2,64,128]{2,1,0:T(8,128)(2,1)S(1)}, bf16[2,64,128]{2,1,0:T(8,128)(2,1)S(1)}, u32[]{:S(2)}, u32[]{:S(2)}) collective-permute-start(bf16[2,64,128]{2,1,0:T(8,128)(2,1)S(1)} %gather_fusion.3), channel_id=1, source_target_pairs={{0,15},{1,0},{2,1},{3,2},{4,3},{5,4},{6,5},{7,6},{8,7},{9,8},{10,9... | collective-permute-start | bytes 98312 | tf_op jit(solution)/shard_map/ppermute | solution.py:18
  25.4 4.0 %copy.14 = bf16[16,4,128,128]{3,2,1,0:T(8,128)(2,1)} copy(bf16[16,4,128,128]{2,3,1,0:T(8,128)(2,1)} %bitcast.43) | data formatting | bytes 4194304 | tf_op jit(solution)/shard_map/transpose | solution.py:104
  31.7 3.0 %shard_map.77.local_ref = f32[16,64,128]{2,1,0:T(8,128)} custom-call(s32[64]{0:T(128)} %reshape.149.cols_ref, bf16[16,64,128]{2,1,0:T(8,128)(2,1)} %copy-done.1, bf16[16,512,128]{2,1,0:T(8,128)(2,1)} %bitcast.25), custom_call_target="tpu_custom_call" | custom-call | tf_op jit(solution)/shard_map/pallas_call | solution.py:43
  35.4 2.6 shard_map.78
  38.0 3.9 %collective-permute-start.4 = (bf16[2,64,128]{2,1,0:T(8,128)(2,1)}, bf16[2,64,128]{2,1,0:T(8,128)(2,1)S(1)}, u32[]{:S(2)}, u32[]{:S(2)}) collective-permute-start(bf16[2,64,128]{2,1,0:T(8,128)(2,1)} %get-tuple-element.51), channel_id=1, source_target_pairs={{0,16},{16,32},{32,48},{48,64},{64,80},{80,96},{96,112},{112,128},... | collective-permute-start | bytes 98312 | tf_op jit(solution)/shard_map/ppermute | solution.py:18
  41.9 4.1 %collective-permute-start.5 = (bf16[2,64,128]{2,1,0:T(8,128)(2,1)}, bf16[2,64,128]{2,1,0:T(8,128)(2,1)S(1)}, u32[]{:S(2)}, u32[]{:S(2)}) collective-permute-start(bf16[2,64,128]{2,1,0:T(8,128)(2,1)} %get-tuple-element.52), channel_id=1, source_target_pairs={{0,496},{16,0},{32,16},{48,32},{64,48},{80,64},{96,80},{112,96},{1... | collective-permute-start | bytes 98312 | tf_op jit(solution)/shard_map/ppermute | solution.py:18
  48.0 4.6 %collective-permute-start.7 = (bf16[2,64,128]{2,1,0:T(8,128)(2,1)}, bf16[2,64,128]{2,1,0:T(8,128)(2,1)S(1)}, u32[]{:S(2)}, u32[]{:S(2)}) collective-permute-start(bf16[2,64,128]{2,1,0:T(8,128)(2,1)} %get-tuple-element.54), channel_id=1, source_target_pairs={{0,15},{1,0},{2,1},{3,2},{4,3},{5,4},{6,5},{7,6},{8,7},{9,8},{10,9... | collective-permute-start | bytes 98312 | tf_op jit(solution)/shard_map/ppermute | solution.py:18
  52.6 3.0 %shard_map.79.local_ref = f32[16,64,128]{2,1,0:T(8,128)} custom-call(s32[64]{0:T(128)} %reshape.149.cols_ref, bf16[16,64,128]{2,1,0:T(8,128)(2,1)} %get-tuple-element.50.rounded_ref, bf16[16,512,128]{2,1,0:T(8,128)(2,1)} %bitcast.26), custom_call_target="tpu_custom_call" | custom-call | tf_op jit(solution)/shard_map/pallas_call | solution.py:43
  56.8 2.6 shard_map.80
  61.3 4.6 %collective-permute-start.11 = (bf16[2,64,128]{2,1,0:T(8,128)(2,1)}, bf16[2,64,128]{2,1,0:T(8,128)(2,1)S(1)}, u32[]{:S(2)}, u32[]{:S(2)}) collective-permute-start(bf16[2,64,128]{2,1,0:T(8,128)(2,1)} %get-tuple-element.60), channel_id=1, source_target_pairs={{0,15},{1,0},{2,1},{3,2},{4,3},{5,4},{6,5},{7,6},{8,7},{9,8},{10,9... | collective-permute-start | bytes 98312 | tf_op jit(solution)/shard_map/ppermute | solution.py:18
  68.5 7.5 %collective-permute-start.9 = (bf16[2,64,128]{2,1,0:T(8,128)(2,1)}, bf16[2,64,128]{2,1,0:T(8,128)(2,1)S(1)}, u32[]{:S(2)}, u32[]{:S(2)}) collective-permute-start(bf16[2,64,128]{2,1,0:T(8,128)(2,1)} %get-tuple-element.58), channel_id=1, source_target_pairs={{0,496},{16,0},{32,16},{48,32},{64,48},{80,64},{96,80},{112,96},{1... | collective-permute-start | bytes 98312 | tf_op jit(solution)/shard_map/ppermute | solution.py:18
  75.9 3.0 %shard_map.81.local_ref = f32[16,64,128]{2,1,0:T(8,128)} custom-call(s32[64]{0:T(128)} %reshape.149.cols_ref, bf16[16,64,128]{2,1,0:T(8,128)(2,1)} %get-tuple-element.55.rounded_ref, bf16[16,512,128]{2,1,0:T(8,128)(2,1)} %bitcast.27), custom_call_target="tpu_custom_call" | custom-call | tf_op jit(solution)/shard_map/pallas_call | solution.py:43
  79.6 2.6 shard_map.82
  84.1 7.0 %collective-permute-start.13 = (bf16[2,64,128]{2,1,0:T(8,128)(2,1)}, bf16[2,64,128]{2,1,0:T(8,128)(2,1)S(1)}, u32[]{:S(2)}, u32[]{:S(2)}) collective-permute-start(bf16[2,64,128]{2,1,0:T(8,128)(2,1)} %get-tuple-element.64), channel_id=1, source_target_pairs={{0,496},{16,0},{32,16},{48,32},{64,48},{80,64},{96,80},{112,96},{1... | collective-permute-start | bytes 98312 | tf_op jit(solution)/shard_map/ppermute | solution.py:18
  93.0 4.6 %collective-permute-start.15 = (bf16[2,64,128]{2,1,0:T(8,128)(2,1)}, bf16[2,64,128]{2,1,0:T(8,128)(2,1)S(1)}, u32[]{:S(2)}, u32[]{:S(2)}) collective-permute-start(bf16[2,64,128]{2,1,0:T(8,128)(2,1)} %get-tuple-element.66), channel_id=1, source_target_pairs={{0,15},{1,0},{2,1},{3,2},{4,3},{5,4},{6,5},{7,6},{8,7},{9,8},{10,9... | collective-permute-start | bytes 98312 | tf_op jit(solution)/shard_map/ppermute | solution.py:18
  97.6 3.0 %shard_map.83.local_ref = f32[16,64,128]{2,1,0:T(8,128)} custom-call(s32[64]{0:T(128)} %reshape.149.cols_ref, bf16[16,64,128]{2,1,0:T(8,128)(2,1)} %get-tuple-element.61.rounded_ref, bf16[16,512,128]{2,1,0:T(8,128)(2,1)} %bitcast.28), custom_call_target="tpu_custom_call" | custom-call | tf_op jit(solution)/shard_map/pallas_call | solution.py:43
  101.2 2.7 shard_map.84
  105.8 7.5 %collective-permute-start.17 = (bf16[2,64,128]{2,1,0:T(8,128)(2,1)}, bf16[2,64,128]{2,1,0:T(8,128)(2,1)S(1)}, u32[]{:S(2)}, u32[]{:S(2)}) collective-permute-start(bf16[2,64,128]{2,1,0:T(8,128)(2,1)} %get-tuple-element.70), channel_id=1, source_target_pairs={{0,496},{16,0},{32,16},{48,32},{64,48},{80,64},{96,80},{112,96},{1... | collective-permute-start | bytes 98312 | tf_op jit(solution)/shard_map/ppermute | solution.py:18
  115.3 4.6 %collective-permute-start.19 = (bf16[2,64,128]{2,1,0:T(8,128)(2,1)}, bf16[2,64,128]{2,1,0:T(8,128)(2,1)S(1)}, u32[]{:S(2)}, u32[]{:S(2)}) collective-permute-start(bf16[2,64,128]{2,1,0:T(8,128)(2,1)} %get-tuple-element.72), channel_id=1, source_target_pairs={{0,15},{1,0},{2,1},{3,2},{4,3},{5,4},{6,5},{7,6},{8,7},{9,8},{10,9... | collective-permute-start | bytes 98312 | tf_op jit(solution)/shard_map/ppermute | solution.py:18
  119.9 3.0 %shard_map.85.local_ref = f32[16,64,128]{2,1,0:T(8,128)} custom-call(s32[64]{0:T(128)} %reshape.149.cols_ref, bf16[16,64,128]{2,1,0:T(8,128)(2,1)} %get-tuple-element.67.rounded_ref, bf16[16,512,128]{2,1,0:T(8,128)(2,1)} %bitcast.29), custom_call_target="tpu_custom_call" | custom-call | tf_op jit(solution)/shard_map/pallas_call | solution.py:43
  123.5 2.7 shard_map.86
  128.1 7.5 %collective-permute-start.21 = (bf16[2,64,128]{2,1,0:T(8,128)(2,1)}, bf16[2,64,128]{2,1,0:T(8,128)(2,1)S(1)}, u32[]{:S(2)}, u32[]{:S(2)}) collective-permute-start(bf16[2,64,128]{2,1,0:T(8,128)(2,1)} %get-tuple-element.76), channel_id=1, source_target_pairs={{0,496},{16,0},{32,16},{48,32},{64,48},{80,64},{96,80},{112,96},{1... | collective-permute-start | bytes 98312 | tf_op jit(solution)/shard_map/ppermute | solution.py:18
  137.5 4.6 %collective-permute-start.23 = (bf16[2,64,128]{2,1,0:T(8,128)(2,1)}, bf16[2,64,128]{2,1,0:T(8,128)(2,1)S(1)}, u32[]{:S(2)}, u32[]{:S(2)}) collective-permute-start(bf16[2,64,128]{2,1,0:T(8,128)(2,1)} %get-tuple-element.78), channel_id=1, source_target_pairs={{0,15},{1,0},{2,1},{3,2},{4,3},{5,4},{6,5},{7,6},{8,7},{9,8},{10,9... | collective-permute-start | bytes 98312 | tf_op jit(solution)/shard_map/ppermute | solution.py:18
  142.1 3.0 %shard_map.87.local_ref = f32[16,64,128]{2,1,0:T(8,128)} custom-call(s32[64]{0:T(128)} %reshape.149.cols_ref, bf16[16,64,128]{2,1,0:T(8,128)(2,1)} %get-tuple-element.73.rounded_ref, bf16[16,512,128]{2,1,0:T(8,128)(2,1)} %bitcast.30), custom_call_target="tpu_custom_call" | custom-call | tf_op jit(solution)/shard_map/pallas_call | solution.py:43
  145.8 2.6 shard_map.88
  150.3 7.5 %collective-permute-start.25 = (bf16[2,64,128]{2,1,0:T(8,128)(2,1)}, bf16[2,64,128]{2,1,0:T(8,128)(2,1)S(1)}, u32[]{:S(2)}, u32[]{:S(2)}) collective-permute-start(bf16[2,64,128]{2,1,0:T(8,128)(2,1)} %get-tuple-element.82), channel_id=1, source_target_pairs={{0,496},{16,0},{32,16},{48,32},{64,48},{80,64},{96,80},{112,96},{1... | collective-permute-start | bytes 98312 | tf_op jit(solution)/shard_map/ppermute | solution.py:18
  159.8 4.6 %collective-permute-start.27 = (bf16[2,64,128]{2,1,0:T(8,128)(2,1)}, bf16[2,64,128]{2,1,0:T(8,128)(2,1)S(1)}, u32[]{:S(2)}, u32[]{:S(2)}) collective-permute-start(bf16[2,64,128]{2,1,0:T(8,128)(2,1)} %get-tuple-element.84), channel_id=1, source_target_pairs={{0,15},{1,0},{2,1},{3,2},{4,3},{5,4},{6,5},{7,6},{8,7},{9,8},{10,9... | collective-permute-start | bytes 98312 | tf_op jit(solution)/shard_map/ppermute | solution.py:18
  164.4 3.0 %shard_map.89.local_ref = f32[16,64,128]{2,1,0:T(8,128)} custom-call(s32[64]{0:T(128)} %reshape.149.cols_ref, bf16[16,64,128]{2,1,0:T(8,128)(2,1)} %get-tuple-element.79.rounded_ref, bf16[16,512,128]{2,1,0:T(8,128)(2,1)} %bitcast.31), custom_call_target="tpu_custom_call" | custom-call | tf_op jit(solution)/shard_map/pallas_call | solution.py:43
  172.6 7.5 %collective-permute-start.29 = (bf16[2,64,128]{2,1,0:T(8,128)(2,1)}, bf16[2,64,128]{2,1,0:T(8,128)(2,1)S(1)}, u32[]{:S(2)}, u32[]{:S(2)}) collective-permute-start(bf16[2,64,128]{2,1,0:T(8,128)(2,1)} %get-tuple-element.88), channel_id=1, source_target_pairs={{0,496},{16,0},{32,16},{48,32},{64,48},{80,64},{96,80},{112,96},{1... | collective-permute-start | bytes 98312 | tf_op jit(solution)/shard_map/ppermute | solution.py:18
  182.0 4.6 %collective-permute-start.31 = (bf16[2,64,128]{2,1,0:T(8,128)(2,1)}, bf16[2,64,128]{2,1,0:T(8,128)(2,1)S(1)}, u32[]{:S(2)}, u32[]{:S(2)}) collective-permute-start(bf16[2,64,128]{2,1,0:T(8,128)(2,1)} %get-tuple-element.90), channel_id=1, source_target_pairs={{0,15},{1,0},{2,1},{3,2},{4,3},{5,4},{6,5},{7,6},{8,7},{9,8},{10,9... | collective-permute-start | bytes 98312 | tf_op jit(solution)/shard_map/ppermute | solution.py:18
  186.6 3.0 %shard_map.91.local_ref = f32[16,64,128]{2,1,0:T(8,128)} custom-call(s32[64]{0:T(128)} %reshape.149.cols_ref, bf16[16,64,128]{2,1,0:T(8,128)(2,1)} %get-tuple-element.85.rounded_ref, bf16[16,512,128]{2,1,0:T(8,128)(2,1)} %bitcast.32), custom_call_target="tpu_custom_call" | custom-call | tf_op jit(solution)/shard_map/pallas_call | solution.py:43
  194.8 7.5 %collective-permute-start.33 = (bf16[2,64,128]{2,1,0:T(8,128)(2,1)}, bf16[2,64,128]{2,1,0:T(8,128)(2,1)S(1)}, u32[]{:S(2)}, u32[]{:S(2)}) collective-permute-start(bf16[2,64,128]{2,1,0:T(8,128)(2,1)} %get-tuple-element.94), channel_id=1, source_target_pairs={{0,496},{16,0},{32,16},{48,32},{64,48},{80,64},{96,80},{112,96},{1... | collective-permute-start | bytes 98312 | tf_op jit(solution)/shard_map/ppermute | solution.py:18
  204.2 4.6 %collective-permute-start.35 = (bf16[2,64,128]{2,1,0:T(8,128)(2,1)}, bf16[2,64,128]{2,1,0:T(8,128)(2,1)S(1)}, u32[]{:S(2)}, u32[]{:S(2)}) collective-permute-start(bf16[2,64,128]{2,1,0:T(8,128)(2,1)} %get-tuple-element.96), channel_id=1, source_target_pairs={{0,15},{1,0},{2,1},{3,2},{4,3},{5,4},{6,5},{7,6},{8,7},{9,8},{10,9... | collective-permute-start | bytes 98312 | tf_op jit(solution)/shard_map/ppermute | solution.py:18
  208.8 3.0 %shard_map.93.local_ref = f32[16,64,128]{2,1,0:T(8,128)} custom-call(s32[64]{0:T(128)} %reshape.149.cols_ref, bf16[16,64,128]{2,1,0:T(8,128)(2,1)} %get-tuple-element.91.rounded_ref, bf16[16,512,128]{2,1,0:T(8,128)(2,1)} %bitcast.33), custom_call_target="tpu_custom_call" | custom-call | tf_op jit(solution)/shard_map/pallas_call | solution.py:43
  212.5 2.6 shard_map.94
  218.9 2.7 collective-permute-done.36
  223.5 3.7 %collective-permute-done.37 = f32[64,64]{1,0:T(8,128)S(1)} collective-permute-done((f32[64,64]{1,0:T(8,128)S(1)}, f32[64,64]{1,0:T(8,128)S(1)}, u32[]{:S(2)}, u32[]{:S(2)}) %collective-permute-start.37) | collective-permute-done | bytes 16416 | tf_op jit(solution)/shard_map/ppermute | solution.py:26
  227.2 4.6 %collective-permute-start.38 = (f32[64,64]{1,0:T(8,128)S(1)}, f32[64,64]{1,0:T(8,128)S(1)}, u32[]{:S(2)}, u32[]{:S(2)}) collective-permute-start(f32[64,64]{1,0:T(8,128)S(1)} %add.94), channel_id=1, source_target_pairs={{0,4},{1,5},{2,6},{3,7},{4,0},{5,1},{6,2},{7,3},{8,12},{9,13},{10,... | collective-permute-start | bytes 49160 | tf_op jit(solution)/shard_map/ppermute | solution.py:26
  231.8 4.3 %collective-permute-done.38 = f32[64,64]{1,0:T(8,128)S(1)} collective-permute-done((f32[64,64]{1,0:T(8,128)S(1)}, f32[64,64]{1,0:T(8,128)S(1)}, u32[]{:S(2)}, u32[]{:S(2)}) %collective-permute-start.38) | collective-permute-done | bytes 16416 | tf_op jit(solution)/shard_map/ppermute | solution.py:26
  236.2 9.2 %collective-permute-start.39 = (f32[64,64]{1,0:T(8,128)S(1)}, f32[64,64]{1,0:T(8,128)S(1)}, u32[]{:S(2)}, u32[]{:S(2)}) collective-permute-start(f32[64,64]{1,0:T(8,128)S(1)} %add.95), channel_id=1, source_target_pairs={{0,8},{1,9},{2,10},{3,11},{4,12},{5,13},{6,14},{7,15},{8,0},{9,1},... | collective-permute-start | bytes 49160 | tf_op jit(solution)/shard_map/ppermute | solution.py:26
  245.3 4.2 %collective-permute-done.39 = f32[64,64]{1,0:T(8,128)S(1)} collective-permute-done((f32[64,64]{1,0:T(8,128)S(1)}, f32[64,64]{1,0:T(8,128)S(1)}, u32[]{:S(2)}, u32[]{:S(2)}) %collective-permute-start.39) | collective-permute-done | bytes 16416 | tf_op jit(solution)/shard_map/ppermute | solution.py:26
  249.5 12.0 %collective-permute-start.40 = (f32[64,64]{1,0:T(8,128)S(1)}, f32[64,64]{1,0:T(8,128)S(1)}, u32[]{:S(2)}, u32[]{:S(2)}) collective-permute-start(f32[64,64]{1,0:T(8,128)S(1)} %add.96), channel_id=1, source_target_pairs={{0,16},{16,0},{32,48},{48,32},{64,80},{80,64},{96,112},{112,96},{1... | collective-permute-start | bytes 49160 | tf_op jit(solution)/shard_map/ppermute | solution.py:26
  264.3 2.7 collective-permute-done.41
  269.0 4.2 %collective-permute-done.42 = f32[64,64]{1,0:T(8,128)S(1)} collective-permute-done((f32[64,64]{1,0:T(8,128)S(1)}, f32[64,64]{1,0:T(8,128)S(1)}, u32[]{:S(2)}, u32[]{:S(2)}) %collective-permute-start.42) | collective-permute-done | bytes 16416 | tf_op jit(solution)/shard_map/ppermute | solution.py:26
  275.1 2.7 collective-permute-done.43
  279.8 4.2 %collective-permute-done.44 = f32[64,64]{1,0:T(8,128)S(1)} collective-permute-done((f32[64,64]{1,0:T(8,128)S(1)}, f32[64,64]{1,0:T(8,128)S(1)}, u32[]{:S(2)}, u32[]{:S(2)}) %collective-permute-start.44) | collective-permute-done | bytes 16416 | tf_op jit(solution)/shard_map/ppermute | solution.py:26
  (173 shorter events, 66.7 us)
Async XLA Ops:
  1.7 27.6 %copy-start.1 = (bf16[16,64,128]{2,1,0:T(8,128)(2,1)}, bf16[16,64,128]{2,1,0:T(8,128)(2,1)S(1)}, u32[]{:S(2)}) copy-start(bf16[16,64,128]{2,1,0:T(8,128)(2,1)S(1)} %convert_element_type.3.rounded_ref) | copy-start | bytes 786436
  3.4 31.3 %collective-permute-start = (bf16[2,64,128]{2,1,0:T(8,128)(2,1)S(1)}, bf16[2,64,128]{2,1,0:T(8,128)(2,1)S(1)}, u32[]{:S(2)}, u32[]{:S(2)}) collective-permute-start(bf16[2,64,128]{2,1,0:T(8,128)(2,1)S(1)} %gather_fusion), channel_id=1, source_target_pairs={{0,16},{16,32},{32,48},{48,64},{64,80},{80,96},{96,112},{112,128},... | collective-permute-start | bytes 98312 | tf_op jit(solution)/shard_map/ppermute | solution.py:18
  8.4 26.3 %collective-permute-start.1 = (bf16[2,64,128]{2,1,0:T(8,128)(2,1)S(1)}, bf16[2,64,128]{2,1,0:T(8,128)(2,1)S(1)}, u32[]{:S(2)}, u32[]{:S(2)}) collective-permute-start(bf16[2,64,128]{2,1,0:T(8,128)(2,1)S(1)} %gather_fusion.1), channel_id=1, source_target_pairs={{0,496},{16,0},{32,16},{48,32},{64,48},{80,64},{96,80},{112,96},{1... | collective-permute-start | bytes 98312 | tf_op jit(solution)/shard_map/ppermute | solution.py:18
  15.2 19.5 %collective-permute-start.2 = (bf16[2,64,128]{2,1,0:T(8,128)(2,1)S(1)}, bf16[2,64,128]{2,1,0:T(8,128)(2,1)S(1)}, u32[]{:S(2)}, u32[]{:S(2)}) collective-permute-start(bf16[2,64,128]{2,1,0:T(8,128)(2,1)S(1)} %gather_fusion.2), channel_id=1, source_target_pairs={{0,1},{1,2},{2,3},{3,4},{4,5},{5,6},{6,7},{7,8},{8,9},{9,10},{10,1... | collective-permute-start | bytes 98312 | tf_op jit(solution)/shard_map/ppermute | solution.py:18
  17.7 17.0 %collective-permute-start.3 = (bf16[2,64,128]{2,1,0:T(8,128)(2,1)S(1)}, bf16[2,64,128]{2,1,0:T(8,128)(2,1)S(1)}, u32[]{:S(2)}, u32[]{:S(2)}) collective-permute-start(bf16[2,64,128]{2,1,0:T(8,128)(2,1)S(1)} %gather_fusion.3), channel_id=1, source_target_pairs={{0,15},{1,0},{2,1},{3,2},{4,3},{5,4},{6,5},{7,6},{8,7},{9,8},{10,9... | collective-permute-start | bytes 98312 | tf_op jit(solution)/shard_map/ppermute | solution.py:18
  25.4 4.7 %copy-start.2 = (bf16[16,128,128]{2,1,0:T(8,128)(2,1)S(1)}, bf16[16,128,128]{2,1,0:T(8,128)(2,1)}, u32[]{:S(2)}) copy-start(bf16[16,128,128]{2,1,0:T(8,128)(2,1)} %param.9) | copy-start | bytes 1572868
  38.0 17.6 %collective-permute-start.4 = (bf16[2,64,128]{2,1,0:T(8,128)(2,1)}, bf16[2,64,128]{2,1,0:T(8,128)(2,1)S(1)}, u32[]{:S(2)}, u32[]{:S(2)}) collective-permute-start(bf16[2,64,128]{2,1,0:T(8,128)(2,1)} %get-tuple-element.51), channel_id=1, source_target_pairs={{0,16},{16,32},{32,48},{48,64},{64,80},{80,96},{96,112},{112,128},... | collective-permute-start | bytes 98312 | tf_op jit(solution)/shard_map/ppermute | solution.py:18
  41.9 13.7 %collective-permute-start.5 = (bf16[2,64,128]{2,1,0:T(8,128)(2,1)}, bf16[2,64,128]{2,1,0:T(8,128)(2,1)S(1)}, u32[]{:S(2)}, u32[]{:S(2)}) collective-permute-start(bf16[2,64,128]{2,1,0:T(8,128)(2,1)} %get-tuple-element.52), channel_id=1, source_target_pairs={{0,496},{16,0},{32,16},{48,32},{64,48},{80,64},{96,80},{112,96},{1... | collective-permute-start | bytes 98312 | tf_op jit(solution)/shard_map/ppermute | solution.py:18
  46.0 9.5 %collective-permute-start.6 = (bf16[2,64,128]{2,1,0:T(8,128)(2,1)}, bf16[2,64,128]{2,1,0:T(8,128)(2,1)S(1)}, u32[]{:S(2)}, u32[]{:S(2)}) collective-permute-start(bf16[2,64,128]{2,1,0:T(8,128)(2,1)} %get-tuple-element.53), channel_id=1, source_target_pairs={{0,1},{1,2},{2,3},{3,4},{4,5},{5,6},{6,7},{7,8},{8,9},{9,10},{10,1... | collective-permute-start | bytes 98312 | tf_op jit(solution)/shard_map/ppermute | solution.py:18
  48.0 7.6 %collective-permute-start.7 = (bf16[2,64,128]{2,1,0:T(8,128)(2,1)}, bf16[2,64,128]{2,1,0:T(8,128)(2,1)S(1)}, u32[]{:S(2)}, u32[]{:S(2)}) collective-permute-start(bf16[2,64,128]{2,1,0:T(8,128)(2,1)} %get-tuple-element.54), channel_id=1, source_target_pairs={{0,15},{1,0},{2,1},{3,2},{4,3},{5,4},{6,5},{7,6},{8,7},{9,8},{10,9... | collective-permute-start | bytes 98312 | tf_op jit(solution)/shard_map/ppermute | solution.py:18
  59.4 19.5 %collective-permute-start.10 = (bf16[2,64,128]{2,1,0:T(8,128)(2,1)}, bf16[2,64,128]{2,1,0:T(8,128)(2,1)S(1)}, u32[]{:S(2)}, u32[]{:S(2)}) collective-permute-start(bf16[2,64,128]{2,1,0:T(8,128)(2,1)} %get-tuple-element.59), channel_id=1, source_target_pairs={{0,1},{1,2},{2,3},{3,4},{4,5},{5,6},{6,7},{7,8},{8,9},{9,10},{10,1... | collective-permute-start | bytes 98312 | tf_op jit(solution)/shard_map/ppermute | solution.py:18
  61.3 17.6 %collective-permute-start.11 = (bf16[2,64,128]{2,1,0:T(8,128)(2,1)}, bf16[2,64,128]{2,1,0:T(8,128)(2,1)S(1)}, u32[]{:S(2)}, u32[]{:S(2)}) collective-permute-start(bf16[2,64,128]{2,1,0:T(8,128)(2,1)} %get-tuple-element.60), channel_id=1, source_target_pairs={{0,15},{1,0},{2,1},{3,2},{4,3},{5,4},{6,5},{7,6},{8,7},{9,8},{10,9... | collective-permute-start | bytes 98312 | tf_op jit(solution)/shard_map/ppermute | solution.py:18
  65.9 13.0 %collective-permute-start.8 = (bf16[2,64,128]{2,1,0:T(8,128)(2,1)}, bf16[2,64,128]{2,1,0:T(8,128)(2,1)S(1)}, u32[]{:S(2)}, u32[]{:S(2)}) collective-permute-start(bf16[2,64,128]{2,1,0:T(8,128)(2,1)} %get-tuple-element.57), channel_id=1, source_target_pairs={{0,16},{16,32},{32,48},{48,64},{64,80},{80,96},{96,112},{112,128},... | collective-permute-start | bytes 98312 | tf_op jit(solution)/shard_map/ppermute | solution.py:18
  68.5 10.5 %collective-permute-start.9 = (bf16[2,64,128]{2,1,0:T(8,128)(2,1)}, bf16[2,64,128]{2,1,0:T(8,128)(2,1)S(1)}, u32[]{:S(2)}, u32[]{:S(2)}) collective-permute-start(bf16[2,64,128]{2,1,0:T(8,128)(2,1)} %get-tuple-element.58), channel_id=1, source_target_pairs={{0,496},{16,0},{32,16},{48,32},{64,48},{80,64},{96,80},{112,96},{1... | collective-permute-start | bytes 98312 | tf_op jit(solution)/shard_map/ppermute | solution.py:18
  82.2 18.4 %collective-permute-start.12 = (bf16[2,64,128]{2,1,0:T(8,128)(2,1)}, bf16[2,64,128]{2,1,0:T(8,128)(2,1)S(1)}, u32[]{:S(2)}, u32[]{:S(2)}) collective-permute-start(bf16[2,64,128]{2,1,0:T(8,128)(2,1)} %get-tuple-element.63), channel_id=1, source_target_pairs={{0,16},{16,32},{32,48},{48,64},{64,80},{80,96},{96,112},{112,128},... | collective-permute-start | bytes 98312 | tf_op jit(solution)/shard_map/ppermute | solution.py:18
  84.1 16.5 %collective-permute-start.13 = (bf16[2,64,128]{2,1,0:T(8,128)(2,1)}, bf16[2,64,128]{2,1,0:T(8,128)(2,1)S(1)}, u32[]{:S(2)}, u32[]{:S(2)}) collective-permute-start(bf16[2,64,128]{2,1,0:T(8,128)(2,1)} %get-tuple-element.64), channel_id=1, source_target_pairs={{0,496},{16,0},{32,16},{48,32},{64,48},{80,64},{96,80},{112,96},{1... | collective-permute-start | bytes 98312 | tf_op jit(solution)/shard_map/ppermute | solution.py:18
  91.1 9.5 %collective-permute-start.14 = (bf16[2,64,128]{2,1,0:T(8,128)(2,1)}, bf16[2,64,128]{2,1,0:T(8,128)(2,1)S(1)}, u32[]{:S(2)}, u32[]{:S(2)}) collective-permute-start(bf16[2,64,128]{2,1,0:T(8,128)(2,1)} %get-tuple-element.65), channel_id=1, source_target_pairs={{0,1},{1,2},{2,3},{3,4},{4,5},{5,6},{6,7},{7,8},{8,9},{9,10},{10,1... | collective-permute-start | bytes 98312 | tf_op jit(solution)/shard_map/ppermute | solution.py:18
  93.0 7.6 %collective-permute-start.15 = (bf16[2,64,128]{2,1,0:T(8,128)(2,1)}, bf16[2,64,128]{2,1,0:T(8,128)(2,1)S(1)}, u32[]{:S(2)}, u32[]{:S(2)}) collective-permute-start(bf16[2,64,128]{2,1,0:T(8,128)(2,1)} %get-tuple-element.66), channel_id=1, source_target_pairs={{0,15},{1,0},{2,1},{3,2},{4,3},{5,4},{6,5},{7,6},{8,7},{9,8},{10,9... | collective-permute-start | bytes 98312 | tf_op jit(solution)/shard_map/ppermute | solution.py:18
  103.9 19.0 %collective-permute-start.16 = (bf16[2,64,128]{2,1,0:T(8,128)(2,1)}, bf16[2,64,128]{2,1,0:T(8,128)(2,1)S(1)}, u32[]{:S(2)}, u32[]{:S(2)}) collective-permute-start(bf16[2,64,128]{2,1,0:T(8,128)(2,1)} %get-tuple-element.69), channel_id=1, source_target_pairs={{0,16},{16,32},{32,48},{48,64},{64,80},{80,96},{96,112},{112,128},... | collective-permute-start | bytes 98312 | tf_op jit(solution)/shard_map/ppermute | solution.py:18
  105.8 17.0 %collective-permute-start.17 = (bf16[2,64,128]{2,1,0:T(8,128)(2,1)}, bf16[2,64,128]{2,1,0:T(8,128)(2,1)S(1)}, u32[]{:S(2)}, u32[]{:S(2)}) collective-permute-start(bf16[2,64,128]{2,1,0:T(8,128)(2,1)} %get-tuple-element.70), channel_id=1, source_target_pairs={{0,496},{16,0},{32,16},{48,32},{64,48},{80,64},{96,80},{112,96},{1... | collective-permute-start | bytes 98312 | tf_op jit(solution)/shard_map/ppermute | solution.py:18
  113.4 9.5 %collective-permute-start.18 = (bf16[2,64,128]{2,1,0:T(8,128)(2,1)}, bf16[2,64,128]{2,1,0:T(8,128)(2,1)S(1)}, u32[]{:S(2)}, u32[]{:S(2)}) collective-permute-start(bf16[2,64,128]{2,1,0:T(8,128)(2,1)} %get-tuple-element.71), channel_id=1, source_target_pairs={{0,1},{1,2},{2,3},{3,4},{4,5},{5,6},{6,7},{7,8},{8,9},{9,10},{10,1... | collective-permute-start | bytes 98312 | tf_op jit(solution)/shard_map/ppermute | solution.py:18
  115.3 7.6 %collective-permute-start.19 = (bf16[2,64,128]{2,1,0:T(8,128)(2,1)}, bf16[2,64,128]{2,1,0:T(8,128)(2,1)S(1)}, u32[]{:S(2)}, u32[]{:S(2)}) collective-permute-start(bf16[2,64,128]{2,1,0:T(8,128)(2,1)} %get-tuple-element.72), channel_id=1, source_target_pairs={{0,15},{1,0},{2,1},{3,2},{4,3},{5,4},{6,5},{7,6},{8,7},{9,8},{10,9... | collective-permute-start | bytes 98312 | tf_op jit(solution)/shard_map/ppermute | solution.py:18
  126.2 19.0 %collective-permute-start.20 = (bf16[2,64,128]{2,1,0:T(8,128)(2,1)}, bf16[2,64,128]{2,1,0:T(8,128)(2,1)S(1)}, u32[]{:S(2)}, u32[]{:S(2)}) collective-permute-start(bf16[2,64,128]{2,1,0:T(8,128)(2,1)} %get-tuple-element.75), channel_id=1, source_target_pairs={{0,16},{16,32},{32,48},{48,64},{64,80},{80,96},{96,112},{112,128},... | collective-permute-start | bytes 98312 | tf_op jit(solution)/shard_map/ppermute | solution.py:18
  128.1 17.1 %collective-permute-start.21 = (bf16[2,64,128]{2,1,0:T(8,128)(2,1)}, bf16[2,64,128]{2,1,0:T(8,128)(2,1)S(1)}, u32[]{:S(2)}, u32[]{:S(2)}) collective-permute-start(bf16[2,64,128]{2,1,0:T(8,128)(2,1)} %get-tuple-element.76), channel_id=1, source_target_pairs={{0,496},{16,0},{32,16},{48,32},{64,48},{80,64},{96,80},{112,96},{1... | collective-permute-start | bytes 98312 | tf_op jit(solution)/shard_map/ppermute | solution.py:18
  135.6 9.5 %collective-permute-start.22 = (bf16[2,64,128]{2,1,0:T(8,128)(2,1)}, bf16[2,64,128]{2,1,0:T(8,128)(2,1)S(1)}, u32[]{:S(2)}, u32[]{:S(2)}) collective-permute-start(bf16[2,64,128]{2,1,0:T(8,128)(2,1)} %get-tuple-element.77), channel_id=1, source_target_pairs={{0,1},{1,2},{2,3},{3,4},{4,5},{5,6},{6,7},{7,8},{8,9},{9,10},{10,1... | collective-permute-start | bytes 98312 | tf_op jit(solution)/shard_map/ppermute | solution.py:18
  137.5 7.6 %collective-permute-start.23 = (bf16[2,64,128]{2,1,0:T(8,128)(2,1)}, bf16[2,64,128]{2,1,0:T(8,128)(2,1)S(1)}, u32[]{:S(2)}, u32[]{:S(2)}) collective-permute-start(bf16[2,64,128]{2,1,0:T(8,128)(2,1)} %get-tuple-element.78), channel_id=1, source_target_pairs={{0,15},{1,0},{2,1},{3,2},{4,3},{5,4},{6,5},{7,6},{8,7},{9,8},{10,9... | collective-permute-start | bytes 98312 | tf_op jit(solution)/shard_map/ppermute | solution.py:18
  148.4 19.0 %collective-permute-start.24 = (bf16[2,64,128]{2,1,0:T(8,128)(2,1)}, bf16[2,64,128]{2,1,0:T(8,128)(2,1)S(1)}, u32[]{:S(2)}, u32[]{:S(2)}) collective-permute-start(bf16[2,64,128]{2,1,0:T(8,128)(2,1)} %get-tuple-element.81), channel_id=1, source_target_pairs={{0,16},{16,32},{32,48},{48,64},{64,80},{80,96},{96,112},{112,128},... | collective-permute-start | bytes 98312 | tf_op jit(solution)/shard_map/ppermute | solution.py:18
  150.3 17.1 %collective-permute-start.25 = (bf16[2,64,128]{2,1,0:T(8,128)(2,1)}, bf16[2,64,128]{2,1,0:T(8,128)(2,1)S(1)}, u32[]{:S(2)}, u32[]{:S(2)}) collective-permute-start(bf16[2,64,128]{2,1,0:T(8,128)(2,1)} %get-tuple-element.82), channel_id=1, source_target_pairs={{0,496},{16,0},{32,16},{48,32},{64,48},{80,64},{96,80},{112,96},{1... | collective-permute-start | bytes 98312 | tf_op jit(solution)/shard_map/ppermute | solution.py:18
  157.9 9.5 %collective-permute-start.26 = (bf16[2,64,128]{2,1,0:T(8,128)(2,1)}, bf16[2,64,128]{2,1,0:T(8,128)(2,1)S(1)}, u32[]{:S(2)}, u32[]{:S(2)}) collective-permute-start(bf16[2,64,128]{2,1,0:T(8,128)(2,1)} %get-tuple-element.83), channel_id=1, source_target_pairs={{0,1},{1,2},{2,3},{3,4},{4,5},{5,6},{6,7},{7,8},{8,9},{9,10},{10,1... | collective-permute-start | bytes 98312 | tf_op jit(solution)/shard_map/ppermute | solution.py:18
  159.8 7.6 %collective-permute-start.27 = (bf16[2,64,128]{2,1,0:T(8,128)(2,1)}, bf16[2,64,128]{2,1,0:T(8,128)(2,1)S(1)}, u32[]{:S(2)}, u32[]{:S(2)}) collective-permute-start(bf16[2,64,128]{2,1,0:T(8,128)(2,1)} %get-tuple-element.84), channel_id=1, source_target_pairs={{0,15},{1,0},{2,1},{3,2},{4,3},{5,4},{6,5},{7,6},{8,7},{9,8},{10,9... | collective-permute-start | bytes 98312 | tf_op jit(solution)/shard_map/ppermute | solution.py:18
  170.6 19.0 %collective-permute-start.28 = (bf16[2,64,128]{2,1,0:T(8,128)(2,1)}, bf16[2,64,128]{2,1,0:T(8,128)(2,1)S(1)}, u32[]{:S(2)}, u32[]{:S(2)}) collective-permute-start(bf16[2,64,128]{2,1,0:T(8,128)(2,1)} %get-tuple-element.87), channel_id=1, source_target_pairs={{0,16},{16,32},{32,48},{48,64},{64,80},{80,96},{96,112},{112,128},... | collective-permute-start | bytes 98312 | tf_op jit(solution)/shard_map/ppermute | solution.py:18
  172.6 17.0 %collective-permute-start.29 = (bf16[2,64,128]{2,1,0:T(8,128)(2,1)}, bf16[2,64,128]{2,1,0:T(8,128)(2,1)S(1)}, u32[]{:S(2)}, u32[]{:S(2)}) collective-permute-start(bf16[2,64,128]{2,1,0:T(8,128)(2,1)} %get-tuple-element.88), channel_id=1, source_target_pairs={{0,496},{16,0},{32,16},{48,32},{64,48},{80,64},{96,80},{112,96},{1... | collective-permute-start | bytes 98312 | tf_op jit(solution)/shard_map/ppermute | solution.py:18
  180.1 9.5 %collective-permute-start.30 = (bf16[2,64,128]{2,1,0:T(8,128)(2,1)}, bf16[2,64,128]{2,1,0:T(8,128)(2,1)S(1)}, u32[]{:S(2)}, u32[]{:S(2)}) collective-permute-start(bf16[2,64,128]{2,1,0:T(8,128)(2,1)} %get-tuple-element.89), channel_id=1, source_target_pairs={{0,1},{1,2},{2,3},{3,4},{4,5},{5,6},{6,7},{7,8},{8,9},{9,10},{10,1... | collective-permute-start | bytes 98312 | tf_op jit(solution)/shard_map/ppermute | solution.py:18
  182.0 7.6 %collective-permute-start.31 = (bf16[2,64,128]{2,1,0:T(8,128)(2,1)}, bf16[2,64,128]{2,1,0:T(8,128)(2,1)S(1)}, u32[]{:S(2)}, u32[]{:S(2)}) collective-permute-start(bf16[2,64,128]{2,1,0:T(8,128)(2,1)} %get-tuple-element.90), channel_id=1, source_target_pairs={{0,15},{1,0},{2,1},{3,2},{4,3},{5,4},{6,5},{7,6},{8,7},{9,8},{10,9... | collective-permute-start | bytes 98312 | tf_op jit(solution)/shard_map/ppermute | solution.py:18
  192.9 19.0 %collective-permute-start.32 = (bf16[2,64,128]{2,1,0:T(8,128)(2,1)}, bf16[2,64,128]{2,1,0:T(8,128)(2,1)S(1)}, u32[]{:S(2)}, u32[]{:S(2)}) collective-permute-start(bf16[2,64,128]{2,1,0:T(8,128)(2,1)} %get-tuple-element.93), channel_id=1, source_target_pairs={{0,16},{16,32},{32,48},{48,64},{64,80},{80,96},{96,112},{112,128},... | collective-permute-start | bytes 98312 | tf_op jit(solution)/shard_map/ppermute | solution.py:18
  194.8 17.0 %collective-permute-start.33 = (bf16[2,64,128]{2,1,0:T(8,128)(2,1)}, bf16[2,64,128]{2,1,0:T(8,128)(2,1)S(1)}, u32[]{:S(2)}, u32[]{:S(2)}) collective-permute-start(bf16[2,64,128]{2,1,0:T(8,128)(2,1)} %get-tuple-element.94), channel_id=1, source_target_pairs={{0,496},{16,0},{32,16},{48,32},{64,48},{80,64},{96,80},{112,96},{1... | collective-permute-start | bytes 98312 | tf_op jit(solution)/shard_map/ppermute | solution.py:18
  202.3 9.5 %collective-permute-start.34 = (bf16[2,64,128]{2,1,0:T(8,128)(2,1)}, bf16[2,64,128]{2,1,0:T(8,128)(2,1)S(1)}, u32[]{:S(2)}, u32[]{:S(2)}) collective-permute-start(bf16[2,64,128]{2,1,0:T(8,128)(2,1)} %get-tuple-element.95), channel_id=1, source_target_pairs={{0,1},{1,2},{2,3},{3,4},{4,5},{5,6},{6,7},{7,8},{8,9},{9,10},{10,1... | collective-permute-start | bytes 98312 | tf_op jit(solution)/shard_map/ppermute | solution.py:18
  204.2 7.6 %collective-permute-start.35 = (bf16[2,64,128]{2,1,0:T(8,128)(2,1)}, bf16[2,64,128]{2,1,0:T(8,128)(2,1)S(1)}, u32[]{:S(2)}, u32[]{:S(2)}) collective-permute-start(bf16[2,64,128]{2,1,0:T(8,128)(2,1)} %get-tuple-element.96), channel_id=1, source_target_pairs={{0,15},{1,0},{2,1},{3,2},{4,3},{5,4},{6,5},{7,6},{8,7},{9,8},{10,9... | collective-permute-start | bytes 98312 | tf_op jit(solution)/shard_map/ppermute | solution.py:18
  215.1 70.4 %copy-start = (f32[16,64,128]{2,1,0:T(8,128)S(1)}, f32[16,64,128]{2,1,0:T(8,128)}, u32[]{:S(2)}) copy-start(f32[16,64,128]{2,1,0:T(8,128)} %get-tuple-element.97) | copy-start | bytes 1572868
  216.9 4.7 %collective-permute-start.36 = (f32[64,64]{1,0:T(8,128)S(1)}, f32[64,64]{1,0:T(8,128)S(1)}, u32[]{:S(2)}, u32[]{:S(2)}) collective-permute-start(f32[64,64]{1,0:T(8,128)S(1)} %convolution_bitcast_fusion), channel_id=1, source_target_pairs={{0,1},{1,0},{2,3},{3,2},{4,5},{5,4},{6,7},{7,6},{8,9},{9,8},{10,11... | collective-permute-start | bytes 49160 | tf_op jit(solution)/shard_map/ppermute | solution.py:26
  221.6 5.6 %collective-permute-start.37 = (f32[64,64]{1,0:T(8,128)S(1)}, f32[64,64]{1,0:T(8,128)S(1)}, u32[]{:S(2)}, u32[]{:S(2)}) collective-permute-start(f32[64,64]{1,0:T(8,128)S(1)} %add.93), channel_id=1, source_target_pairs={{0,2},{1,3},{2,0},{3,1},{4,6},{5,7},{6,4},{7,5},{8,10},{9,11},{10,... | collective-permute-start | bytes 49160 | tf_op jit(solution)/shard_map/ppermute | solution.py:26
  227.2 8.9 %collective-permute-start.38 = (f32[64,64]{1,0:T(8,128)S(1)}, f32[64,64]{1,0:T(8,128)S(1)}, u32[]{:S(2)}, u32[]{:S(2)}) collective-permute-start(f32[64,64]{1,0:T(8,128)S(1)} %add.94), channel_id=1, source_target_pairs={{0,4},{1,5},{2,6},{3,7},{4,0},{5,1},{6,2},{7,3},{8,12},{9,13},{10,... | collective-permute-start | bytes 49160 | tf_op jit(solution)/shard_map/ppermute | solution.py:26
  236.2 13.4 %collective-permute-start.39 = (f32[64,64]{1,0:T(8,128)S(1)}, f32[64,64]{1,0:T(8,128)S(1)}, u32[]{:S(2)}, u32[]{:S(2)}) collective-permute-start(f32[64,64]{1,0:T(8,128)S(1)} %add.95), channel_id=1, source_target_pairs={{0,8},{1,9},{2,10},{3,11},{4,12},{5,13},{6,14},{7,15},{8,0},{9,1},... | collective-permute-start | bytes 49160 | tf_op jit(solution)/shard_map/ppermute | solution.py:26
  249.5 12.9 %collective-permute-start.40 = (f32[64,64]{1,0:T(8,128)S(1)}, f32[64,64]{1,0:T(8,128)S(1)}, u32[]{:S(2)}, u32[]{:S(2)}) collective-permute-start(f32[64,64]{1,0:T(8,128)S(1)} %add.96), channel_id=1, source_target_pairs={{0,16},{16,0},{32,48},{48,32},{64,80},{80,64},{96,112},{112,96},{1... | collective-permute-start | bytes 49160 | tf_op jit(solution)/shard_map/ppermute | solution.py:26
  262.4 4.6 %collective-permute-start.41 = (f32[64,64]{1,0:T(8,128)S(1)}, f32[64,64]{1,0:T(8,128)S(1)}, u32[]{:S(2)}, u32[]{:S(2)}) collective-permute-start(f32[64,64]{1,0:T(8,128)S(1)} %add.97), channel_id=1, source_target_pairs={{0,32},{16,48},{32,0},{48,16},{64,96},{80,112},{96,64},{112,80},{1... | collective-permute-start | bytes 49160 | tf_op jit(solution)/shard_map/ppermute | solution.py:26
  267.0 6.2 %collective-permute-start.42 = (f32[64,64]{1,0:T(8,128)S(1)}, f32[64,64]{1,0:T(8,128)S(1)}, u32[]{:S(2)}, u32[]{:S(2)}) collective-permute-start(f32[64,64]{1,0:T(8,128)S(1)} %add.98), channel_id=1, source_target_pairs={{0,64},{16,80},{32,96},{48,112},{64,0},{80,16},{96,32},{112,48},{1... | collective-permute-start | bytes 49160 | tf_op jit(solution)/shard_map/ppermute | solution.py:26
  273.2 4.6 %collective-permute-start.43 = (f32[64,64]{1,0:T(8,128)S(1)}, f32[64,64]{1,0:T(8,128)S(1)}, u32[]{:S(2)}, u32[]{:S(2)}) collective-permute-start(f32[64,64]{1,0:T(8,128)S(1)} %add.99), channel_id=1, source_target_pairs={{0,128},{16,144},{32,160},{48,176},{64,192},{80,208},{96,224},{112... | collective-permute-start | bytes 49160 | tf_op jit(solution)/shard_map/ppermute | solution.py:26
  277.9 6.2 %collective-permute-start.44 = (f32[64,64]{1,0:T(8,128)S(1)}, f32[64,64]{1,0:T(8,128)S(1)}, u32[]{:S(2)}, u32[]{:S(2)}) collective-permute-start(f32[64,64]{1,0:T(8,128)S(1)} %add.100), channel_id=1, source_target_pairs={{0,256},{16,272},{32,288},{48,304},{64,320},{80,336},{96,352},{112... | collective-permute-start | bytes 49160 | tf_op jit(solution)/shard_map/ppermute | solution.py:26
  (37 other events, 25.9 us)

commit v7 on v6

v7 whole, which is shorter than its diff:
```python
import functools

import jax
import jax.numpy as jnp
from jax import lax
from jax.experimental import pallas as pl
from jax.experimental.pallas import tpu as pltpu
from jax.sharding import PartitionSpec as P


DEG = 9
INTERPRET = False


def from_behind(value, axis, steps):
    count = lax.axis_size(axis)
    pairs = [(source, (source + steps) % count) for source in range(count)]
    return lax.ppermute(value, axis, pairs)


def butterfly_sum(value, axis):
    count = lax.axis_size(axis)
    stride = 1
    while stride < count:
        pairs = [(source, source ^ stride) for source in range(count)]
        value = value + lax.ppermute(value, axis, pairs)
        stride *= 2
    return value


def _local_kernel(cols_ref, picks_ref, rounded_ref, stacked_ref, *refs, scale, with_older):
    if with_older:
        older_ref, part_ref, edge_ref = refs
    else:
        part_ref, edge_ref = refs
    rows = stacked_ref.shape[0]
    per_row = stacked_ref.shape[1] // rounded_ref.shape[2]
    for r in range(rows):
        blocks = [rounded_ref[cols_ref[r * per_row + t]] for t in range(per_row)]
        value = jnp.dot(
            jnp.concatenate(blocks, axis=1), stacked_ref[r], preferred_element_type=jnp.float32
        )
        if with_older:
            value = scale * value - older_ref[r]
        part_ref[r] = value
    for e in range(edge_ref.shape[0]):
        edge_ref[e] = part_ref[picks_ref[e]]


def local_part(rounded, stacked, cols, picks, older, scale):
    vmem = pl.BlockSpec(memory_space=pltpu.VMEM)
    smem = pl.BlockSpec(memory_space=pltpu.SMEM)
    with_older = older is not None
    shape = (stacked.shape[0],) + rounded.shape[1:]
    kernel = functools.partial(_local_kernel, scale=scale, with_older=with_older)
    operands = (cols.reshape(-1), picks, rounded, stacked) + ((older,) if with_older else ())
    return pl.pallas_call(
        kernel,
        out_shape=(
            jax.ShapeDtypeStruct(shape, jnp.float32),
            jax.ShapeDtypeStruct((picks.shape[0],) + shape[1:], jnp.float32),
        ),
        in_specs=[smem, smem] + [vmem] * (len(operands) - 2),
        out_specs=(vmem, vmem),
        interpret=INTERPRET,
    )(*operands)


def _halo_kernel(slot_ref, part_ref, halo_ref, *refs, scale, rounded_only):
    pieces, outs, received_ref = refs[:4], refs[4:-1], refs[-1]
    per_list = pieces[0].shape[0]
    for d in range(4):
        for i in range(per_list):
            received_ref[d * per_list + i] = pieces[d][i]
    for r in range(part_ref.shape[0]):
        block = received_ref[slot_ref[r]]
        coupled = jnp.dot(block, halo_ref[r], preferred_element_type=jnp.float32)
        value = part_ref[r] + (coupled if scale == 1.0 else scale * coupled)
        if rounded_only:
            outs[r // per_list][r % per_list] = value.astype(jnp.bfloat16)
        else:
            outs[0][r] = value
            outs[1][r] = value.astype(jnp.bfloat16)


def halo_add(part, pieces, halo, slot, scale, rounded_only):
    vmem = pl.BlockSpec(memory_space=pltpu.VMEM)
    smem = pl.BlockSpec(memory_space=pltpu.SMEM)
    per_list = pieces[0].shape[0]
    if rounded_only:
        out_shape = (jax.ShapeDtypeStruct(pieces[0].shape, jnp.bfloat16),) * 4
    else:
        out_shape = (
            jax.ShapeDtypeStruct(part.shape, jnp.float32),
            jax.ShapeDtypeStruct(part.shape, jnp.bfloat16),
        )
    kernel = functools.partial(_halo_kernel, scale=scale, rounded_only=rounded_only)
    outs = pl.pallas_call(
        kernel,
        out_shape=out_shape,
        in_specs=[smem] + [vmem] * 6,
        out_specs=(vmem,) * len(out_shape),
        scratch_shapes=[pltpu.VMEM((4 * per_list,) + pieces[0].shape[1:], jnp.bfloat16)],
        interpret=INTERPRET,
    )(slot, part, halo, *pieces)
    return list(outs)


def exchange(pieces):
    from_yhigh = from_behind(pieces[3], "py", -1)
    from_ylow = from_behind(pieces[2], "py", 1)
    from_xhigh = from_behind(pieces[1], "px", -1)
    from_xlow = from_behind(pieces[0], "px", 1)
    return [from_xlow, from_xhigh, from_ylow, from_yhigh]


def shards(start_vecs, local_tiles, local_cols, halo_tiles, halo_slot, boundary):
    picks = boundary.reshape(-1)
    rounded = start_vecs.astype(jnp.bfloat16)
    outgoing = [rounded[boundary[d]] for d in range(4)]
    rows, per_row, size = local_tiles.shape[0], local_tiles.shape[1], local_tiles.shape[3]
    stacked = jnp.swapaxes(local_tiles, 2, 3).reshape(rows, per_row * size, size)
    halo_t = jnp.swapaxes(halo_tiles, 1, 2)
    edge_halo = halo_t[picks]
    edge_slot = halo_slot[picks]
    outgoing = [rounded[boundary[d]] for d in range(4)]
    received = exchange(outgoing)
    part, edge_part = local_part(rounded, stacked, local_cols, picks, None, 1.0)
    previous = start_vecs
    for step in range(1, DEG + 1):
        scale = 1.0 if step == 1 else 2.0
        if step < DEG:
            outgoing = halo_add(edge_part, received, edge_halo, edge_slot, scale, True)
            received_next = exchange(outgoing)
        current, rounded = halo_add(part, received, halo_t, halo_slot, scale, False)
        if step < DEG:
            part, edge_part = local_part(rounded, stacked, local_cols, picks, previous, 2.0)
        if step < DEG:
            received = received_next
        previous = current

    total_rows = current.shape[0] * current.shape[2] * lax.axis_size("px") * lax.axis_size("py")
    partial_gram = jnp.einsum("rkj,rlj->kl", current, current, precision=lax.Precision.HIGHEST)
    raw_gram = butterfly_sum(butterfly_sum(partial_gram, "py"), "px")
    squares = jnp.diagonal(raw_gram)
    scales = lax.rsqrt(squares / total_rows + 1e-06)
    filtered = current * scales[None, :, None]
    gram_matrix = raw_gram * scales[:, None] * scales[None, :] / total_rows
    return (filtered, gram_matrix)


def solution(mesh):
    return jax.shard_map(
        shards,
        mesh=mesh,
        in_specs=(
            P(("px", "py"), None, None),
            P(("px", "py"), None, None, None),
            P(("px", "py"), None),
            P(("px", "py"), None, None),
            P(("px", "py")),
            P(("px", "py"), None),
        ),
        out_specs=(P(("px", "py"), None, None), P()),
        check_vma=False,
    )
```

time: 290 us -> 306 us (1.055)
  Pallas kernels: 50.7 us -> 65.3 us
    pallas_call x18 -> x26, Pallas kernels: 50.7 us -> 65.3 us  [the longest x17 36.7 us: halo_add(): pl.pallas_call(kernel, out_shape=out_shape, in_specs=[smem] + [vmem] * 6,...]
    unnamed x83 -> x87, local copies, waits for them, and re-layouts: 7.85 us -> 6.68 us
  transfers between devices with their start and end apart: 45 -> 45, of which waited for: 9 -> 9; matrix products, arithmetic and copies ran while one was open for 3% -> 3% of each run, Pallas kernels for 9% -> 16%
where the time goes in v7:
time: 306 us; the launch traced here: 302 us
  starting transfers between devices  181 us (59%)
  Pallas kernels  65.3 us (21%)
  waiting for transfers between devices  31.3 us (10%)
  local copies, waits for them, and re-layouts  18.5 us (6%)
    ppermute x36, starting transfers between devices, from_behind(): return lax.ppermute(value, axis, pairs)  145 us
    pallas_call x17, Pallas kernels, halo_add(): pl.pallas_call(kernel, out_shape=out_shape, in_specs=[smem] + [vmem] * 6,...  36.7 us
    ppermute x9, starting transfers between devices, butterfly_sum(): value = value + lax.ppermute(value, axis, pairs)  35.6 us
    ppermute x9, waiting for transfers between devices, butterfly_sum(): value = value + lax.ppermute(value, axis, pairs)  31.2 us
    pallas_call x9, Pallas kernels, local_part(): pl.pallas_call(kernel, out_shape=(jax.ShapeDtypeStruct(shape, jnp.float32...  28.5 us
    unnamed x87, local copies, waits for them, and re-layouts  6.68 us
  transfers between devices with their start and end apart: 45, of which 9 were waited for; matrix products, arithmetic and copies ran while one was open for 3% of the time, Pallas kernels for 16%

profile of v7, /device:TPU:1, one launch (start us, length us, event | category | flops | bytes accessed | tf_op | source)
XLA Modules:
  0.0 302.2 jit_solution(256901755510133150)
XLA Ops:
  3.4 4.5 %collective-permute-start = (bf16[2,64,128]{2,1,0:T(8,128)(2,1)S(1)}, bf16[2,64,128]{2,1,0:T(8,128)(2,1)S(1)}, u32[]{:S(2)}, u32[]{:S(2)}) collective-permute-start(bf16[2,64,128]{2,1,0:T(8,128)(2,1)S(1)} %gather_fusion), channel_id=1, source_target_pairs={{0,16},{16,32},{32,48},{48,64},{64,80},{80,96},{96,112},{112,128},... | collective-permute-start | bytes 98312 | tf_op jit(solution)/shard_map/ppermute | solution.py:18
  8.4 6.2 %collective-permute-start.1 = (bf16[2,64,128]{2,1,0:T(8,128)(2,1)S(1)}, bf16[2,64,128]{2,1,0:T(8,128)(2,1)S(1)}, u32[]{:S(2)}, u32[]{:S(2)}) collective-permute-start(bf16[2,64,128]{2,1,0:T(8,128)(2,1)S(1)} %gather_fusion.1), channel_id=1, source_target_pairs={{0,496},{16,0},{32,16},{48,32},{64,48},{80,64},{96,80},{112,96},{1... | collective-permute-start | bytes 98312 | tf_op jit(solution)/shard_map/ppermute | solution.py:18
  17.7 6.9 %collective-permute-start.3 = (bf16[2,64,128]{2,1,0:T(8,128)(2,1)S(1)}, bf16[2,64,128]{2,1,0:T(8,128)(2,1)S(1)}, u32[]{:S(2)}, u32[]{:S(2)}) collective-permute-start(bf16[2,64,128]{2,1,0:T(8,128)(2,1)S(1)} %gather_fusion.3), channel_id=1, source_target_pairs={{0,15},{1,0},{2,1},{3,2},{4,3},{5,4},{6,5},{7,6},{8,7},{9,8},{10,9... | collective-permute-start | bytes 98312 | tf_op jit(solution)/shard_map/ppermute | solution.py:18
  26.0 4.0 %copy.15 = bf16[16,4,128,128]{3,2,1,0:T(8,128)(2,1)} copy(bf16[16,4,128,128]{2,3,1,0:T(8,128)(2,1)} %bitcast.46) | data formatting | bytes 4194304 | tf_op jit(solution)/shard_map/transpose | solution.py:122
  33.5 3.1 %shard_map.77 = (f32[16,64,128]{2,1,0:T(8,128)}, f32[8,64,128]{2,1,0:T(8,128)}) custom-call(s32[64]{0:T(128)} %reshape.178.cols_ref, s32[8]{0:T(128)} %reshape.179.picks_ref, bf16[16,64,128]{2,1,0:T(8,128)(2,1)} %copy-done.3, bf16[16,512,128]{2,1,0:T(8,128)(2,1)} %bitcast.27), custom_call_target="tpu_custom_call" | custom-call | tf_op jit(solution)/shard_map/pallas_call | solution.py:57
  39.1 3.9 %collective-permute-start.4 = (bf16[2,64,128]{2,1,0:T(8,128)(2,1)}, bf16[2,64,128]{2,1,0:T(8,128)(2,1)S(1)}, u32[]{:S(2)}, u32[]{:S(2)}) collective-permute-start(bf16[2,64,128]{2,1,0:T(8,128)(2,1)} %get-tuple-element.71), channel_id=1, source_target_pairs={{0,16},{16,32},{32,48},{48,64},{64,80},{80,96},{96,112},{112,128},... | collective-permute-start | bytes 98312 | tf_op jit(solution)/shard_map/ppermute | solution.py:18
  43.0 4.1 %collective-permute-start.5 = (bf16[2,64,128]{2,1,0:T(8,128)(2,1)}, bf16[2,64,128]{2,1,0:T(8,128)(2,1)S(1)}, u32[]{:S(2)}, u32[]{:S(2)}) collective-permute-start(bf16[2,64,128]{2,1,0:T(8,128)(2,1)} %get-tuple-element.72), channel_id=1, source_target_pairs={{0,496},{16,0},{32,16},{48,32},{64,48},{80,64},{96,80},{112,96},{1... | collective-permute-start | bytes 98312 | tf_op jit(solution)/shard_map/ppermute | solution.py:18
  49.1 4.6 %collective-permute-start.7 = (bf16[2,64,128]{2,1,0:T(8,128)(2,1)}, bf16[2,64,128]{2,1,0:T(8,128)(2,1)S(1)}, u32[]{:S(2)}, u32[]{:S(2)}) collective-permute-start(bf16[2,64,128]{2,1,0:T(8,128)(2,1)} %get-tuple-element.74), channel_id=1, source_target_pairs={{0,15},{1,0},{2,1},{3,2},{4,3},{5,4},{6,5},{7,6},{8,7},{9,8},{10,9... | collective-permute-start | bytes 98312 | tf_op jit(solution)/shard_map/ppermute | solution.py:18
  56.1 3.2 %shard_map.79 = (f32[16,64,128]{2,1,0:T(8,128)}, f32[8,64,128]{2,1,0:T(8,128)}) custom-call(s32[64]{0:T(128)} %reshape.178.cols_ref, s32[8]{0:T(128)} %reshape.179.picks_ref, bf16[16,64,128]{2,1,0:T(8,128)(2,1)} %get-tuple-element.68.rounded_ref, bf16[16,512,128]{2,1,0:T(8,128)(2,1)} %bitcast.28, f32[16,64,128]{2,1,0:T(8,128)} %refs_0_.1), custom_call_target="tpu_custom_call" | custom-call | tf_op jit(solution)/shard_map/pallas_call | solution.py:57
  63.7 4.6 %collective-permute-start.11 = (bf16[2,64,128]{2,1,0:T(8,128)(2,1)}, bf16[2,64,128]{2,1,0:T(8,128)(2,1)S(1)}, u32[]{:S(2)}, u32[]{:S(2)}) collective-permute-start(bf16[2,64,128]{2,1,0:T(8,128)(2,1)} %get-tuple-element.82), channel_id=1, source_target_pairs={{0,15},{1,0},{2,1},{3,2},{4,3},{5,4},{6,5},{7,6},{8,7},{9,8},{10,9... | collective-permute-start | bytes 98312 | tf_op jit(solution)/shard_map/ppermute | solution.py:18
  68.3 2.5 collective-permute-start.8
  70.9 7.5 %collective-permute-start.9 = (bf16[2,64,128]{2,1,0:T(8,128)(2,1)}, bf16[2,64,128]{2,1,0:T(8,128)(2,1)S(1)}, u32[]{:S(2)}, u32[]{:S(2)}) collective-permute-start(bf16[2,64,128]{2,1,0:T(8,128)(2,1)} %get-tuple-element.80), channel_id=1, source_target_pairs={{0,496},{16,0},{32,16},{48,32},{64,48},{80,64},{96,80},{112,96},{1... | collective-permute-start | bytes 98312 | tf_op jit(solution)/shard_map/ppermute | solution.py:18
  78.3 2.4 shard_map.81
  80.7 3.2 %shard_map.82 = (f32[16,64,128]{2,1,0:T(8,128)}, f32[8,64,128]{2,1,0:T(8,128)}) custom-call(s32[64]{0:T(128)} %reshape.178.cols_ref, s32[8]{0:T(128)} %reshape.179.picks_ref, bf16[16,64,128]{2,1,0:T(8,128)(2,1)} %get-tuple-element.75.rounded_ref, bf16[16,512,128]{2,1,0:T(8,128)(2,1)} %bitcast.29, f32[16,64,128]{2,1,0:T(8,128)} %get-tuple-element.76.refs_0_), custom_call_target="tpu_custom_call" | custom-call | tf_op jit(solution)/shard_map/pallas_call | solution.py:57
  88.4 7.0 %collective-permute-start.13 = (bf16[2,64,128]{2,1,0:T(8,128)(2,1)}, bf16[2,64,128]{2,1,0:T(8,128)(2,1)S(1)}, u32[]{:S(2)}, u32[]{:S(2)}) collective-permute-start(bf16[2,64,128]{2,1,0:T(8,128)(2,1)} %get-tuple-element.88), channel_id=1, source_target_pairs={{0,496},{16,0},{32,16},{48,32},{64,48},{80,64},{96,80},{112,96},{1... | collective-permute-start | bytes 98312 | tf_op jit(solution)/shard_map/ppermute | solution.py:18
  97.3 4.6 %collective-permute-start.15 = (bf16[2,64,128]{2,1,0:T(8,128)(2,1)}, bf16[2,64,128]{2,1,0:T(8,128)(2,1)S(1)}, u32[]{:S(2)}, u32[]{:S(2)}) collective-permute-start(bf16[2,64,128]{2,1,0:T(8,128)(2,1)} %get-tuple-element.90), channel_id=1, source_target_pairs={{0,15},{1,0},{2,1},{3,2},{4,3},{5,4},{6,5},{7,6},{8,7},{9,8},{10,9... | collective-permute-start | bytes 98312 | tf_op jit(solution)/shard_map/ppermute | solution.py:18
  101.9 2.4 shard_map.84
  104.3 3.2 %shard_map.85 = (f32[16,64,128]{2,1,0:T(8,128)}, f32[8,64,128]{2,1,0:T(8,128)}) custom-call(s32[64]{0:T(128)} %reshape.178.cols_ref, s32[8]{0:T(128)} %reshape.179.picks_ref, bf16[16,64,128]{2,1,0:T(8,128)(2,1)} %get-tuple-element.83.rounded_ref, bf16[16,512,128]{2,1,0:T(8,128)(2,1)} %bitcast.30, f32[16,64,128]{2,1,0:T(8,128)} %get-tuple-element.84.refs_0_), custom_call_target="tpu_custom_call" | custom-call | tf_op jit(solution)/shard_map/pallas_call | solution.py:57
  111.9 7.5 %collective-permute-start.17 = (bf16[2,64,128]{2,1,0:T(8,128)(2,1)}, bf16[2,64,128]{2,1,0:T(8,128)(2,1)S(1)}, u32[]{:S(2)}, u32[]{:S(2)}) collective-permute-start(bf16[2,64,128]{2,1,0:T(8,128)(2,1)} %get-tuple-element.96), channel_id=1, source_target_pairs={{0,496},{16,0},{32,16},{48,32},{64,48},{80,64},{96,80},{112,96},{1... | collective-permute-start | bytes 98312 | tf_op jit(solution)/shard_map/ppermute | solution.py:18
  121.4 4.6 %collective-permute-start.19 = (bf16[2,64,128]{2,1,0:T(8,128)(2,1)}, bf16[2,64,128]{2,1,0:T(8,128)(2,1)S(1)}, u32[]{:S(2)}, u32[]{:S(2)}) collective-permute-start(bf16[2,64,128]{2,1,0:T(8,128)(2,1)} %get-tuple-element.98), channel_id=1, source_target_pairs={{0,15},{1,0},{2,1},{3,2},{4,3},{5,4},{6,5},{7,6},{8,7},{9,8},{10,9... | collective-permute-start | bytes 98312 | tf_op jit(solution)/shard_map/ppermute | solution.py:18
  126.0 2.4 shard_map.87
  128.4 3.2 %shard_map.88 = (f32[16,64,128]{2,1,0:T(8,128)}, f32[8,64,128]{2,1,0:T(8,128)}) custom-call(s32[64]{0:T(128)} %reshape.178.cols_ref, s32[8]{0:T(128)} %reshape.179.picks_ref, bf16[16,64,128]{2,1,0:T(8,128)(2,1)} %get-tuple-element.91.rounded_ref, bf16[16,512,128]{2,1,0:T(8,128)(2,1)} %bitcast.31, f32[16,64,128]{2,1,0:T(8,128)} %get-tuple-element.92.refs_0_), custom_call_target="tpu_custom_call" | custom-call | tf_op jit(solution)/shard_map/pallas_call | solution.py:57
  136.0 7.5 %collective-permute-start.21 = (bf16[2,64,128]{2,1,0:T(8,128)(2,1)}, bf16[2,64,128]{2,1,0:T(8,128)(2,1)S(1)}, u32[]{:S(2)}, u32[]{:S(2)}) collective-permute-start(bf16[2,64,128]{2,1,0:T(8,128)(2,1)} %get-tuple-element.104), channel_id=1, source_target_pairs={{0,496},{16,0},{32,16},{48,32},{64,48},{80,64},{96,80},{112,96},{1... | collective-permute-start | bytes 98312 | tf_op jit(solution)/shard_map/ppermute | solution.py:18
  145.5 4.6 %collective-permute-start.23 = (bf16[2,64,128]{2,1,0:T(8,128)(2,1)}, bf16[2,64,128]{2,1,0:T(8,128)(2,1)S(1)}, u32[]{:S(2)}, u32[]{:S(2)}) collective-permute-start(bf16[2,64,128]{2,1,0:T(8,128)(2,1)} %get-tuple-element.106), channel_id=1, source_target_pairs={{0,15},{1,0},{2,1},{3,2},{4,3},{5,4},{6,5},{7,6},{8,7},{9,8},{10,9... | collective-permute-start | bytes 98312 | tf_op jit(solution)/shard_map/ppermute | solution.py:18
  152.4 3.2 %shard_map.91 = (f32[16,64,128]{2,1,0:T(8,128)}, f32[8,64,128]{2,1,0:T(8,128)}) custom-call(s32[64]{0:T(128)} %reshape.178.cols_ref, s32[8]{0:T(128)} %reshape.179.picks_ref, bf16[16,64,128]{2,1,0:T(8,128)(2,1)} %get-tuple-element.99.rounded_ref, bf16[16,512,128]{2,1,0:T(8,128)(2,1)} %bitcast.32, f32[16,64,128]{2,1,0:T(8,128)} %get-tuple-element.100.refs_0_), custom_call_target="tpu_custom_call" | custom-call | tf_op jit(solution)/shard_map/pallas_call | solution.py:57
  160.1 7.5 %collective-permute-start.25 = (bf16[2,64,128]{2,1,0:T(8,128)(2,1)}, bf16[2,64,128]{2,1,0:T(8,128)(2,1)S(1)}, u32[]{:S(2)}, u32[]{:S(2)}) collective-permute-start(bf16[2,64,128]{2,1,0:T(8,128)(2,1)} %get-tuple-element.112), channel_id=1, source_target_pairs={{0,496},{16,0},{32,16},{48,32},{64,48},{80,64},{96,80},{112,96},{1... | collective-permute-start | bytes 98312 | tf_op jit(solution)/shard_map/ppermute | solution.py:18
  169.6 4.6 %collective-permute-start.27 = (bf16[2,64,128]{2,1,0:T(8,128)(2,1)}, bf16[2,64,128]{2,1,0:T(8,128)(2,1)S(1)}, u32[]{:S(2)}, u32[]{:S(2)}) collective-permute-start(bf16[2,64,128]{2,1,0:T(8,128)(2,1)} %get-tuple-element.114), channel_id=1, source_target_pairs={{0,15},{1,0},{2,1},{3,2},{4,3},{5,4},{6,5},{7,6},{8,7},{9,8},{10,9... | collective-permute-start | bytes 98312 | tf_op jit(solution)/shard_map/ppermute | solution.py:18
  174.1 2.4 shard_map.93
  176.6 3.2 %shard_map.94 = (f32[16,64,128]{2,1,0:T(8,128)}, f32[8,64,128]{2,1,0:T(8,128)}) custom-call(s32[64]{0:T(128)} %reshape.178.cols_ref, s32[8]{0:T(128)} %reshape.179.picks_ref, bf16[16,64,128]{2,1,0:T(8,128)(2,1)} %get-tuple-element.107.rounded_ref, bf16[16,512,128]{2,1,0:T(8,128)(2,1)} %bitcast.33, f32[16,64,128]{2,1,0:T(8,128)} %get-tuple-element.108.refs_0_), custom_call_target="tpu_custom_call" | custom-call | tf_op jit(solution)/shard_map/pallas_call | solution.py:57
  184.2 7.5 %collective-permute-start.29 = (bf16[2,64,128]{2,1,0:T(8,128)(2,1)}, bf16[2,64,128]{2,1,0:T(8,128)(2,1)S(1)}, u32[]{:S(2)}, u32[]{:S(2)}) collective-permute-start(bf16[2,64,128]{2,1,0:T(8,128)(2,1)} %get-tuple-element.120), channel_id=1, source_target_pairs={{0,496},{16,0},{32,16},{48,32},{64,48},{80,64},{96,80},{112,96},{1... | collective-permute-start | bytes 98312 | tf_op jit(solution)/shard_map/ppermute | solution.py:18
  193.6 4.6 %collective-permute-start.31 = (bf16[2,64,128]{2,1,0:T(8,128)(2,1)}, bf16[2,64,128]{2,1,0:T(8,128)(2,1)S(1)}, u32[]{:S(2)}, u32[]{:S(2)}) collective-permute-start(bf16[2,64,128]{2,1,0:T(8,128)(2,1)} %get-tuple-element.122), channel_id=1, source_target_pairs={{0,15},{1,0},{2,1},{3,2},{4,3},{5,4},{6,5},{7,6},{8,7},{9,8},{10,9... | collective-permute-start | bytes 98312 | tf_op jit(solution)/shard_map/ppermute | solution.py:18
  198.2 2.4 shard_map.96
  200.6 3.2 %shard_map.97 = (f32[16,64,128]{2,1,0:T(8,128)}, f32[8,64,128]{2,1,0:T(8,128)}) custom-call(s32[64]{0:T(128)} %reshape.178.cols_ref, s32[8]{0:T(128)} %reshape.179.picks_ref, bf16[16,64,128]{2,1,0:T(8,128)(2,1)} %get-tuple-element.115.rounded_ref, bf16[16,512,128]{2,1,0:T(8,128)(2,1)} %bitcast.34, f32[16,64,128]{2,1,0:T(8,128)} %get-tuple-element.116.refs_0_), custom_call_target="tpu_custom_call" | custom-call | tf_op jit(solution)/shard_map/pallas_call | solution.py:57
  208.3 7.5 %collective-permute-start.33 = (bf16[2,64,128]{2,1,0:T(8,128)(2,1)}, bf16[2,64,128]{2,1,0:T(8,128)(2,1)S(1)}, u32[]{:S(2)}, u32[]{:S(2)}) collective-permute-start(bf16[2,64,128]{2,1,0:T(8,128)(2,1)} %get-tuple-element.128), channel_id=1, source_target_pairs={{0,496},{16,0},{32,16},{48,32},{64,48},{80,64},{96,80},{112,96},{1... | collective-permute-start | bytes 98312 | tf_op jit(solution)/shard_map/ppermute | solution.py:18
  217.8 4.6 %collective-permute-start.35 = (bf16[2,64,128]{2,1,0:T(8,128)(2,1)}, bf16[2,64,128]{2,1,0:T(8,128)(2,1)S(1)}, u32[]{:S(2)}, u32[]{:S(2)}) collective-permute-start(bf16[2,64,128]{2,1,0:T(8,128)(2,1)} %get-tuple-element.130), channel_id=1, source_target_pairs={{0,15},{1,0},{2,1},{3,2},{4,3},{5,4},{6,5},{7,6},{8,7},{9,8},{10,9... | collective-permute-start | bytes 98312 | tf_op jit(solution)/shard_map/ppermute | solution.py:18
  222.3 2.4 shard_map.99
  224.8 3.2 %shard_map.100 = (f32[16,64,128]{2,1,0:T(8,128)}, f32[8,64,128]{2,1,0:T(8,128)}) custom-call(s32[64]{0:T(128)} %reshape.178.cols_ref, s32[8]{0:T(128)} %reshape.179.picks_ref, bf16[16,64,128]{2,1,0:T(8,128)(2,1)} %get-tuple-element.123.rounded_ref, bf16[16,512,128]{2,1,0:T(8,128)(2,1)} %bitcast.35, f32[16,64,128]{2,1,0:T(8,128)} %get-tuple-element.124.refs_0_), custom_call_target="tpu_custom_call" | custom-call | tf_op jit(solution)/shard_map/pallas_call | solution.py:57
  234.8 2.7 collective-permute-done.36
  239.4 3.7 %collective-permute-done.37 = f32[64,64]{1,0:T(8,128)S(1)} collective-permute-done((f32[64,64]{1,0:T(8,128)S(1)}, f32[64,64]{1,0:T(8,128)S(1)}, u32[]{:S(2)}, u32[]{:S(2)}) %collective-permute-start.37) | collective-permute-done | bytes 16416 | tf_op jit(solution)/shard_map/ppermute | solution.py:26
  243.1 3.5 %collective-permute-start.38 = (f32[64,64]{1,0:T(8,128)S(1)}, f32[64,64]{1,0:T(8,128)S(1)}, u32[]{:S(2)}, u32[]{:S(2)}) collective-permute-start(f32[64,64]{1,0:T(8,128)S(1)} %add.106), channel_id=1, source_target_pairs={{0,4},{1,5},{2,6},{3,7},{4,0},{5,1},{6,2},{7,3},{8,12},{9,13},{10,... | collective-permute-start | bytes 49160 | tf_op jit(solution)/shard_map/ppermute | solution.py:26
  246.6 5.7 %collective-permute-done.38 = f32[64,64]{1,0:T(8,128)S(1)} collective-permute-done((f32[64,64]{1,0:T(8,128)S(1)}, f32[64,64]{1,0:T(8,128)S(1)}, u32[]{:S(2)}, u32[]{:S(2)}) %collective-permute-start.38) | collective-permute-done | bytes 16416 | tf_op jit(solution)/shard_map/ppermute | solution.py:26
  252.3 9.0 %collective-permute-start.39 = (f32[64,64]{1,0:T(8,128)S(1)}, f32[64,64]{1,0:T(8,128)S(1)}, u32[]{:S(2)}, u32[]{:S(2)}) collective-permute-start(f32[64,64]{1,0:T(8,128)S(1)} %add.107), channel_id=1, source_target_pairs={{0,8},{1,9},{2,10},{3,11},{4,12},{5,13},{6,14},{7,15},{8,0},{9,1},... | collective-permute-start | bytes 49160 | tf_op jit(solution)/shard_map/ppermute | solution.py:26
  261.3 4.3 %collective-permute-done.39 = f32[64,64]{1,0:T(8,128)S(1)} collective-permute-done((f32[64,64]{1,0:T(8,128)S(1)}, f32[64,64]{1,0:T(8,128)S(1)}, u32[]{:S(2)}, u32[]{:S(2)}) %collective-permute-start.39) | collective-permute-done | bytes 16416 | tf_op jit(solution)/shard_map/ppermute | solution.py:26
  265.7 11.6 %collective-permute-start.40 = (f32[64,64]{1,0:T(8,128)S(1)}, f32[64,64]{1,0:T(8,128)S(1)}, u32[]{:S(2)}, u32[]{:S(2)}) collective-permute-start(f32[64,64]{1,0:T(8,128)S(1)} %add.108), channel_id=1, source_target_pairs={{0,16},{16,0},{32,48},{48,32},{64,80},{80,64},{96,112},{112,96},{1... | collective-permute-start | bytes 49160 | tf_op jit(solution)/shard_map/ppermute | solution.py:26
  280.1 2.7 collective-permute-done.41
  284.7 4.2 %collective-permute-done.42 = f32[64,64]{1,0:T(8,128)S(1)} collective-permute-done((f32[64,64]{1,0:T(8,128)S(1)}, f32[64,64]{1,0:T(8,128)S(1)}, u32[]{:S(2)}, u32[]{:S(2)}) %collective-permute-start.42) | collective-permute-done | bytes 16416 | tf_op jit(solution)/shard_map/ppermute | solution.py:26
  290.9 2.7 collective-permute-done.43
  295.5 4.2 %collective-permute-done.44 = f32[64,64]{1,0:T(8,128)S(1)} collective-permute-done((f32[64,64]{1,0:T(8,128)S(1)}, f32[64,64]{1,0:T(8,128)S(1)}, u32[]{:S(2)}, u32[]{:S(2)}) %collective-permute-start.44) | collective-permute-done | bytes 16416 | tf_op jit(solution)/shard_map/ppermute | solution.py:26
  (190 shorter events, 82.5 us)
Async XLA Ops:
  1.7 28.3 %copy-start.3 = (bf16[16,64,128]{2,1,0:T(8,128)(2,1)}, bf16[16,64,128]{2,1,0:T(8,128)(2,1)S(1)}, u32[]{:S(2)}) copy-start(bf16[16,64,128]{2,1,0:T(8,128)(2,1)S(1)} %convert_element_type.3.rounded_ref) | copy-start | bytes 786436
  3.4 33.2 %collective-permute-start = (bf16[2,64,128]{2,1,0:T(8,128)(2,1)S(1)}, bf16[2,64,128]{2,1,0:T(8,128)(2,1)S(1)}, u32[]{:S(2)}, u32[]{:S(2)}) collective-permute-start(bf16[2,64,128]{2,1,0:T(8,128)(2,1)S(1)} %gather_fusion), channel_id=1, source_target_pairs={{0,16},{16,32},{32,48},{48,64},{64,80},{80,96},{96,112},{112,128},... | collective-permute-start | bytes 98312 | tf_op jit(solution)/shard_map/ppermute | solution.py:18
  8.4 28.1 %collective-permute-start.1 = (bf16[2,64,128]{2,1,0:T(8,128)(2,1)S(1)}, bf16[2,64,128]{2,1,0:T(8,128)(2,1)S(1)}, u32[]{:S(2)}, u32[]{:S(2)}) collective-permute-start(bf16[2,64,128]{2,1,0:T(8,128)(2,1)S(1)} %gather_fusion.1), channel_id=1, source_target_pairs={{0,496},{16,0},{32,16},{48,32},{64,48},{80,64},{96,80},{112,96},{1... | collective-permute-start | bytes 98312 | tf_op jit(solution)/shard_map/ppermute | solution.py:18
  15.2 21.4 %collective-permute-start.2 = (bf16[2,64,128]{2,1,0:T(8,128)(2,1)S(1)}, bf16[2,64,128]{2,1,0:T(8,128)(2,1)S(1)}, u32[]{:S(2)}, u32[]{:S(2)}) collective-permute-start(bf16[2,64,128]{2,1,0:T(8,128)(2,1)S(1)} %gather_fusion.2), channel_id=1, source_target_pairs={{0,1},{1,2},{2,3},{3,4},{4,5},{5,6},{6,7},{7,8},{8,9},{9,10},{10,1... | collective-permute-start | bytes 98312 | tf_op jit(solution)/shard_map/ppermute | solution.py:18
  17.7 18.9 %collective-permute-start.3 = (bf16[2,64,128]{2,1,0:T(8,128)(2,1)S(1)}, bf16[2,64,128]{2,1,0:T(8,128)(2,1)S(1)}, u32[]{:S(2)}, u32[]{:S(2)}) collective-permute-start(bf16[2,64,128]{2,1,0:T(8,128)(2,1)S(1)} %gather_fusion.3), channel_id=1, source_target_pairs={{0,15},{1,0},{2,1},{3,2},{4,3},{5,4},{6,5},{7,6},{8,7},{9,8},{10,9... | collective-permute-start | bytes 98312 | tf_op jit(solution)/shard_map/ppermute | solution.py:18
  31.0 22.7 %copy-start.1 = (bf16[16,128,128]{1,2,0:T(8,128)(2,1)}, bf16[16,128,128]{1,2,0:T(8,128)(2,1)S(1)}, u32[]{:S(2)}) copy-start(bf16[16,128,128]{1,2,0:T(8,128)(2,1)S(1)} %copy.16) | copy-start | bytes 1572868
  39.1 20.1 %collective-permute-start.4 = (bf16[2,64,128]{2,1,0:T(8,128)(2,1)}, bf16[2,64,128]{2,1,0:T(8,128)(2,1)S(1)}, u32[]{:S(2)}, u32[]{:S(2)}) collective-permute-start(bf16[2,64,128]{2,1,0:T(8,128)(2,1)} %get-tuple-element.71), channel_id=1, source_target_pairs={{0,16},{16,32},{32,48},{48,64},{64,80},{80,96},{96,112},{112,128},... | collective-permute-start | bytes 98312 | tf_op jit(solution)/shard_map/ppermute | solution.py:18
  43.0 16.2 %collective-permute-start.5 = (bf16[2,64,128]{2,1,0:T(8,128)(2,1)}, bf16[2,64,128]{2,1,0:T(8,128)(2,1)S(1)}, u32[]{:S(2)}, u32[]{:S(2)}) collective-permute-start(bf16[2,64,128]{2,1,0:T(8,128)(2,1)} %get-tuple-element.72), channel_id=1, source_target_pairs={{0,496},{16,0},{32,16},{48,32},{64,48},{80,64},{96,80},{112,96},{1... | collective-permute-start | bytes 98312 | tf_op jit(solution)/shard_map/ppermute | solution.py:18
  47.2 12.1 %collective-permute-start.6 = (bf16[2,64,128]{2,1,0:T(8,128)(2,1)}, bf16[2,64,128]{2,1,0:T(8,128)(2,1)S(1)}, u32[]{:S(2)}, u32[]{:S(2)}) collective-permute-start(bf16[2,64,128]{2,1,0:T(8,128)(2,1)} %get-tuple-element.73), channel_id=1, source_target_pairs={{0,1},{1,2},{2,3},{3,4},{4,5},{5,6},{6,7},{7,8},{8,9},{9,10},{10,1... | collective-permute-start | bytes 98312 | tf_op jit(solution)/shard_map/ppermute | solution.py:18
  49.1 10.2 %collective-permute-start.7 = (bf16[2,64,128]{2,1,0:T(8,128)(2,1)}, bf16[2,64,128]{2,1,0:T(8,128)(2,1)S(1)}, u32[]{:S(2)}, u32[]{:S(2)}) collective-permute-start(bf16[2,64,128]{2,1,0:T(8,128)(2,1)} %get-tuple-element.74), channel_id=1, source_target_pairs={{0,15},{1,0},{2,1},{3,2},{4,3},{5,4},{6,5},{7,6},{8,7},{9,8},{10,9... | collective-permute-start | bytes 98312 | tf_op jit(solution)/shard_map/ppermute | solution.py:18
  61.8 22.1 %collective-permute-start.10 = (bf16[2,64,128]{2,1,0:T(8,128)(2,1)}, bf16[2,64,128]{2,1,0:T(8,128)(2,1)S(1)}, u32[]{:S(2)}, u32[]{:S(2)}) collective-permute-start(bf16[2,64,128]{2,1,0:T(8,128)(2,1)} %get-tuple-element.81), channel_id=1, source_target_pairs={{0,1},{1,2},{2,3},{3,4},{4,5},{5,6},{6,7},{7,8},{8,9},{9,10},{10,1... | collective-permute-start | bytes 98312 | tf_op jit(solution)/shard_map/ppermute | solution.py:18
  63.7 20.2 %collective-permute-start.11 = (bf16[2,64,128]{2,1,0:T(8,128)(2,1)}, bf16[2,64,128]{2,1,0:T(8,128)(2,1)S(1)}, u32[]{:S(2)}, u32[]{:S(2)}) collective-permute-start(bf16[2,64,128]{2,1,0:T(8,128)(2,1)} %get-tuple-element.82), channel_id=1, source_target_pairs={{0,15},{1,0},{2,1},{3,2},{4,3},{5,4},{6,5},{7,6},{8,7},{9,8},{10,9... | collective-permute-start | bytes 98312 | tf_op jit(solution)/shard_map/ppermute | solution.py:18
  68.3 15.6 %collective-permute-start.8 = (bf16[2,64,128]{2,1,0:T(8,128)(2,1)}, bf16[2,64,128]{2,1,0:T(8,128)(2,1)S(1)}, u32[]{:S(2)}, u32[]{:S(2)}) collective-permute-start(bf16[2,64,128]{2,1,0:T(8,128)(2,1)} %get-tuple-element.79), channel_id=1, source_target_pairs={{0,16},{16,32},{32,48},{48,64},{64,80},{80,96},{96,112},{112,128},... | collective-permute-start | bytes 98312 | tf_op jit(solution)/shard_map/ppermute | solution.py:18
  70.9 13.1 %collective-permute-start.9 = (bf16[2,64,128]{2,1,0:T(8,128)(2,1)}, bf16[2,64,128]{2,1,0:T(8,128)(2,1)S(1)}, u32[]{:S(2)}, u32[]{:S(2)}) collective-permute-start(bf16[2,64,128]{2,1,0:T(8,128)(2,1)} %get-tuple-element.80), channel_id=1, source_target_pairs={{0,496},{16,0},{32,16},{48,32},{64,48},{80,64},{96,80},{112,96},{1... | collective-permute-start | bytes 98312 | tf_op jit(solution)/shard_map/ppermute | solution.py:18
  86.5 21.0 %collective-permute-start.12 = (bf16[2,64,128]{2,1,0:T(8,128)(2,1)}, bf16[2,64,128]{2,1,0:T(8,128)(2,1)S(1)}, u32[]{:S(2)}, u32[]{:S(2)}) collective-permute-start(bf16[2,64,128]{2,1,0:T(8,128)(2,1)} %get-tuple-element.87), channel_id=1, source_target_pairs={{0,16},{16,32},{32,48},{48,64},{64,80},{80,96},{96,112},{112,128},... | collective-permute-start | bytes 98312 | tf_op jit(solution)/shard_map/ppermute | solution.py:18
  88.4 19.1 %collective-permute-start.13 = (bf16[2,64,128]{2,1,0:T(8,128)(2,1)}, bf16[2,64,128]{2,1,0:T(8,128)(2,1)S(1)}, u32[]{:S(2)}, u32[]{:S(2)}) collective-permute-start(bf16[2,64,128]{2,1,0:T(8,128)(2,1)} %get-tuple-element.88), channel_id=1, source_target_pairs={{0,496},{16,0},{32,16},{48,32},{64,48},{80,64},{96,80},{112,96},{1... | collective-permute-start | bytes 98312 | tf_op jit(solution)/shard_map/ppermute | solution.py:18
  95.4 12.1 %collective-permute-start.14 = (bf16[2,64,128]{2,1,0:T(8,128)(2,1)}, bf16[2,64,128]{2,1,0:T(8,128)(2,1)S(1)}, u32[]{:S(2)}, u32[]{:S(2)}) collective-permute-start(bf16[2,64,128]{2,1,0:T(8,128)(2,1)} %get-tuple-element.89), channel_id=1, source_target_pairs={{0,1},{1,2},{2,3},{3,4},{4,5},{5,6},{6,7},{7,8},{8,9},{9,10},{10,1... | collective-permute-start | bytes 98312 | tf_op jit(solution)/shard_map/ppermute | solution.py:18
  97.3 10.2 %collective-permute-start.15 = (bf16[2,64,128]{2,1,0:T(8,128)(2,1)}, bf16[2,64,128]{2,1,0:T(8,128)(2,1)S(1)}, u32[]{:S(2)}, u32[]{:S(2)}) collective-permute-start(bf16[2,64,128]{2,1,0:T(8,128)(2,1)} %get-tuple-element.90), channel_id=1, source_target_pairs={{0,15},{1,0},{2,1},{3,2},{4,3},{5,4},{6,5},{7,6},{8,7},{9,8},{10,9... | collective-permute-start | bytes 98312 | tf_op jit(solution)/shard_map/ppermute | solution.py:18
  110.0 21.5 %collective-permute-start.16 = (bf16[2,64,128]{2,1,0:T(8,128)(2,1)}, bf16[2,64,128]{2,1,0:T(8,128)(2,1)S(1)}, u32[]{:S(2)}, u32[]{:S(2)}) collective-permute-start(bf16[2,64,128]{2,1,0:T(8,128)(2,1)} %get-tuple-element.95), channel_id=1, source_target_pairs={{0,16},{16,32},{32,48},{48,64},{64,80},{80,96},{96,112},{112,128},... | collective-permute-start | bytes 98312 | tf_op jit(solution)/shard_map/ppermute | solution.py:18
  111.9 19.6 %collective-permute-start.17 = (bf16[2,64,128]{2,1,0:T(8,128)(2,1)}, bf16[2,64,128]{2,1,0:T(8,128)(2,1)S(1)}, u32[]{:S(2)}, u32[]{:S(2)}) collective-permute-start(bf16[2,64,128]{2,1,0:T(8,128)(2,1)} %get-tuple-element.96), channel_id=1, source_target_pairs={{0,496},{16,0},{32,16},{48,32},{64,48},{80,64},{96,80},{112,96},{1... | collective-permute-start | bytes 98312 | tf_op jit(solution)/shard_map/ppermute | solution.py:18
  119.5 12.1 %collective-permute-start.18 = (bf16[2,64,128]{2,1,0:T(8,128)(2,1)}, bf16[2,64,128]{2,1,0:T(8,128)(2,1)S(1)}, u32[]{:S(2)}, u32[]{:S(2)}) collective-permute-start(bf16[2,64,128]{2,1,0:T(8,128)(2,1)} %get-tuple-element.97), channel_id=1, source_target_pairs={{0,1},{1,2},{2,3},{3,4},{4,5},{5,6},{6,7},{7,8},{8,9},{9,10},{10,1... | collective-permute-start | bytes 98312 | tf_op jit(solution)/shard_map/ppermute | solution.py:18
  121.4 10.2 %collective-permute-start.19 = (bf16[2,64,128]{2,1,0:T(8,128)(2,1)}, bf16[2,64,128]{2,1,0:T(8,128)(2,1)S(1)}, u32[]{:S(2)}, u32[]{:S(2)}) collective-permute-start(bf16[2,64,128]{2,1,0:T(8,128)(2,1)} %get-tuple-element.98), channel_id=1, source_target_pairs={{0,15},{1,0},{2,1},{3,2},{4,3},{5,4},{6,5},{7,6},{8,7},{9,8},{10,9... | collective-permute-start | bytes 98312 | tf_op jit(solution)/shard_map/ppermute | solution.py:18
  134.1 21.5 %collective-permute-start.20 = (bf16[2,64,128]{2,1,0:T(8,128)(2,1)}, bf16[2,64,128]{2,1,0:T(8,128)(2,1)S(1)}, u32[]{:S(2)}, u32[]{:S(2)}) collective-permute-start(bf16[2,64,128]{2,1,0:T(8,128)(2,1)} %get-tuple-element.103), channel_id=1, source_target_pairs={{0,16},{16,32},{32,48},{48,64},{64,80},{80,96},{96,112},{112,128},... | collective-permute-start | bytes 98312 | tf_op jit(solution)/shard_map/ppermute | solution.py:18
  136.0 19.6 %collective-permute-start.21 = (bf16[2,64,128]{2,1,0:T(8,128)(2,1)}, bf16[2,64,128]{2,1,0:T(8,128)(2,1)S(1)}, u32[]{:S(2)}, u32[]{:S(2)}) collective-permute-start(bf16[2,64,128]{2,1,0:T(8,128)(2,1)} %get-tuple-element.104), channel_id=1, source_target_pairs={{0,496},{16,0},{32,16},{48,32},{64,48},{80,64},{96,80},{112,96},{1... | collective-permute-start | bytes 98312 | tf_op jit(solution)/shard_map/ppermute | solution.py:18
  143.5 12.1 %collective-permute-start.22 = (bf16[2,64,128]{2,1,0:T(8,128)(2,1)}, bf16[2,64,128]{2,1,0:T(8,128)(2,1)S(1)}, u32[]{:S(2)}, u32[]{:S(2)}) collective-permute-start(bf16[2,64,128]{2,1,0:T(8,128)(2,1)} %get-tuple-element.105), channel_id=1, source_target_pairs={{0,1},{1,2},{2,3},{3,4},{4,5},{5,6},{6,7},{7,8},{8,9},{9,10},{10,1... | collective-permute-start | bytes 98312 | tf_op jit(solution)/shard_map/ppermute | solution.py:18
  145.5 10.2 %collective-permute-start.23 = (bf16[2,64,128]{2,1,0:T(8,128)(2,1)}, bf16[2,64,128]{2,1,0:T(8,128)(2,1)S(1)}, u32[]{:S(2)}, u32[]{:S(2)}) collective-permute-start(bf16[2,64,128]{2,1,0:T(8,128)(2,1)} %get-tuple-element.106), channel_id=1, source_target_pairs={{0,15},{1,0},{2,1},{3,2},{4,3},{5,4},{6,5},{7,6},{8,7},{9,8},{10,9... | collective-permute-start | bytes 98312 | tf_op jit(solution)/shard_map/ppermute | solution.py:18
  158.2 21.5 %collective-permute-start.24 = (bf16[2,64,128]{2,1,0:T(8,128)(2,1)}, bf16[2,64,128]{2,1,0:T(8,128)(2,1)S(1)}, u32[]{:S(2)}, u32[]{:S(2)}) collective-permute-start(bf16[2,64,128]{2,1,0:T(8,128)(2,1)} %get-tuple-element.111), channel_id=1, source_target_pairs={{0,16},{16,32},{32,48},{48,64},{64,80},{80,96},{96,112},{112,128},... | collective-permute-start | bytes 98312 | tf_op jit(solution)/shard_map/ppermute | solution.py:18
  160.1 19.6 %collective-permute-start.25 = (bf16[2,64,128]{2,1,0:T(8,128)(2,1)}, bf16[2,64,128]{2,1,0:T(8,128)(2,1)S(1)}, u32[]{:S(2)}, u32[]{:S(2)}) collective-permute-start(bf16[2,64,128]{2,1,0:T(8,128)(2,1)} %get-tuple-element.112), channel_id=1, source_target_pairs={{0,496},{16,0},{32,16},{48,32},{64,48},{80,64},{96,80},{112,96},{1... | collective-permute-start | bytes 98312 | tf_op jit(solution)/shard_map/ppermute | solution.py:18
  167.6 12.1 %collective-permute-start.26 = (bf16[2,64,128]{2,1,0:T(8,128)(2,1)}, bf16[2,64,128]{2,1,0:T(8,128)(2,1)S(1)}, u32[]{:S(2)}, u32[]{:S(2)}) collective-permute-start(bf16[2,64,128]{2,1,0:T(8,128)(2,1)} %get-tuple-element.113), channel_id=1, source_target_pairs={{0,1},{1,2},{2,3},{3,4},{4,5},{5,6},{6,7},{7,8},{8,9},{9,10},{10,1... | collective-permute-start | bytes 98312 | tf_op jit(solution)/shard_map/ppermute | solution.py:18
  169.6 10.2 %collective-permute-start.27 = (bf16[2,64,128]{2,1,0:T(8,128)(2,1)}, bf16[2,64,128]{2,1,0:T(8,128)(2,1)S(1)}, u32[]{:S(2)}, u32[]{:S(2)}) collective-permute-start(bf16[2,64,128]{2,1,0:T(8,128)(2,1)} %get-tuple-element.114), channel_id=1, source_target_pairs={{0,15},{1,0},{2,1},{3,2},{4,3},{5,4},{6,5},{7,6},{8,7},{9,8},{10,9... | collective-permute-start | bytes 98312 | tf_op jit(solution)/shard_map/ppermute | solution.py:18
  182.3 21.5 %collective-permute-start.28 = (bf16[2,64,128]{2,1,0:T(8,128)(2,1)}, bf16[2,64,128]{2,1,0:T(8,128)(2,1)S(1)}, u32[]{:S(2)}, u32[]{:S(2)}) collective-permute-start(bf16[2,64,128]{2,1,0:T(8,128)(2,1)} %get-tuple-element.119), channel_id=1, source_target_pairs={{0,16},{16,32},{32,48},{48,64},{64,80},{80,96},{96,112},{112,128},... | collective-permute-start | bytes 98312 | tf_op jit(solution)/shard_map/ppermute | solution.py:18
  184.2 19.6 %collective-permute-start.29 = (bf16[2,64,128]{2,1,0:T(8,128)(2,1)}, bf16[2,64,128]{2,1,0:T(8,128)(2,1)S(1)}, u32[]{:S(2)}, u32[]{:S(2)}) collective-permute-start(bf16[2,64,128]{2,1,0:T(8,128)(2,1)} %get-tuple-element.120), channel_id=1, source_target_pairs={{0,496},{16,0},{32,16},{48,32},{64,48},{80,64},{96,80},{112,96},{1... | collective-permute-start | bytes 98312 | tf_op jit(solution)/shard_map/ppermute | solution.py:18
  191.7 12.1 %collective-permute-start.30 = (bf16[2,64,128]{2,1,0:T(8,128)(2,1)}, bf16[2,64,128]{2,1,0:T(8,128)(2,1)S(1)}, u32[]{:S(2)}, u32[]{:S(2)}) collective-permute-start(bf16[2,64,128]{2,1,0:T(8,128)(2,1)} %get-tuple-element.121), channel_id=1, source_target_pairs={{0,1},{1,2},{2,3},{3,4},{4,5},{5,6},{6,7},{7,8},{8,9},{9,10},{10,1... | collective-permute-start | bytes 98312 | tf_op jit(solution)/shard_map/ppermute | solution.py:18
  193.6 10.2 %collective-permute-start.31 = (bf16[2,64,128]{2,1,0:T(8,128)(2,1)}, bf16[2,64,128]{2,1,0:T(8,128)(2,1)S(1)}, u32[]{:S(2)}, u32[]{:S(2)}) collective-permute-start(bf16[2,64,128]{2,1,0:T(8,128)(2,1)} %get-tuple-element.122), channel_id=1, source_target_pairs={{0,15},{1,0},{2,1},{3,2},{4,3},{5,4},{6,5},{7,6},{8,7},{9,8},{10,9... | collective-permute-start | bytes 98312 | tf_op jit(solution)/shard_map/ppermute | solution.py:18
  206.4 21.6 %collective-permute-start.32 = (bf16[2,64,128]{2,1,0:T(8,128)(2,1)}, bf16[2,64,128]{2,1,0:T(8,128)(2,1)S(1)}, u32[]{:S(2)}, u32[]{:S(2)}) collective-permute-start(bf16[2,64,128]{2,1,0:T(8,128)(2,1)} %get-tuple-element.127), channel_id=1, source_target_pairs={{0,16},{16,32},{32,48},{48,64},{64,80},{80,96},{96,112},{112,128},... | collective-permute-start | bytes 98312 | tf_op jit(solution)/shard_map/ppermute | solution.py:18
  208.3 19.7 %collective-permute-start.33 = (bf16[2,64,128]{2,1,0:T(8,128)(2,1)}, bf16[2,64,128]{2,1,0:T(8,128)(2,1)S(1)}, u32[]{:S(2)}, u32[]{:S(2)}) collective-permute-start(bf16[2,64,128]{2,1,0:T(8,128)(2,1)} %get-tuple-element.128), channel_id=1, source_target_pairs={{0,496},{16,0},{32,16},{48,32},{64,48},{80,64},{96,80},{112,96},{1... | collective-permute-start | bytes 98312 | tf_op jit(solution)/shard_map/ppermute | solution.py:18
  215.8 12.2 %collective-permute-start.34 = (bf16[2,64,128]{2,1,0:T(8,128)(2,1)}, bf16[2,64,128]{2,1,0:T(8,128)(2,1)S(1)}, u32[]{:S(2)}, u32[]{:S(2)}) collective-permute-start(bf16[2,64,128]{2,1,0:T(8,128)(2,1)} %get-tuple-element.129), channel_id=1, source_target_pairs={{0,1},{1,2},{2,3},{3,4},{4,5},{5,6},{6,7},{7,8},{8,9},{9,10},{10,1... | collective-permute-start | bytes 98312 | tf_op jit(solution)/shard_map/ppermute | solution.py:18
  217.8 10.2 %collective-permute-start.35 = (bf16[2,64,128]{2,1,0:T(8,128)(2,1)}, bf16[2,64,128]{2,1,0:T(8,128)(2,1)S(1)}, u32[]{:S(2)}, u32[]{:S(2)}) collective-permute-start(bf16[2,64,128]{2,1,0:T(8,128)(2,1)} %get-tuple-element.130), channel_id=1, source_target_pairs={{0,15},{1,0},{2,1},{3,2},{4,3},{5,4},{6,5},{7,6},{8,7},{9,8},{10,9... | collective-permute-start | bytes 98312 | tf_op jit(solution)/shard_map/ppermute | solution.py:18
  231.0 70.3 %copy-start.2 = (f32[16,64,128]{2,1,0:T(8,128)S(1)}, f32[16,64,128]{2,1,0:T(8,128)}, u32[]{:S(2)}) copy-start(f32[16,64,128]{2,1,0:T(8,128)} %get-tuple-element.131) | copy-start | bytes 1572868
  232.8 4.7 %collective-permute-start.36 = (f32[64,64]{1,0:T(8,128)S(1)}, f32[64,64]{1,0:T(8,128)S(1)}, u32[]{:S(2)}, u32[]{:S(2)}) collective-permute-start(f32[64,64]{1,0:T(8,128)S(1)} %convolution_bitcast_fusion), channel_id=1, source_target_pairs={{0,1},{1,0},{2,3},{3,2},{4,5},{5,4},{6,7},{7,6},{8,9},{9,8},{10,11... | collective-permute-start | bytes 49160 | tf_op jit(solution)/shard_map/ppermute | solution.py:26
  237.5 5.6 %collective-permute-start.37 = (f32[64,64]{1,0:T(8,128)S(1)}, f32[64,64]{1,0:T(8,128)S(1)}, u32[]{:S(2)}, u32[]{:S(2)}) collective-permute-start(f32[64,64]{1,0:T(8,128)S(1)} %add.105), channel_id=1, source_target_pairs={{0,2},{1,3},{2,0},{3,1},{4,6},{5,7},{6,4},{7,5},{8,10},{9,11},{10,... | collective-permute-start | bytes 49160 | tf_op jit(solution)/shard_map/ppermute | solution.py:26
  243.1 9.1 %collective-permute-start.38 = (f32[64,64]{1,0:T(8,128)S(1)}, f32[64,64]{1,0:T(8,128)S(1)}, u32[]{:S(2)}, u32[]{:S(2)}) collective-permute-start(f32[64,64]{1,0:T(8,128)S(1)} %add.106), channel_id=1, source_target_pairs={{0,4},{1,5},{2,6},{3,7},{4,0},{5,1},{6,2},{7,3},{8,12},{9,13},{10,... | collective-permute-start | bytes 49160 | tf_op jit(solution)/shard_map/ppermute | solution.py:26
  252.3 13.4 %collective-permute-start.39 = (f32[64,64]{1,0:T(8,128)S(1)}, f32[64,64]{1,0:T(8,128)S(1)}, u32[]{:S(2)}, u32[]{:S(2)}) collective-permute-start(f32[64,64]{1,0:T(8,128)S(1)} %add.107), channel_id=1, source_target_pairs={{0,8},{1,9},{2,10},{3,11},{4,12},{5,13},{6,14},{7,15},{8,0},{9,1},... | collective-permute-start | bytes 49160 | tf_op jit(solution)/shard_map/ppermute | solution.py:26
  265.7 12.5 %collective-permute-start.40 = (f32[64,64]{1,0:T(8,128)S(1)}, f32[64,64]{1,0:T(8,128)S(1)}, u32[]{:S(2)}, u32[]{:S(2)}) collective-permute-start(f32[64,64]{1,0:T(8,128)S(1)} %add.108), channel_id=1, source_target_pairs={{0,16},{16,0},{32,48},{48,32},{64,80},{80,64},{96,112},{112,96},{1... | collective-permute-start | bytes 49160 | tf_op jit(solution)/shard_map/ppermute | solution.py:26
  278.1 4.6 %collective-permute-start.41 = (f32[64,64]{1,0:T(8,128)S(1)}, f32[64,64]{1,0:T(8,128)S(1)}, u32[]{:S(2)}, u32[]{:S(2)}) collective-permute-start(f32[64,64]{1,0:T(8,128)S(1)} %add.109), channel_id=1, source_target_pairs={{0,32},{16,48},{32,0},{48,16},{64,96},{80,112},{96,64},{112,80},{1... | collective-permute-start | bytes 49160 | tf_op jit(solution)/shard_map/ppermute | solution.py:26
  282.8 6.2 %collective-permute-start.42 = (f32[64,64]{1,0:T(8,128)S(1)}, f32[64,64]{1,0:T(8,128)S(1)}, u32[]{:S(2)}, u32[]{:S(2)}) collective-permute-start(f32[64,64]{1,0:T(8,128)S(1)} %add.110), channel_id=1, source_target_pairs={{0,64},{16,80},{32,96},{48,112},{64,0},{80,16},{96,32},{112,48},{1... | collective-permute-start | bytes 49160 | tf_op jit(solution)/shard_map/ppermute | solution.py:26
  289.0 4.6 %collective-permute-start.43 = (f32[64,64]{1,0:T(8,128)S(1)}, f32[64,64]{1,0:T(8,128)S(1)}, u32[]{:S(2)}, u32[]{:S(2)}) collective-permute-start(f32[64,64]{1,0:T(8,128)S(1)} %add.111), channel_id=1, source_target_pairs={{0,128},{16,144},{32,160},{48,176},{64,192},{80,208},{96,224},{112... | collective-permute-start | bytes 49160 | tf_op jit(solution)/shard_map/ppermute | solution.py:26
  293.6 6.2 %collective-permute-start.44 = (f32[64,64]{1,0:T(8,128)S(1)}, f32[64,64]{1,0:T(8,128)S(1)}, u32[]{:S(2)}, u32[]{:S(2)}) collective-permute-start(f32[64,64]{1,0:T(8,128)S(1)} %add.112), channel_id=1, source_target_pairs={{0,256},{16,272},{32,288},{48,304},{64,320},{80,336},{96,352},{112... | collective-permute-start | bytes 49160 | tf_op jit(solution)/shard_map/ppermute | solution.py:26
  (39 other events, 37.1 us)

commit v8 on v1

--- a/solution.py
+++ b/solution.py
@@ -47,11 +47,9 @@
 
     first_vecs = step_apply(start_vecs)
 
-    def advance(step_index, state_pair):
-        older_vec, newer_vec = state_pair
-        return (newer_vec, 2.0 * step_apply(newer_vec) - older_vec)
-
-    previous, current = lax.fori_loop(0, DEG - 1, advance, (start_vecs, first_vecs))
+    previous, current = start_vecs, first_vecs
+    for step_index in range(DEG - 1):
+        previous, current = current, 2.0 * step_apply(current) - previous
     total_rows = current.shape[0] * current.shape[2] * lax.axis_size("px") * lax.axis_size("py")
     partial_gram = jnp.einsum("rkj,rlj->kl", current, current, precision=lax.Precision.HIGHEST)
     raw_gram = butterfly_sum(butterfly_sum(partial_gram, "py"), "px")

time: 288 us -> 298 us (1.035)
  matrix products: 38.7 us -> 44.1 us
  waiting for transfers between devices: 31.8 us -> 35.2 us
    while x48 -> x0, local copies, waits for them, and re-layouts: 9.86 us -> none
    gather x9, local copies, waits for them, and re-layouts: 7.68 us -> 15.3 us  [operator_apply(): gathered = rounded[local_cols]]
    gather x9, local copies, waits for them, and re-layouts: 5.38 us -> 10.9 us  [operator_apply(): received[halo_slot]]
    ppermute x36, starting transfers between devices: 140 us -> 143 us  [from_behind(): return lax.ppermute(value, axis, pairs)]
    dot_general x9, matrix products: 16 us -> 19.2 us  [operator_apply(): jnp.einsum('rkj,rij->rki', received[halo_slot], halo_tiles, preferred_ele...]
  transfers between devices with their start and end apart: 45 -> 45, of which waited for: 9 -> 10; matrix products, arithmetic and copies ran while one was open for 11% -> 9% of each run, Pallas kernels for 0% -> 0%
where the time goes in v8:
time: 298 us; the launch traced here: 294 us
  starting transfers between devices  176 us (59%)
  matrix products  44.1 us (15%)
  waiting for transfers between devices  35.2 us (12%)
  local copies, waits for them, and re-layouts  32.6 us (11%)
  other arithmetic  4.5 us (2%)
    ppermute x36, starting transfers between devices, from_behind(): return lax.ppermute(value, axis, pairs)  143 us
    ppermute x9, waiting for transfers between devices, butterfly_sum(): value = value + lax.ppermute(value, axis, pairs)  33.6 us
    ppermute x9, starting transfers between devices, butterfly_sum(): value = value + lax.ppermute(value, axis, pairs)  32.4 us
    dot_general x9, matrix products, operator_apply(): jnp.einsum('rtkj,rtij->rki', gathered, local_tiles, preferred_element_typ...  24.3 us
    dot_general x9, matrix products, operator_apply(): jnp.einsum('rkj,rij->rki', received[halo_slot], halo_tiles, preferred_ele...  19.2 us
    gather x9, local copies, waits for them, and re-layouts, operator_apply(): gathered = rounded[local_cols]  15.3 us
    gather x9, local copies, waits for them, and re-layouts, operator_apply(): received[halo_slot]  10.9 us
  transfers between devices with their start and end apart: 45, of which 10 were waited for; matrix products, arithmetic and copies ran while one was open for 9% of the time, Pallas kernels for 0%

profile of v8, /device:TPU:1, one launch (start us, length us, event | category | flops | bytes accessed | tf_op | source)
XLA Modules:
  0.0 293.7 jit_solution(7858088929634347542)
XLA Ops:
  3.4 11.9 %collective-permute-start.3 = (bf16[2,64,128]{2,1,0:T(8,128)(2,1)S(1)}, bf16[2,64,128]{2,1,0:T(8,128)(2,1)S(1)}, u32[]{:S(2)}, u32[]{:S(2)}) collective-permute-start(bf16[2,64,128]{2,1,0:T(8,128)(2,1)S(1)} %get-tuple-element.37), channel_id=1, source_target_pairs={{0,15},{1,0},{2,1},{3,2},{4,3},{5,4},{6,5},{7,6},{8,7},{9,8},{10,9... | collective-permute-start | bytes 98312 | tf_op jit(solution)/shard_map/ppermute | solution.py:12
  15.3 1.9 collective-permute-start.2
  17.2 2.9 collective-permute-start.1
  20.1 3.0 %collective-permute-start = (bf16[2,64,128]{2,1,0:T(8,128)(2,1)S(1)}, bf16[2,64,128]{2,1,0:T(8,128)(2,1)S(1)}, u32[]{:S(2)}, u32[]{:S(2)}) collective-permute-start(bf16[2,64,128]{2,1,0:T(8,128)(2,1)S(1)} %get-tuple-element.34), channel_id=1, source_target_pairs={{0,16},{16,32},{32,48},{48,64},{64,80},{80,96},{96,112},{112,128},... | collective-permute-start | bytes 98312 | tf_op jit(solution)/shard_map/ppermute | solution.py:12
  25.7 2.1 convolution_bitcast_fusion.8
  29.2 2.2 fusion.26
  33.7 4.9 %collective-permute-start.7 = (bf16[2,64,128]{2,1,0:T(8,128)(2,1)S(1)}, bf16[2,64,128]{2,1,0:T(8,128)(2,1)S(1)}, u32[]{:S(2)}, u32[]{:S(2)}) collective-permute-start(bf16[2,64,128]{2,1,0:T(8,128)(2,1)S(1)} %get-tuple-element.33), channel_id=1, source_target_pairs={{0,15},{1,0},{2,1},{3,2},{4,3},{5,4},{6,5},{7,6},{8,7},{9,8},{10,9... | collective-permute-start | bytes 98312 | tf_op jit(solution)/shard_map/ppermute | solution.py:12
  40.5 7.0 %collective-permute-start.5 = (bf16[2,64,128]{2,1,0:T(8,128)(2,1)S(1)}, bf16[2,64,128]{2,1,0:T(8,128)(2,1)S(1)}, u32[]{:S(2)}, u32[]{:S(2)}) collective-permute-start(bf16[2,64,128]{2,1,0:T(8,128)(2,1)S(1)} %get-tuple-element.32), channel_id=1, source_target_pairs={{0,496},{16,0},{32,16},{48,32},{64,48},{80,64},{96,80},{112,96},{1... | collective-permute-start | bytes 98312 | tf_op jit(solution)/shard_map/ppermute | solution.py:12
  49.5 2.0 convolution_bitcast_fusion.7
  54.4 2.4 fusion.27
  59.1 4.6 %collective-permute-start.11 = (bf16[2,64,128]{2,1,0:T(8,128)(2,1)S(1)}, bf16[2,64,128]{2,1,0:T(8,128)(2,1)S(1)}, u32[]{:S(2)}, u32[]{:S(2)}) collective-permute-start(bf16[2,64,128]{2,1,0:T(8,128)(2,1)S(1)} %get-tuple-element.29), channel_id=1, source_target_pairs={{0,15},{1,0},{2,1},{3,2},{4,3},{5,4},{6,5},{7,6},{8,7},{9,8},{10,9... | collective-permute-start | bytes 98312 | tf_op jit(solution)/shard_map/ppermute | solution.py:12
  65.6 8.1 %collective-permute-start.9 = (bf16[2,64,128]{2,1,0:T(8,128)(2,1)S(1)}, bf16[2,64,128]{2,1,0:T(8,128)(2,1)S(1)}, u32[]{:S(2)}, u32[]{:S(2)}) collective-permute-start(bf16[2,64,128]{2,1,0:T(8,128)(2,1)S(1)} %get-tuple-element.28), channel_id=1, source_target_pairs={{0,496},{16,0},{32,16},{48,32},{64,48},{80,64},{96,80},{112,96},{1... | collective-permute-start | bytes 98312 | tf_op jit(solution)/shard_map/ppermute | solution.py:12
  73.7 1.9 collective-permute-start.8
  75.6 2.9 convolution_bitcast_fusion.6
  83.9 4.8 %collective-permute-start.15 = (bf16[2,64,128]{2,1,0:T(8,128)(2,1)S(1)}, bf16[2,64,128]{2,1,0:T(8,128)(2,1)S(1)}, u32[]{:S(2)}, u32[]{:S(2)}) collective-permute-start(bf16[2,64,128]{2,1,0:T(8,128)(2,1)S(1)} %get-tuple-element.25), channel_id=1, source_target_pairs={{0,15},{1,0},{2,1},{3,2},{4,3},{5,4},{6,5},{7,6},{8,7},{9,8},{10,9... | collective-permute-start | bytes 98312 | tf_op jit(solution)/shard_map/ppermute | solution.py:12
  88.7 1.9 collective-permute-start.14
  90.7 5.9 %collective-permute-start.13 = (bf16[2,64,128]{2,1,0:T(8,128)(2,1)S(1)}, bf16[2,64,128]{2,1,0:T(8,128)(2,1)S(1)}, u32[]{:S(2)}, u32[]{:S(2)}) collective-permute-start(bf16[2,64,128]{2,1,0:T(8,128)(2,1)S(1)} %get-tuple-element.24), channel_id=1, source_target_pairs={{0,496},{16,0},{32,16},{48,32},{64,48},{80,64},{96,80},{112,96},{1... | collective-permute-start | bytes 98312 | tf_op jit(solution)/shard_map/ppermute | solution.py:12
  98.5 2.8 convolution_bitcast_fusion.5
  102.7 2.5 fusion.29
  107.6 4.8 %collective-permute-start.19 = (bf16[2,64,128]{2,1,0:T(8,128)(2,1)S(1)}, bf16[2,64,128]{2,1,0:T(8,128)(2,1)S(1)}, u32[]{:S(2)}, u32[]{:S(2)}) collective-permute-start(bf16[2,64,128]{2,1,0:T(8,128)(2,1)S(1)} %get-tuple-element.21), channel_id=1, source_target_pairs={{0,15},{1,0},{2,1},{3,2},{4,3},{5,4},{6,5},{7,6},{8,7},{9,8},{10,9... | collective-permute-start | bytes 98312 | tf_op jit(solution)/shard_map/ppermute | solution.py:12
  114.3 6.7 %collective-permute-start.17 = (bf16[2,64,128]{2,1,0:T(8,128)(2,1)S(1)}, bf16[2,64,128]{2,1,0:T(8,128)(2,1)S(1)}, u32[]{:S(2)}, u32[]{:S(2)}) collective-permute-start(bf16[2,64,128]{2,1,0:T(8,128)(2,1)S(1)} %get-tuple-element.20), channel_id=1, source_target_pairs={{0,496},{16,0},{32,16},{48,32},{64,48},{80,64},{96,80},{112,96},{1... | collective-permute-start | bytes 98312 | tf_op jit(solution)/shard_map/ppermute | solution.py:12
  123.0 2.9 convolution_bitcast_fusion.4
  127.2 2.4 fusion.30
  131.8 4.9 %collective-permute-start.23 = (bf16[2,64,128]{2,1,0:T(8,128)(2,1)S(1)}, bf16[2,64,128]{2,1,0:T(8,128)(2,1)S(1)}, u32[]{:S(2)}, u32[]{:S(2)}) collective-permute-start(bf16[2,64,128]{2,1,0:T(8,128)(2,1)S(1)} %get-tuple-element.17), channel_id=1, source_target_pairs={{0,15},{1,0},{2,1},{3,2},{4,3},{5,4},{6,5},{7,6},{8,7},{9,8},{10,9... | collective-permute-start | bytes 98312 | tf_op jit(solution)/shard_map/ppermute | solution.py:12
  138.6 6.7 %collective-permute-start.21 = (bf16[2,64,128]{2,1,0:T(8,128)(2,1)S(1)}, bf16[2,64,128]{2,1,0:T(8,128)(2,1)S(1)}, u32[]{:S(2)}, u32[]{:S(2)}) collective-permute-start(bf16[2,64,128]{2,1,0:T(8,128)(2,1)S(1)} %get-tuple-element.16), channel_id=1, source_target_pairs={{0,496},{16,0},{32,16},{48,32},{64,48},{80,64},{96,80},{112,96},{1... | collective-permute-start | bytes 98312 | tf_op jit(solution)/shard_map/ppermute | solution.py:12
  147.3 2.9 convolution_bitcast_fusion.3
  151.5 2.4 fusion.31
  156.2 4.8 %collective-permute-start.27 = (bf16[2,64,128]{2,1,0:T(8,128)(2,1)S(1)}, bf16[2,64,128]{2,1,0:T(8,128)(2,1)S(1)}, u32[]{:S(2)}, u32[]{:S(2)}) collective-permute-start(bf16[2,64,128]{2,1,0:T(8,128)(2,1)S(1)} %get-tuple-element.13), channel_id=1, source_target_pairs={{0,15},{1,0},{2,1},{3,2},{4,3},{5,4},{6,5},{7,6},{8,7},{9,8},{10,9... | collective-permute-start | bytes 98312 | tf_op jit(solution)/shard_map/ppermute | solution.py:12
  163.0 6.6 %collective-permute-start.25 = (bf16[2,64,128]{2,1,0:T(8,128)(2,1)S(1)}, bf16[2,64,128]{2,1,0:T(8,128)(2,1)S(1)}, u32[]{:S(2)}, u32[]{:S(2)}) collective-permute-start(bf16[2,64,128]{2,1,0:T(8,128)(2,1)S(1)} %get-tuple-element.12), channel_id=1, source_target_pairs={{0,496},{16,0},{32,16},{48,32},{64,48},{80,64},{96,80},{112,96},{1... | collective-permute-start | bytes 98312 | tf_op jit(solution)/shard_map/ppermute | solution.py:12
  171.5 2.9 convolution_bitcast_fusion.2
  175.8 2.4 fusion.32
  180.4 4.9 %collective-permute-start.31 = (bf16[2,64,128]{2,1,0:T(8,128)(2,1)S(1)}, bf16[2,64,128]{2,1,0:T(8,128)(2,1)S(1)}, u32[]{:S(2)}, u32[]{:S(2)}) collective-permute-start(bf16[2,64,128]{2,1,0:T(8,128)(2,1)S(1)} %get-tuple-element.9), channel_id=1, source_target_pairs={{0,15},{1,0},{2,1},{3,2},{4,3},{5,4},{6,5},{7,6},{8,7},{9,8},{10,9... | collective-permute-start | bytes 98312 | tf_op jit(solution)/shard_map/ppermute | solution.py:12
  187.2 6.7 %collective-permute-start.29 = (bf16[2,64,128]{2,1,0:T(8,128)(2,1)S(1)}, bf16[2,64,128]{2,1,0:T(8,128)(2,1)S(1)}, u32[]{:S(2)}, u32[]{:S(2)}) collective-permute-start(bf16[2,64,128]{2,1,0:T(8,128)(2,1)S(1)} %get-tuple-element.8), channel_id=1, source_target_pairs={{0,496},{16,0},{32,16},{48,32},{64,48},{80,64},{96,80},{112,96},{1... | collective-permute-start | bytes 98312 | tf_op jit(solution)/shard_map/ppermute | solution.py:12
  195.9 2.9 convolution_bitcast_fusion.1
  204.0 4.8 %collective-permute-start.35 = (bf16[2,64,128]{2,1,0:T(8,128)(2,1)S(1)}, bf16[2,64,128]{2,1,0:T(8,128)(2,1)S(1)}, u32[]{:S(2)}, u32[]{:S(2)}) collective-permute-start(bf16[2,64,128]{2,1,0:T(8,128)(2,1)S(1)} %get-tuple-element.5), channel_id=1, source_target_pairs={{0,15},{1,0},{2,1},{3,2},{4,3},{5,4},{6,5},{7,6},{8,7},{9,8},{10,9... | collective-permute-start | bytes 98312 | tf_op jit(solution)/shard_map/ppermute | solution.py:12
  210.8 6.7 %collective-permute-start.33 = (bf16[2,64,128]{2,1,0:T(8,128)(2,1)S(1)}, bf16[2,64,128]{2,1,0:T(8,128)(2,1)S(1)}, u32[]{:S(2)}, u32[]{:S(2)}) collective-permute-start(bf16[2,64,128]{2,1,0:T(8,128)(2,1)S(1)} %get-tuple-element.4), channel_id=1, source_target_pairs={{0,496},{16,0},{32,16},{48,32},{64,48},{80,64},{96,80},{112,96},{1... | collective-permute-start | bytes 98312 | tf_op jit(solution)/shard_map/ppermute | solution.py:12
  219.4 2.8 convolution_bitcast_fusion
  227.1 2.7 collective-permute-done.36
  231.7 3.7 %collective-permute-done.37 = f32[64,64]{1,0:T(8,128)S(1)} collective-permute-done((f32[64,64]{1,0:T(8,128)S(1)}, f32[64,64]{1,0:T(8,128)S(1)}, u32[]{:S(2)}, u32[]{:S(2)}) %collective-permute-start.37) | collective-permute-done | bytes 16416 | tf_op jit(solution)/shard_map/ppermute | solution.py:20
  235.5 3.4 %collective-permute-start.38 = (f32[64,64]{1,0:T(8,128)S(1)}, f32[64,64]{1,0:T(8,128)S(1)}, u32[]{:S(2)}, u32[]{:S(2)}) collective-permute-start(f32[64,64]{1,0:T(8,128)S(1)} %add.122), channel_id=1, source_target_pairs={{0,4},{1,5},{2,6},{3,7},{4,0},{5,1},{6,2},{7,3},{8,12},{9,13},{10,... | collective-permute-start | bytes 49160 | tf_op jit(solution)/shard_map/ppermute | solution.py:20
  238.9 5.7 %collective-permute-done.38 = f32[64,64]{1,0:T(8,128)S(1)} collective-permute-done((f32[64,64]{1,0:T(8,128)S(1)}, f32[64,64]{1,0:T(8,128)S(1)}, u32[]{:S(2)}, u32[]{:S(2)}) %collective-permute-start.38) | collective-permute-done | bytes 16416 | tf_op jit(solution)/shard_map/ppermute | solution.py:20
  244.6 6.6 %collective-permute-start.39 = (f32[64,64]{1,0:T(8,128)S(1)}, f32[64,64]{1,0:T(8,128)S(1)}, u32[]{:S(2)}, u32[]{:S(2)}) collective-permute-start(f32[64,64]{1,0:T(8,128)S(1)} %add.123), channel_id=1, source_target_pairs={{0,8},{1,9},{2,10},{3,11},{4,12},{5,13},{6,14},{7,15},{8,0},{9,1},... | collective-permute-start | bytes 49160 | tf_op jit(solution)/shard_map/ppermute | solution.py:20
  251.2 6.7 %collective-permute-done.39 = f32[64,64]{1,0:T(8,128)S(1)} collective-permute-done((f32[64,64]{1,0:T(8,128)S(1)}, f32[64,64]{1,0:T(8,128)S(1)}, u32[]{:S(2)}, u32[]{:S(2)}) %collective-permute-start.39) | collective-permute-done | bytes 16416 | tf_op jit(solution)/shard_map/ppermute | solution.py:20
  257.9 10.8 %collective-permute-start.40 = (f32[64,64]{1,0:T(8,128)S(1)}, f32[64,64]{1,0:T(8,128)S(1)}, u32[]{:S(2)}, u32[]{:S(2)}) collective-permute-start(f32[64,64]{1,0:T(8,128)S(1)} %add.124), channel_id=1, source_target_pairs={{0,16},{16,0},{32,48},{48,32},{64,80},{80,64},{96,112},{112,96},{1... | collective-permute-start | bytes 49160 | tf_op jit(solution)/shard_map/ppermute | solution.py:20
  271.5 2.7 collective-permute-done.41
  276.2 4.2 %collective-permute-done.42 = f32[64,64]{1,0:T(8,128)S(1)} collective-permute-done((f32[64,64]{1,0:T(8,128)S(1)}, f32[64,64]{1,0:T(8,128)S(1)}, u32[]{:S(2)}, u32[]{:S(2)}) %collective-permute-start.42) | collective-permute-done | bytes 16416 | tf_op jit(solution)/shard_map/ppermute | solution.py:20
  282.4 2.7 collective-permute-done.43
  287.0 4.2 %collective-permute-done.44 = f32[64,64]{1,0:T(8,128)S(1)} collective-permute-done((f32[64,64]{1,0:T(8,128)S(1)}, f32[64,64]{1,0:T(8,128)S(1)}, u32[]{:S(2)}, u32[]{:S(2)}) %collective-permute-start.44) | collective-permute-done | bytes 16416 | tf_op jit(solution)/shard_map/ppermute | solution.py:20
  (143 shorter events, 83.4 us)
Async XLA Ops:
  0.6 25.1 %copy-start = (bf16[16,4,128,128]{3,2,1,0:T(8,128)(2,1)S(1)}, bf16[16,4,128,128]{3,2,1,0:T(8,128)(2,1)}, u32[]{:S(2)}) copy-start(bf16[16,4,128,128]{3,2,1,0:T(8,128)(2,1)} %param.7) | copy-start | bytes 6291460
  0.6 25.1 %copy-start.5 = (s32[16]{0:T(128)S(1)}, s32[16]{0:T(128)}, u32[]{:S(2)}) copy-start(s32[16]{0:T(128)} %param.10) | copy-start | bytes 196
  3.4 24.5 %collective-permute-start.3 = (bf16[2,64,128]{2,1,0:T(8,128)(2,1)S(1)}, bf16[2,64,128]{2,1,0:T(8,128)(2,1)S(1)}, u32[]{:S(2)}, u32[]{:S(2)}) collective-permute-start(bf16[2,64,128]{2,1,0:T(8,128)(2,1)S(1)} %get-tuple-element.37), channel_id=1, source_target_pairs={{0,15},{1,0},{2,1},{3,2},{4,3},{5,4},{6,5},{7,6},{8,7},{9,8},{10,9... | collective-permute-start | bytes 98312 | tf_op jit(solution)/shard_map/ppermute | solution.py:12
  15.3 12.6 %collective-permute-start.2 = (bf16[2,64,128]{2,1,0:T(8,128)(2,1)S(1)}, bf16[2,64,128]{2,1,0:T(8,128)(2,1)S(1)}, u32[]{:S(2)}, u32[]{:S(2)}) collective-permute-start(bf16[2,64,128]{2,1,0:T(8,128)(2,1)S(1)} %get-tuple-element.35), channel_id=1, source_target_pairs={{0,1},{1,2},{2,3},{3,4},{4,5},{5,6},{6,7},{7,8},{8,9},{9,10},{10,1... | collective-permute-start | bytes 98312 | tf_op jit(solution)/shard_map/ppermute | solution.py:12
  17.2 10.6 %collective-permute-start.1 = (bf16[2,64,128]{2,1,0:T(8,128)(2,1)S(1)}, bf16[2,64,128]{2,1,0:T(8,128)(2,1)S(1)}, u32[]{:S(2)}, u32[]{:S(2)}) collective-permute-start(bf16[2,64,128]{2,1,0:T(8,128)(2,1)S(1)} %get-tuple-element.36), channel_id=1, source_target_pairs={{0,496},{16,0},{32,16},{48,32},{64,48},{80,64},{96,80},{112,96},{1... | collective-permute-start | bytes 98312 | tf_op jit(solution)/shard_map/ppermute | solution.py:12
  20.1 7.8 %collective-permute-start = (bf16[2,64,128]{2,1,0:T(8,128)(2,1)S(1)}, bf16[2,64,128]{2,1,0:T(8,128)(2,1)S(1)}, u32[]{:S(2)}, u32[]{:S(2)}) collective-permute-start(bf16[2,64,128]{2,1,0:T(8,128)(2,1)S(1)} %get-tuple-element.34), channel_id=1, source_target_pairs={{0,16},{16,32},{32,48},{48,64},{64,80},{80,96},{96,112},{112,128},... | collective-permute-start | bytes 98312 | tf_op jit(solution)/shard_map/ppermute | solution.py:12
  33.7 17.8 %collective-permute-start.7 = (bf16[2,64,128]{2,1,0:T(8,128)(2,1)S(1)}, bf16[2,64,128]{2,1,0:T(8,128)(2,1)S(1)}, u32[]{:S(2)}, u32[]{:S(2)}) collective-permute-start(bf16[2,64,128]{2,1,0:T(8,128)(2,1)S(1)} %get-tuple-element.33), channel_id=1, source_target_pairs={{0,15},{1,0},{2,1},{3,2},{4,3},{5,4},{6,5},{7,6},{8,7},{9,8},{10,9... | collective-permute-start | bytes 98312 | tf_op jit(solution)/shard_map/ppermute | solution.py:12
  38.6 13.0 %collective-permute-start.6 = (bf16[2,64,128]{2,1,0:T(8,128)(2,1)S(1)}, bf16[2,64,128]{2,1,0:T(8,128)(2,1)S(1)}, u32[]{:S(2)}, u32[]{:S(2)}) collective-permute-start(bf16[2,64,128]{2,1,0:T(8,128)(2,1)S(1)} %get-tuple-element.31), channel_id=1, source_target_pairs={{0,1},{1,2},{2,3},{3,4},{4,5},{5,6},{6,7},{7,8},{8,9},{9,10},{10,1... | collective-permute-start | bytes 98312 | tf_op jit(solution)/shard_map/ppermute | solution.py:12
  40.5 11.0 %collective-permute-start.5 = (bf16[2,64,128]{2,1,0:T(8,128)(2,1)S(1)}, bf16[2,64,128]{2,1,0:T(8,128)(2,1)S(1)}, u32[]{:S(2)}, u32[]{:S(2)}) collective-permute-start(bf16[2,64,128]{2,1,0:T(8,128)(2,1)S(1)} %get-tuple-element.32), channel_id=1, source_target_pairs={{0,496},{16,0},{32,16},{48,32},{64,48},{80,64},{96,80},{112,96},{1... | collective-permute-start | bytes 98312 | tf_op jit(solution)/shard_map/ppermute | solution.py:12
  47.6 5.5 %collective-permute-start.4 = (bf16[2,64,128]{2,1,0:T(8,128)(2,1)S(1)}, bf16[2,64,128]{2,1,0:T(8,128)(2,1)S(1)}, u32[]{:S(2)}, u32[]{:S(2)}) collective-permute-start(bf16[2,64,128]{2,1,0:T(8,128)(2,1)S(1)} %get-tuple-element.30), channel_id=1, source_target_pairs={{0,16},{16,32},{32,48},{48,64},{64,80},{80,96},{96,112},{112,128},... | collective-permute-start | bytes 98312 | tf_op jit(solution)/shard_map/ppermute | solution.py:12
  59.1 19.4 %collective-permute-start.11 = (bf16[2,64,128]{2,1,0:T(8,128)(2,1)S(1)}, bf16[2,64,128]{2,1,0:T(8,128)(2,1)S(1)}, u32[]{:S(2)}, u32[]{:S(2)}) collective-permute-start(bf16[2,64,128]{2,1,0:T(8,128)(2,1)S(1)} %get-tuple-element.29), channel_id=1, source_target_pairs={{0,15},{1,0},{2,1},{3,2},{4,3},{5,4},{6,5},{7,6},{8,7},{9,8},{10,9... | collective-permute-start | bytes 98312 | tf_op jit(solution)/shard_map/ppermute | solution.py:12
  63.6 14.9 %collective-permute-start.10 = (bf16[2,64,128]{2,1,0:T(8,128)(2,1)S(1)}, bf16[2,64,128]{2,1,0:T(8,128)(2,1)S(1)}, u32[]{:S(2)}, u32[]{:S(2)}) collective-permute-start(bf16[2,64,128]{2,1,0:T(8,128)(2,1)S(1)} %get-tuple-element.27), channel_id=1, source_target_pairs={{0,1},{1,2},{2,3},{3,4},{4,5},{5,6},{6,7},{7,8},{8,9},{9,10},{10,1... | collective-permute-start | bytes 98312 | tf_op jit(solution)/shard_map/ppermute | solution.py:12
  65.6 12.9 %collective-permute-start.9 = (bf16[2,64,128]{2,1,0:T(8,128)(2,1)S(1)}, bf16[2,64,128]{2,1,0:T(8,128)(2,1)S(1)}, u32[]{:S(2)}, u32[]{:S(2)}) collective-permute-start(bf16[2,64,128]{2,1,0:T(8,128)(2,1)S(1)} %get-tuple-element.28), channel_id=1, source_target_pairs={{0,496},{16,0},{32,16},{48,32},{64,48},{80,64},{96,80},{112,96},{1... | collective-permute-start | bytes 98312 | tf_op jit(solution)/shard_map/ppermute | solution.py:12
  73.7 4.8 %collective-permute-start.8 = (bf16[2,64,128]{2,1,0:T(8,128)(2,1)S(1)}, bf16[2,64,128]{2,1,0:T(8,128)(2,1)S(1)}, u32[]{:S(2)}, u32[]{:S(2)}) collective-permute-start(bf16[2,64,128]{2,1,0:T(8,128)(2,1)S(1)} %get-tuple-element.26), channel_id=1, source_target_pairs={{0,16},{16,32},{32,48},{48,64},{64,80},{80,96},{96,112},{112,128},... | collective-permute-start | bytes 98312 | tf_op jit(solution)/shard_map/ppermute | solution.py:12
  83.9 17.5 %collective-permute-start.15 = (bf16[2,64,128]{2,1,0:T(8,128)(2,1)S(1)}, bf16[2,64,128]{2,1,0:T(8,128)(2,1)S(1)}, u32[]{:S(2)}, u32[]{:S(2)}) collective-permute-start(bf16[2,64,128]{2,1,0:T(8,128)(2,1)S(1)} %get-tuple-element.25), channel_id=1, source_target_pairs={{0,15},{1,0},{2,1},{3,2},{4,3},{5,4},{6,5},{7,6},{8,7},{9,8},{10,9... | collective-permute-start | bytes 98312 | tf_op jit(solution)/shard_map/ppermute | solution.py:12
  88.7 12.7 %collective-permute-start.14 = (bf16[2,64,128]{2,1,0:T(8,128)(2,1)S(1)}, bf16[2,64,128]{2,1,0:T(8,128)(2,1)S(1)}, u32[]{:S(2)}, u32[]{:S(2)}) collective-permute-start(bf16[2,64,128]{2,1,0:T(8,128)(2,1)S(1)} %get-tuple-element.23), channel_id=1, source_target_pairs={{0,1},{1,2},{2,3},{3,4},{4,5},{5,6},{6,7},{7,8},{8,9},{9,10},{10,1... | collective-permute-start | bytes 98312 | tf_op jit(solution)/shard_map/ppermute | solution.py:12
  90.7 10.7 %collective-permute-start.13 = (bf16[2,64,128]{2,1,0:T(8,128)(2,1)S(1)}, bf16[2,64,128]{2,1,0:T(8,128)(2,1)S(1)}, u32[]{:S(2)}, u32[]{:S(2)}) collective-permute-start(bf16[2,64,128]{2,1,0:T(8,128)(2,1)S(1)} %get-tuple-element.24), channel_id=1, source_target_pairs={{0,496},{16,0},{32,16},{48,32},{64,48},{80,64},{96,80},{112,96},{1... | collective-permute-start | bytes 98312 | tf_op jit(solution)/shard_map/ppermute | solution.py:12
  96.6 4.8 %collective-permute-start.12 = (bf16[2,64,128]{2,1,0:T(8,128)(2,1)S(1)}, bf16[2,64,128]{2,1,0:T(8,128)(2,1)S(1)}, u32[]{:S(2)}, u32[]{:S(2)}) collective-permute-start(bf16[2,64,128]{2,1,0:T(8,128)(2,1)S(1)} %get-tuple-element.22), channel_id=1, source_target_pairs={{0,16},{16,32},{32,48},{48,64},{64,80},{80,96},{96,112},{112,128},... | collective-permute-start | bytes 98312 | tf_op jit(solution)/shard_map/ppermute | solution.py:12
  107.6 18.3 %collective-permute-start.19 = (bf16[2,64,128]{2,1,0:T(8,128)(2,1)S(1)}, bf16[2,64,128]{2,1,0:T(8,128)(2,1)S(1)}, u32[]{:S(2)}, u32[]{:S(2)}) collective-permute-start(bf16[2,64,128]{2,1,0:T(8,128)(2,1)S(1)} %get-tuple-element.21), channel_id=1, source_target_pairs={{0,15},{1,0},{2,1},{3,2},{4,3},{5,4},{6,5},{7,6},{8,7},{9,8},{10,9... | collective-permute-start | bytes 98312 | tf_op jit(solution)/shard_map/ppermute | solution.py:12
  112.4 13.4 %collective-permute-start.18 = (bf16[2,64,128]{2,1,0:T(8,128)(2,1)S(1)}, bf16[2,64,128]{2,1,0:T(8,128)(2,1)S(1)}, u32[]{:S(2)}, u32[]{:S(2)}) collective-permute-start(bf16[2,64,128]{2,1,0:T(8,128)(2,1)S(1)} %get-tuple-element.19), channel_id=1, source_target_pairs={{0,1},{1,2},{2,3},{3,4},{4,5},{5,6},{6,7},{7,8},{8,9},{9,10},{10,1... | collective-permute-start | bytes 98312 | tf_op jit(solution)/shard_map/ppermute | solution.py:12
  114.3 11.5 %collective-permute-start.17 = (bf16[2,64,128]{2,1,0:T(8,128)(2,1)S(1)}, bf16[2,64,128]{2,1,0:T(8,128)(2,1)S(1)}, u32[]{:S(2)}, u32[]{:S(2)}) collective-permute-start(bf16[2,64,128]{2,1,0:T(8,128)(2,1)S(1)} %get-tuple-element.20), channel_id=1, source_target_pairs={{0,496},{16,0},{32,16},{48,32},{64,48},{80,64},{96,80},{112,96},{1... | collective-permute-start | bytes 98312 | tf_op jit(solution)/shard_map/ppermute | solution.py:12
  121.0 4.8 %collective-permute-start.16 = (bf16[2,64,128]{2,1,0:T(8,128)(2,1)S(1)}, bf16[2,64,128]{2,1,0:T(8,128)(2,1)S(1)}, u32[]{:S(2)}, u32[]{:S(2)}) collective-permute-start(bf16[2,64,128]{2,1,0:T(8,128)(2,1)S(1)} %get-tuple-element.18), channel_id=1, source_target_pairs={{0,16},{16,32},{32,48},{48,64},{64,80},{80,96},{96,112},{112,128},... | collective-permute-start | bytes 98312 | tf_op jit(solution)/shard_map/ppermute | solution.py:12
  131.8 18.3 %collective-permute-start.23 = (bf16[2,64,128]{2,1,0:T(8,128)(2,1)S(1)}, bf16[2,64,128]{2,1,0:T(8,128)(2,1)S(1)}, u32[]{:S(2)}, u32[]{:S(2)}) collective-permute-start(bf16[2,64,128]{2,1,0:T(8,128)(2,1)S(1)} %get-tuple-element.17), channel_id=1, source_target_pairs={{0,15},{1,0},{2,1},{3,2},{4,3},{5,4},{6,5},{7,6},{8,7},{9,8},{10,9... | collective-permute-start | bytes 98312 | tf_op jit(solution)/shard_map/ppermute | solution.py:12
  136.7 13.5 %collective-permute-start.22 = (bf16[2,64,128]{2,1,0:T(8,128)(2,1)S(1)}, bf16[2,64,128]{2,1,0:T(8,128)(2,1)S(1)}, u32[]{:S(2)}, u32[]{:S(2)}) collective-permute-start(bf16[2,64,128]{2,1,0:T(8,128)(2,1)S(1)} %get-tuple-element.15), channel_id=1, source_target_pairs={{0,1},{1,2},{2,3},{3,4},{4,5},{5,6},{6,7},{7,8},{8,9},{9,10},{10,1... | collective-permute-start | bytes 98312 | tf_op jit(solution)/shard_map/ppermute | solution.py:12
  138.6 11.5 %collective-permute-start.21 = (bf16[2,64,128]{2,1,0:T(8,128)(2,1)S(1)}, bf16[2,64,128]{2,1,0:T(8,128)(2,1)S(1)}, u32[]{:S(2)}, u32[]{:S(2)}) collective-permute-start(bf16[2,64,128]{2,1,0:T(8,128)(2,1)S(1)} %get-tuple-element.16), channel_id=1, source_target_pairs={{0,496},{16,0},{32,16},{48,32},{64,48},{80,64},{96,80},{112,96},{1... | collective-permute-start | bytes 98312 | tf_op jit(solution)/shard_map/ppermute | solution.py:12
  145.3 4.9 %collective-permute-start.20 = (bf16[2,64,128]{2,1,0:T(8,128)(2,1)S(1)}, bf16[2,64,128]{2,1,0:T(8,128)(2,1)S(1)}, u32[]{:S(2)}, u32[]{:S(2)}) collective-permute-start(bf16[2,64,128]{2,1,0:T(8,128)(2,1)S(1)} %get-tuple-element.14), channel_id=1, source_target_pairs={{0,16},{16,32},{32,48},{48,64},{64,80},{80,96},{96,112},{112,128},... | collective-permute-start | bytes 98312 | tf_op jit(solution)/shard_map/ppermute | solution.py:12
  156.2 18.3 %collective-permute-start.27 = (bf16[2,64,128]{2,1,0:T(8,128)(2,1)S(1)}, bf16[2,64,128]{2,1,0:T(8,128)(2,1)S(1)}, u32[]{:S(2)}, u32[]{:S(2)}) collective-permute-start(bf16[2,64,128]{2,1,0:T(8,128)(2,1)S(1)} %get-tuple-element.13), channel_id=1, source_target_pairs={{0,15},{1,0},{2,1},{3,2},{4,3},{5,4},{6,5},{7,6},{8,7},{9,8},{10,9... | collective-permute-start | bytes 98312 | tf_op jit(solution)/shard_map/ppermute | solution.py:12
  161.0 13.4 %collective-permute-start.26 = (bf16[2,64,128]{2,1,0:T(8,128)(2,1)S(1)}, bf16[2,64,128]{2,1,0:T(8,128)(2,1)S(1)}, u32[]{:S(2)}, u32[]{:S(2)}) collective-permute-start(bf16[2,64,128]{2,1,0:T(8,128)(2,1)S(1)} %get-tuple-element.11), channel_id=1, source_target_pairs={{0,1},{1,2},{2,3},{3,4},{4,5},{5,6},{6,7},{7,8},{8,9},{9,10},{10,1... | collective-permute-start | bytes 98312 | tf_op jit(solution)/shard_map/ppermute | solution.py:12
  163.0 11.5 %collective-permute-start.25 = (bf16[2,64,128]{2,1,0:T(8,128)(2,1)S(1)}, bf16[2,64,128]{2,1,0:T(8,128)(2,1)S(1)}, u32[]{:S(2)}, u32[]{:S(2)}) collective-permute-start(bf16[2,64,128]{2,1,0:T(8,128)(2,1)S(1)} %get-tuple-element.12), channel_id=1, source_target_pairs={{0,496},{16,0},{32,16},{48,32},{64,48},{80,64},{96,80},{112,96},{1... | collective-permute-start | bytes 98312 | tf_op jit(solution)/shard_map/ppermute | solution.py:12
  169.6 4.9 %collective-permute-start.24 = (bf16[2,64,128]{2,1,0:T(8,128)(2,1)S(1)}, bf16[2,64,128]{2,1,0:T(8,128)(2,1)S(1)}, u32[]{:S(2)}, u32[]{:S(2)}) collective-permute-start(bf16[2,64,128]{2,1,0:T(8,128)(2,1)S(1)} %get-tuple-element.10), channel_id=1, source_target_pairs={{0,16},{16,32},{32,48},{48,64},{64,80},{80,96},{96,112},{112,128},... | collective-permute-start | bytes 98312 | tf_op jit(solution)/shard_map/ppermute | solution.py:12
  180.4 18.3 %collective-permute-start.31 = (bf16[2,64,128]{2,1,0:T(8,128)(2,1)S(1)}, bf16[2,64,128]{2,1,0:T(8,128)(2,1)S(1)}, u32[]{:S(2)}, u32[]{:S(2)}) collective-permute-start(bf16[2,64,128]{2,1,0:T(8,128)(2,1)S(1)} %get-tuple-element.9), channel_id=1, source_target_pairs={{0,15},{1,0},{2,1},{3,2},{4,3},{5,4},{6,5},{7,6},{8,7},{9,8},{10,9... | collective-permute-start | bytes 98312 | tf_op jit(solution)/shard_map/ppermute | solution.py:12
  185.3 13.5 %collective-permute-start.30 = (bf16[2,64,128]{2,1,0:T(8,128)(2,1)S(1)}, bf16[2,64,128]{2,1,0:T(8,128)(2,1)S(1)}, u32[]{:S(2)}, u32[]{:S(2)}) collective-permute-start(bf16[2,64,128]{2,1,0:T(8,128)(2,1)S(1)} %get-tuple-element.7), channel_id=1, source_target_pairs={{0,1},{1,2},{2,3},{3,4},{4,5},{5,6},{6,7},{7,8},{8,9},{9,10},{10,1... | collective-permute-start | bytes 98312 | tf_op jit(solution)/shard_map/ppermute | solution.py:12
  187.2 11.6 %collective-permute-start.29 = (bf16[2,64,128]{2,1,0:T(8,128)(2,1)S(1)}, bf16[2,64,128]{2,1,0:T(8,128)(2,1)S(1)}, u32[]{:S(2)}, u32[]{:S(2)}) collective-permute-start(bf16[2,64,128]{2,1,0:T(8,128)(2,1)S(1)} %get-tuple-element.8), channel_id=1, source_target_pairs={{0,496},{16,0},{32,16},{48,32},{64,48},{80,64},{96,80},{112,96},{1... | collective-permute-start | bytes 98312 | tf_op jit(solution)/shard_map/ppermute | solution.py:12
  193.9 4.9 %collective-permute-start.28 = (bf16[2,64,128]{2,1,0:T(8,128)(2,1)S(1)}, bf16[2,64,128]{2,1,0:T(8,128)(2,1)S(1)}, u32[]{:S(2)}, u32[]{:S(2)}) collective-permute-start(bf16[2,64,128]{2,1,0:T(8,128)(2,1)S(1)} %get-tuple-element.6), channel_id=1, source_target_pairs={{0,16},{16,32},{32,48},{48,64},{64,80},{80,96},{96,112},{112,128},... | collective-permute-start | bytes 98312 | tf_op jit(solution)/shard_map/ppermute | solution.py:12
  195.9 4.3 %copy-start.4 = (f32[16,64,128]{2,1,0:T(8,128)S(1)}, f32[16,64,128]{2,1,0:T(8,128)}, u32[]{:S(2)}) copy-start(f32[16,64,128]{2,1,0:T(8,128)} %get-tuple-element.49) | copy-start | bytes 1572868
  204.0 18.2 %collective-permute-start.35 = (bf16[2,64,128]{2,1,0:T(8,128)(2,1)S(1)}, bf16[2,64,128]{2,1,0:T(8,128)(2,1)S(1)}, u32[]{:S(2)}, u32[]{:S(2)}) collective-permute-start(bf16[2,64,128]{2,1,0:T(8,128)(2,1)S(1)} %get-tuple-element.5), channel_id=1, source_target_pairs={{0,15},{1,0},{2,1},{3,2},{4,3},{5,4},{6,5},{7,6},{8,7},{9,8},{10,9... | collective-permute-start | bytes 98312 | tf_op jit(solution)/shard_map/ppermute | solution.py:12
  208.9 13.4 %collective-permute-start.34 = (bf16[2,64,128]{2,1,0:T(8,128)(2,1)S(1)}, bf16[2,64,128]{2,1,0:T(8,128)(2,1)S(1)}, u32[]{:S(2)}, u32[]{:S(2)}) collective-permute-start(bf16[2,64,128]{2,1,0:T(8,128)(2,1)S(1)} %get-tuple-element.3), channel_id=1, source_target_pairs={{0,1},{1,2},{2,3},{3,4},{4,5},{5,6},{6,7},{7,8},{8,9},{9,10},{10,1... | collective-permute-start | bytes 98312 | tf_op jit(solution)/shard_map/ppermute | solution.py:12
  210.8 11.5 %collective-permute-start.33 = (bf16[2,64,128]{2,1,0:T(8,128)(2,1)S(1)}, bf16[2,64,128]{2,1,0:T(8,128)(2,1)S(1)}, u32[]{:S(2)}, u32[]{:S(2)}) collective-permute-start(bf16[2,64,128]{2,1,0:T(8,128)(2,1)S(1)} %get-tuple-element.4), channel_id=1, source_target_pairs={{0,496},{16,0},{32,16},{48,32},{64,48},{80,64},{96,80},{112,96},{1... | collective-permute-start | bytes 98312 | tf_op jit(solution)/shard_map/ppermute | solution.py:12
  217.5 4.8 %collective-permute-start.32 = (bf16[2,64,128]{2,1,0:T(8,128)(2,1)S(1)}, bf16[2,64,128]{2,1,0:T(8,128)(2,1)S(1)}, u32[]{:S(2)}, u32[]{:S(2)}) collective-permute-start(bf16[2,64,128]{2,1,0:T(8,128)(2,1)S(1)} %get-tuple-element.2), channel_id=1, source_target_pairs={{0,16},{16,32},{32,48},{48,64},{64,80},{80,96},{96,112},{112,128},... | collective-permute-start | bytes 98312 | tf_op jit(solution)/shard_map/ppermute | solution.py:12
  225.1 4.7 %collective-permute-start.36 = (f32[64,64]{1,0:T(8,128)S(1)}, f32[64,64]{1,0:T(8,128)S(1)}, u32[]{:S(2)}, u32[]{:S(2)}) collective-permute-start(f32[64,64]{1,0:T(8,128)S(1)} %convolution_bitcast_fusion.9), channel_id=1, source_target_pairs={{0,1},{1,0},{2,3},{3,2},{4,5},{5,4},{6,7},{7,6},{8,9},{9,8},{10,11... | collective-permute-start | bytes 49160 | tf_op jit(solution)/shard_map/ppermute | solution.py:20
  229.8 5.7 %collective-permute-start.37 = (f32[64,64]{1,0:T(8,128)S(1)}, f32[64,64]{1,0:T(8,128)S(1)}, u32[]{:S(2)}, u32[]{:S(2)}) collective-permute-start(f32[64,64]{1,0:T(8,128)S(1)} %add.121), channel_id=1, source_target_pairs={{0,2},{1,3},{2,0},{3,1},{4,6},{5,7},{6,4},{7,5},{8,10},{9,11},{10,... | collective-permute-start | bytes 49160 | tf_op jit(solution)/shard_map/ppermute | solution.py:20
  235.5 9.1 %collective-permute-start.38 = (f32[64,64]{1,0:T(8,128)S(1)}, f32[64,64]{1,0:T(8,128)S(1)}, u32[]{:S(2)}, u32[]{:S(2)}) collective-permute-start(f32[64,64]{1,0:T(8,128)S(1)} %add.122), channel_id=1, source_target_pairs={{0,4},{1,5},{2,6},{3,7},{4,0},{5,1},{6,2},{7,3},{8,12},{9,13},{10,... | collective-permute-start | bytes 49160 | tf_op jit(solution)/shard_map/ppermute | solution.py:20
  244.6 13.4 %collective-permute-start.39 = (f32[64,64]{1,0:T(8,128)S(1)}, f32[64,64]{1,0:T(8,128)S(1)}, u32[]{:S(2)}, u32[]{:S(2)}) collective-permute-start(f32[64,64]{1,0:T(8,128)S(1)} %add.123), channel_id=1, source_target_pairs={{0,8},{1,9},{2,10},{3,11},{4,12},{5,13},{6,14},{7,15},{8,0},{9,1},... | collective-permute-start | bytes 49160 | tf_op jit(solution)/shard_map/ppermute | solution.py:20
  257.9 11.7 %collective-permute-start.40 = (f32[64,64]{1,0:T(8,128)S(1)}, f32[64,64]{1,0:T(8,128)S(1)}, u32[]{:S(2)}, u32[]{:S(2)}) collective-permute-start(f32[64,64]{1,0:T(8,128)S(1)} %add.124), channel_id=1, source_target_pairs={{0,16},{16,0},{32,48},{48,32},{64,80},{80,64},{96,112},{112,96},{1... | collective-permute-start | bytes 49160 | tf_op jit(solution)/shard_map/ppermute | solution.py:20
  269.6 4.6 %collective-permute-start.41 = (f32[64,64]{1,0:T(8,128)S(1)}, f32[64,64]{1,0:T(8,128)S(1)}, u32[]{:S(2)}, u32[]{:S(2)}) collective-permute-start(f32[64,64]{1,0:T(8,128)S(1)} %add.125), channel_id=1, source_target_pairs={{0,32},{16,48},{32,0},{48,16},{64,96},{80,112},{96,64},{112,80},{1... | collective-permute-start | bytes 49160 | tf_op jit(solution)/shard_map/ppermute | solution.py:20
  274.3 6.2 %collective-permute-start.42 = (f32[64,64]{1,0:T(8,128)S(1)}, f32[64,64]{1,0:T(8,128)S(1)}, u32[]{:S(2)}, u32[]{:S(2)}) collective-permute-start(f32[64,64]{1,0:T(8,128)S(1)} %add.126), channel_id=1, source_target_pairs={{0,64},{16,80},{32,96},{48,112},{64,0},{80,16},{96,32},{112,48},{1... | collective-permute-start | bytes 49160 | tf_op jit(solution)/shard_map/ppermute | solution.py:20
  280.4 4.6 %collective-permute-start.43 = (f32[64,64]{1,0:T(8,128)S(1)}, f32[64,64]{1,0:T(8,128)S(1)}, u32[]{:S(2)}, u32[]{:S(2)}) collective-permute-start(f32[64,64]{1,0:T(8,128)S(1)} %add.127), channel_id=1, source_target_pairs={{0,128},{16,144},{32,160},{48,176},{64,192},{80,208},{96,224},{112... | collective-permute-start | bytes 49160 | tf_op jit(solution)/shard_map/ppermute | solution.py:20
  285.1 6.2 %collective-permute-start.44 = (f32[64,64]{1,0:T(8,128)S(1)}, f32[64,64]{1,0:T(8,128)S(1)}, u32[]{:S(2)}, u32[]{:S(2)}) collective-permute-start(f32[64,64]{1,0:T(8,128)S(1)} %add.128), channel_id=1, source_target_pairs={{0,256},{16,272},{32,288},{48,304},{64,320},{80,336},{96,352},{112... | collective-permute-start | bytes 49160 | tf_op jit(solution)/shard_map/ppermute | solution.py:20
  (3 other events, 12.0 us)

commit v9 on v0

--- a/solution.py
+++ b/solution.py
@@ -10,6 +10,10 @@
     count = lax.axis_size(axis)
     pairs = [(source, (source + steps) % count) for source in range(count)]
     return lax.ppermute(value, axis, pairs)
+
+
+def gathered_sum(value, axis):
+    return jnp.sum(lax.all_gather(value, axis), axis=0)
 
 
 def operator_apply(current, local_tiles, local_cols, halo_tiles, halo_slot, boundary):
@@ -43,11 +47,12 @@
 
     previous, current = lax.fori_loop(0, DEG - 1, advance, (start_vecs, first_vecs))
     total_rows = current.shape[0] * current.shape[2] * lax.axis_size("px") * lax.axis_size("py")
-    squares = lax.psum(jnp.sum(current * current, axis=(0, 2)), ("px", "py"))
+    partial_gram = jnp.einsum("rkj,rlj->kl", current, current, precision=lax.Precision.HIGHEST)
+    raw_gram = gathered_sum(gathered_sum(partial_gram, "py"), "px")
+    squares = jnp.diagonal(raw_gram)
     scales = lax.rsqrt(squares / total_rows + 1e-06)
     filtered = current * scales[None, :, None]
-    partial_gram = jnp.einsum("rkj,rlj->kl", filtered, filtered, precision=lax.Precision.HIGHEST)
-    gram_matrix = lax.psum(partial_gram, ("px", "py")) / total_rows
+    gram_matrix = raw_gram * scales[:, None] * scales[None, :] / total_rows
     return (filtered, gram_matrix)
 
 

time: 421 us -> 279 us (0.66)
  blocking collectives: 204 us -> 58.5 us
    psum x2 -> x0, blocking collectives: 204 us -> none  [the longest x1 105 us: shards(): squares = lax.psum(jnp.sum(current * current, axis=(0, 2)), ('px', 'py'))]
    all_gather x0 -> x2, blocking collectives: none -> 58.5 us  [gathered_sum(): return jnp.sum(lax.all_gather(value, axis), axis=0)]
  transfers between devices with their start and end apart: 36 -> 36, of which waited for: 0 -> 0; matrix products, arithmetic and copies ran while one was open for 8% -> 11% of each run, Pallas kernels for 0% -> 0%
where the time goes in v9:
time: 279 us; the launch traced here: 277 us
  starting transfers between devices  140 us (50%)
  blocking collectives  58.5 us (21%)
  matrix products  38.9 us (14%)
  local copies, waits for them, and re-layouts  34 us (12%)
  other arithmetic  3.31 us (1%)
    ppermute x36, starting transfers between devices, from_behind(): return lax.ppermute(value, axis, pairs)  140 us
    all_gather x2, blocking collectives, gathered_sum(): return jnp.sum(lax.all_gather(value, axis), axis=0)  58.5 us
    dot_general x9, matrix products, operator_apply(): jnp.einsum('rtkj,rtij->rki', gathered, local_tiles, preferred_element_typ...  22.3 us
    dot_general x9, matrix products, operator_apply(): jnp.einsum('rkj,rij->rki', received[halo_slot], halo_tiles, preferred_ele...  16 us
    while x48, local copies, waits for them, and re-layouts  9.86 us
    gather x9, local copies, waits for them, and re-layouts, operator_apply(): gathered = rounded[local_cols]  7.64 us
    gather x9, local copies, waits for them, and re-layouts, operator_apply(): received[halo_slot]  6.05 us
  transfers between devices with their start and end apart: 36, of which 0 were waited for; matrix products, arithmetic and copies ran while one was open for 11% of the time, Pallas kernels for 0%

profile of v9, /device:TPU:1, one launch (start us, length us, event | category | flops | bytes accessed | tf_op | source)
XLA Modules:
  0.0 276.9 jit_solution(5358862406760999810)
XLA Ops:
  3.4 4.5 %collective-permute-start.4 = (bf16[2,64,128]{2,1,0:T(8,128)(2,1)S(1)}, bf16[2,64,128]{2,1,0:T(8,128)(2,1)S(1)}, u32[]{:S(2)}, u32[]{:S(2)}) collective-permute-start(bf16[2,64,128]{2,1,0:T(8,128)(2,1)S(1)} %get-tuple-element.65), channel_id=1, source_target_pairs={{0,16},{16,32},{32,48},{48,64},{64,80},{80,96},{96,112},{112,128},... | collective-permute-start | bytes 98312 | tf_op jit(solution)/shard_map/ppermute | solution.py:12
  7.9 6.2 %collective-permute-start.5 = (bf16[2,64,128]{2,1,0:T(8,128)(2,1)S(1)}, bf16[2,64,128]{2,1,0:T(8,128)(2,1)S(1)}, u32[]{:S(2)}, u32[]{:S(2)}) collective-permute-start(bf16[2,64,128]{2,1,0:T(8,128)(2,1)S(1)} %get-tuple-element.67), channel_id=1, source_target_pairs={{0,496},{16,0},{32,16},{48,32},{64,48},{80,64},{96,80},{112,96},{1... | collective-permute-start | bytes 98312 | tf_op jit(solution)/shard_map/ppermute | solution.py:12
  14.1 1.9 collective-permute-start.6
  16.0 6.9 %collective-permute-start.7 = (bf16[2,64,128]{2,1,0:T(8,128)(2,1)S(1)}, bf16[2,64,128]{2,1,0:T(8,128)(2,1)S(1)}, u32[]{:S(2)}, u32[]{:S(2)}) collective-permute-start(bf16[2,64,128]{2,1,0:T(8,128)(2,1)S(1)} %get-tuple-element.68), channel_id=1, source_target_pairs={{0,15},{1,0},{2,1},{3,2},{4,3},{5,4},{6,5},{7,6},{8,7},{9,8},{10,9... | collective-permute-start | bytes 98312 | tf_op jit(solution)/shard_map/ppermute | solution.py:12
  24.8 2.9 %convolution_bitcast_fusion.1 = f32[16,64,128]{2,1,0:T(8,128)} fusion(bf16[16,4,64,128]{3,2,1,0:T(8,128)(2,1)} %bitcast.57, bf16[16,4,128,128]{3,2,1,0:T(8,128)(2,1)S(1)} %copy-done), kind=kOutput, calls=%fused_computation.19 | convolution fusion | flops 134217728 | bytes 3670016 | tf_op jit(solution)/shard_map/rtkj,rtij->rki/dot_general | solution.py:28
  30.7 184.5 %while.12 = (s32[]{:T(128)}, f32[16,64,128]{2,1,0:T(8,128)}, f32[16,64,128]{2,1,0:T(8,128)S(1)}, s32[16,4]{0,1:T(4,128)S(1)}, bf16[16,4,128,128]{3,2,1,0:T(8,128...) while((s32[]{:T(128)}, f32[16,64,128]{2,1,0:T(8,128)}, ...), condition=%wide.region_1.0_spmd, body=%wide.region_0.0_spmd.sunk | while | flops 168496400 | bytes 23345988 | solution.py:48
  31.6 3.4 %collective-permute-start = (bf16[2,64,128]{2,1,0:T(8,128)(2,1)S(1)}, bf16[2,64,128]{2,1,0:T(8,128)(2,1)S(1)}, u32[]{:S(2)}, u32[]{:S(2)}) collective-permute-start(bf16[2,64,128]{2,1,0:T(8,128)(2,1)S(1)} %get-tuple-element.122), channel_id=1, source_target_pairs={{0,15},{1,0},{2,1},{3,2},{4,3},{5,4},{6,5},{7,6},{8,7},{9,8},{10,9... | collective-permute-start | bytes 98312 | tf_op jit(solution)/shard_map/while/body/eval_jaxpr/ppermute | solution.py:12
  34.9 1.9 collective-permute-start.1
  36.9 6.7 %collective-permute-start.2 = (bf16[2,64,128]{2,1,0:T(8,128)(2,1)S(1)}, bf16[2,64,128]{2,1,0:T(8,128)(2,1)S(1)}, u32[]{:S(2)}, u32[]{:S(2)}) collective-permute-start(bf16[2,64,128]{2,1,0:T(8,128)(2,1)S(1)} %get-tuple-element.124), channel_id=1, source_target_pairs={{0,496},{16,0},{32,16},{48,32},{64,48},{80,64},{96,80},{112,96},{1... | collective-permute-start | bytes 98312 | tf_op jit(solution)/shard_map/while/body/eval_jaxpr/ppermute | solution.py:12
  43.6 1.9 collective-permute-start.3
  46.5 2.4 convolution_bitcast_fusion.4
  53.5 4.8 %collective-permute-start = (bf16[2,64,128]{2,1,0:T(8,128)(2,1)S(1)}, bf16[2,64,128]{2,1,0:T(8,128)(2,1)S(1)}, u32[]{:S(2)}, u32[]{:S(2)}) collective-permute-start(bf16[2,64,128]{2,1,0:T(8,128)(2,1)S(1)} %get-tuple-element.122), channel_id=1, source_target_pairs={{0,15},{1,0},{2,1},{3,2},{4,3},{5,4},{6,5},{7,6},{8,7},{9,8},{10,9... | collective-permute-start | bytes 98312 | tf_op jit(solution)/shard_map/while/body/eval_jaxpr/ppermute | solution.py:12
  58.4 1.9 collective-permute-start.1
  60.3 5.4 %collective-permute-start.2 = (bf16[2,64,128]{2,1,0:T(8,128)(2,1)S(1)}, bf16[2,64,128]{2,1,0:T(8,128)(2,1)S(1)}, u32[]{:S(2)}, u32[]{:S(2)}) collective-permute-start(bf16[2,64,128]{2,1,0:T(8,128)(2,1)S(1)} %get-tuple-element.124), channel_id=1, source_target_pairs={{0,496},{16,0},{32,16},{48,32},{64,48},{80,64},{96,80},{112,96},{1... | collective-permute-start | bytes 98312 | tf_op jit(solution)/shard_map/while/body/eval_jaxpr/ppermute | solution.py:12
  65.7 1.9 collective-permute-start.3
  68.6 2.4 convolution_bitcast_fusion.4
  75.6 4.8 %collective-permute-start = (bf16[2,64,128]{2,1,0:T(8,128)(2,1)S(1)}, bf16[2,64,128]{2,1,0:T(8,128)(2,1)S(1)}, u32[]{:S(2)}, u32[]{:S(2)}) collective-permute-start(bf16[2,64,128]{2,1,0:T(8,128)(2,1)S(1)} %get-tuple-element.122), channel_id=1, source_target_pairs={{0,15},{1,0},{2,1},{3,2},{4,3},{5,4},{6,5},{7,6},{8,7},{9,8},{10,9... | collective-permute-start | bytes 98312 | tf_op jit(solution)/shard_map/while/body/eval_jaxpr/ppermute | solution.py:12
  80.5 1.9 collective-permute-start.1
  82.4 6.7 %collective-permute-start.2 = (bf16[2,64,128]{2,1,0:T(8,128)(2,1)S(1)}, bf16[2,64,128]{2,1,0:T(8,128)(2,1)S(1)}, u32[]{:S(2)}, u32[]{:S(2)}) collective-permute-start(bf16[2,64,128]{2,1,0:T(8,128)(2,1)S(1)} %get-tuple-element.124), channel_id=1, source_target_pairs={{0,496},{16,0},{32,16},{48,32},{64,48},{80,64},{96,80},{112,96},{1... | collective-permute-start | bytes 98312 | tf_op jit(solution)/shard_map/while/body/eval_jaxpr/ppermute | solution.py:12
  89.1 1.9 collective-permute-start.3
  92.0 2.4 convolution_bitcast_fusion.4
  99.0 4.9 %collective-permute-start = (bf16[2,64,128]{2,1,0:T(8,128)(2,1)S(1)}, bf16[2,64,128]{2,1,0:T(8,128)(2,1)S(1)}, u32[]{:S(2)}, u32[]{:S(2)}) collective-permute-start(bf16[2,64,128]{2,1,0:T(8,128)(2,1)S(1)} %get-tuple-element.122), channel_id=1, source_target_pairs={{0,15},{1,0},{2,1},{3,2},{4,3},{5,4},{6,5},{7,6},{8,7},{9,8},{10,9... | collective-permute-start | bytes 98312 | tf_op jit(solution)/shard_map/while/body/eval_jaxpr/ppermute | solution.py:12
  103.9 1.9 collective-permute-start.1
  105.8 6.7 %collective-permute-start.2 = (bf16[2,64,128]{2,1,0:T(8,128)(2,1)S(1)}, bf16[2,64,128]{2,1,0:T(8,128)(2,1)S(1)}, u32[]{:S(2)}, u32[]{:S(2)}) collective-permute-start(bf16[2,64,128]{2,1,0:T(8,128)(2,1)S(1)} %get-tuple-element.124), channel_id=1, source_target_pairs={{0,496},{16,0},{32,16},{48,32},{64,48},{80,64},{96,80},{112,96},{1... | collective-permute-start | bytes 98312 | tf_op jit(solution)/shard_map/while/body/eval_jaxpr/ppermute | solution.py:12
  112.5 1.9 collective-permute-start.3
  115.4 2.4 convolution_bitcast_fusion.4
  122.4 4.9 %collective-permute-start = (bf16[2,64,128]{2,1,0:T(8,128)(2,1)S(1)}, bf16[2,64,128]{2,1,0:T(8,128)(2,1)S(1)}, u32[]{:S(2)}, u32[]{:S(2)}) collective-permute-start(bf16[2,64,128]{2,1,0:T(8,128)(2,1)S(1)} %get-tuple-element.122), channel_id=1, source_target_pairs={{0,15},{1,0},{2,1},{3,2},{4,3},{5,4},{6,5},{7,6},{8,7},{9,8},{10,9... | collective-permute-start | bytes 98312 | tf_op jit(solution)/shard_map/while/body/eval_jaxpr/ppermute | solution.py:12
  127.3 1.9 collective-permute-start.1
  129.2 6.7 %collective-permute-start.2 = (bf16[2,64,128]{2,1,0:T(8,128)(2,1)S(1)}, bf16[2,64,128]{2,1,0:T(8,128)(2,1)S(1)}, u32[]{:S(2)}, u32[]{:S(2)}) collective-permute-start(bf16[2,64,128]{2,1,0:T(8,128)(2,1)S(1)} %get-tuple-element.124), channel_id=1, source_target_pairs={{0,496},{16,0},{32,16},{48,32},{64,48},{80,64},{96,80},{112,96},{1... | collective-permute-start | bytes 98312 | tf_op jit(solution)/shard_map/while/body/eval_jaxpr/ppermute | solution.py:12
  135.9 1.9 collective-permute-start.3
  138.8 2.4 convolution_bitcast_fusion.4
  145.8 4.9 %collective-permute-start = (bf16[2,64,128]{2,1,0:T(8,128)(2,1)S(1)}, bf16[2,64,128]{2,1,0:T(8,128)(2,1)S(1)}, u32[]{:S(2)}, u32[]{:S(2)}) collective-permute-start(bf16[2,64,128]{2,1,0:T(8,128)(2,1)S(1)} %get-tuple-element.122), channel_id=1, source_target_pairs={{0,15},{1,0},{2,1},{3,2},{4,3},{5,4},{6,5},{7,6},{8,7},{9,8},{10,9... | collective-permute-start | bytes 98312 | tf_op jit(solution)/shard_map/while/body/eval_jaxpr/ppermute | solution.py:12
  150.7 1.9 collective-permute-start.1
  152.6 6.7 %collective-permute-start.2 = (bf16[2,64,128]{2,1,0:T(8,128)(2,1)S(1)}, bf16[2,64,128]{2,1,0:T(8,128)(2,1)S(1)}, u32[]{:S(2)}, u32[]{:S(2)}) collective-permute-start(bf16[2,64,128]{2,1,0:T(8,128)(2,1)S(1)} %get-tuple-element.124), channel_id=1, source_target_pairs={{0,496},{16,0},{32,16},{48,32},{64,48},{80,64},{96,80},{112,96},{1... | collective-permute-start | bytes 98312 | tf_op jit(solution)/shard_map/while/body/eval_jaxpr/ppermute | solution.py:12
  159.3 1.9 collective-permute-start.3
  162.2 2.4 convolution_bitcast_fusion.4
  169.3 4.9 %collective-permute-start = (bf16[2,64,128]{2,1,0:T(8,128)(2,1)S(1)}, bf16[2,64,128]{2,1,0:T(8,128)(2,1)S(1)}, u32[]{:S(2)}, u32[]{:S(2)}) collective-permute-start(bf16[2,64,128]{2,1,0:T(8,128)(2,1)S(1)} %get-tuple-element.122), channel_id=1, source_target_pairs={{0,15},{1,0},{2,1},{3,2},{4,3},{5,4},{6,5},{7,6},{8,7},{9,8},{10,9... | collective-permute-start | bytes 98312 | tf_op jit(solution)/shard_map/while/body/eval_jaxpr/ppermute | solution.py:12
  174.1 1.9 collective-permute-start.1
  176.1 6.7 %collective-permute-start.2 = (bf16[2,64,128]{2,1,0:T(8,128)(2,1)S(1)}, bf16[2,64,128]{2,1,0:T(8,128)(2,1)S(1)}, u32[]{:S(2)}, u32[]{:S(2)}) collective-permute-start(bf16[2,64,128]{2,1,0:T(8,128)(2,1)S(1)} %get-tuple-element.124), channel_id=1, source_target_pairs={{0,496},{16,0},{32,16},{48,32},{64,48},{80,64},{96,80},{112,96},{1... | collective-permute-start | bytes 98312 | tf_op jit(solution)/shard_map/while/body/eval_jaxpr/ppermute | solution.py:12
  182.7 1.9 collective-permute-start.3
  185.6 2.4 convolution_bitcast_fusion.4
  192.7 4.9 %collective-permute-start = (bf16[2,64,128]{2,1,0:T(8,128)(2,1)S(1)}, bf16[2,64,128]{2,1,0:T(8,128)(2,1)S(1)}, u32[]{:S(2)}, u32[]{:S(2)}) collective-permute-start(bf16[2,64,128]{2,1,0:T(8,128)(2,1)S(1)} %get-tuple-element.122), channel_id=1, source_target_pairs={{0,15},{1,0},{2,1},{3,2},{4,3},{5,4},{6,5},{7,6},{8,7},{9,8},{10,9... | collective-permute-start | bytes 98312 | tf_op jit(solution)/shard_map/while/body/eval_jaxpr/ppermute | solution.py:12
  197.5 1.9 collective-permute-start.1
  199.5 6.7 %collective-permute-start.2 = (bf16[2,64,128]{2,1,0:T(8,128)(2,1)S(1)}, bf16[2,64,128]{2,1,0:T(8,128)(2,1)S(1)}, u32[]{:S(2)}, u32[]{:S(2)}) collective-permute-start(bf16[2,64,128]{2,1,0:T(8,128)(2,1)S(1)} %get-tuple-element.124), channel_id=1, source_target_pairs={{0,496},{16,0},{32,16},{48,32},{64,48},{80,64},{96,80},{112,96},{1... | collective-permute-start | bytes 98312 | tf_op jit(solution)/shard_map/while/body/eval_jaxpr/ppermute | solution.py:12
  206.2 1.9 collective-permute-start.3
  209.0 2.4 convolution_bitcast_fusion.4
  215.8 24.7 %all-gather = f32[1024,64]{1,0:T(8,128)S(1)} all-gather(f32[64,64]{1,0:T(8,128)S(1)} %convolution_bitcast_fusion.2), channel_id=2, replica_groups=mesh['px'=32,'py'=16] {'py'}, dimensions={0}, use_global_device_ids=true | all-gather | bytes 278528 | tf_op jit(solution)/shard_map/all_gather | solution.py:16
  240.6 33.8 %all-gather.1 = f32[2048,64]{1,0:T(8,128)S(1)} all-gather(f32[64,64]{1,0:T(8,128)S(1)} %reduce_sum.18), channel_id=3, replica_groups=mesh['px'=32,'py'=16] {'px'}, dimensions={0}, use_global_device_ids=true | all-gather | bytes 540672 | tf_op jit(solution)/shard_map/all_gather | solution.py:16
  (258 shorter events, 54.0 us)
Async XLA Ops:
  0.6 24.2 %copy-start = (bf16[16,4,128,128]{3,2,1,0:T(8,128)(2,1)S(1)}, bf16[16,4,128,128]{3,2,1,0:T(8,128)(2,1)}, u32[]{:S(2)}) copy-start(bf16[16,4,128,128]{3,2,1,0:T(8,128)(2,1)} %param.9) | copy-start | bytes 6291460
  0.6 22.3 %copy-start.5 = (s32[16,4]{0,1:T(4,128)S(1)}, s32[16,4]{0,1:T(4,128)}, u32[]{:S(2)}) copy-start(s32[16,4]{0,1:T(4,128)} %param.10) | copy-start | bytes 772
  0.7 22.3 %copy-start.7 = (s32[16]{0:T(128)S(1)}, s32[16]{0:T(128)}, u32[]{:S(2)}) copy-start(s32[16]{0:T(128)} %param.12) | copy-start | bytes 196
  1.9 25.9 %copy-start.2 = (f32[16,64,128]{2,1,0:T(8,128)}, f32[16,64,128]{2,1,0:T(8,128)S(1)}, u32[]{:S(2)}) copy-start(f32[16,64,128]{2,1,0:T(8,128)S(1)} %copy.41) | copy-start | bytes 1572868
  3.4 24.4 %collective-permute-start.4 = (bf16[2,64,128]{2,1,0:T(8,128)(2,1)S(1)}, bf16[2,64,128]{2,1,0:T(8,128)(2,1)S(1)}, u32[]{:S(2)}, u32[]{:S(2)}) collective-permute-start(bf16[2,64,128]{2,1,0:T(8,128)(2,1)S(1)} %get-tuple-element.65), channel_id=1, source_target_pairs={{0,16},{16,32},{32,48},{48,64},{64,80},{80,96},{96,112},{112,128},... | collective-permute-start | bytes 98312 | tf_op jit(solution)/shard_map/ppermute | solution.py:12
  7.9 19.9 %collective-permute-start.5 = (bf16[2,64,128]{2,1,0:T(8,128)(2,1)S(1)}, bf16[2,64,128]{2,1,0:T(8,128)(2,1)S(1)}, u32[]{:S(2)}, u32[]{:S(2)}) collective-permute-start(bf16[2,64,128]{2,1,0:T(8,128)(2,1)S(1)} %get-tuple-element.67), channel_id=1, source_target_pairs={{0,496},{16,0},{32,16},{48,32},{64,48},{80,64},{96,80},{112,96},{1... | collective-permute-start | bytes 98312 | tf_op jit(solution)/shard_map/ppermute | solution.py:12
  14.1 13.7 %collective-permute-start.6 = (bf16[2,64,128]{2,1,0:T(8,128)(2,1)S(1)}, bf16[2,64,128]{2,1,0:T(8,128)(2,1)S(1)}, u32[]{:S(2)}, u32[]{:S(2)}) collective-permute-start(bf16[2,64,128]{2,1,0:T(8,128)(2,1)S(1)} %get-tuple-element.66), channel_id=1, source_target_pairs={{0,1},{1,2},{2,3},{3,4},{4,5},{5,6},{6,7},{7,8},{8,9},{9,10},{10,1... | collective-permute-start | bytes 98312 | tf_op jit(solution)/shard_map/ppermute | solution.py:12
  16.0 11.8 %collective-permute-start.7 = (bf16[2,64,128]{2,1,0:T(8,128)(2,1)S(1)}, bf16[2,64,128]{2,1,0:T(8,128)(2,1)S(1)}, u32[]{:S(2)}, u32[]{:S(2)}) collective-permute-start(bf16[2,64,128]{2,1,0:T(8,128)(2,1)S(1)} %get-tuple-element.68), channel_id=1, source_target_pairs={{0,15},{1,0},{2,1},{3,2},{4,3},{5,4},{6,5},{7,6},{8,7},{9,8},{10,9... | collective-permute-start | bytes 98312 | tf_op jit(solution)/shard_map/ppermute | solution.py:12
  24.8 4.3 %copy-start.3 = (bf16[16,128,128]{2,1,0:T(8,128)(2,1)S(1)}, bf16[16,128,128]{2,1,0:T(8,128)(2,1)}, u32[]{:S(2)}) copy-start(bf16[16,128,128]{2,1,0:T(8,128)(2,1)} %param.11) | copy-start | bytes 1572868
  27.8 2.9 %copy-start.6 = (s32[4,2]{0,1:T(2,128)S(1)}, s32[4,2]{0,1:T(2,128)}, u32[]{:S(2)}) copy-start(s32[4,2]{0,1:T(2,128)} %param.13) | copy-start | bytes 100
  31.6 17.3 %collective-permute-start = (bf16[2,64,128]{2,1,0:T(8,128)(2,1)S(1)}, bf16[2,64,128]{2,1,0:T(8,128)(2,1)S(1)}, u32[]{:S(2)}, u32[]{:S(2)}) collective-permute-start(bf16[2,64,128]{2,1,0:T(8,128)(2,1)S(1)} %get-tuple-element.122), channel_id=1, source_target_pairs={{0,15},{1,0},{2,1},{3,2},{4,3},{5,4},{6,5},{7,6},{8,7},{9,8},{10,9... | collective-permute-start | bytes 98312 | tf_op jit(solution)/shard_map/while/body/eval_jaxpr/ppermute | solution.py:12
  34.9 14.0 %collective-permute-start.1 = (bf16[2,64,128]{2,1,0:T(8,128)(2,1)S(1)}, bf16[2,64,128]{2,1,0:T(8,128)(2,1)S(1)}, u32[]{:S(2)}, u32[]{:S(2)}) collective-permute-start(bf16[2,64,128]{2,1,0:T(8,128)(2,1)S(1)} %get-tuple-element.123), channel_id=1, source_target_pairs={{0,1},{1,2},{2,3},{3,4},{4,5},{5,6},{6,7},{7,8},{8,9},{9,10},{10,1... | collective-permute-start | bytes 98312 | tf_op jit(solution)/shard_map/while/body/eval_jaxpr/ppermute | solution.py:12
  36.9 12.1 %collective-permute-start.2 = (bf16[2,64,128]{2,1,0:T(8,128)(2,1)S(1)}, bf16[2,64,128]{2,1,0:T(8,128)(2,1)S(1)}, u32[]{:S(2)}, u32[]{:S(2)}) collective-permute-start(bf16[2,64,128]{2,1,0:T(8,128)(2,1)S(1)} %get-tuple-element.124), channel_id=1, source_target_pairs={{0,496},{16,0},{32,16},{48,32},{64,48},{80,64},{96,80},{112,96},{1... | collective-permute-start | bytes 98312 | tf_op jit(solution)/shard_map/while/body/eval_jaxpr/ppermute | solution.py:12
  43.6 5.4 %collective-permute-start.3 = (bf16[2,64,128]{2,1,0:T(8,128)(2,1)S(1)}, bf16[2,64,128]{2,1,0:T(8,128)(2,1)S(1)}, u32[]{:S(2)}, u32[]{:S(2)}) collective-permute-start(bf16[2,64,128]{2,1,0:T(8,128)(2,1)S(1)} %get-tuple-element.125), channel_id=1, source_target_pairs={{0,16},{16,32},{32,48},{48,64},{64,80},{80,96},{96,112},{112,128},... | collective-permute-start | bytes 98312 | tf_op jit(solution)/shard_map/while/body/eval_jaxpr/ppermute | solution.py:12
  49.6 2.7 copy-start.1
  53.5 17.5 %collective-permute-start = (bf16[2,64,128]{2,1,0:T(8,128)(2,1)S(1)}, bf16[2,64,128]{2,1,0:T(8,128)(2,1)S(1)}, u32[]{:S(2)}, u32[]{:S(2)}) collective-permute-start(bf16[2,64,128]{2,1,0:T(8,128)(2,1)S(1)} %get-tuple-element.122), channel_id=1, source_target_pairs={{0,15},{1,0},{2,1},{3,2},{4,3},{5,4},{6,5},{7,6},{8,7},{9,8},{10,9... | collective-permute-start | bytes 98312 | tf_op jit(solution)/shard_map/while/body/eval_jaxpr/ppermute | solution.py:12
  58.4 12.7 %collective-permute-start.1 = (bf16[2,64,128]{2,1,0:T(8,128)(2,1)S(1)}, bf16[2,64,128]{2,1,0:T(8,128)(2,1)S(1)}, u32[]{:S(2)}, u32[]{:S(2)}) collective-permute-start(bf16[2,64,128]{2,1,0:T(8,128)(2,1)S(1)} %get-tuple-element.123), channel_id=1, source_target_pairs={{0,1},{1,2},{2,3},{3,4},{4,5},{5,6},{6,7},{7,8},{8,9},{9,10},{10,1... | collective-permute-start | bytes 98312 | tf_op jit(solution)/shard_map/while/body/eval_jaxpr/ppermute | solution.py:12
  60.3 10.7 %collective-permute-start.2 = (bf16[2,64,128]{2,1,0:T(8,128)(2,1)S(1)}, bf16[2,64,128]{2,1,0:T(8,128)(2,1)S(1)}, u32[]{:S(2)}, u32[]{:S(2)}) collective-permute-start(bf16[2,64,128]{2,1,0:T(8,128)(2,1)S(1)} %get-tuple-element.124), channel_id=1, source_target_pairs={{0,496},{16,0},{32,16},{48,32},{64,48},{80,64},{96,80},{112,96},{1... | collective-permute-start | bytes 98312 | tf_op jit(solution)/shard_map/while/body/eval_jaxpr/ppermute | solution.py:12
  65.7 5.4 %collective-permute-start.3 = (bf16[2,64,128]{2,1,0:T(8,128)(2,1)S(1)}, bf16[2,64,128]{2,1,0:T(8,128)(2,1)S(1)}, u32[]{:S(2)}, u32[]{:S(2)}) collective-permute-start(bf16[2,64,128]{2,1,0:T(8,128)(2,1)S(1)} %get-tuple-element.125), channel_id=1, source_target_pairs={{0,16},{16,32},{32,48},{48,64},{64,80},{80,96},{96,112},{112,128},... | collective-permute-start | bytes 98312 | tf_op jit(solution)/shard_map/while/body/eval_jaxpr/ppermute | solution.py:12
  71.7 2.7 copy-start.1
  75.6 18.8 %collective-permute-start = (bf16[2,64,128]{2,1,0:T(8,128)(2,1)S(1)}, bf16[2,64,128]{2,1,0:T(8,128)(2,1)S(1)}, u32[]{:S(2)}, u32[]{:S(2)}) collective-permute-start(bf16[2,64,128]{2,1,0:T(8,128)(2,1)S(1)} %get-tuple-element.122), channel_id=1, source_target_pairs={{0,15},{1,0},{2,1},{3,2},{4,3},{5,4},{6,5},{7,6},{8,7},{9,8},{10,9... | collective-permute-start | bytes 98312 | tf_op jit(solution)/shard_map/while/body/eval_jaxpr/ppermute | solution.py:12
  80.5 14.0 %collective-permute-start.1 = (bf16[2,64,128]{2,1,0:T(8,128)(2,1)S(1)}, bf16[2,64,128]{2,1,0:T(8,128)(2,1)S(1)}, u32[]{:S(2)}, u32[]{:S(2)}) collective-permute-start(bf16[2,64,128]{2,1,0:T(8,128)(2,1)S(1)} %get-tuple-element.123), channel_id=1, source_target_pairs={{0,1},{1,2},{2,3},{3,4},{4,5},{5,6},{6,7},{7,8},{8,9},{9,10},{10,1... | collective-permute-start | bytes 98312 | tf_op jit(solution)/shard_map/while/body/eval_jaxpr/ppermute | solution.py:12
  82.4 12.0 %collective-permute-start.2 = (bf16[2,64,128]{2,1,0:T(8,128)(2,1)S(1)}, bf16[2,64,128]{2,1,0:T(8,128)(2,1)S(1)}, u32[]{:S(2)}, u32[]{:S(2)}) collective-permute-start(bf16[2,64,128]{2,1,0:T(8,128)(2,1)S(1)} %get-tuple-element.124), channel_id=1, source_target_pairs={{0,496},{16,0},{32,16},{48,32},{64,48},{80,64},{96,80},{112,96},{1... | collective-permute-start | bytes 98312 | tf_op jit(solution)/shard_map/while/body/eval_jaxpr/ppermute | solution.py:12
  89.1 5.4 %collective-permute-start.3 = (bf16[2,64,128]{2,1,0:T(8,128)(2,1)S(1)}, bf16[2,64,128]{2,1,0:T(8,128)(2,1)S(1)}, u32[]{:S(2)}, u32[]{:S(2)}) collective-permute-start(bf16[2,64,128]{2,1,0:T(8,128)(2,1)S(1)} %get-tuple-element.125), channel_id=1, source_target_pairs={{0,16},{16,32},{32,48},{48,64},{64,80},{80,96},{96,112},{112,128},... | collective-permute-start | bytes 98312 | tf_op jit(solution)/shard_map/while/body/eval_jaxpr/ppermute | solution.py:12
  95.1 2.7 copy-start.1
  99.0 18.8 %collective-permute-start = (bf16[2,64,128]{2,1,0:T(8,128)(2,1)S(1)}, bf16[2,64,128]{2,1,0:T(8,128)(2,1)S(1)}, u32[]{:S(2)}, u32[]{:S(2)}) collective-permute-start(bf16[2,64,128]{2,1,0:T(8,128)(2,1)S(1)} %get-tuple-element.122), channel_id=1, source_target_pairs={{0,15},{1,0},{2,1},{3,2},{4,3},{5,4},{6,5},{7,6},{8,7},{9,8},{10,9... | collective-permute-start | bytes 98312 | tf_op jit(solution)/shard_map/while/body/eval_jaxpr/ppermute | solution.py:12
  103.9 14.0 %collective-permute-start.1 = (bf16[2,64,128]{2,1,0:T(8,128)(2,1)S(1)}, bf16[2,64,128]{2,1,0:T(8,128)(2,1)S(1)}, u32[]{:S(2)}, u32[]{:S(2)}) collective-permute-start(bf16[2,64,128]{2,1,0:T(8,128)(2,1)S(1)} %get-tuple-element.123), channel_id=1, source_target_pairs={{0,1},{1,2},{2,3},{3,4},{4,5},{5,6},{6,7},{7,8},{8,9},{9,10},{10,1... | collective-permute-start | bytes 98312 | tf_op jit(solution)/shard_map/while/body/eval_jaxpr/ppermute | solution.py:12
  105.8 12.0 %collective-permute-start.2 = (bf16[2,64,128]{2,1,0:T(8,128)(2,1)S(1)}, bf16[2,64,128]{2,1,0:T(8,128)(2,1)S(1)}, u32[]{:S(2)}, u32[]{:S(2)}) collective-permute-start(bf16[2,64,128]{2,1,0:T(8,128)(2,1)S(1)} %get-tuple-element.124), channel_id=1, source_target_pairs={{0,496},{16,0},{32,16},{48,32},{64,48},{80,64},{96,80},{112,96},{1... | collective-permute-start | bytes 98312 | tf_op jit(solution)/shard_map/while/body/eval_jaxpr/ppermute | solution.py:12
  112.5 5.4 %collective-permute-start.3 = (bf16[2,64,128]{2,1,0:T(8,128)(2,1)S(1)}, bf16[2,64,128]{2,1,0:T(8,128)(2,1)S(1)}, u32[]{:S(2)}, u32[]{:S(2)}) collective-permute-start(bf16[2,64,128]{2,1,0:T(8,128)(2,1)S(1)} %get-tuple-element.125), channel_id=1, source_target_pairs={{0,16},{16,32},{32,48},{48,64},{64,80},{80,96},{96,112},{112,128},... | collective-permute-start | bytes 98312 | tf_op jit(solution)/shard_map/while/body/eval_jaxpr/ppermute | solution.py:12
  122.4 18.8 %collective-permute-start = (bf16[2,64,128]{2,1,0:T(8,128)(2,1)S(1)}, bf16[2,64,128]{2,1,0:T(8,128)(2,1)S(1)}, u32[]{:S(2)}, u32[]{:S(2)}) collective-permute-start(bf16[2,64,128]{2,1,0:T(8,128)(2,1)S(1)} %get-tuple-element.122), channel_id=1, source_target_pairs={{0,15},{1,0},{2,1},{3,2},{4,3},{5,4},{6,5},{7,6},{8,7},{9,8},{10,9... | collective-permute-start | bytes 98312 | tf_op jit(solution)/shard_map/while/body/eval_jaxpr/ppermute | solution.py:12
  127.3 14.0 %collective-permute-start.1 = (bf16[2,64,128]{2,1,0:T(8,128)(2,1)S(1)}, bf16[2,64,128]{2,1,0:T(8,128)(2,1)S(1)}, u32[]{:S(2)}, u32[]{:S(2)}) collective-permute-start(bf16[2,64,128]{2,1,0:T(8,128)(2,1)S(1)} %get-tuple-element.123), channel_id=1, source_target_pairs={{0,1},{1,2},{2,3},{3,4},{4,5},{5,6},{6,7},{7,8},{8,9},{9,10},{10,1... | collective-permute-start | bytes 98312 | tf_op jit(solution)/shard_map/while/body/eval_jaxpr/ppermute | solution.py:12
  129.2 12.0 %collective-permute-start.2 = (bf16[2,64,128]{2,1,0:T(8,128)(2,1)S(1)}, bf16[2,64,128]{2,1,0:T(8,128)(2,1)S(1)}, u32[]{:S(2)}, u32[]{:S(2)}) collective-permute-start(bf16[2,64,128]{2,1,0:T(8,128)(2,1)S(1)} %get-tuple-element.124), channel_id=1, source_target_pairs={{0,496},{16,0},{32,16},{48,32},{64,48},{80,64},{96,80},{112,96},{1... | collective-permute-start | bytes 98312 | tf_op jit(solution)/shard_map/while/body/eval_jaxpr/ppermute | solution.py:12
  135.9 5.4 %collective-permute-start.3 = (bf16[2,64,128]{2,1,0:T(8,128)(2,1)S(1)}, bf16[2,64,128]{2,1,0:T(8,128)(2,1)S(1)}, u32[]{:S(2)}, u32[]{:S(2)}) collective-permute-start(bf16[2,64,128]{2,1,0:T(8,128)(2,1)S(1)} %get-tuple-element.125), channel_id=1, source_target_pairs={{0,16},{16,32},{32,48},{48,64},{64,80},{80,96},{96,112},{112,128},... | collective-permute-start | bytes 98312 | tf_op jit(solution)/shard_map/while/body/eval_jaxpr/ppermute | solution.py:12
  141.9 2.7 copy-start.1
  145.8 18.8 %collective-permute-start = (bf16[2,64,128]{2,1,0:T(8,128)(2,1)S(1)}, bf16[2,64,128]{2,1,0:T(8,128)(2,1)S(1)}, u32[]{:S(2)}, u32[]{:S(2)}) collective-permute-start(bf16[2,64,128]{2,1,0:T(8,128)(2,1)S(1)} %get-tuple-element.122), channel_id=1, source_target_pairs={{0,15},{1,0},{2,1},{3,2},{4,3},{5,4},{6,5},{7,6},{8,7},{9,8},{10,9... | collective-permute-start | bytes 98312 | tf_op jit(solution)/shard_map/while/body/eval_jaxpr/ppermute | solution.py:12
  150.7 14.0 %collective-permute-start.1 = (bf16[2,64,128]{2,1,0:T(8,128)(2,1)S(1)}, bf16[2,64,128]{2,1,0:T(8,128)(2,1)S(1)}, u32[]{:S(2)}, u32[]{:S(2)}) collective-permute-start(bf16[2,64,128]{2,1,0:T(8,128)(2,1)S(1)} %get-tuple-element.123), channel_id=1, source_target_pairs={{0,1},{1,2},{2,3},{3,4},{4,5},{5,6},{6,7},{7,8},{8,9},{9,10},{10,1... | collective-permute-start | bytes 98312 | tf_op jit(solution)/shard_map/while/body/eval_jaxpr/ppermute | solution.py:12
  152.6 12.0 %collective-permute-start.2 = (bf16[2,64,128]{2,1,0:T(8,128)(2,1)S(1)}, bf16[2,64,128]{2,1,0:T(8,128)(2,1)S(1)}, u32[]{:S(2)}, u32[]{:S(2)}) collective-permute-start(bf16[2,64,128]{2,1,0:T(8,128)(2,1)S(1)} %get-tuple-element.124), channel_id=1, source_target_pairs={{0,496},{16,0},{32,16},{48,32},{64,48},{80,64},{96,80},{112,96},{1... | collective-permute-start | bytes 98312 | tf_op jit(solution)/shard_map/while/body/eval_jaxpr/ppermute | solution.py:12
  159.3 5.4 %collective-permute-start.3 = (bf16[2,64,128]{2,1,0:T(8,128)(2,1)S(1)}, bf16[2,64,128]{2,1,0:T(8,128)(2,1)S(1)}, u32[]{:S(2)}, u32[]{:S(2)}) collective-permute-start(bf16[2,64,128]{2,1,0:T(8,128)(2,1)S(1)} %get-tuple-element.125), channel_id=1, source_target_pairs={{0,16},{16,32},{32,48},{48,64},{64,80},{80,96},{96,112},{112,128},... | collective-permute-start | bytes 98312 | tf_op jit(solution)/shard_map/while/body/eval_jaxpr/ppermute | solution.py:12
  165.3 2.7 copy-start.1
  169.3 18.8 %collective-permute-start = (bf16[2,64,128]{2,1,0:T(8,128)(2,1)S(1)}, bf16[2,64,128]{2,1,0:T(8,128)(2,1)S(1)}, u32[]{:S(2)}, u32[]{:S(2)}) collective-permute-start(bf16[2,64,128]{2,1,0:T(8,128)(2,1)S(1)} %get-tuple-element.122), channel_id=1, source_target_pairs={{0,15},{1,0},{2,1},{3,2},{4,3},{5,4},{6,5},{7,6},{8,7},{9,8},{10,9... | collective-permute-start | bytes 98312 | tf_op jit(solution)/shard_map/while/body/eval_jaxpr/ppermute | solution.py:12
  174.1 14.0 %collective-permute-start.1 = (bf16[2,64,128]{2,1,0:T(8,128)(2,1)S(1)}, bf16[2,64,128]{2,1,0:T(8,128)(2,1)S(1)}, u32[]{:S(2)}, u32[]{:S(2)}) collective-permute-start(bf16[2,64,128]{2,1,0:T(8,128)(2,1)S(1)} %get-tuple-element.123), channel_id=1, source_target_pairs={{0,1},{1,2},{2,3},{3,4},{4,5},{5,6},{6,7},{7,8},{8,9},{9,10},{10,1... | collective-permute-start | bytes 98312 | tf_op jit(solution)/shard_map/while/body/eval_jaxpr/ppermute | solution.py:12
  176.1 12.0 %collective-permute-start.2 = (bf16[2,64,128]{2,1,0:T(8,128)(2,1)S(1)}, bf16[2,64,128]{2,1,0:T(8,128)(2,1)S(1)}, u32[]{:S(2)}, u32[]{:S(2)}) collective-permute-start(bf16[2,64,128]{2,1,0:T(8,128)(2,1)S(1)} %get-tuple-element.124), channel_id=1, source_target_pairs={{0,496},{16,0},{32,16},{48,32},{64,48},{80,64},{96,80},{112,96},{1... | collective-permute-start | bytes 98312 | tf_op jit(solution)/shard_map/while/body/eval_jaxpr/ppermute | solution.py:12
  182.7 5.4 %collective-permute-start.3 = (bf16[2,64,128]{2,1,0:T(8,128)(2,1)S(1)}, bf16[2,64,128]{2,1,0:T(8,128)(2,1)S(1)}, u32[]{:S(2)}, u32[]{:S(2)}) collective-permute-start(bf16[2,64,128]{2,1,0:T(8,128)(2,1)S(1)} %get-tuple-element.125), channel_id=1, source_target_pairs={{0,16},{16,32},{32,48},{48,64},{64,80},{80,96},{96,112},{112,128},... | collective-permute-start | bytes 98312 | tf_op jit(solution)/shard_map/while/body/eval_jaxpr/ppermute | solution.py:12
  192.7 18.8 %collective-permute-start = (bf16[2,64,128]{2,1,0:T(8,128)(2,1)S(1)}, bf16[2,64,128]{2,1,0:T(8,128)(2,1)S(1)}, u32[]{:S(2)}, u32[]{:S(2)}) collective-permute-start(bf16[2,64,128]{2,1,0:T(8,128)(2,1)S(1)} %get-tuple-element.122), channel_id=1, source_target_pairs={{0,15},{1,0},{2,1},{3,2},{4,3},{5,4},{6,5},{7,6},{8,7},{9,8},{10,9... | collective-permute-start | bytes 98312 | tf_op jit(solution)/shard_map/while/body/eval_jaxpr/ppermute | solution.py:12
  197.5 14.0 %collective-permute-start.1 = (bf16[2,64,128]{2,1,0:T(8,128)(2,1)S(1)}, bf16[2,64,128]{2,1,0:T(8,128)(2,1)S(1)}, u32[]{:S(2)}, u32[]{:S(2)}) collective-permute-start(bf16[2,64,128]{2,1,0:T(8,128)(2,1)S(1)} %get-tuple-element.123), channel_id=1, source_target_pairs={{0,1},{1,2},{2,3},{3,4},{4,5},{5,6},{6,7},{7,8},{8,9},{9,10},{10,1... | collective-permute-start | bytes 98312 | tf_op jit(solution)/shard_map/while/body/eval_jaxpr/ppermute | solution.py:12
  199.5 12.0 %collective-permute-start.2 = (bf16[2,64,128]{2,1,0:T(8,128)(2,1)S(1)}, bf16[2,64,128]{2,1,0:T(8,128)(2,1)S(1)}, u32[]{:S(2)}, u32[]{:S(2)}) collective-permute-start(bf16[2,64,128]{2,1,0:T(8,128)(2,1)S(1)} %get-tuple-element.124), channel_id=1, source_target_pairs={{0,496},{16,0},{32,16},{48,32},{64,48},{80,64},{96,80},{112,96},{1... | collective-permute-start | bytes 98312 | tf_op jit(solution)/shard_map/while/body/eval_jaxpr/ppermute | solution.py:12
  206.2 5.4 %collective-permute-start.3 = (bf16[2,64,128]{2,1,0:T(8,128)(2,1)S(1)}, bf16[2,64,128]{2,1,0:T(8,128)(2,1)S(1)}, u32[]{:S(2)}, u32[]{:S(2)}) collective-permute-start(bf16[2,64,128]{2,1,0:T(8,128)(2,1)S(1)} %get-tuple-element.125), channel_id=1, source_target_pairs={{0,16},{16,32},{32,48},{48,64},{64,80},{80,96},{96,112},{112,128},... | collective-permute-start | bytes 98312 | tf_op jit(solution)/shard_map/while/body/eval_jaxpr/ppermute | solution.py:12
  212.2 2.7 copy-start.1
  (10 other events, 15.4 us)

commit v10 on v9

--- a/solution.py
+++ b/solution.py
@@ -14,6 +14,26 @@
 
 def gathered_sum(value, axis):
     return jnp.sum(lax.all_gather(value, axis), axis=0)
+
+
+def fold_symmetric(gram):
+    half = gram.shape[0] // 2
+    top, side, low = gram[:half, :half], gram[:half, half:], gram[half:, half:]
+    upper = jnp.arange(half)[:, None] <= jnp.arange(half)[None, :]
+    mixed = jnp.where(upper, top, low)
+    return jnp.concatenate([side, mixed, jnp.diagonal(low)[None, :]], axis=0)
+
+
+def unfold_symmetric(folded):
+    half = folded.shape[1]
+    side, mixed, low_diag = folded[:half], folded[half:2 * half], folded[2 * half]
+    rows, cols = jnp.arange(half)[:, None], jnp.arange(half)[None, :]
+    top = jnp.where(rows <= cols, mixed, mixed.T)
+    low = jnp.where(rows > cols, mixed, mixed.T)
+    low = jnp.where(rows == cols, low_diag[None, :], low)
+    return jnp.concatenate(
+        [jnp.concatenate([top, side], axis=1), jnp.concatenate([side.T, low], axis=1)], axis=0
+    )
 
 
 def operator_apply(current, local_tiles, local_cols, halo_tiles, halo_slot, boundary):
@@ -48,7 +68,7 @@
     previous, current = lax.fori_loop(0, DEG - 1, advance, (start_vecs, first_vecs))
     total_rows = current.shape[0] * current.shape[2] * lax.axis_size("px") * lax.axis_size("py")
     partial_gram = jnp.einsum("rkj,rlj->kl", current, current, precision=lax.Precision.HIGHEST)
-    raw_gram = gathered_sum(gathered_sum(partial_gram, "py"), "px")
+    raw_gram = unfold_symmetric(gathered_sum(gathered_sum(fold_symmetric(partial_gram), "py"), "px"))
     squares = jnp.diagonal(raw_gram)
     scales = lax.rsqrt(squares / total_rows + 1e-06)
     filtered = current * scales[None, :, None]

time: 279 us -> 278 us (level)
  no operation moved by 1% of the time
where the time goes in v10:
time: 278 us; the launch traced here: 277 us
  starting transfers between devices  140 us (50%)
  blocking collectives  56.8 us (20%)
  matrix products  38.8 us (14%)
  local copies, waits for them, and re-layouts  35.9 us (13%)
  other arithmetic  2.98 us (1%)
    ppermute x36, starting transfers between devices, from_behind(): return lax.ppermute(value, axis, pairs)  140 us
    all_gather x2, blocking collectives, gathered_sum(): return jnp.sum(lax.all_gather(value, axis), axis=0)  56.8 us
    dot_general x9, matrix products, operator_apply(): jnp.einsum('rtkj,rtij->rki', gathered, local_tiles, preferred_element_typ...  22.2 us
    dot_general x9, matrix products, operator_apply(): jnp.einsum('rkj,rij->rki', received[halo_slot], halo_tiles, preferred_ele...  16 us
    while x48, local copies, waits for them, and re-layouts  9.86 us
    gather x9, local copies, waits for them, and re-layouts, operator_apply(): gathered = rounded[local_cols]  7.65 us
    gather x9, local copies, waits for them, and re-layouts, operator_apply(): received[halo_slot]  6.06 us
  transfers between devices with their start and end apart: 36, of which 0 were waited for; matrix products, arithmetic and copies ran while one was open for 11% of the time, Pallas kernels for 0%

profile of v10, /device:TPU:1, one launch (start us, length us, event | category | flops | bytes accessed | tf_op | source)
XLA Modules:
  0.0 276.7 jit_solution(8490852862072744960)
XLA Ops:
  3.4 4.5 %collective-permute-start.4 = (bf16[2,64,128]{2,1,0:T(8,128)(2,1)S(1)}, bf16[2,64,128]{2,1,0:T(8,128)(2,1)S(1)}, u32[]{:S(2)}, u32[]{:S(2)}) collective-permute-start(bf16[2,64,128]{2,1,0:T(8,128)(2,1)S(1)} %get-tuple-element.75), channel_id=1, source_target_pairs={{0,16},{16,32},{32,48},{48,64},{64,80},{80,96},{96,112},{112,128},... | collective-permute-start | bytes 98312 | tf_op jit(solution)/shard_map/ppermute | solution.py:12
  7.9 6.2 %collective-permute-start.5 = (bf16[2,64,128]{2,1,0:T(8,128)(2,1)S(1)}, bf16[2,64,128]{2,1,0:T(8,128)(2,1)S(1)}, u32[]{:S(2)}, u32[]{:S(2)}) collective-permute-start(bf16[2,64,128]{2,1,0:T(8,128)(2,1)S(1)} %get-tuple-element.77), channel_id=1, source_target_pairs={{0,496},{16,0},{32,16},{48,32},{64,48},{80,64},{96,80},{112,96},{1... | collective-permute-start | bytes 98312 | tf_op jit(solution)/shard_map/ppermute | solution.py:12
  14.1 1.9 collective-permute-start.6
  16.0 6.9 %collective-permute-start.7 = (bf16[2,64,128]{2,1,0:T(8,128)(2,1)S(1)}, bf16[2,64,128]{2,1,0:T(8,128)(2,1)S(1)}, u32[]{:S(2)}, u32[]{:S(2)}) collective-permute-start(bf16[2,64,128]{2,1,0:T(8,128)(2,1)S(1)} %get-tuple-element.78), channel_id=1, source_target_pairs={{0,15},{1,0},{2,1},{3,2},{4,3},{5,4},{6,5},{7,6},{8,7},{9,8},{10,9... | collective-permute-start | bytes 98312 | tf_op jit(solution)/shard_map/ppermute | solution.py:12
  24.8 2.9 %convolution_bitcast_fusion.1 = f32[16,64,128]{2,1,0:T(8,128)} fusion(bf16[16,4,64,128]{3,2,1,0:T(8,128)(2,1)} %bitcast.67, bf16[16,4,128,128]{3,2,1,0:T(8,128)(2,1)S(1)} %copy-done), kind=kOutput, calls=%fused_computation.20 | convolution fusion | flops 134217728 | bytes 3670016 | tf_op jit(solution)/shard_map/rtkj,rtij->rki/dot_general | solution.py:48
  30.7 184.5 %while.12 = (s32[]{:T(128)}, f32[16,64,128]{2,1,0:T(8,128)}, f32[16,64,128]{2,1,0:T(8,128)S(1)}, s32[16,4]{0,1:T(4,128)S(1)}, bf16[16,4,128,128]{3,2,1,0:T(8,128...) while((s32[]{:T(128)}, f32[16,64,128]{2,1,0:T(8,128)}, ...), condition=%wide.region_1.0_spmd, body=%wide.region_0.0_spmd.sunk | while | flops 168496400 | bytes 23345988 | solution.py:68
  31.6 3.4 %collective-permute-start = (bf16[2,64,128]{2,1,0:T(8,128)(2,1)S(1)}, bf16[2,64,128]{2,1,0:T(8,128)(2,1)S(1)}, u32[]{:S(2)}, u32[]{:S(2)}) collective-permute-start(bf16[2,64,128]{2,1,0:T(8,128)(2,1)S(1)} %get-tuple-element.138), channel_id=1, source_target_pairs={{0,15},{1,0},{2,1},{3,2},{4,3},{5,4},{6,5},{7,6},{8,7},{9,8},{10,9... | collective-permute-start | bytes 98312 | tf_op jit(solution)/shard_map/while/body/eval_jaxpr/ppermute | solution.py:12
  34.9 1.9 collective-permute-start.1
  36.9 6.7 %collective-permute-start.2 = (bf16[2,64,128]{2,1,0:T(8,128)(2,1)S(1)}, bf16[2,64,128]{2,1,0:T(8,128)(2,1)S(1)}, u32[]{:S(2)}, u32[]{:S(2)}) collective-permute-start(bf16[2,64,128]{2,1,0:T(8,128)(2,1)S(1)} %get-tuple-element.140), channel_id=1, source_target_pairs={{0,496},{16,0},{32,16},{48,32},{64,48},{80,64},{96,80},{112,96},{1... | collective-permute-start | bytes 98312 | tf_op jit(solution)/shard_map/while/body/eval_jaxpr/ppermute | solution.py:12
  43.6 1.9 collective-permute-start.3
  46.5 2.4 convolution_bitcast_fusion.4
  53.5 4.8 %collective-permute-start = (bf16[2,64,128]{2,1,0:T(8,128)(2,1)S(1)}, bf16[2,64,128]{2,1,0:T(8,128)(2,1)S(1)}, u32[]{:S(2)}, u32[]{:S(2)}) collective-permute-start(bf16[2,64,128]{2,1,0:T(8,128)(2,1)S(1)} %get-tuple-element.138), channel_id=1, source_target_pairs={{0,15},{1,0},{2,1},{3,2},{4,3},{5,4},{6,5},{7,6},{8,7},{9,8},{10,9... | collective-permute-start | bytes 98312 | tf_op jit(solution)/shard_map/while/body/eval_jaxpr/ppermute | solution.py:12
  58.4 1.9 collective-permute-start.1
  60.3 5.4 %collective-permute-start.2 = (bf16[2,64,128]{2,1,0:T(8,128)(2,1)S(1)}, bf16[2,64,128]{2,1,0:T(8,128)(2,1)S(1)}, u32[]{:S(2)}, u32[]{:S(2)}) collective-permute-start(bf16[2,64,128]{2,1,0:T(8,128)(2,1)S(1)} %get-tuple-element.140), channel_id=1, source_target_pairs={{0,496},{16,0},{32,16},{48,32},{64,48},{80,64},{96,80},{112,96},{1... | collective-permute-start | bytes 98312 | tf_op jit(solution)/shard_map/while/body/eval_jaxpr/ppermute | solution.py:12
  65.7 1.9 collective-permute-start.3
  68.6 2.4 convolution_bitcast_fusion.4
  75.6 4.8 %collective-permute-start = (bf16[2,64,128]{2,1,0:T(8,128)(2,1)S(1)}, bf16[2,64,128]{2,1,0:T(8,128)(2,1)S(1)}, u32[]{:S(2)}, u32[]{:S(2)}) collective-permute-start(bf16[2,64,128]{2,1,0:T(8,128)(2,1)S(1)} %get-tuple-element.138), channel_id=1, source_target_pairs={{0,15},{1,0},{2,1},{3,2},{4,3},{5,4},{6,5},{7,6},{8,7},{9,8},{10,9... | collective-permute-start | bytes 98312 | tf_op jit(solution)/shard_map/while/body/eval_jaxpr/ppermute | solution.py:12
  80.5 1.9 collective-permute-start.1
  82.4 6.7 %collective-permute-start.2 = (bf16[2,64,128]{2,1,0:T(8,128)(2,1)S(1)}, bf16[2,64,128]{2,1,0:T(8,128)(2,1)S(1)}, u32[]{:S(2)}, u32[]{:S(2)}) collective-permute-start(bf16[2,64,128]{2,1,0:T(8,128)(2,1)S(1)} %get-tuple-element.140), channel_id=1, source_target_pairs={{0,496},{16,0},{32,16},{48,32},{64,48},{80,64},{96,80},{112,96},{1... | collective-permute-start | bytes 98312 | tf_op jit(solution)/shard_map/while/body/eval_jaxpr/ppermute | solution.py:12
  89.1 1.9 collective-permute-start.3
  92.0 2.4 convolution_bitcast_fusion.4
  99.0 4.9 %collective-permute-start = (bf16[2,64,128]{2,1,0:T(8,128)(2,1)S(1)}, bf16[2,64,128]{2,1,0:T(8,128)(2,1)S(1)}, u32[]{:S(2)}, u32[]{:S(2)}) collective-permute-start(bf16[2,64,128]{2,1,0:T(8,128)(2,1)S(1)} %get-tuple-element.138), channel_id=1, source_target_pairs={{0,15},{1,0},{2,1},{3,2},{4,3},{5,4},{6,5},{7,6},{8,7},{9,8},{10,9... | collective-permute-start | bytes 98312 | tf_op jit(solution)/shard_map/while/body/eval_jaxpr/ppermute | solution.py:12
  103.9 1.9 collective-permute-start.1
  105.8 6.7 %collective-permute-start.2 = (bf16[2,64,128]{2,1,0:T(8,128)(2,1)S(1)}, bf16[2,64,128]{2,1,0:T(8,128)(2,1)S(1)}, u32[]{:S(2)}, u32[]{:S(2)}) collective-permute-start(bf16[2,64,128]{2,1,0:T(8,128)(2,1)S(1)} %get-tuple-element.140), channel_id=1, source_target_pairs={{0,496},{16,0},{32,16},{48,32},{64,48},{80,64},{96,80},{112,96},{1... | collective-permute-start | bytes 98312 | tf_op jit(solution)/shard_map/while/body/eval_jaxpr/ppermute | solution.py:12
  112.5 1.9 collective-permute-start.3
  115.4 2.4 convolution_bitcast_fusion.4
  122.4 4.9 %collective-permute-start = (bf16[2,64,128]{2,1,0:T(8,128)(2,1)S(1)}, bf16[2,64,128]{2,1,0:T(8,128)(2,1)S(1)}, u32[]{:S(2)}, u32[]{:S(2)}) collective-permute-start(bf16[2,64,128]{2,1,0:T(8,128)(2,1)S(1)} %get-tuple-element.138), channel_id=1, source_target_pairs={{0,15},{1,0},{2,1},{3,2},{4,3},{5,4},{6,5},{7,6},{8,7},{9,8},{10,9... | collective-permute-start | bytes 98312 | tf_op jit(solution)/shard_map/while/body/eval_jaxpr/ppermute | solution.py:12
  127.3 1.9 collective-permute-start.1
  129.2 6.7 %collective-permute-start.2 = (bf16[2,64,128]{2,1,0:T(8,128)(2,1)S(1)}, bf16[2,64,128]{2,1,0:T(8,128)(2,1)S(1)}, u32[]{:S(2)}, u32[]{:S(2)}) collective-permute-start(bf16[2,64,128]{2,1,0:T(8,128)(2,1)S(1)} %get-tuple-element.140), channel_id=1, source_target_pairs={{0,496},{16,0},{32,16},{48,32},{64,48},{80,64},{96,80},{112,96},{1... | collective-permute-start | bytes 98312 | tf_op jit(solution)/shard_map/while/body/eval_jaxpr/ppermute | solution.py:12
  135.9 1.9 collective-permute-start.3
  138.8 2.4 convolution_bitcast_fusion.4
  145.9 4.9 %collective-permute-start = (bf16[2,64,128]{2,1,0:T(8,128)(2,1)S(1)}, bf16[2,64,128]{2,1,0:T(8,128)(2,1)S(1)}, u32[]{:S(2)}, u32[]{:S(2)}) collective-permute-start(bf16[2,64,128]{2,1,0:T(8,128)(2,1)S(1)} %get-tuple-element.138), channel_id=1, source_target_pairs={{0,15},{1,0},{2,1},{3,2},{4,3},{5,4},{6,5},{7,6},{8,7},{9,8},{10,9... | collective-permute-start | bytes 98312 | tf_op jit(solution)/shard_map/while/body/eval_jaxpr/ppermute | solution.py:12
  150.7 1.9 collective-permute-start.1
  152.6 6.7 %collective-permute-start.2 = (bf16[2,64,128]{2,1,0:T(8,128)(2,1)S(1)}, bf16[2,64,128]{2,1,0:T(8,128)(2,1)S(1)}, u32[]{:S(2)}, u32[]{:S(2)}) collective-permute-start(bf16[2,64,128]{2,1,0:T(8,128)(2,1)S(1)} %get-tuple-element.140), channel_id=1, source_target_pairs={{0,496},{16,0},{32,16},{48,32},{64,48},{80,64},{96,80},{112,96},{1... | collective-permute-start | bytes 98312 | tf_op jit(solution)/shard_map/while/body/eval_jaxpr/ppermute | solution.py:12
  159.3 1.9 collective-permute-start.3
  162.2 2.4 convolution_bitcast_fusion.4
  169.3 4.9 %collective-permute-start = (bf16[2,64,128]{2,1,0:T(8,128)(2,1)S(1)}, bf16[2,64,128]{2,1,0:T(8,128)(2,1)S(1)}, u32[]{:S(2)}, u32[]{:S(2)}) collective-permute-start(bf16[2,64,128]{2,1,0:T(8,128)(2,1)S(1)} %get-tuple-element.138), channel_id=1, source_target_pairs={{0,15},{1,0},{2,1},{3,2},{4,3},{5,4},{6,5},{7,6},{8,7},{9,8},{10,9... | collective-permute-start | bytes 98312 | tf_op jit(solution)/shard_map/while/body/eval_jaxpr/ppermute | solution.py:12
  174.1 1.9 collective-permute-start.1
  176.1 6.7 %collective-permute-start.2 = (bf16[2,64,128]{2,1,0:T(8,128)(2,1)S(1)}, bf16[2,64,128]{2,1,0:T(8,128)(2,1)S(1)}, u32[]{:S(2)}, u32[]{:S(2)}) collective-permute-start(bf16[2,64,128]{2,1,0:T(8,128)(2,1)S(1)} %get-tuple-element.140), channel_id=1, source_target_pairs={{0,496},{16,0},{32,16},{48,32},{64,48},{80,64},{96,80},{112,96},{1... | collective-permute-start | bytes 98312 | tf_op jit(solution)/shard_map/while/body/eval_jaxpr/ppermute | solution.py:12
  182.7 1.9 collective-permute-start.3
  185.6 2.4 convolution_bitcast_fusion.4
  192.7 4.9 %collective-permute-start = (bf16[2,64,128]{2,1,0:T(8,128)(2,1)S(1)}, bf16[2,64,128]{2,1,0:T(8,128)(2,1)S(1)}, u32[]{:S(2)}, u32[]{:S(2)}) collective-permute-start(bf16[2,64,128]{2,1,0:T(8,128)(2,1)S(1)} %get-tuple-element.138), channel_id=1, source_target_pairs={{0,15},{1,0},{2,1},{3,2},{4,3},{5,4},{6,5},{7,6},{8,7},{9,8},{10,9... | collective-permute-start | bytes 98312 | tf_op jit(solution)/shard_map/while/body/eval_jaxpr/ppermute | solution.py:12
  197.5 1.9 collective-permute-start.1
  199.5 6.7 %collective-permute-start.2 = (bf16[2,64,128]{2,1,0:T(8,128)(2,1)S(1)}, bf16[2,64,128]{2,1,0:T(8,128)(2,1)S(1)}, u32[]{:S(2)}, u32[]{:S(2)}) collective-permute-start(bf16[2,64,128]{2,1,0:T(8,128)(2,1)S(1)} %get-tuple-element.140), channel_id=1, source_target_pairs={{0,496},{16,0},{32,16},{48,32},{64,48},{80,64},{96,80},{112,96},{1... | collective-permute-start | bytes 98312 | tf_op jit(solution)/shard_map/while/body/eval_jaxpr/ppermute | solution.py:12
  206.2 1.9 collective-permute-start.3
  209.1 2.4 convolution_bitcast_fusion.4
  216.8 23.7 %all-gather.2 = f32[16,65,32]{1,2,0:T(8,128)S(1)} all-gather(f32[1,65,32]{1,2,0:T(8,128)S(1)} %maximum_bitcast_fusion), channel_id=2, replica_groups=mesh['px'=32,'py'=16] {'py'}, dimensions={0}, use_global_device_ids=true | all-gather | bytes 141440 | tf_op jit(solution)/shard_map/all_gather | solution.py:16
  240.5 33.0 %all-gather.3 = f32[32,65,32]{1,2,0:T(8,128)S(1)} all-gather(f32[1,65,32]{1,2,0:T(8,128)S(1)} %bitcast.70), channel_id=3, replica_groups=mesh['px'=32,'py'=16] {'px'}, dimensions={0}, use_global_device_ids=true | all-gather | bytes 274560 | tf_op jit(solution)/shard_map/all_gather | solution.py:16
  (270 shorter events, 55.6 us)
Async XLA Ops:
  0.6 24.2 %copy-start = (bf16[16,4,128,128]{3,2,1,0:T(8,128)(2,1)S(1)}, bf16[16,4,128,128]{3,2,1,0:T(8,128)(2,1)}, u32[]{:S(2)}) copy-start(bf16[16,4,128,128]{3,2,1,0:T(8,128)(2,1)} %param.9) | copy-start | bytes 6291460
  0.6 22.3 %copy-start.5 = (s32[16,4]{0,1:T(4,128)S(1)}, s32[16,4]{0,1:T(4,128)}, u32[]{:S(2)}) copy-start(s32[16,4]{0,1:T(4,128)} %param.10) | copy-start | bytes 772
  0.7 22.3 %copy-start.7 = (s32[16]{0:T(128)S(1)}, s32[16]{0:T(128)}, u32[]{:S(2)}) copy-start(s32[16]{0:T(128)} %param.12) | copy-start | bytes 196
  1.9 25.9 %copy-start.2 = (f32[16,64,128]{2,1,0:T(8,128)}, f32[16,64,128]{2,1,0:T(8,128)S(1)}, u32[]{:S(2)}) copy-start(f32[16,64,128]{2,1,0:T(8,128)S(1)} %copy.76) | copy-start | bytes 1572868
  3.4 24.4 %collective-permute-start.4 = (bf16[2,64,128]{2,1,0:T(8,128)(2,1)S(1)}, bf16[2,64,128]{2,1,0:T(8,128)(2,1)S(1)}, u32[]{:S(2)}, u32[]{:S(2)}) collective-permute-start(bf16[2,64,128]{2,1,0:T(8,128)(2,1)S(1)} %get-tuple-element.75), channel_id=1, source_target_pairs={{0,16},{16,32},{32,48},{48,64},{64,80},{80,96},{96,112},{112,128},... | collective-permute-start | bytes 98312 | tf_op jit(solution)/shard_map/ppermute | solution.py:12
  7.9 19.9 %collective-permute-start.5 = (bf16[2,64,128]{2,1,0:T(8,128)(2,1)S(1)}, bf16[2,64,128]{2,1,0:T(8,128)(2,1)S(1)}, u32[]{:S(2)}, u32[]{:S(2)}) collective-permute-start(bf16[2,64,128]{2,1,0:T(8,128)(2,1)S(1)} %get-tuple-element.77), channel_id=1, source_target_pairs={{0,496},{16,0},{32,16},{48,32},{64,48},{80,64},{96,80},{112,96},{1... | collective-permute-start | bytes 98312 | tf_op jit(solution)/shard_map/ppermute | solution.py:12
  14.1 13.7 %collective-permute-start.6 = (bf16[2,64,128]{2,1,0:T(8,128)(2,1)S(1)}, bf16[2,64,128]{2,1,0:T(8,128)(2,1)S(1)}, u32[]{:S(2)}, u32[]{:S(2)}) collective-permute-start(bf16[2,64,128]{2,1,0:T(8,128)(2,1)S(1)} %get-tuple-element.76), channel_id=1, source_target_pairs={{0,1},{1,2},{2,3},{3,4},{4,5},{5,6},{6,7},{7,8},{8,9},{9,10},{10,1... | collective-permute-start | bytes 98312 | tf_op jit(solution)/shard_map/ppermute | solution.py:12
  16.0 11.8 %collective-permute-start.7 = (bf16[2,64,128]{2,1,0:T(8,128)(2,1)S(1)}, bf16[2,64,128]{2,1,0:T(8,128)(2,1)S(1)}, u32[]{:S(2)}, u32[]{:S(2)}) collective-permute-start(bf16[2,64,128]{2,1,0:T(8,128)(2,1)S(1)} %get-tuple-element.78), channel_id=1, source_target_pairs={{0,15},{1,0},{2,1},{3,2},{4,3},{5,4},{6,5},{7,6},{8,7},{9,8},{10,9... | collective-permute-start | bytes 98312 | tf_op jit(solution)/shard_map/ppermute | solution.py:12
  24.8 4.3 %copy-start.3 = (bf16[16,128,128]{2,1,0:T(8,128)(2,1)S(1)}, bf16[16,128,128]{2,1,0:T(8,128)(2,1)}, u32[]{:S(2)}) copy-start(bf16[16,128,128]{2,1,0:T(8,128)(2,1)} %param.11) | copy-start | bytes 1572868
  27.8 3.0 %copy-start.6 = (s32[4,2]{0,1:T(2,128)S(1)}, s32[4,2]{0,1:T(2,128)}, u32[]{:S(2)}) copy-start(s32[4,2]{0,1:T(2,128)} %param.13) | copy-start | bytes 100
  31.6 17.3 %collective-permute-start = (bf16[2,64,128]{2,1,0:T(8,128)(2,1)S(1)}, bf16[2,64,128]{2,1,0:T(8,128)(2,1)S(1)}, u32[]{:S(2)}, u32[]{:S(2)}) collective-permute-start(bf16[2,64,128]{2,1,0:T(8,128)(2,1)S(1)} %get-tuple-element.138), channel_id=1, source_target_pairs={{0,15},{1,0},{2,1},{3,2},{4,3},{5,4},{6,5},{7,6},{8,7},{9,8},{10,9... | collective-permute-start | bytes 98312 | tf_op jit(solution)/shard_map/while/body/eval_jaxpr/ppermute | solution.py:12
  34.9 14.0 %collective-permute-start.1 = (bf16[2,64,128]{2,1,0:T(8,128)(2,1)S(1)}, bf16[2,64,128]{2,1,0:T(8,128)(2,1)S(1)}, u32[]{:S(2)}, u32[]{:S(2)}) collective-permute-start(bf16[2,64,128]{2,1,0:T(8,128)(2,1)S(1)} %get-tuple-element.139), channel_id=1, source_target_pairs={{0,1},{1,2},{2,3},{3,4},{4,5},{5,6},{6,7},{7,8},{8,9},{9,10},{10,1... | collective-permute-start | bytes 98312 | tf_op jit(solution)/shard_map/while/body/eval_jaxpr/ppermute | solution.py:12
  36.9 12.1 %collective-permute-start.2 = (bf16[2,64,128]{2,1,0:T(8,128)(2,1)S(1)}, bf16[2,64,128]{2,1,0:T(8,128)(2,1)S(1)}, u32[]{:S(2)}, u32[]{:S(2)}) collective-permute-start(bf16[2,64,128]{2,1,0:T(8,128)(2,1)S(1)} %get-tuple-element.140), channel_id=1, source_target_pairs={{0,496},{16,0},{32,16},{48,32},{64,48},{80,64},{96,80},{112,96},{1... | collective-permute-start | bytes 98312 | tf_op jit(solution)/shard_map/while/body/eval_jaxpr/ppermute | solution.py:12
  43.6 5.4 %collective-permute-start.3 = (bf16[2,64,128]{2,1,0:T(8,128)(2,1)S(1)}, bf16[2,64,128]{2,1,0:T(8,128)(2,1)S(1)}, u32[]{:S(2)}, u32[]{:S(2)}) collective-permute-start(bf16[2,64,128]{2,1,0:T(8,128)(2,1)S(1)} %get-tuple-element.141), channel_id=1, source_target_pairs={{0,16},{16,32},{32,48},{48,64},{64,80},{80,96},{96,112},{112,128},... | collective-permute-start | bytes 98312 | tf_op jit(solution)/shard_map/while/body/eval_jaxpr/ppermute | solution.py:12
  49.6 2.7 copy-start.1
  53.5 17.5 %collective-permute-start = (bf16[2,64,128]{2,1,0:T(8,128)(2,1)S(1)}, bf16[2,64,128]{2,1,0:T(8,128)(2,1)S(1)}, u32[]{:S(2)}, u32[]{:S(2)}) collective-permute-start(bf16[2,64,128]{2,1,0:T(8,128)(2,1)S(1)} %get-tuple-element.138), channel_id=1, source_target_pairs={{0,15},{1,0},{2,1},{3,2},{4,3},{5,4},{6,5},{7,6},{8,7},{9,8},{10,9... | collective-permute-start | bytes 98312 | tf_op jit(solution)/shard_map/while/body/eval_jaxpr/ppermute | solution.py:12
  58.4 12.7 %collective-permute-start.1 = (bf16[2,64,128]{2,1,0:T(8,128)(2,1)S(1)}, bf16[2,64,128]{2,1,0:T(8,128)(2,1)S(1)}, u32[]{:S(2)}, u32[]{:S(2)}) collective-permute-start(bf16[2,64,128]{2,1,0:T(8,128)(2,1)S(1)} %get-tuple-element.139), channel_id=1, source_target_pairs={{0,1},{1,2},{2,3},{3,4},{4,5},{5,6},{6,7},{7,8},{8,9},{9,10},{10,1... | collective-permute-start | bytes 98312 | tf_op jit(solution)/shard_map/while/body/eval_jaxpr/ppermute | solution.py:12
  60.3 10.7 %collective-permute-start.2 = (bf16[2,64,128]{2,1,0:T(8,128)(2,1)S(1)}, bf16[2,64,128]{2,1,0:T(8,128)(2,1)S(1)}, u32[]{:S(2)}, u32[]{:S(2)}) collective-permute-start(bf16[2,64,128]{2,1,0:T(8,128)(2,1)S(1)} %get-tuple-element.140), channel_id=1, source_target_pairs={{0,496},{16,0},{32,16},{48,32},{64,48},{80,64},{96,80},{112,96},{1... | collective-permute-start | bytes 98312 | tf_op jit(solution)/shard_map/while/body/eval_jaxpr/ppermute | solution.py:12
  65.7 5.4 %collective-permute-start.3 = (bf16[2,64,128]{2,1,0:T(8,128)(2,1)S(1)}, bf16[2,64,128]{2,1,0:T(8,128)(2,1)S(1)}, u32[]{:S(2)}, u32[]{:S(2)}) collective-permute-start(bf16[2,64,128]{2,1,0:T(8,128)(2,1)S(1)} %get-tuple-element.141), channel_id=1, source_target_pairs={{0,16},{16,32},{32,48},{48,64},{64,80},{80,96},{96,112},{112,128},... | collective-permute-start | bytes 98312 | tf_op jit(solution)/shard_map/while/body/eval_jaxpr/ppermute | solution.py:12
  71.7 2.7 copy-start.1
  75.6 18.8 %collective-permute-start = (bf16[2,64,128]{2,1,0:T(8,128)(2,1)S(1)}, bf16[2,64,128]{2,1,0:T(8,128)(2,1)S(1)}, u32[]{:S(2)}, u32[]{:S(2)}) collective-permute-start(bf16[2,64,128]{2,1,0:T(8,128)(2,1)S(1)} %get-tuple-element.138), channel_id=1, source_target_pairs={{0,15},{1,0},{2,1},{3,2},{4,3},{5,4},{6,5},{7,6},{8,7},{9,8},{10,9... | collective-permute-start | bytes 98312 | tf_op jit(solution)/shard_map/while/body/eval_jaxpr/ppermute | solution.py:12
  80.5 14.0 %collective-permute-start.1 = (bf16[2,64,128]{2,1,0:T(8,128)(2,1)S(1)}, bf16[2,64,128]{2,1,0:T(8,128)(2,1)S(1)}, u32[]{:S(2)}, u32[]{:S(2)}) collective-permute-start(bf16[2,64,128]{2,1,0:T(8,128)(2,1)S(1)} %get-tuple-element.139), channel_id=1, source_target_pairs={{0,1},{1,2},{2,3},{3,4},{4,5},{5,6},{6,7},{7,8},{8,9},{9,10},{10,1... | collective-permute-start | bytes 98312 | tf_op jit(solution)/shard_map/while/body/eval_jaxpr/ppermute | solution.py:12
  82.4 12.0 %collective-permute-start.2 = (bf16[2,64,128]{2,1,0:T(8,128)(2,1)S(1)}, bf16[2,64,128]{2,1,0:T(8,128)(2,1)S(1)}, u32[]{:S(2)}, u32[]{:S(2)}) collective-permute-start(bf16[2,64,128]{2,1,0:T(8,128)(2,1)S(1)} %get-tuple-element.140), channel_id=1, source_target_pairs={{0,496},{16,0},{32,16},{48,32},{64,48},{80,64},{96,80},{112,96},{1... | collective-permute-start | bytes 98312 | tf_op jit(solution)/shard_map/while/body/eval_jaxpr/ppermute | solution.py:12
  89.1 5.4 %collective-permute-start.3 = (bf16[2,64,128]{2,1,0:T(8,128)(2,1)S(1)}, bf16[2,64,128]{2,1,0:T(8,128)(2,1)S(1)}, u32[]{:S(2)}, u32[]{:S(2)}) collective-permute-start(bf16[2,64,128]{2,1,0:T(8,128)(2,1)S(1)} %get-tuple-element.141), channel_id=1, source_target_pairs={{0,16},{16,32},{32,48},{48,64},{64,80},{80,96},{96,112},{112,128},... | collective-permute-start | bytes 98312 | tf_op jit(solution)/shard_map/while/body/eval_jaxpr/ppermute | solution.py:12
  95.1 2.7 copy-start.1
  99.0 18.8 %collective-permute-start = (bf16[2,64,128]{2,1,0:T(8,128)(2,1)S(1)}, bf16[2,64,128]{2,1,0:T(8,128)(2,1)S(1)}, u32[]{:S(2)}, u32[]{:S(2)}) collective-permute-start(bf16[2,64,128]{2,1,0:T(8,128)(2,1)S(1)} %get-tuple-element.138), channel_id=1, source_target_pairs={{0,15},{1,0},{2,1},{3,2},{4,3},{5,4},{6,5},{7,6},{8,7},{9,8},{10,9... | collective-permute-start | bytes 98312 | tf_op jit(solution)/shard_map/while/body/eval_jaxpr/ppermute | solution.py:12
  103.9 14.0 %collective-permute-start.1 = (bf16[2,64,128]{2,1,0:T(8,128)(2,1)S(1)}, bf16[2,64,128]{2,1,0:T(8,128)(2,1)S(1)}, u32[]{:S(2)}, u32[]{:S(2)}) collective-permute-start(bf16[2,64,128]{2,1,0:T(8,128)(2,1)S(1)} %get-tuple-element.139), channel_id=1, source_target_pairs={{0,1},{1,2},{2,3},{3,4},{4,5},{5,6},{6,7},{7,8},{8,9},{9,10},{10,1... | collective-permute-start | bytes 98312 | tf_op jit(solution)/shard_map/while/body/eval_jaxpr/ppermute | solution.py:12
  105.8 12.0 %collective-permute-start.2 = (bf16[2,64,128]{2,1,0:T(8,128)(2,1)S(1)}, bf16[2,64,128]{2,1,0:T(8,128)(2,1)S(1)}, u32[]{:S(2)}, u32[]{:S(2)}) collective-permute-start(bf16[2,64,128]{2,1,0:T(8,128)(2,1)S(1)} %get-tuple-element.140), channel_id=1, source_target_pairs={{0,496},{16,0},{32,16},{48,32},{64,48},{80,64},{96,80},{112,96},{1... | collective-permute-start | bytes 98312 | tf_op jit(solution)/shard_map/while/body/eval_jaxpr/ppermute | solution.py:12
  112.5 5.4 %collective-permute-start.3 = (bf16[2,64,128]{2,1,0:T(8,128)(2,1)S(1)}, bf16[2,64,128]{2,1,0:T(8,128)(2,1)S(1)}, u32[]{:S(2)}, u32[]{:S(2)}) collective-permute-start(bf16[2,64,128]{2,1,0:T(8,128)(2,1)S(1)} %get-tuple-element.141), channel_id=1, source_target_pairs={{0,16},{16,32},{32,48},{48,64},{64,80},{80,96},{96,112},{112,128},... | collective-permute-start | bytes 98312 | tf_op jit(solution)/shard_map/while/body/eval_jaxpr/ppermute | solution.py:12
  118.5 2.7 copy-start.1
  122.4 18.8 %collective-permute-start = (bf16[2,64,128]{2,1,0:T(8,128)(2,1)S(1)}, bf16[2,64,128]{2,1,0:T(8,128)(2,1)S(1)}, u32[]{:S(2)}, u32[]{:S(2)}) collective-permute-start(bf16[2,64,128]{2,1,0:T(8,128)(2,1)S(1)} %get-tuple-element.138), channel_id=1, source_target_pairs={{0,15},{1,0},{2,1},{3,2},{4,3},{5,4},{6,5},{7,6},{8,7},{9,8},{10,9... | collective-permute-start | bytes 98312 | tf_op jit(solution)/shard_map/while/body/eval_jaxpr/ppermute | solution.py:12
  127.3 14.0 %collective-permute-start.1 = (bf16[2,64,128]{2,1,0:T(8,128)(2,1)S(1)}, bf16[2,64,128]{2,1,0:T(8,128)(2,1)S(1)}, u32[]{:S(2)}, u32[]{:S(2)}) collective-permute-start(bf16[2,64,128]{2,1,0:T(8,128)(2,1)S(1)} %get-tuple-element.139), channel_id=1, source_target_pairs={{0,1},{1,2},{2,3},{3,4},{4,5},{5,6},{6,7},{7,8},{8,9},{9,10},{10,1... | collective-permute-start | bytes 98312 | tf_op jit(solution)/shard_map/while/body/eval_jaxpr/ppermute | solution.py:12
  129.2 12.0 %collective-permute-start.2 = (bf16[2,64,128]{2,1,0:T(8,128)(2,1)S(1)}, bf16[2,64,128]{2,1,0:T(8,128)(2,1)S(1)}, u32[]{:S(2)}, u32[]{:S(2)}) collective-permute-start(bf16[2,64,128]{2,1,0:T(8,128)(2,1)S(1)} %get-tuple-element.140), channel_id=1, source_target_pairs={{0,496},{16,0},{32,16},{48,32},{64,48},{80,64},{96,80},{112,96},{1... | collective-permute-start | bytes 98312 | tf_op jit(solution)/shard_map/while/body/eval_jaxpr/ppermute | solution.py:12
  135.9 5.4 %collective-permute-start.3 = (bf16[2,64,128]{2,1,0:T(8,128)(2,1)S(1)}, bf16[2,64,128]{2,1,0:T(8,128)(2,1)S(1)}, u32[]{:S(2)}, u32[]{:S(2)}) collective-permute-start(bf16[2,64,128]{2,1,0:T(8,128)(2,1)S(1)} %get-tuple-element.141), channel_id=1, source_target_pairs={{0,16},{16,32},{32,48},{48,64},{64,80},{80,96},{96,112},{112,128},... | collective-permute-start | bytes 98312 | tf_op jit(solution)/shard_map/while/body/eval_jaxpr/ppermute | solution.py:12
  141.9 2.7 copy-start.1
  145.9 18.8 %collective-permute-start = (bf16[2,64,128]{2,1,0:T(8,128)(2,1)S(1)}, bf16[2,64,128]{2,1,0:T(8,128)(2,1)S(1)}, u32[]{:S(2)}, u32[]{:S(2)}) collective-permute-start(bf16[2,64,128]{2,1,0:T(8,128)(2,1)S(1)} %get-tuple-element.138), channel_id=1, source_target_pairs={{0,15},{1,0},{2,1},{3,2},{4,3},{5,4},{6,5},{7,6},{8,7},{9,8},{10,9... | collective-permute-start | bytes 98312 | tf_op jit(solution)/shard_map/while/body/eval_jaxpr/ppermute | solution.py:12
  150.7 14.0 %collective-permute-start.1 = (bf16[2,64,128]{2,1,0:T(8,128)(2,1)S(1)}, bf16[2,64,128]{2,1,0:T(8,128)(2,1)S(1)}, u32[]{:S(2)}, u32[]{:S(2)}) collective-permute-start(bf16[2,64,128]{2,1,0:T(8,128)(2,1)S(1)} %get-tuple-element.139), channel_id=1, source_target_pairs={{0,1},{1,2},{2,3},{3,4},{4,5},{5,6},{6,7},{7,8},{8,9},{9,10},{10,1... | collective-permute-start | bytes 98312 | tf_op jit(solution)/shard_map/while/body/eval_jaxpr/ppermute | solution.py:12
  152.6 12.0 %collective-permute-start.2 = (bf16[2,64,128]{2,1,0:T(8,128)(2,1)S(1)}, bf16[2,64,128]{2,1,0:T(8,128)(2,1)S(1)}, u32[]{:S(2)}, u32[]{:S(2)}) collective-permute-start(bf16[2,64,128]{2,1,0:T(8,128)(2,1)S(1)} %get-tuple-element.140), channel_id=1, source_target_pairs={{0,496},{16,0},{32,16},{48,32},{64,48},{80,64},{96,80},{112,96},{1... | collective-permute-start | bytes 98312 | tf_op jit(solution)/shard_map/while/body/eval_jaxpr/ppermute | solution.py:12
  159.3 5.4 %collective-permute-start.3 = (bf16[2,64,128]{2,1,0:T(8,128)(2,1)S(1)}, bf16[2,64,128]{2,1,0:T(8,128)(2,1)S(1)}, u32[]{:S(2)}, u32[]{:S(2)}) collective-permute-start(bf16[2,64,128]{2,1,0:T(8,128)(2,1)S(1)} %get-tuple-element.141), channel_id=1, source_target_pairs={{0,16},{16,32},{32,48},{48,64},{64,80},{80,96},{96,112},{112,128},... | collective-permute-start | bytes 98312 | tf_op jit(solution)/shard_map/while/body/eval_jaxpr/ppermute | solution.py:12
  165.3 2.7 copy-start.1
  169.3 18.8 %collective-permute-start = (bf16[2,64,128]{2,1,0:T(8,128)(2,1)S(1)}, bf16[2,64,128]{2,1,0:T(8,128)(2,1)S(1)}, u32[]{:S(2)}, u32[]{:S(2)}) collective-permute-start(bf16[2,64,128]{2,1,0:T(8,128)(2,1)S(1)} %get-tuple-element.138), channel_id=1, source_target_pairs={{0,15},{1,0},{2,1},{3,2},{4,3},{5,4},{6,5},{7,6},{8,7},{9,8},{10,9... | collective-permute-start | bytes 98312 | tf_op jit(solution)/shard_map/while/body/eval_jaxpr/ppermute | solution.py:12
  174.1 14.0 %collective-permute-start.1 = (bf16[2,64,128]{2,1,0:T(8,128)(2,1)S(1)}, bf16[2,64,128]{2,1,0:T(8,128)(2,1)S(1)}, u32[]{:S(2)}, u32[]{:S(2)}) collective-permute-start(bf16[2,64,128]{2,1,0:T(8,128)(2,1)S(1)} %get-tuple-element.139), channel_id=1, source_target_pairs={{0,1},{1,2},{2,3},{3,4},{4,5},{5,6},{6,7},{7,8},{8,9},{9,10},{10,1... | collective-permute-start | bytes 98312 | tf_op jit(solution)/shard_map/while/body/eval_jaxpr/ppermute | solution.py:12
  176.1 12.0 %collective-permute-start.2 = (bf16[2,64,128]{2,1,0:T(8,128)(2,1)S(1)}, bf16[2,64,128]{2,1,0:T(8,128)(2,1)S(1)}, u32[]{:S(2)}, u32[]{:S(2)}) collective-permute-start(bf16[2,64,128]{2,1,0:T(8,128)(2,1)S(1)} %get-tuple-element.140), channel_id=1, source_target_pairs={{0,496},{16,0},{32,16},{48,32},{64,48},{80,64},{96,80},{112,96},{1... | collective-permute-start | bytes 98312 | tf_op jit(solution)/shard_map/while/body/eval_jaxpr/ppermute | solution.py:12
  182.7 5.4 %collective-permute-start.3 = (bf16[2,64,128]{2,1,0:T(8,128)(2,1)S(1)}, bf16[2,64,128]{2,1,0:T(8,128)(2,1)S(1)}, u32[]{:S(2)}, u32[]{:S(2)}) collective-permute-start(bf16[2,64,128]{2,1,0:T(8,128)(2,1)S(1)} %get-tuple-element.141), channel_id=1, source_target_pairs={{0,16},{16,32},{32,48},{48,64},{64,80},{80,96},{96,112},{112,128},... | collective-permute-start | bytes 98312 | tf_op jit(solution)/shard_map/while/body/eval_jaxpr/ppermute | solution.py:12
  192.7 18.8 %collective-permute-start = (bf16[2,64,128]{2,1,0:T(8,128)(2,1)S(1)}, bf16[2,64,128]{2,1,0:T(8,128)(2,1)S(1)}, u32[]{:S(2)}, u32[]{:S(2)}) collective-permute-start(bf16[2,64,128]{2,1,0:T(8,128)(2,1)S(1)} %get-tuple-element.138), channel_id=1, source_target_pairs={{0,15},{1,0},{2,1},{3,2},{4,3},{5,4},{6,5},{7,6},{8,7},{9,8},{10,9... | collective-permute-start | bytes 98312 | tf_op jit(solution)/shard_map/while/body/eval_jaxpr/ppermute | solution.py:12
  197.5 14.0 %collective-permute-start.1 = (bf16[2,64,128]{2,1,0:T(8,128)(2,1)S(1)}, bf16[2,64,128]{2,1,0:T(8,128)(2,1)S(1)}, u32[]{:S(2)}, u32[]{:S(2)}) collective-permute-start(bf16[2,64,128]{2,1,0:T(8,128)(2,1)S(1)} %get-tuple-element.139), channel_id=1, source_target_pairs={{0,1},{1,2},{2,3},{3,4},{4,5},{5,6},{6,7},{7,8},{8,9},{9,10},{10,1... | collective-permute-start | bytes 98312 | tf_op jit(solution)/shard_map/while/body/eval_jaxpr/ppermute | solution.py:12
  199.5 12.0 %collective-permute-start.2 = (bf16[2,64,128]{2,1,0:T(8,128)(2,1)S(1)}, bf16[2,64,128]{2,1,0:T(8,128)(2,1)S(1)}, u32[]{:S(2)}, u32[]{:S(2)}) collective-permute-start(bf16[2,64,128]{2,1,0:T(8,128)(2,1)S(1)} %get-tuple-element.140), channel_id=1, source_target_pairs={{0,496},{16,0},{32,16},{48,32},{64,48},{80,64},{96,80},{112,96},{1... | collective-permute-start | bytes 98312 | tf_op jit(solution)/shard_map/while/body/eval_jaxpr/ppermute | solution.py:12
  206.2 5.4 %collective-permute-start.3 = (bf16[2,64,128]{2,1,0:T(8,128)(2,1)S(1)}, bf16[2,64,128]{2,1,0:T(8,128)(2,1)S(1)}, u32[]{:S(2)}, u32[]{:S(2)}) collective-permute-start(bf16[2,64,128]{2,1,0:T(8,128)(2,1)S(1)} %get-tuple-element.141), channel_id=1, source_target_pairs={{0,16},{16,32},{32,48},{48,64},{64,80},{80,96},{96,112},{112,128},... | collective-permute-start | bytes 98312 | tf_op jit(solution)/shard_map/while/body/eval_jaxpr/ppermute | solution.py:12
  (10 other events, 15.4 us)

commit v11 on v10

--- a/solution.py
+++ b/solution.py
@@ -68,7 +68,7 @@
     previous, current = lax.fori_loop(0, DEG - 1, advance, (start_vecs, first_vecs))
     total_rows = current.shape[0] * current.shape[2] * lax.axis_size("px") * lax.axis_size("py")
     partial_gram = jnp.einsum("rkj,rlj->kl", current, current, precision=lax.Precision.HIGHEST)
-    raw_gram = unfold_symmetric(gathered_sum(gathered_sum(fold_symmetric(partial_gram), "py"), "px"))
+    raw_gram = unfold_symmetric(gathered_sum(fold_symmetric(partial_gram), ("px", "py")))
     squares = jnp.diagonal(raw_gram)
     scales = lax.rsqrt(squares / total_rows + 1e-06)
     filtered = current * scales[None, :, None]

time: 278 us -> 450 us (1.62)
  waiting for transfers between devices: 0.09 us -> 211 us
  blocking collectives: 56.8 us -> 0 us
  between operations: 0.85 us -> 14.3 us
  other arithmetic: 2.98 us -> 7.49 us
    all_gather x0 -> x1, waiting for transfers between devices: none -> 211 us  [gathered_sum(): return jnp.sum(lax.all_gather(value, axis), axis=0)]
    all_gather x2 -> x0, blocking collectives: 56.8 us -> none  [gathered_sum(): return jnp.sum(lax.all_gather(value, axis), axis=0)]
  transfers between devices with their start and end apart: 36 -> 37, of which waited for: 0 -> 1; matrix products, arithmetic and copies ran while one was open for 11% -> 7% of each run, Pallas kernels for 0% -> 0%
where the time goes in v11:
time: 450 us; the launch traced here: 448 us
  waiting for transfers between devices  211 us (47%)
  starting transfers between devices  140 us (31%)
  matrix products  38.8 us (9%)
  local copies, waits for them, and re-layouts  35.2 us (8%)
  between operations  14.3 us (3%)
  other arithmetic  7.49 us (2%)
    all_gather x1, waiting for transfers between devices, gathered_sum(): return jnp.sum(lax.all_gather(value, axis), axis=0)  211 us
    ppermute x36, starting transfers between devices, from_behind(): return lax.ppermute(value, axis, pairs)  140 us
    dot_general x9, matrix products, operator_apply(): jnp.einsum('rtkj,rtij->rki', gathered, local_tiles, preferred_element_typ...  22.3 us
    dot_general x9, matrix products, operator_apply(): jnp.einsum('rkj,rij->rki', received[halo_slot], halo_tiles, preferred_ele...  16 us
    while x48, local copies, waits for them, and re-layouts  9.86 us
  transfers between devices with their start and end apart: 37, of which 1 were waited for; matrix products, arithmetic and copies ran while one was open for 7% of the time, Pallas kernels for 0%

profile of v11, /device:TPU:1, one launch (start us, length us, event | category | flops | bytes accessed | tf_op | source)
XLA Modules:
  0.0 447.9 jit_solution(2697448135411598029)
XLA Ops:
  10.0 4.5 %collective-permute-start.4 = (bf16[2,64,128]{2,1,0:T(8,128)(2,1)S(1)}, bf16[2,64,128]{2,1,0:T(8,128)(2,1)S(1)}, u32[]{:S(2)}, u32[]{:S(2)}) collective-permute-start(bf16[2,64,128]{2,1,0:T(8,128)(2,1)S(1)} %get-tuple-element.73), channel_id=1, source_target_pairs={{0,16},{16,32},{32,48},{48,64},{64,80},{80,96},{96,112},{112,128},... | collective-permute-start | bytes 98312 | tf_op jit(solution)/shard_map/ppermute | solution.py:12
  14.5 6.2 %collective-permute-start.5 = (bf16[2,64,128]{2,1,0:T(8,128)(2,1)S(1)}, bf16[2,64,128]{2,1,0:T(8,128)(2,1)S(1)}, u32[]{:S(2)}, u32[]{:S(2)}) collective-permute-start(bf16[2,64,128]{2,1,0:T(8,128)(2,1)S(1)} %get-tuple-element.75), channel_id=1, source_target_pairs={{0,496},{16,0},{32,16},{48,32},{64,48},{80,64},{96,80},{112,96},{1... | collective-permute-start | bytes 98312 | tf_op jit(solution)/shard_map/ppermute | solution.py:12
  20.7 1.9 collective-permute-start.6
  22.6 6.9 %collective-permute-start.7 = (bf16[2,64,128]{2,1,0:T(8,128)(2,1)S(1)}, bf16[2,64,128]{2,1,0:T(8,128)(2,1)S(1)}, u32[]{:S(2)}, u32[]{:S(2)}) collective-permute-start(bf16[2,64,128]{2,1,0:T(8,128)(2,1)S(1)} %get-tuple-element.76), channel_id=1, source_target_pairs={{0,15},{1,0},{2,1},{3,2},{4,3},{5,4},{6,5},{7,6},{8,7},{9,8},{10,9... | collective-permute-start | bytes 98312 | tf_op jit(solution)/shard_map/ppermute | solution.py:12
  31.4 2.9 convolution_bitcast_fusion.1
  36.5 184.5 %while.12 = (s32[]{:T(128)}, f32[16,64,128]{2,1,0:T(8,128)}, f32[16,64,128]{2,1,0:T(8,128)S(1)}, s32[16,4]{0,1:T(4,128)S(1)}, bf16[16,4,128,128]{3,2,1,0:T(8,128...) while((s32[]{:T(128)}, f32[16,64,128]{2,1,0:T(8,128)}, ...), condition=%wide.region_1.0_spmd, body=%wide.region_0.0_spmd.sunk | while | flops 168496400 | bytes 23345988 | solution.py:68
  37.4 3.4 collective-permute-start
  40.8 1.9 collective-permute-start.1
  42.7 6.7 %collective-permute-start.2 = (bf16[2,64,128]{2,1,0:T(8,128)(2,1)S(1)}, bf16[2,64,128]{2,1,0:T(8,128)(2,1)S(1)}, u32[]{:S(2)}, u32[]{:S(2)}) collective-permute-start(bf16[2,64,128]{2,1,0:T(8,128)(2,1)S(1)} %get-tuple-element.138), channel_id=1, source_target_pairs={{0,496},{16,0},{32,16},{48,32},{64,48},{80,64},{96,80},{112,96},{1... | collective-permute-start | bytes 98312 | tf_op jit(solution)/shard_map/while/body/eval_jaxpr/ppermute | solution.py:12
  49.4 1.9 collective-permute-start.3
  52.3 2.4 convolution_bitcast_fusion.4
  59.3 4.9 %collective-permute-start = (bf16[2,64,128]{2,1,0:T(8,128)(2,1)S(1)}, bf16[2,64,128]{2,1,0:T(8,128)(2,1)S(1)}, u32[]{:S(2)}, u32[]{:S(2)}) collective-permute-start(bf16[2,64,128]{2,1,0:T(8,128)(2,1)S(1)} %get-tuple-element.136), channel_id=1, source_target_pairs={{0,15},{1,0},{2,1},{3,2},{4,3},{5,4},{6,5},{7,6},{8,7},{9,8},{10,9... | collective-permute-start | bytes 98312 | tf_op jit(solution)/shard_map/while/body/eval_jaxpr/ppermute | solution.py:12
  64.2 1.9 collective-permute-start.1
  66.1 5.4 %collective-permute-start.2 = (bf16[2,64,128]{2,1,0:T(8,128)(2,1)S(1)}, bf16[2,64,128]{2,1,0:T(8,128)(2,1)S(1)}, u32[]{:S(2)}, u32[]{:S(2)}) collective-permute-start(bf16[2,64,128]{2,1,0:T(8,128)(2,1)S(1)} %get-tuple-element.138), channel_id=1, source_target_pairs={{0,496},{16,0},{32,16},{48,32},{64,48},{80,64},{96,80},{112,96},{1... | collective-permute-start | bytes 98312 | tf_op jit(solution)/shard_map/while/body/eval_jaxpr/ppermute | solution.py:12
  71.5 1.9 collective-permute-start.3
  74.4 2.4 convolution_bitcast_fusion.4
  81.4 4.9 %collective-permute-start = (bf16[2,64,128]{2,1,0:T(8,128)(2,1)S(1)}, bf16[2,64,128]{2,1,0:T(8,128)(2,1)S(1)}, u32[]{:S(2)}, u32[]{:S(2)}) collective-permute-start(bf16[2,64,128]{2,1,0:T(8,128)(2,1)S(1)} %get-tuple-element.136), channel_id=1, source_target_pairs={{0,15},{1,0},{2,1},{3,2},{4,3},{5,4},{6,5},{7,6},{8,7},{9,8},{10,9... | collective-permute-start | bytes 98312 | tf_op jit(solution)/shard_map/while/body/eval_jaxpr/ppermute | solution.py:12
  86.3 1.9 collective-permute-start.1
  88.2 6.7 %collective-permute-start.2 = (bf16[2,64,128]{2,1,0:T(8,128)(2,1)S(1)}, bf16[2,64,128]{2,1,0:T(8,128)(2,1)S(1)}, u32[]{:S(2)}, u32[]{:S(2)}) collective-permute-start(bf16[2,64,128]{2,1,0:T(8,128)(2,1)S(1)} %get-tuple-element.138), channel_id=1, source_target_pairs={{0,496},{16,0},{32,16},{48,32},{64,48},{80,64},{96,80},{112,96},{1... | collective-permute-start | bytes 98312 | tf_op jit(solution)/shard_map/while/body/eval_jaxpr/ppermute | solution.py:12
  94.9 1.9 collective-permute-start.3
  97.8 2.4 convolution_bitcast_fusion.4
  104.8 4.9 %collective-permute-start = (bf16[2,64,128]{2,1,0:T(8,128)(2,1)S(1)}, bf16[2,64,128]{2,1,0:T(8,128)(2,1)S(1)}, u32[]{:S(2)}, u32[]{:S(2)}) collective-permute-start(bf16[2,64,128]{2,1,0:T(8,128)(2,1)S(1)} %get-tuple-element.136), channel_id=1, source_target_pairs={{0,15},{1,0},{2,1},{3,2},{4,3},{5,4},{6,5},{7,6},{8,7},{9,8},{10,9... | collective-permute-start | bytes 98312 | tf_op jit(solution)/shard_map/while/body/eval_jaxpr/ppermute | solution.py:12
  109.7 1.9 collective-permute-start.1
  111.6 6.7 %collective-permute-start.2 = (bf16[2,64,128]{2,1,0:T(8,128)(2,1)S(1)}, bf16[2,64,128]{2,1,0:T(8,128)(2,1)S(1)}, u32[]{:S(2)}, u32[]{:S(2)}) collective-permute-start(bf16[2,64,128]{2,1,0:T(8,128)(2,1)S(1)} %get-tuple-element.138), channel_id=1, source_target_pairs={{0,496},{16,0},{32,16},{48,32},{64,48},{80,64},{96,80},{112,96},{1... | collective-permute-start | bytes 98312 | tf_op jit(solution)/shard_map/while/body/eval_jaxpr/ppermute | solution.py:12
  118.3 1.9 collective-permute-start.3
  121.2 2.4 convolution_bitcast_fusion.4
  128.3 4.9 %collective-permute-start = (bf16[2,64,128]{2,1,0:T(8,128)(2,1)S(1)}, bf16[2,64,128]{2,1,0:T(8,128)(2,1)S(1)}, u32[]{:S(2)}, u32[]{:S(2)}) collective-permute-start(bf16[2,64,128]{2,1,0:T(8,128)(2,1)S(1)} %get-tuple-element.136), channel_id=1, source_target_pairs={{0,15},{1,0},{2,1},{3,2},{4,3},{5,4},{6,5},{7,6},{8,7},{9,8},{10,9... | collective-permute-start | bytes 98312 | tf_op jit(solution)/shard_map/while/body/eval_jaxpr/ppermute | solution.py:12
  133.1 1.9 collective-permute-start.1
  135.0 6.7 %collective-permute-start.2 = (bf16[2,64,128]{2,1,0:T(8,128)(2,1)S(1)}, bf16[2,64,128]{2,1,0:T(8,128)(2,1)S(1)}, u32[]{:S(2)}, u32[]{:S(2)}) collective-permute-start(bf16[2,64,128]{2,1,0:T(8,128)(2,1)S(1)} %get-tuple-element.138), channel_id=1, source_target_pairs={{0,496},{16,0},{32,16},{48,32},{64,48},{80,64},{96,80},{112,96},{1... | collective-permute-start | bytes 98312 | tf_op jit(solution)/shard_map/while/body/eval_jaxpr/ppermute | solution.py:12
  141.7 1.9 collective-permute-start.3
  144.6 2.4 convolution_bitcast_fusion.4
  151.7 4.9 %collective-permute-start = (bf16[2,64,128]{2,1,0:T(8,128)(2,1)S(1)}, bf16[2,64,128]{2,1,0:T(8,128)(2,1)S(1)}, u32[]{:S(2)}, u32[]{:S(2)}) collective-permute-start(bf16[2,64,128]{2,1,0:T(8,128)(2,1)S(1)} %get-tuple-element.136), channel_id=1, source_target_pairs={{0,15},{1,0},{2,1},{3,2},{4,3},{5,4},{6,5},{7,6},{8,7},{9,8},{10,9... | collective-permute-start | bytes 98312 | tf_op jit(solution)/shard_map/while/body/eval_jaxpr/ppermute | solution.py:12
  156.5 1.9 collective-permute-start.1
  158.5 6.7 %collective-permute-start.2 = (bf16[2,64,128]{2,1,0:T(8,128)(2,1)S(1)}, bf16[2,64,128]{2,1,0:T(8,128)(2,1)S(1)}, u32[]{:S(2)}, u32[]{:S(2)}) collective-permute-start(bf16[2,64,128]{2,1,0:T(8,128)(2,1)S(1)} %get-tuple-element.138), channel_id=1, source_target_pairs={{0,496},{16,0},{32,16},{48,32},{64,48},{80,64},{96,80},{112,96},{1... | collective-permute-start | bytes 98312 | tf_op jit(solution)/shard_map/while/body/eval_jaxpr/ppermute | solution.py:12
  165.1 1.9 collective-permute-start.3
  168.0 2.4 convolution_bitcast_fusion.4
  175.1 4.9 %collective-permute-start = (bf16[2,64,128]{2,1,0:T(8,128)(2,1)S(1)}, bf16[2,64,128]{2,1,0:T(8,128)(2,1)S(1)}, u32[]{:S(2)}, u32[]{:S(2)}) collective-permute-start(bf16[2,64,128]{2,1,0:T(8,128)(2,1)S(1)} %get-tuple-element.136), channel_id=1, source_target_pairs={{0,15},{1,0},{2,1},{3,2},{4,3},{5,4},{6,5},{7,6},{8,7},{9,8},{10,9... | collective-permute-start | bytes 98312 | tf_op jit(solution)/shard_map/while/body/eval_jaxpr/ppermute | solution.py:12
  179.9 1.9 collective-permute-start.1
  181.9 6.7 %collective-permute-start.2 = (bf16[2,64,128]{2,1,0:T(8,128)(2,1)S(1)}, bf16[2,64,128]{2,1,0:T(8,128)(2,1)S(1)}, u32[]{:S(2)}, u32[]{:S(2)}) collective-permute-start(bf16[2,64,128]{2,1,0:T(8,128)(2,1)S(1)} %get-tuple-element.138), channel_id=1, source_target_pairs={{0,496},{16,0},{32,16},{48,32},{64,48},{80,64},{96,80},{112,96},{1... | collective-permute-start | bytes 98312 | tf_op jit(solution)/shard_map/while/body/eval_jaxpr/ppermute | solution.py:12
  188.6 1.9 collective-permute-start.3
  191.5 2.4 convolution_bitcast_fusion.4
  198.5 4.9 %collective-permute-start = (bf16[2,64,128]{2,1,0:T(8,128)(2,1)S(1)}, bf16[2,64,128]{2,1,0:T(8,128)(2,1)S(1)}, u32[]{:S(2)}, u32[]{:S(2)}) collective-permute-start(bf16[2,64,128]{2,1,0:T(8,128)(2,1)S(1)} %get-tuple-element.136), channel_id=1, source_target_pairs={{0,15},{1,0},{2,1},{3,2},{4,3},{5,4},{6,5},{7,6},{8,7},{9,8},{10,9... | collective-permute-start | bytes 98312 | tf_op jit(solution)/shard_map/while/body/eval_jaxpr/ppermute | solution.py:12
  203.3 1.9 collective-permute-start.1
  205.3 6.7 %collective-permute-start.2 = (bf16[2,64,128]{2,1,0:T(8,128)(2,1)S(1)}, bf16[2,64,128]{2,1,0:T(8,128)(2,1)S(1)}, u32[]{:S(2)}, u32[]{:S(2)}) collective-permute-start(bf16[2,64,128]{2,1,0:T(8,128)(2,1)S(1)} %get-tuple-element.138), channel_id=1, source_target_pairs={{0,496},{16,0},{32,16},{48,32},{64,48},{80,64},{96,80},{112,96},{1... | collective-permute-start | bytes 98312 | tf_op jit(solution)/shard_map/while/body/eval_jaxpr/ppermute | solution.py:12
  212.0 1.9 collective-permute-start.3
  214.9 2.4 convolution_bitcast_fusion.4
  223.2 210.7 %all-gather.4.cloned.1.call-done = f32[512,65,32]{1,2,0:T(8,128)} async-done(((f32[1,65,32]{1,2,0:T(8,128)}), f32[512,65,32]{1,2,0:T(8,128)}) %all-gather.4.cloned.1.call-update) | async-done | bytes 4259856 | tf_op jit(solution)/shard_map/all_gather | solution.py:16
  433.9 4.0 reduce_sum.9
  (270 shorter events, 55.4 us)
Async XLA Ops:
  7.2 24.2 %copy-start = (bf16[16,4,128,128]{3,2,1,0:T(8,128)(2,1)S(1)}, bf16[16,4,128,128]{3,2,1,0:T(8,128)(2,1)}, u32[]{:S(2)}) copy-start(bf16[16,4,128,128]{3,2,1,0:T(8,128)(2,1)} %param.9) | copy-start | bytes 6291460
  7.2 22.3 %copy-start.5 = (s32[16,4]{0,1:T(4,128)S(1)}, s32[16,4]{0,1:T(4,128)}, u32[]{:S(2)}) copy-start(s32[16,4]{0,1:T(4,128)} %param.10) | copy-start | bytes 772
  7.2 22.3 %copy-start.7 = (s32[16]{0:T(128)S(1)}, s32[16]{0:T(128)}, u32[]{:S(2)}) copy-start(s32[16]{0:T(128)} %param.12) | copy-start | bytes 196
  7.2 426.8 %all-gather.4.cloned.1.call-start = ((), (), s32[]{:S(2)}) async-start(), calls=%async_computation | async-start | bytes 8404992 | tf_op jit(solution)/shard_map/all_gather | solution.py:16
  8.4 25.9 %copy-start.2 = (f32[16,64,128]{2,1,0:T(8,128)}, f32[16,64,128]{2,1,0:T(8,128)S(1)}, u32[]{:S(2)}) copy-start(f32[16,64,128]{2,1,0:T(8,128)S(1)} %copy.67) | copy-start | bytes 1572868
  10.0 24.4 %collective-permute-start.4 = (bf16[2,64,128]{2,1,0:T(8,128)(2,1)S(1)}, bf16[2,64,128]{2,1,0:T(8,128)(2,1)S(1)}, u32[]{:S(2)}, u32[]{:S(2)}) collective-permute-start(bf16[2,64,128]{2,1,0:T(8,128)(2,1)S(1)} %get-tuple-element.73), channel_id=1, source_target_pairs={{0,16},{16,32},{32,48},{48,64},{64,80},{80,96},{96,112},{112,128},... | collective-permute-start | bytes 98312 | tf_op jit(solution)/shard_map/ppermute | solution.py:12
  14.5 19.9 %collective-permute-start.5 = (bf16[2,64,128]{2,1,0:T(8,128)(2,1)S(1)}, bf16[2,64,128]{2,1,0:T(8,128)(2,1)S(1)}, u32[]{:S(2)}, u32[]{:S(2)}) collective-permute-start(bf16[2,64,128]{2,1,0:T(8,128)(2,1)S(1)} %get-tuple-element.75), channel_id=1, source_target_pairs={{0,496},{16,0},{32,16},{48,32},{64,48},{80,64},{96,80},{112,96},{1... | collective-permute-start | bytes 98312 | tf_op jit(solution)/shard_map/ppermute | solution.py:12
  20.7 13.7 %collective-permute-start.6 = (bf16[2,64,128]{2,1,0:T(8,128)(2,1)S(1)}, bf16[2,64,128]{2,1,0:T(8,128)(2,1)S(1)}, u32[]{:S(2)}, u32[]{:S(2)}) collective-permute-start(bf16[2,64,128]{2,1,0:T(8,128)(2,1)S(1)} %get-tuple-element.74), channel_id=1, source_target_pairs={{0,1},{1,2},{2,3},{3,4},{4,5},{5,6},{6,7},{7,8},{8,9},{9,10},{10,1... | collective-permute-start | bytes 98312 | tf_op jit(solution)/shard_map/ppermute | solution.py:12
  22.6 11.8 %collective-permute-start.7 = (bf16[2,64,128]{2,1,0:T(8,128)(2,1)S(1)}, bf16[2,64,128]{2,1,0:T(8,128)(2,1)S(1)}, u32[]{:S(2)}, u32[]{:S(2)}) collective-permute-start(bf16[2,64,128]{2,1,0:T(8,128)(2,1)S(1)} %get-tuple-element.76), channel_id=1, source_target_pairs={{0,15},{1,0},{2,1},{3,2},{4,3},{5,4},{6,5},{7,6},{8,7},{9,8},{10,9... | collective-permute-start | bytes 98312 | tf_op jit(solution)/shard_map/ppermute | solution.py:12
  31.4 3.6 copy-start.3
  37.4 17.3 %collective-permute-start = (bf16[2,64,128]{2,1,0:T(8,128)(2,1)S(1)}, bf16[2,64,128]{2,1,0:T(8,128)(2,1)S(1)}, u32[]{:S(2)}, u32[]{:S(2)}) collective-permute-start(bf16[2,64,128]{2,1,0:T(8,128)(2,1)S(1)} %get-tuple-element.136), channel_id=1, source_target_pairs={{0,15},{1,0},{2,1},{3,2},{4,3},{5,4},{6,5},{7,6},{8,7},{9,8},{10,9... | collective-permute-start | bytes 98312 | tf_op jit(solution)/shard_map/while/body/eval_jaxpr/ppermute | solution.py:12
  40.8 14.0 %collective-permute-start.1 = (bf16[2,64,128]{2,1,0:T(8,128)(2,1)S(1)}, bf16[2,64,128]{2,1,0:T(8,128)(2,1)S(1)}, u32[]{:S(2)}, u32[]{:S(2)}) collective-permute-start(bf16[2,64,128]{2,1,0:T(8,128)(2,1)S(1)} %get-tuple-element.137), channel_id=1, source_target_pairs={{0,1},{1,2},{2,3},{3,4},{4,5},{5,6},{6,7},{7,8},{8,9},{9,10},{10,1... | collective-permute-start | bytes 98312 | tf_op jit(solution)/shard_map/while/body/eval_jaxpr/ppermute | solution.py:12
  42.7 12.1 %collective-permute-start.2 = (bf16[2,64,128]{2,1,0:T(8,128)(2,1)S(1)}, bf16[2,64,128]{2,1,0:T(8,128)(2,1)S(1)}, u32[]{:S(2)}, u32[]{:S(2)}) collective-permute-start(bf16[2,64,128]{2,1,0:T(8,128)(2,1)S(1)} %get-tuple-element.138), channel_id=1, source_target_pairs={{0,496},{16,0},{32,16},{48,32},{64,48},{80,64},{96,80},{112,96},{1... | collective-permute-start | bytes 98312 | tf_op jit(solution)/shard_map/while/body/eval_jaxpr/ppermute | solution.py:12
  49.4 5.4 %collective-permute-start.3 = (bf16[2,64,128]{2,1,0:T(8,128)(2,1)S(1)}, bf16[2,64,128]{2,1,0:T(8,128)(2,1)S(1)}, u32[]{:S(2)}, u32[]{:S(2)}) collective-permute-start(bf16[2,64,128]{2,1,0:T(8,128)(2,1)S(1)} %get-tuple-element.139), channel_id=1, source_target_pairs={{0,16},{16,32},{32,48},{48,64},{64,80},{80,96},{96,112},{112,128},... | collective-permute-start | bytes 98312 | tf_op jit(solution)/shard_map/while/body/eval_jaxpr/ppermute | solution.py:12
  55.4 2.7 copy-start.1
  59.3 17.5 %collective-permute-start = (bf16[2,64,128]{2,1,0:T(8,128)(2,1)S(1)}, bf16[2,64,128]{2,1,0:T(8,128)(2,1)S(1)}, u32[]{:S(2)}, u32[]{:S(2)}) collective-permute-start(bf16[2,64,128]{2,1,0:T(8,128)(2,1)S(1)} %get-tuple-element.136), channel_id=1, source_target_pairs={{0,15},{1,0},{2,1},{3,2},{4,3},{5,4},{6,5},{7,6},{8,7},{9,8},{10,9... | collective-permute-start | bytes 98312 | tf_op jit(solution)/shard_map/while/body/eval_jaxpr/ppermute | solution.py:12
  64.2 12.7 %collective-permute-start.1 = (bf16[2,64,128]{2,1,0:T(8,128)(2,1)S(1)}, bf16[2,64,128]{2,1,0:T(8,128)(2,1)S(1)}, u32[]{:S(2)}, u32[]{:S(2)}) collective-permute-start(bf16[2,64,128]{2,1,0:T(8,128)(2,1)S(1)} %get-tuple-element.137), channel_id=1, source_target_pairs={{0,1},{1,2},{2,3},{3,4},{4,5},{5,6},{6,7},{7,8},{8,9},{9,10},{10,1... | collective-permute-start | bytes 98312 | tf_op jit(solution)/shard_map/while/body/eval_jaxpr/ppermute | solution.py:12
  66.1 10.7 %collective-permute-start.2 = (bf16[2,64,128]{2,1,0:T(8,128)(2,1)S(1)}, bf16[2,64,128]{2,1,0:T(8,128)(2,1)S(1)}, u32[]{:S(2)}, u32[]{:S(2)}) collective-permute-start(bf16[2,64,128]{2,1,0:T(8,128)(2,1)S(1)} %get-tuple-element.138), channel_id=1, source_target_pairs={{0,496},{16,0},{32,16},{48,32},{64,48},{80,64},{96,80},{112,96},{1... | collective-permute-start | bytes 98312 | tf_op jit(solution)/shard_map/while/body/eval_jaxpr/ppermute | solution.py:12
  71.5 5.4 %collective-permute-start.3 = (bf16[2,64,128]{2,1,0:T(8,128)(2,1)S(1)}, bf16[2,64,128]{2,1,0:T(8,128)(2,1)S(1)}, u32[]{:S(2)}, u32[]{:S(2)}) collective-permute-start(bf16[2,64,128]{2,1,0:T(8,128)(2,1)S(1)} %get-tuple-element.139), channel_id=1, source_target_pairs={{0,16},{16,32},{32,48},{48,64},{64,80},{80,96},{96,112},{112,128},... | collective-permute-start | bytes 98312 | tf_op jit(solution)/shard_map/while/body/eval_jaxpr/ppermute | solution.py:12
  77.5 2.7 copy-start.1
  81.4 18.8 %collective-permute-start = (bf16[2,64,128]{2,1,0:T(8,128)(2,1)S(1)}, bf16[2,64,128]{2,1,0:T(8,128)(2,1)S(1)}, u32[]{:S(2)}, u32[]{:S(2)}) collective-permute-start(bf16[2,64,128]{2,1,0:T(8,128)(2,1)S(1)} %get-tuple-element.136), channel_id=1, source_target_pairs={{0,15},{1,0},{2,1},{3,2},{4,3},{5,4},{6,5},{7,6},{8,7},{9,8},{10,9... | collective-permute-start | bytes 98312 | tf_op jit(solution)/shard_map/while/body/eval_jaxpr/ppermute | solution.py:12
  86.3 14.0 %collective-permute-start.1 = (bf16[2,64,128]{2,1,0:T(8,128)(2,1)S(1)}, bf16[2,64,128]{2,1,0:T(8,128)(2,1)S(1)}, u32[]{:S(2)}, u32[]{:S(2)}) collective-permute-start(bf16[2,64,128]{2,1,0:T(8,128)(2,1)S(1)} %get-tuple-element.137), channel_id=1, source_target_pairs={{0,1},{1,2},{2,3},{3,4},{4,5},{5,6},{6,7},{7,8},{8,9},{9,10},{10,1... | collective-permute-start | bytes 98312 | tf_op jit(solution)/shard_map/while/body/eval_jaxpr/ppermute | solution.py:12
  88.2 12.0 %collective-permute-start.2 = (bf16[2,64,128]{2,1,0:T(8,128)(2,1)S(1)}, bf16[2,64,128]{2,1,0:T(8,128)(2,1)S(1)}, u32[]{:S(2)}, u32[]{:S(2)}) collective-permute-start(bf16[2,64,128]{2,1,0:T(8,128)(2,1)S(1)} %get-tuple-element.138), channel_id=1, source_target_pairs={{0,496},{16,0},{32,16},{48,32},{64,48},{80,64},{96,80},{112,96},{1... | collective-permute-start | bytes 98312 | tf_op jit(solution)/shard_map/while/body/eval_jaxpr/ppermute | solution.py:12
  94.9 5.4 %collective-permute-start.3 = (bf16[2,64,128]{2,1,0:T(8,128)(2,1)S(1)}, bf16[2,64,128]{2,1,0:T(8,128)(2,1)S(1)}, u32[]{:S(2)}, u32[]{:S(2)}) collective-permute-start(bf16[2,64,128]{2,1,0:T(8,128)(2,1)S(1)} %get-tuple-element.139), channel_id=1, source_target_pairs={{0,16},{16,32},{32,48},{48,64},{64,80},{80,96},{96,112},{112,128},... | collective-permute-start | bytes 98312 | tf_op jit(solution)/shard_map/while/body/eval_jaxpr/ppermute | solution.py:12
  100.9 2.7 copy-start.1
  104.8 18.8 %collective-permute-start = (bf16[2,64,128]{2,1,0:T(8,128)(2,1)S(1)}, bf16[2,64,128]{2,1,0:T(8,128)(2,1)S(1)}, u32[]{:S(2)}, u32[]{:S(2)}) collective-permute-start(bf16[2,64,128]{2,1,0:T(8,128)(2,1)S(1)} %get-tuple-element.136), channel_id=1, source_target_pairs={{0,15},{1,0},{2,1},{3,2},{4,3},{5,4},{6,5},{7,6},{8,7},{9,8},{10,9... | collective-permute-start | bytes 98312 | tf_op jit(solution)/shard_map/while/body/eval_jaxpr/ppermute | solution.py:12
  109.7 14.0 %collective-permute-start.1 = (bf16[2,64,128]{2,1,0:T(8,128)(2,1)S(1)}, bf16[2,64,128]{2,1,0:T(8,128)(2,1)S(1)}, u32[]{:S(2)}, u32[]{:S(2)}) collective-permute-start(bf16[2,64,128]{2,1,0:T(8,128)(2,1)S(1)} %get-tuple-element.137), channel_id=1, source_target_pairs={{0,1},{1,2},{2,3},{3,4},{4,5},{5,6},{6,7},{7,8},{8,9},{9,10},{10,1... | collective-permute-start | bytes 98312 | tf_op jit(solution)/shard_map/while/body/eval_jaxpr/ppermute | solution.py:12
  111.6 12.0 %collective-permute-start.2 = (bf16[2,64,128]{2,1,0:T(8,128)(2,1)S(1)}, bf16[2,64,128]{2,1,0:T(8,128)(2,1)S(1)}, u32[]{:S(2)}, u32[]{:S(2)}) collective-permute-start(bf16[2,64,128]{2,1,0:T(8,128)(2,1)S(1)} %get-tuple-element.138), channel_id=1, source_target_pairs={{0,496},{16,0},{32,16},{48,32},{64,48},{80,64},{96,80},{112,96},{1... | collective-permute-start | bytes 98312 | tf_op jit(solution)/shard_map/while/body/eval_jaxpr/ppermute | solution.py:12
  118.3 5.4 %collective-permute-start.3 = (bf16[2,64,128]{2,1,0:T(8,128)(2,1)S(1)}, bf16[2,64,128]{2,1,0:T(8,128)(2,1)S(1)}, u32[]{:S(2)}, u32[]{:S(2)}) collective-permute-start(bf16[2,64,128]{2,1,0:T(8,128)(2,1)S(1)} %get-tuple-element.139), channel_id=1, source_target_pairs={{0,16},{16,32},{32,48},{48,64},{64,80},{80,96},{96,112},{112,128},... | collective-permute-start | bytes 98312 | tf_op jit(solution)/shard_map/while/body/eval_jaxpr/ppermute | solution.py:12
  124.3 2.7 copy-start.1
  128.3 18.8 %collective-permute-start = (bf16[2,64,128]{2,1,0:T(8,128)(2,1)S(1)}, bf16[2,64,128]{2,1,0:T(8,128)(2,1)S(1)}, u32[]{:S(2)}, u32[]{:S(2)}) collective-permute-start(bf16[2,64,128]{2,1,0:T(8,128)(2,1)S(1)} %get-tuple-element.136), channel_id=1, source_target_pairs={{0,15},{1,0},{2,1},{3,2},{4,3},{5,4},{6,5},{7,6},{8,7},{9,8},{10,9... | collective-permute-start | bytes 98312 | tf_op jit(solution)/shard_map/while/body/eval_jaxpr/ppermute | solution.py:12
  133.1 14.0 %collective-permute-start.1 = (bf16[2,64,128]{2,1,0:T(8,128)(2,1)S(1)}, bf16[2,64,128]{2,1,0:T(8,128)(2,1)S(1)}, u32[]{:S(2)}, u32[]{:S(2)}) collective-permute-start(bf16[2,64,128]{2,1,0:T(8,128)(2,1)S(1)} %get-tuple-element.137), channel_id=1, source_target_pairs={{0,1},{1,2},{2,3},{3,4},{4,5},{5,6},{6,7},{7,8},{8,9},{9,10},{10,1... | collective-permute-start | bytes 98312 | tf_op jit(solution)/shard_map/while/body/eval_jaxpr/ppermute | solution.py:12
  135.0 12.0 %collective-permute-start.2 = (bf16[2,64,128]{2,1,0:T(8,128)(2,1)S(1)}, bf16[2,64,128]{2,1,0:T(8,128)(2,1)S(1)}, u32[]{:S(2)}, u32[]{:S(2)}) collective-permute-start(bf16[2,64,128]{2,1,0:T(8,128)(2,1)S(1)} %get-tuple-element.138), channel_id=1, source_target_pairs={{0,496},{16,0},{32,16},{48,32},{64,48},{80,64},{96,80},{112,96},{1... | collective-permute-start | bytes 98312 | tf_op jit(solution)/shard_map/while/body/eval_jaxpr/ppermute | solution.py:12
  141.7 5.4 %collective-permute-start.3 = (bf16[2,64,128]{2,1,0:T(8,128)(2,1)S(1)}, bf16[2,64,128]{2,1,0:T(8,128)(2,1)S(1)}, u32[]{:S(2)}, u32[]{:S(2)}) collective-permute-start(bf16[2,64,128]{2,1,0:T(8,128)(2,1)S(1)} %get-tuple-element.139), channel_id=1, source_target_pairs={{0,16},{16,32},{32,48},{48,64},{64,80},{80,96},{96,112},{112,128},... | collective-permute-start | bytes 98312 | tf_op jit(solution)/shard_map/while/body/eval_jaxpr/ppermute | solution.py:12
  147.7 2.7 copy-start.1
  151.7 18.8 %collective-permute-start = (bf16[2,64,128]{2,1,0:T(8,128)(2,1)S(1)}, bf16[2,64,128]{2,1,0:T(8,128)(2,1)S(1)}, u32[]{:S(2)}, u32[]{:S(2)}) collective-permute-start(bf16[2,64,128]{2,1,0:T(8,128)(2,1)S(1)} %get-tuple-element.136), channel_id=1, source_target_pairs={{0,15},{1,0},{2,1},{3,2},{4,3},{5,4},{6,5},{7,6},{8,7},{9,8},{10,9... | collective-permute-start | bytes 98312 | tf_op jit(solution)/shard_map/while/body/eval_jaxpr/ppermute | solution.py:12
  156.5 14.0 %collective-permute-start.1 = (bf16[2,64,128]{2,1,0:T(8,128)(2,1)S(1)}, bf16[2,64,128]{2,1,0:T(8,128)(2,1)S(1)}, u32[]{:S(2)}, u32[]{:S(2)}) collective-permute-start(bf16[2,64,128]{2,1,0:T(8,128)(2,1)S(1)} %get-tuple-element.137), channel_id=1, source_target_pairs={{0,1},{1,2},{2,3},{3,4},{4,5},{5,6},{6,7},{7,8},{8,9},{9,10},{10,1... | collective-permute-start | bytes 98312 | tf_op jit(solution)/shard_map/while/body/eval_jaxpr/ppermute | solution.py:12
  158.5 12.0 %collective-permute-start.2 = (bf16[2,64,128]{2,1,0:T(8,128)(2,1)S(1)}, bf16[2,64,128]{2,1,0:T(8,128)(2,1)S(1)}, u32[]{:S(2)}, u32[]{:S(2)}) collective-permute-start(bf16[2,64,128]{2,1,0:T(8,128)(2,1)S(1)} %get-tuple-element.138), channel_id=1, source_target_pairs={{0,496},{16,0},{32,16},{48,32},{64,48},{80,64},{96,80},{112,96},{1... | collective-permute-start | bytes 98312 | tf_op jit(solution)/shard_map/while/body/eval_jaxpr/ppermute | solution.py:12
  165.1 5.4 %collective-permute-start.3 = (bf16[2,64,128]{2,1,0:T(8,128)(2,1)S(1)}, bf16[2,64,128]{2,1,0:T(8,128)(2,1)S(1)}, u32[]{:S(2)}, u32[]{:S(2)}) collective-permute-start(bf16[2,64,128]{2,1,0:T(8,128)(2,1)S(1)} %get-tuple-element.139), channel_id=1, source_target_pairs={{0,16},{16,32},{32,48},{48,64},{64,80},{80,96},{96,112},{112,128},... | collective-permute-start | bytes 98312 | tf_op jit(solution)/shard_map/while/body/eval_jaxpr/ppermute | solution.py:12
  175.1 18.8 %collective-permute-start = (bf16[2,64,128]{2,1,0:T(8,128)(2,1)S(1)}, bf16[2,64,128]{2,1,0:T(8,128)(2,1)S(1)}, u32[]{:S(2)}, u32[]{:S(2)}) collective-permute-start(bf16[2,64,128]{2,1,0:T(8,128)(2,1)S(1)} %get-tuple-element.136), channel_id=1, source_target_pairs={{0,15},{1,0},{2,1},{3,2},{4,3},{5,4},{6,5},{7,6},{8,7},{9,8},{10,9... | collective-permute-start | bytes 98312 | tf_op jit(solution)/shard_map/while/body/eval_jaxpr/ppermute | solution.py:12
  179.9 14.0 %collective-permute-start.1 = (bf16[2,64,128]{2,1,0:T(8,128)(2,1)S(1)}, bf16[2,64,128]{2,1,0:T(8,128)(2,1)S(1)}, u32[]{:S(2)}, u32[]{:S(2)}) collective-permute-start(bf16[2,64,128]{2,1,0:T(8,128)(2,1)S(1)} %get-tuple-element.137), channel_id=1, source_target_pairs={{0,1},{1,2},{2,3},{3,4},{4,5},{5,6},{6,7},{7,8},{8,9},{9,10},{10,1... | collective-permute-start | bytes 98312 | tf_op jit(solution)/shard_map/while/body/eval_jaxpr/ppermute | solution.py:12
  181.9 12.0 %collective-permute-start.2 = (bf16[2,64,128]{2,1,0:T(8,128)(2,1)S(1)}, bf16[2,64,128]{2,1,0:T(8,128)(2,1)S(1)}, u32[]{:S(2)}, u32[]{:S(2)}) collective-permute-start(bf16[2,64,128]{2,1,0:T(8,128)(2,1)S(1)} %get-tuple-element.138), channel_id=1, source_target_pairs={{0,496},{16,0},{32,16},{48,32},{64,48},{80,64},{96,80},{112,96},{1... | collective-permute-start | bytes 98312 | tf_op jit(solution)/shard_map/while/body/eval_jaxpr/ppermute | solution.py:12
  188.6 5.4 %collective-permute-start.3 = (bf16[2,64,128]{2,1,0:T(8,128)(2,1)S(1)}, bf16[2,64,128]{2,1,0:T(8,128)(2,1)S(1)}, u32[]{:S(2)}, u32[]{:S(2)}) collective-permute-start(bf16[2,64,128]{2,1,0:T(8,128)(2,1)S(1)} %get-tuple-element.139), channel_id=1, source_target_pairs={{0,16},{16,32},{32,48},{48,64},{64,80},{80,96},{96,112},{112,128},... | collective-permute-start | bytes 98312 | tf_op jit(solution)/shard_map/while/body/eval_jaxpr/ppermute | solution.py:12
  194.6 2.7 copy-start.1
  198.5 18.8 %collective-permute-start = (bf16[2,64,128]{2,1,0:T(8,128)(2,1)S(1)}, bf16[2,64,128]{2,1,0:T(8,128)(2,1)S(1)}, u32[]{:S(2)}, u32[]{:S(2)}) collective-permute-start(bf16[2,64,128]{2,1,0:T(8,128)(2,1)S(1)} %get-tuple-element.136), channel_id=1, source_target_pairs={{0,15},{1,0},{2,1},{3,2},{4,3},{5,4},{6,5},{7,6},{8,7},{9,8},{10,9... | collective-permute-start | bytes 98312 | tf_op jit(solution)/shard_map/while/body/eval_jaxpr/ppermute | solution.py:12
  203.3 14.0 %collective-permute-start.1 = (bf16[2,64,128]{2,1,0:T(8,128)(2,1)S(1)}, bf16[2,64,128]{2,1,0:T(8,128)(2,1)S(1)}, u32[]{:S(2)}, u32[]{:S(2)}) collective-permute-start(bf16[2,64,128]{2,1,0:T(8,128)(2,1)S(1)} %get-tuple-element.137), channel_id=1, source_target_pairs={{0,1},{1,2},{2,3},{3,4},{4,5},{5,6},{6,7},{7,8},{8,9},{9,10},{10,1... | collective-permute-start | bytes 98312 | tf_op jit(solution)/shard_map/while/body/eval_jaxpr/ppermute | solution.py:12
  205.3 12.0 %collective-permute-start.2 = (bf16[2,64,128]{2,1,0:T(8,128)(2,1)S(1)}, bf16[2,64,128]{2,1,0:T(8,128)(2,1)S(1)}, u32[]{:S(2)}, u32[]{:S(2)}) collective-permute-start(bf16[2,64,128]{2,1,0:T(8,128)(2,1)S(1)} %get-tuple-element.138), channel_id=1, source_target_pairs={{0,496},{16,0},{32,16},{48,32},{64,48},{80,64},{96,80},{112,96},{1... | collective-permute-start | bytes 98312 | tf_op jit(solution)/shard_map/while/body/eval_jaxpr/ppermute | solution.py:12
  212.0 5.4 %collective-permute-start.3 = (bf16[2,64,128]{2,1,0:T(8,128)(2,1)S(1)}, bf16[2,64,128]{2,1,0:T(8,128)(2,1)S(1)}, u32[]{:S(2)}, u32[]{:S(2)}) collective-permute-start(bf16[2,64,128]{2,1,0:T(8,128)(2,1)S(1)} %get-tuple-element.139), channel_id=1, source_target_pairs={{0,16},{16,32},{32,48},{48,64},{64,80},{80,96},{96,112},{112,128},... | collective-permute-start | bytes 98312 | tf_op jit(solution)/shard_map/while/body/eval_jaxpr/ppermute | solution.py:12
  (11 other events, 17.6 us)
Sparse Core Ops, SparseCore 0:
  223.3 210.5 all-gather.3

commit v12 on v9

--- a/solution.py
+++ b/solution.py
@@ -48,7 +48,7 @@
     previous, current = lax.fori_loop(0, DEG - 1, advance, (start_vecs, first_vecs))
     total_rows = current.shape[0] * current.shape[2] * lax.axis_size("px") * lax.axis_size("py")
     partial_gram = jnp.einsum("rkj,rlj->kl", current, current, precision=lax.Precision.HIGHEST)
-    raw_gram = gathered_sum(gathered_sum(partial_gram, "py"), "px")
+    raw_gram = gathered_sum(gathered_sum(partial_gram, "px"), "py")
     squares = jnp.diagonal(raw_gram)
     scales = lax.rsqrt(squares / total_rows + 1e-06)
     filtered = current * scales[None, :, None]

time: 279 us -> 278 us (level)
  the two profiles are of different devices: /device:TPU:1 before, /device:TPU:2 now
where the time goes in v12:
time: 278 us; the launch traced here: 276 us
  starting transfers between devices  116 us (42%)
  blocking collectives  60.2 us (22%)
  matrix products  38.9 us (14%)
  local copies, waits for them, and re-layouts  34 us (12%)
  waiting for transfers between devices  20.8 us (7%)
  other arithmetic  3.29 us (1%)
    ppermute x36, starting transfers between devices, from_behind(): return lax.ppermute(value, axis, pairs)  116 us
    all_gather x2, blocking collectives, gathered_sum(): return jnp.sum(lax.all_gather(value, axis), axis=0)  60.2 us
    dot_general x9, matrix products, operator_apply(): jnp.einsum('rtkj,rtij->rki', gathered, local_tiles, preferred_element_typ...  22.3 us
    ppermute x36, waiting for transfers between devices, from_behind(): return lax.ppermute(value, axis, pairs)  20.8 us
    dot_general x9, matrix products, operator_apply(): jnp.einsum('rkj,rij->rki', received[halo_slot], halo_tiles, preferred_ele...  16 us
    while x48, local copies, waits for them, and re-layouts  9.86 us
    gather x9, local copies, waits for them, and re-layouts, operator_apply(): gathered = rounded[local_cols]  7.64 us
    gather x9, local copies, waits for them, and re-layouts, operator_apply(): received[halo_slot]  6.05 us
  transfers between devices with their start and end apart: 36, of which 8 were waited for; matrix products, arithmetic and copies ran while one was open for 11% of the time, Pallas kernels for 0%

profile of v12, /device:TPU:2, one launch (start us, length us, event | category | flops | bytes accessed | tf_op | source)
XLA Modules:
  0.0 275.9 jit_solution(1905905658108546140)
XLA Ops:
  3.4 1.9 collective-permute-start.4
  5.4 3.6 %collective-permute-start.5 = (bf16[2,64,128]{2,1,0:T(8,128)(2,1)S(1)}, bf16[2,64,128]{2,1,0:T(8,128)(2,1)S(1)}, u32[]{:S(2)}, u32[]{:S(2)}) collective-permute-start(bf16[2,64,128]{2,1,0:T(8,128)(2,1)S(1)} %get-tuple-element.67), channel_id=1, source_target_pairs={{0,496},{16,0},{32,16},{48,32},{64,48},{80,64},{96,80},{112,96},{1... | collective-permute-start | bytes 98312 | tf_op jit(solution)/shard_map/ppermute | solution.py:12
  9.0 3.8 %collective-permute-start.6 = (bf16[2,64,128]{2,1,0:T(8,128)(2,1)S(1)}, bf16[2,64,128]{2,1,0:T(8,128)(2,1)S(1)}, u32[]{:S(2)}, u32[]{:S(2)}) collective-permute-start(bf16[2,64,128]{2,1,0:T(8,128)(2,1)S(1)} %get-tuple-element.66), channel_id=1, source_target_pairs={{0,1},{1,2},{2,3},{3,4},{4,5},{5,6},{6,7},{7,8},{8,9},{9,10},{10,1... | collective-permute-start | bytes 98312 | tf_op jit(solution)/shard_map/ppermute | solution.py:12
  12.8 9.5 %collective-permute-start.7 = (bf16[2,64,128]{2,1,0:T(8,128)(2,1)S(1)}, bf16[2,64,128]{2,1,0:T(8,128)(2,1)S(1)}, u32[]{:S(2)}, u32[]{:S(2)}) collective-permute-start(bf16[2,64,128]{2,1,0:T(8,128)(2,1)S(1)} %get-tuple-element.68), channel_id=1, source_target_pairs={{0,15},{1,0},{2,1},{3,2},{4,3},{5,4},{6,5},{7,6},{8,7},{9,8},{10,9... | collective-permute-start | bytes 98312 | tf_op jit(solution)/shard_map/ppermute | solution.py:12
  24.2 2.9 %convolution_bitcast_fusion.1 = f32[16,64,128]{2,1,0:T(8,128)} fusion(bf16[16,4,64,128]{3,2,1,0:T(8,128)(2,1)} %bitcast.57, bf16[16,4,128,128]{3,2,1,0:T(8,128)(2,1)S(1)} %copy-done), kind=kOutput, calls=%fused_computation.19 | convolution fusion | flops 134217728 | bytes 3670016 | tf_op jit(solution)/shard_map/rtkj,rtij->rki/dot_general | solution.py:28
  30.1 182.4 %while.12 = (s32[]{:T(128)}, f32[16,64,128]{2,1,0:T(8,128)}, f32[16,64,128]{2,1,0:T(8,128)S(1)}, s32[16,4]{0,1:T(4,128)S(1)}, bf16[16,4,128,128]{3,2,1,0:T(8,128...) while((s32[]{:T(128)}, f32[16,64,128]{2,1,0:T(8,128)}, ...), condition=%wide.region_1.0_spmd, body=%wide.region_0.0_spmd.sunk | while | flops 168496400 | bytes 23345988 | solution.py:48
  31.0 3.9 %collective-permute-start = (bf16[2,64,128]{2,1,0:T(8,128)(2,1)S(1)}, bf16[2,64,128]{2,1,0:T(8,128)(2,1)S(1)}, u32[]{:S(2)}, u32[]{:S(2)}) collective-permute-start(bf16[2,64,128]{2,1,0:T(8,128)(2,1)S(1)} %get-tuple-element.122), channel_id=1, source_target_pairs={{0,15},{1,0},{2,1},{3,2},{4,3},{5,4},{6,5},{7,6},{8,7},{9,8},{10,9... | collective-permute-start | bytes 98312 | tf_op jit(solution)/shard_map/while/body/eval_jaxpr/ppermute | solution.py:12
  34.9 1.9 collective-permute-start.1
  36.9 1.9 collective-permute-start.2
  38.8 2.4 collective-permute-start.3
  42.2 2.4 convolution_bitcast_fusion.4
  50.8 5.1 %collective-permute-start = (bf16[2,64,128]{2,1,0:T(8,128)(2,1)S(1)}, bf16[2,64,128]{2,1,0:T(8,128)(2,1)S(1)}, u32[]{:S(2)}, u32[]{:S(2)}) collective-permute-start(bf16[2,64,128]{2,1,0:T(8,128)(2,1)S(1)} %get-tuple-element.122), channel_id=1, source_target_pairs={{0,15},{1,0},{2,1},{3,2},{4,3},{5,4},{6,5},{7,6},{8,7},{9,8},{10,9... | collective-permute-start | bytes 98312 | tf_op jit(solution)/shard_map/while/body/eval_jaxpr/ppermute | solution.py:12
  55.9 1.9 collective-permute-start.1
  57.9 3.5 %collective-permute-start.2 = (bf16[2,64,128]{2,1,0:T(8,128)(2,1)S(1)}, bf16[2,64,128]{2,1,0:T(8,128)(2,1)S(1)}, u32[]{:S(2)}, u32[]{:S(2)}) collective-permute-start(bf16[2,64,128]{2,1,0:T(8,128)(2,1)S(1)} %get-tuple-element.124), channel_id=1, source_target_pairs={{0,496},{16,0},{32,16},{48,32},{64,48},{80,64},{96,80},{112,96},{1... | collective-permute-start | bytes 98312 | tf_op jit(solution)/shard_map/while/body/eval_jaxpr/ppermute | solution.py:12
  61.4 1.9 collective-permute-start.3
  64.3 2.4 convolution_bitcast_fusion.4
  72.9 5.1 %collective-permute-start = (bf16[2,64,128]{2,1,0:T(8,128)(2,1)S(1)}, bf16[2,64,128]{2,1,0:T(8,128)(2,1)S(1)}, u32[]{:S(2)}, u32[]{:S(2)}) collective-permute-start(bf16[2,64,128]{2,1,0:T(8,128)(2,1)S(1)} %get-tuple-element.122), channel_id=1, source_target_pairs={{0,15},{1,0},{2,1},{3,2},{4,3},{5,4},{6,5},{7,6},{8,7},{9,8},{10,9... | collective-permute-start | bytes 98312 | tf_op jit(solution)/shard_map/while/body/eval_jaxpr/ppermute | solution.py:12
  78.0 1.9 collective-permute-start.1
  80.0 3.5 %collective-permute-start.2 = (bf16[2,64,128]{2,1,0:T(8,128)(2,1)S(1)}, bf16[2,64,128]{2,1,0:T(8,128)(2,1)S(1)}, u32[]{:S(2)}, u32[]{:S(2)}) collective-permute-start(bf16[2,64,128]{2,1,0:T(8,128)(2,1)S(1)} %get-tuple-element.124), channel_id=1, source_target_pairs={{0,496},{16,0},{32,16},{48,32},{64,48},{80,64},{96,80},{112,96},{1... | collective-permute-start | bytes 98312 | tf_op jit(solution)/shard_map/while/body/eval_jaxpr/ppermute | solution.py:12
  83.5 1.9 collective-permute-start.3
  86.4 2.4 convolution_bitcast_fusion.4
  88.8 2.9 %collective-permute-done.3 = bf16[2,64,128]{2,1,0:T(8,128)(2,1)S(1)} collective-permute-done((bf16[2,64,128]{2,1,0:T(8,128)(2,1)S(1)}, bf16[2,64,128]{2,1,0:T(8,128)(2,1)S(1)}, u32[]{:S(2)}, u32[]{:S(2)}) %collective-permute-start.3) | collective-permute-done | bytes 32800 | tf_op jit(solution)/shard_map/while/body/eval_jaxpr/ppermute | solution.py:12
  96.3 5.1 %collective-permute-start = (bf16[2,64,128]{2,1,0:T(8,128)(2,1)S(1)}, bf16[2,64,128]{2,1,0:T(8,128)(2,1)S(1)}, u32[]{:S(2)}, u32[]{:S(2)}) collective-permute-start(bf16[2,64,128]{2,1,0:T(8,128)(2,1)S(1)} %get-tuple-element.122), channel_id=1, source_target_pairs={{0,15},{1,0},{2,1},{3,2},{4,3},{5,4},{6,5},{7,6},{8,7},{9,8},{10,9... | collective-permute-start | bytes 98312 | tf_op jit(solution)/shard_map/while/body/eval_jaxpr/ppermute | solution.py:12
  101.4 1.9 collective-permute-start.1
  103.4 3.5 %collective-permute-start.2 = (bf16[2,64,128]{2,1,0:T(8,128)(2,1)S(1)}, bf16[2,64,128]{2,1,0:T(8,128)(2,1)S(1)}, u32[]{:S(2)}, u32[]{:S(2)}) collective-permute-start(bf16[2,64,128]{2,1,0:T(8,128)(2,1)S(1)} %get-tuple-element.124), channel_id=1, source_target_pairs={{0,496},{16,0},{32,16},{48,32},{64,48},{80,64},{96,80},{112,96},{1... | collective-permute-start | bytes 98312 | tf_op jit(solution)/shard_map/while/body/eval_jaxpr/ppermute | solution.py:12
  109.8 2.4 convolution_bitcast_fusion.4
  112.3 2.9 %collective-permute-done.3 = bf16[2,64,128]{2,1,0:T(8,128)(2,1)S(1)} collective-permute-done((bf16[2,64,128]{2,1,0:T(8,128)(2,1)S(1)}, bf16[2,64,128]{2,1,0:T(8,128)(2,1)S(1)}, u32[]{:S(2)}, u32[]{:S(2)}) %collective-permute-start.3) | collective-permute-done | bytes 32800 | tf_op jit(solution)/shard_map/while/body/eval_jaxpr/ppermute | solution.py:12
  119.7 5.1 %collective-permute-start = (bf16[2,64,128]{2,1,0:T(8,128)(2,1)S(1)}, bf16[2,64,128]{2,1,0:T(8,128)(2,1)S(1)}, u32[]{:S(2)}, u32[]{:S(2)}) collective-permute-start(bf16[2,64,128]{2,1,0:T(8,128)(2,1)S(1)} %get-tuple-element.122), channel_id=1, source_target_pairs={{0,15},{1,0},{2,1},{3,2},{4,3},{5,4},{6,5},{7,6},{8,7},{9,8},{10,9... | collective-permute-start | bytes 98312 | tf_op jit(solution)/shard_map/while/body/eval_jaxpr/ppermute | solution.py:12
  126.8 3.5 %collective-permute-start.2 = (bf16[2,64,128]{2,1,0:T(8,128)(2,1)S(1)}, bf16[2,64,128]{2,1,0:T(8,128)(2,1)S(1)}, u32[]{:S(2)}, u32[]{:S(2)}) collective-permute-start(bf16[2,64,128]{2,1,0:T(8,128)(2,1)S(1)} %get-tuple-element.124), channel_id=1, source_target_pairs={{0,496},{16,0},{32,16},{48,32},{64,48},{80,64},{96,80},{112,96},{1... | collective-permute-start | bytes 98312 | tf_op jit(solution)/shard_map/while/body/eval_jaxpr/ppermute | solution.py:12
  130.3 1.9 collective-permute-start.3
  133.2 2.4 convolution_bitcast_fusion.4
  135.7 2.9 %collective-permute-done.3 = bf16[2,64,128]{2,1,0:T(8,128)(2,1)S(1)} collective-permute-done((bf16[2,64,128]{2,1,0:T(8,128)(2,1)S(1)}, bf16[2,64,128]{2,1,0:T(8,128)(2,1)S(1)}, u32[]{:S(2)}, u32[]{:S(2)}) %collective-permute-start.3) | collective-permute-done | bytes 32800 | tf_op jit(solution)/shard_map/while/body/eval_jaxpr/ppermute | solution.py:12
  143.1 5.1 %collective-permute-start = (bf16[2,64,128]{2,1,0:T(8,128)(2,1)S(1)}, bf16[2,64,128]{2,1,0:T(8,128)(2,1)S(1)}, u32[]{:S(2)}, u32[]{:S(2)}) collective-permute-start(bf16[2,64,128]{2,1,0:T(8,128)(2,1)S(1)} %get-tuple-element.122), channel_id=1, source_target_pairs={{0,15},{1,0},{2,1},{3,2},{4,3},{5,4},{6,5},{7,6},{8,7},{9,8},{10,9... | collective-permute-start | bytes 98312 | tf_op jit(solution)/shard_map/while/body/eval_jaxpr/ppermute | solution.py:12
  150.2 3.5 %collective-permute-start.2 = (bf16[2,64,128]{2,1,0:T(8,128)(2,1)S(1)}, bf16[2,64,128]{2,1,0:T(8,128)(2,1)S(1)}, u32[]{:S(2)}, u32[]{:S(2)}) collective-permute-start(bf16[2,64,128]{2,1,0:T(8,128)(2,1)S(1)} %get-tuple-element.124), channel_id=1, source_target_pairs={{0,496},{16,0},{32,16},{48,32},{64,48},{80,64},{96,80},{112,96},{1... | collective-permute-start | bytes 98312 | tf_op jit(solution)/shard_map/while/body/eval_jaxpr/ppermute | solution.py:12
  156.6 2.4 convolution_bitcast_fusion.4
  159.1 2.9 %collective-permute-done.3 = bf16[2,64,128]{2,1,0:T(8,128)(2,1)S(1)} collective-permute-done((bf16[2,64,128]{2,1,0:T(8,128)(2,1)S(1)}, bf16[2,64,128]{2,1,0:T(8,128)(2,1)S(1)}, u32[]{:S(2)}, u32[]{:S(2)}) %collective-permute-start.3) | collective-permute-done | bytes 32800 | tf_op jit(solution)/shard_map/while/body/eval_jaxpr/ppermute | solution.py:12
  166.5 5.1 %collective-permute-start = (bf16[2,64,128]{2,1,0:T(8,128)(2,1)S(1)}, bf16[2,64,128]{2,1,0:T(8,128)(2,1)S(1)}, u32[]{:S(2)}, u32[]{:S(2)}) collective-permute-start(bf16[2,64,128]{2,1,0:T(8,128)(2,1)S(1)} %get-tuple-element.122), channel_id=1, source_target_pairs={{0,15},{1,0},{2,1},{3,2},{4,3},{5,4},{6,5},{7,6},{8,7},{9,8},{10,9... | collective-permute-start | bytes 98312 | tf_op jit(solution)/shard_map/while/body/eval_jaxpr/ppermute | solution.py:12
  171.7 1.9 collective-permute-start.1
  173.6 3.5 %collective-permute-start.2 = (bf16[2,64,128]{2,1,0:T(8,128)(2,1)S(1)}, bf16[2,64,128]{2,1,0:T(8,128)(2,1)S(1)}, u32[]{:S(2)}, u32[]{:S(2)}) collective-permute-start(bf16[2,64,128]{2,1,0:T(8,128)(2,1)S(1)} %get-tuple-element.124), channel_id=1, source_target_pairs={{0,496},{16,0},{32,16},{48,32},{64,48},{80,64},{96,80},{112,96},{1... | collective-permute-start | bytes 98312 | tf_op jit(solution)/shard_map/while/body/eval_jaxpr/ppermute | solution.py:12
  180.0 2.4 convolution_bitcast_fusion.4
  182.5 2.9 %collective-permute-done.3 = bf16[2,64,128]{2,1,0:T(8,128)(2,1)S(1)} collective-permute-done((bf16[2,64,128]{2,1,0:T(8,128)(2,1)S(1)}, bf16[2,64,128]{2,1,0:T(8,128)(2,1)S(1)}, u32[]{:S(2)}, u32[]{:S(2)}) %collective-permute-start.3) | collective-permute-done | bytes 32800 | tf_op jit(solution)/shard_map/while/body/eval_jaxpr/ppermute | solution.py:12
  190.0 5.1 %collective-permute-start = (bf16[2,64,128]{2,1,0:T(8,128)(2,1)S(1)}, bf16[2,64,128]{2,1,0:T(8,128)(2,1)S(1)}, u32[]{:S(2)}, u32[]{:S(2)}) collective-permute-start(bf16[2,64,128]{2,1,0:T(8,128)(2,1)S(1)} %get-tuple-element.122), channel_id=1, source_target_pairs={{0,15},{1,0},{2,1},{3,2},{4,3},{5,4},{6,5},{7,6},{8,7},{9,8},{10,9... | collective-permute-start | bytes 98312 | tf_op jit(solution)/shard_map/while/body/eval_jaxpr/ppermute | solution.py:12
  197.0 3.5 %collective-permute-start.2 = (bf16[2,64,128]{2,1,0:T(8,128)(2,1)S(1)}, bf16[2,64,128]{2,1,0:T(8,128)(2,1)S(1)}, u32[]{:S(2)}, u32[]{:S(2)}) collective-permute-start(bf16[2,64,128]{2,1,0:T(8,128)(2,1)S(1)} %get-tuple-element.124), channel_id=1, source_target_pairs={{0,496},{16,0},{32,16},{48,32},{64,48},{80,64},{96,80},{112,96},{1... | collective-permute-start | bytes 98312 | tf_op jit(solution)/shard_map/while/body/eval_jaxpr/ppermute | solution.py:12
  200.5 1.9 collective-permute-start.3
  203.4 2.4 convolution_bitcast_fusion.4
  205.9 2.9 %collective-permute-done.3 = bf16[2,64,128]{2,1,0:T(8,128)(2,1)S(1)} collective-permute-done((bf16[2,64,128]{2,1,0:T(8,128)(2,1)S(1)}, bf16[2,64,128]{2,1,0:T(8,128)(2,1)S(1)}, u32[]{:S(2)}, u32[]{:S(2)}) %collective-permute-start.3) | collective-permute-done | bytes 32800 | tf_op jit(solution)/shard_map/while/body/eval_jaxpr/ppermute | solution.py:12
  213.1 28.4 %all-gather = f32[2048,64]{1,0:T(8,128)S(1)} all-gather(f32[64,64]{1,0:T(8,128)S(1)} %convolution_bitcast_fusion.2), channel_id=2, replica_groups=mesh['px'=32,'py'=16] {'px'}, dimensions={0}, use_global_device_ids=true | all-gather | bytes 540672 | tf_op jit(solution)/shard_map/all_gather | solution.py:16
  241.6 31.8 %all-gather.1 = f32[1024,64]{1,0:T(8,128)S(1)} all-gather(f32[64,64]{1,0:T(8,128)S(1)} %reduce_sum.18), channel_id=3, replica_groups=mesh['px'=32,'py'=16] {'py'}, dimensions={0}, use_global_device_ids=true | all-gather | bytes 278528 | tf_op jit(solution)/shard_map/all_gather | solution.py:16
  (258 shorter events, 68.7 us)
Async XLA Ops:
  0.6 23.6 %copy-start = (bf16[16,4,128,128]{3,2,1,0:T(8,128)(2,1)S(1)}, bf16[16,4,128,128]{3,2,1,0:T(8,128)(2,1)}, u32[]{:S(2)}) copy-start(bf16[16,4,128,128]{3,2,1,0:T(8,128)(2,1)} %param.9) | copy-start | bytes 6291460
  0.6 21.7 %copy-start.5 = (s32[16,4]{0,1:T(4,128)S(1)}, s32[16,4]{0,1:T(4,128)}, u32[]{:S(2)}) copy-start(s32[16,4]{0,1:T(4,128)} %param.10) | copy-start | bytes 772
  0.7 21.7 %copy-start.7 = (s32[16]{0:T(128)S(1)}, s32[16]{0:T(128)}, u32[]{:S(2)}) copy-start(s32[16]{0:T(128)} %param.12) | copy-start | bytes 196
  1.9 25.3 %copy-start.2 = (f32[16,64,128]{2,1,0:T(8,128)}, f32[16,64,128]{2,1,0:T(8,128)S(1)}, u32[]{:S(2)}) copy-start(f32[16,64,128]{2,1,0:T(8,128)S(1)} %copy.41) | copy-start | bytes 1572868
  3.4 23.8 %collective-permute-start.4 = (bf16[2,64,128]{2,1,0:T(8,128)(2,1)S(1)}, bf16[2,64,128]{2,1,0:T(8,128)(2,1)S(1)}, u32[]{:S(2)}, u32[]{:S(2)}) collective-permute-start(bf16[2,64,128]{2,1,0:T(8,128)(2,1)S(1)} %get-tuple-element.65), channel_id=1, source_target_pairs={{0,16},{16,32},{32,48},{48,64},{64,80},{80,96},{96,112},{112,128},... | collective-permute-start | bytes 98312 | tf_op jit(solution)/shard_map/ppermute | solution.py:12
  5.4 21.9 %collective-permute-start.5 = (bf16[2,64,128]{2,1,0:T(8,128)(2,1)S(1)}, bf16[2,64,128]{2,1,0:T(8,128)(2,1)S(1)}, u32[]{:S(2)}, u32[]{:S(2)}) collective-permute-start(bf16[2,64,128]{2,1,0:T(8,128)(2,1)S(1)} %get-tuple-element.67), channel_id=1, source_target_pairs={{0,496},{16,0},{32,16},{48,32},{64,48},{80,64},{96,80},{112,96},{1... | collective-permute-start | bytes 98312 | tf_op jit(solution)/shard_map/ppermute | solution.py:12
  9.0 18.2 %collective-permute-start.6 = (bf16[2,64,128]{2,1,0:T(8,128)(2,1)S(1)}, bf16[2,64,128]{2,1,0:T(8,128)(2,1)S(1)}, u32[]{:S(2)}, u32[]{:S(2)}) collective-permute-start(bf16[2,64,128]{2,1,0:T(8,128)(2,1)S(1)} %get-tuple-element.66), channel_id=1, source_target_pairs={{0,1},{1,2},{2,3},{3,4},{4,5},{5,6},{6,7},{7,8},{8,9},{9,10},{10,1... | collective-permute-start | bytes 98312 | tf_op jit(solution)/shard_map/ppermute | solution.py:12
  12.8 14.4 %collective-permute-start.7 = (bf16[2,64,128]{2,1,0:T(8,128)(2,1)S(1)}, bf16[2,64,128]{2,1,0:T(8,128)(2,1)S(1)}, u32[]{:S(2)}, u32[]{:S(2)}) collective-permute-start(bf16[2,64,128]{2,1,0:T(8,128)(2,1)S(1)} %get-tuple-element.68), channel_id=1, source_target_pairs={{0,15},{1,0},{2,1},{3,2},{4,3},{5,4},{6,5},{7,6},{8,7},{9,8},{10,9... | collective-permute-start | bytes 98312 | tf_op jit(solution)/shard_map/ppermute | solution.py:12
  24.2 4.3 %copy-start.3 = (bf16[16,128,128]{2,1,0:T(8,128)(2,1)S(1)}, bf16[16,128,128]{2,1,0:T(8,128)(2,1)}, u32[]{:S(2)}) copy-start(bf16[16,128,128]{2,1,0:T(8,128)(2,1)} %param.11) | copy-start | bytes 1572868
  27.2 2.9 %copy-start.6 = (s32[4,2]{0,1:T(2,128)S(1)}, s32[4,2]{0,1:T(2,128)}, u32[]{:S(2)}) copy-start(s32[4,2]{0,1:T(2,128)} %param.13) | copy-start | bytes 100
  31.0 13.6 %collective-permute-start = (bf16[2,64,128]{2,1,0:T(8,128)(2,1)S(1)}, bf16[2,64,128]{2,1,0:T(8,128)(2,1)S(1)}, u32[]{:S(2)}, u32[]{:S(2)}) collective-permute-start(bf16[2,64,128]{2,1,0:T(8,128)(2,1)S(1)} %get-tuple-element.122), channel_id=1, source_target_pairs={{0,15},{1,0},{2,1},{3,2},{4,3},{5,4},{6,5},{7,6},{8,7},{9,8},{10,9... | collective-permute-start | bytes 98312 | tf_op jit(solution)/shard_map/while/body/eval_jaxpr/ppermute | solution.py:12
  34.9 9.7 %collective-permute-start.1 = (bf16[2,64,128]{2,1,0:T(8,128)(2,1)S(1)}, bf16[2,64,128]{2,1,0:T(8,128)(2,1)S(1)}, u32[]{:S(2)}, u32[]{:S(2)}) collective-permute-start(bf16[2,64,128]{2,1,0:T(8,128)(2,1)S(1)} %get-tuple-element.123), channel_id=1, source_target_pairs={{0,1},{1,2},{2,3},{3,4},{4,5},{5,6},{6,7},{7,8},{8,9},{9,10},{10,1... | collective-permute-start | bytes 98312 | tf_op jit(solution)/shard_map/while/body/eval_jaxpr/ppermute | solution.py:12
  36.9 7.8 %collective-permute-start.2 = (bf16[2,64,128]{2,1,0:T(8,128)(2,1)S(1)}, bf16[2,64,128]{2,1,0:T(8,128)(2,1)S(1)}, u32[]{:S(2)}, u32[]{:S(2)}) collective-permute-start(bf16[2,64,128]{2,1,0:T(8,128)(2,1)S(1)} %get-tuple-element.124), channel_id=1, source_target_pairs={{0,496},{16,0},{32,16},{48,32},{64,48},{80,64},{96,80},{112,96},{1... | collective-permute-start | bytes 98312 | tf_op jit(solution)/shard_map/while/body/eval_jaxpr/ppermute | solution.py:12
  38.8 7.5 %collective-permute-start.3 = (bf16[2,64,128]{2,1,0:T(8,128)(2,1)S(1)}, bf16[2,64,128]{2,1,0:T(8,128)(2,1)S(1)}, u32[]{:S(2)}, u32[]{:S(2)}) collective-permute-start(bf16[2,64,128]{2,1,0:T(8,128)(2,1)S(1)} %get-tuple-element.125), channel_id=1, source_target_pairs={{0,16},{16,32},{32,48},{48,64},{64,80},{80,96},{96,112},{112,128},... | collective-permute-start | bytes 98312 | tf_op jit(solution)/shard_map/while/body/eval_jaxpr/ppermute | solution.py:12
  46.9 2.7 copy-start.1
  50.8 15.9 %collective-permute-start = (bf16[2,64,128]{2,1,0:T(8,128)(2,1)S(1)}, bf16[2,64,128]{2,1,0:T(8,128)(2,1)S(1)}, u32[]{:S(2)}, u32[]{:S(2)}) collective-permute-start(bf16[2,64,128]{2,1,0:T(8,128)(2,1)S(1)} %get-tuple-element.122), channel_id=1, source_target_pairs={{0,15},{1,0},{2,1},{3,2},{4,3},{5,4},{6,5},{7,6},{8,7},{9,8},{10,9... | collective-permute-start | bytes 98312 | tf_op jit(solution)/shard_map/while/body/eval_jaxpr/ppermute | solution.py:12
  55.9 10.8 %collective-permute-start.1 = (bf16[2,64,128]{2,1,0:T(8,128)(2,1)S(1)}, bf16[2,64,128]{2,1,0:T(8,128)(2,1)S(1)}, u32[]{:S(2)}, u32[]{:S(2)}) collective-permute-start(bf16[2,64,128]{2,1,0:T(8,128)(2,1)S(1)} %get-tuple-element.123), channel_id=1, source_target_pairs={{0,1},{1,2},{2,3},{3,4},{4,5},{5,6},{6,7},{7,8},{8,9},{9,10},{10,1... | collective-permute-start | bytes 98312 | tf_op jit(solution)/shard_map/while/body/eval_jaxpr/ppermute | solution.py:12
  57.9 8.9 %collective-permute-start.2 = (bf16[2,64,128]{2,1,0:T(8,128)(2,1)S(1)}, bf16[2,64,128]{2,1,0:T(8,128)(2,1)S(1)}, u32[]{:S(2)}, u32[]{:S(2)}) collective-permute-start(bf16[2,64,128]{2,1,0:T(8,128)(2,1)S(1)} %get-tuple-element.124), channel_id=1, source_target_pairs={{0,496},{16,0},{32,16},{48,32},{64,48},{80,64},{96,80},{112,96},{1... | collective-permute-start | bytes 98312 | tf_op jit(solution)/shard_map/while/body/eval_jaxpr/ppermute | solution.py:12
  61.4 7.0 %collective-permute-start.3 = (bf16[2,64,128]{2,1,0:T(8,128)(2,1)S(1)}, bf16[2,64,128]{2,1,0:T(8,128)(2,1)S(1)}, u32[]{:S(2)}, u32[]{:S(2)}) collective-permute-start(bf16[2,64,128]{2,1,0:T(8,128)(2,1)S(1)} %get-tuple-element.125), channel_id=1, source_target_pairs={{0,16},{16,32},{32,48},{48,64},{64,80},{80,96},{96,112},{112,128},... | collective-permute-start | bytes 98312 | tf_op jit(solution)/shard_map/while/body/eval_jaxpr/ppermute | solution.py:12
  69.0 2.7 copy-start.1
  72.9 15.9 %collective-permute-start = (bf16[2,64,128]{2,1,0:T(8,128)(2,1)S(1)}, bf16[2,64,128]{2,1,0:T(8,128)(2,1)S(1)}, u32[]{:S(2)}, u32[]{:S(2)}) collective-permute-start(bf16[2,64,128]{2,1,0:T(8,128)(2,1)S(1)} %get-tuple-element.122), channel_id=1, source_target_pairs={{0,15},{1,0},{2,1},{3,2},{4,3},{5,4},{6,5},{7,6},{8,7},{9,8},{10,9... | collective-permute-start | bytes 98312 | tf_op jit(solution)/shard_map/while/body/eval_jaxpr/ppermute | solution.py:12
  78.0 10.8 %collective-permute-start.1 = (bf16[2,64,128]{2,1,0:T(8,128)(2,1)S(1)}, bf16[2,64,128]{2,1,0:T(8,128)(2,1)S(1)}, u32[]{:S(2)}, u32[]{:S(2)}) collective-permute-start(bf16[2,64,128]{2,1,0:T(8,128)(2,1)S(1)} %get-tuple-element.123), channel_id=1, source_target_pairs={{0,1},{1,2},{2,3},{3,4},{4,5},{5,6},{6,7},{7,8},{8,9},{9,10},{10,1... | collective-permute-start | bytes 98312 | tf_op jit(solution)/shard_map/while/body/eval_jaxpr/ppermute | solution.py:12
  80.0 8.9 %collective-permute-start.2 = (bf16[2,64,128]{2,1,0:T(8,128)(2,1)S(1)}, bf16[2,64,128]{2,1,0:T(8,128)(2,1)S(1)}, u32[]{:S(2)}, u32[]{:S(2)}) collective-permute-start(bf16[2,64,128]{2,1,0:T(8,128)(2,1)S(1)} %get-tuple-element.124), channel_id=1, source_target_pairs={{0,496},{16,0},{32,16},{48,32},{64,48},{80,64},{96,80},{112,96},{1... | collective-permute-start | bytes 98312 | tf_op jit(solution)/shard_map/while/body/eval_jaxpr/ppermute | solution.py:12
  83.5 8.3 %collective-permute-start.3 = (bf16[2,64,128]{2,1,0:T(8,128)(2,1)S(1)}, bf16[2,64,128]{2,1,0:T(8,128)(2,1)S(1)}, u32[]{:S(2)}, u32[]{:S(2)}) collective-permute-start(bf16[2,64,128]{2,1,0:T(8,128)(2,1)S(1)} %get-tuple-element.125), channel_id=1, source_target_pairs={{0,16},{16,32},{32,48},{48,64},{64,80},{80,96},{96,112},{112,128},... | collective-permute-start | bytes 98312 | tf_op jit(solution)/shard_map/while/body/eval_jaxpr/ppermute | solution.py:12
  92.4 2.7 copy-start.1
  96.3 15.9 %collective-permute-start = (bf16[2,64,128]{2,1,0:T(8,128)(2,1)S(1)}, bf16[2,64,128]{2,1,0:T(8,128)(2,1)S(1)}, u32[]{:S(2)}, u32[]{:S(2)}) collective-permute-start(bf16[2,64,128]{2,1,0:T(8,128)(2,1)S(1)} %get-tuple-element.122), channel_id=1, source_target_pairs={{0,15},{1,0},{2,1},{3,2},{4,3},{5,4},{6,5},{7,6},{8,7},{9,8},{10,9... | collective-permute-start | bytes 98312 | tf_op jit(solution)/shard_map/while/body/eval_jaxpr/ppermute | solution.py:12
  101.4 10.8 %collective-permute-start.1 = (bf16[2,64,128]{2,1,0:T(8,128)(2,1)S(1)}, bf16[2,64,128]{2,1,0:T(8,128)(2,1)S(1)}, u32[]{:S(2)}, u32[]{:S(2)}) collective-permute-start(bf16[2,64,128]{2,1,0:T(8,128)(2,1)S(1)} %get-tuple-element.123), channel_id=1, source_target_pairs={{0,1},{1,2},{2,3},{3,4},{4,5},{5,6},{6,7},{7,8},{8,9},{9,10},{10,1... | collective-permute-start | bytes 98312 | tf_op jit(solution)/shard_map/while/body/eval_jaxpr/ppermute | solution.py:12
  103.4 8.9 %collective-permute-start.2 = (bf16[2,64,128]{2,1,0:T(8,128)(2,1)S(1)}, bf16[2,64,128]{2,1,0:T(8,128)(2,1)S(1)}, u32[]{:S(2)}, u32[]{:S(2)}) collective-permute-start(bf16[2,64,128]{2,1,0:T(8,128)(2,1)S(1)} %get-tuple-element.124), channel_id=1, source_target_pairs={{0,496},{16,0},{32,16},{48,32},{64,48},{80,64},{96,80},{112,96},{1... | collective-permute-start | bytes 98312 | tf_op jit(solution)/shard_map/while/body/eval_jaxpr/ppermute | solution.py:12
  106.9 8.3 %collective-permute-start.3 = (bf16[2,64,128]{2,1,0:T(8,128)(2,1)S(1)}, bf16[2,64,128]{2,1,0:T(8,128)(2,1)S(1)}, u32[]{:S(2)}, u32[]{:S(2)}) collective-permute-start(bf16[2,64,128]{2,1,0:T(8,128)(2,1)S(1)} %get-tuple-element.125), channel_id=1, source_target_pairs={{0,16},{16,32},{32,48},{48,64},{64,80},{80,96},{96,112},{112,128},... | collective-permute-start | bytes 98312 | tf_op jit(solution)/shard_map/while/body/eval_jaxpr/ppermute | solution.py:12
  115.8 2.7 copy-start.1
  119.7 15.9 %collective-permute-start = (bf16[2,64,128]{2,1,0:T(8,128)(2,1)S(1)}, bf16[2,64,128]{2,1,0:T(8,128)(2,1)S(1)}, u32[]{:S(2)}, u32[]{:S(2)}) collective-permute-start(bf16[2,64,128]{2,1,0:T(8,128)(2,1)S(1)} %get-tuple-element.122), channel_id=1, source_target_pairs={{0,15},{1,0},{2,1},{3,2},{4,3},{5,4},{6,5},{7,6},{8,7},{9,8},{10,9... | collective-permute-start | bytes 98312 | tf_op jit(solution)/shard_map/while/body/eval_jaxpr/ppermute | solution.py:12
  124.9 10.8 %collective-permute-start.1 = (bf16[2,64,128]{2,1,0:T(8,128)(2,1)S(1)}, bf16[2,64,128]{2,1,0:T(8,128)(2,1)S(1)}, u32[]{:S(2)}, u32[]{:S(2)}) collective-permute-start(bf16[2,64,128]{2,1,0:T(8,128)(2,1)S(1)} %get-tuple-element.123), channel_id=1, source_target_pairs={{0,1},{1,2},{2,3},{3,4},{4,5},{5,6},{6,7},{7,8},{8,9},{9,10},{10,1... | collective-permute-start | bytes 98312 | tf_op jit(solution)/shard_map/while/body/eval_jaxpr/ppermute | solution.py:12
  126.8 8.9 %collective-permute-start.2 = (bf16[2,64,128]{2,1,0:T(8,128)(2,1)S(1)}, bf16[2,64,128]{2,1,0:T(8,128)(2,1)S(1)}, u32[]{:S(2)}, u32[]{:S(2)}) collective-permute-start(bf16[2,64,128]{2,1,0:T(8,128)(2,1)S(1)} %get-tuple-element.124), channel_id=1, source_target_pairs={{0,496},{16,0},{32,16},{48,32},{64,48},{80,64},{96,80},{112,96},{1... | collective-permute-start | bytes 98312 | tf_op jit(solution)/shard_map/while/body/eval_jaxpr/ppermute | solution.py:12
  130.3 8.3 %collective-permute-start.3 = (bf16[2,64,128]{2,1,0:T(8,128)(2,1)S(1)}, bf16[2,64,128]{2,1,0:T(8,128)(2,1)S(1)}, u32[]{:S(2)}, u32[]{:S(2)}) collective-permute-start(bf16[2,64,128]{2,1,0:T(8,128)(2,1)S(1)} %get-tuple-element.125), channel_id=1, source_target_pairs={{0,16},{16,32},{32,48},{48,64},{64,80},{80,96},{96,112},{112,128},... | collective-permute-start | bytes 98312 | tf_op jit(solution)/shard_map/while/body/eval_jaxpr/ppermute | solution.py:12
  139.2 2.7 copy-start.1
  143.1 15.9 %collective-permute-start = (bf16[2,64,128]{2,1,0:T(8,128)(2,1)S(1)}, bf16[2,64,128]{2,1,0:T(8,128)(2,1)S(1)}, u32[]{:S(2)}, u32[]{:S(2)}) collective-permute-start(bf16[2,64,128]{2,1,0:T(8,128)(2,1)S(1)} %get-tuple-element.122), channel_id=1, source_target_pairs={{0,15},{1,0},{2,1},{3,2},{4,3},{5,4},{6,5},{7,6},{8,7},{9,8},{10,9... | collective-permute-start | bytes 98312 | tf_op jit(solution)/shard_map/while/body/eval_jaxpr/ppermute | solution.py:12
  148.3 10.8 %collective-permute-start.1 = (bf16[2,64,128]{2,1,0:T(8,128)(2,1)S(1)}, bf16[2,64,128]{2,1,0:T(8,128)(2,1)S(1)}, u32[]{:S(2)}, u32[]{:S(2)}) collective-permute-start(bf16[2,64,128]{2,1,0:T(8,128)(2,1)S(1)} %get-tuple-element.123), channel_id=1, source_target_pairs={{0,1},{1,2},{2,3},{3,4},{4,5},{5,6},{6,7},{7,8},{8,9},{9,10},{10,1... | collective-permute-start | bytes 98312 | tf_op jit(solution)/shard_map/while/body/eval_jaxpr/ppermute | solution.py:12
  150.2 8.9 %collective-permute-start.2 = (bf16[2,64,128]{2,1,0:T(8,128)(2,1)S(1)}, bf16[2,64,128]{2,1,0:T(8,128)(2,1)S(1)}, u32[]{:S(2)}, u32[]{:S(2)}) collective-permute-start(bf16[2,64,128]{2,1,0:T(8,128)(2,1)S(1)} %get-tuple-element.124), channel_id=1, source_target_pairs={{0,496},{16,0},{32,16},{48,32},{64,48},{80,64},{96,80},{112,96},{1... | collective-permute-start | bytes 98312 | tf_op jit(solution)/shard_map/while/body/eval_jaxpr/ppermute | solution.py:12
  153.7 8.3 %collective-permute-start.3 = (bf16[2,64,128]{2,1,0:T(8,128)(2,1)S(1)}, bf16[2,64,128]{2,1,0:T(8,128)(2,1)S(1)}, u32[]{:S(2)}, u32[]{:S(2)}) collective-permute-start(bf16[2,64,128]{2,1,0:T(8,128)(2,1)S(1)} %get-tuple-element.125), channel_id=1, source_target_pairs={{0,16},{16,32},{32,48},{48,64},{64,80},{80,96},{96,112},{112,128},... | collective-permute-start | bytes 98312 | tf_op jit(solution)/shard_map/while/body/eval_jaxpr/ppermute | solution.py:12
  166.5 15.9 %collective-permute-start = (bf16[2,64,128]{2,1,0:T(8,128)(2,1)S(1)}, bf16[2,64,128]{2,1,0:T(8,128)(2,1)S(1)}, u32[]{:S(2)}, u32[]{:S(2)}) collective-permute-start(bf16[2,64,128]{2,1,0:T(8,128)(2,1)S(1)} %get-tuple-element.122), channel_id=1, source_target_pairs={{0,15},{1,0},{2,1},{3,2},{4,3},{5,4},{6,5},{7,6},{8,7},{9,8},{10,9... | collective-permute-start | bytes 98312 | tf_op jit(solution)/shard_map/while/body/eval_jaxpr/ppermute | solution.py:12
  171.7 10.8 %collective-permute-start.1 = (bf16[2,64,128]{2,1,0:T(8,128)(2,1)S(1)}, bf16[2,64,128]{2,1,0:T(8,128)(2,1)S(1)}, u32[]{:S(2)}, u32[]{:S(2)}) collective-permute-start(bf16[2,64,128]{2,1,0:T(8,128)(2,1)S(1)} %get-tuple-element.123), channel_id=1, source_target_pairs={{0,1},{1,2},{2,3},{3,4},{4,5},{5,6},{6,7},{7,8},{8,9},{9,10},{10,1... | collective-permute-start | bytes 98312 | tf_op jit(solution)/shard_map/while/body/eval_jaxpr/ppermute | solution.py:12
  173.6 8.9 %collective-permute-start.2 = (bf16[2,64,128]{2,1,0:T(8,128)(2,1)S(1)}, bf16[2,64,128]{2,1,0:T(8,128)(2,1)S(1)}, u32[]{:S(2)}, u32[]{:S(2)}) collective-permute-start(bf16[2,64,128]{2,1,0:T(8,128)(2,1)S(1)} %get-tuple-element.124), channel_id=1, source_target_pairs={{0,496},{16,0},{32,16},{48,32},{64,48},{80,64},{96,80},{112,96},{1... | collective-permute-start | bytes 98312 | tf_op jit(solution)/shard_map/while/body/eval_jaxpr/ppermute | solution.py:12
  177.1 8.3 %collective-permute-start.3 = (bf16[2,64,128]{2,1,0:T(8,128)(2,1)S(1)}, bf16[2,64,128]{2,1,0:T(8,128)(2,1)S(1)}, u32[]{:S(2)}, u32[]{:S(2)}) collective-permute-start(bf16[2,64,128]{2,1,0:T(8,128)(2,1)S(1)} %get-tuple-element.125), channel_id=1, source_target_pairs={{0,16},{16,32},{32,48},{48,64},{64,80},{80,96},{96,112},{112,128},... | collective-permute-start | bytes 98312 | tf_op jit(solution)/shard_map/while/body/eval_jaxpr/ppermute | solution.py:12
  186.0 2.7 copy-start.1
  190.0 15.9 %collective-permute-start = (bf16[2,64,128]{2,1,0:T(8,128)(2,1)S(1)}, bf16[2,64,128]{2,1,0:T(8,128)(2,1)S(1)}, u32[]{:S(2)}, u32[]{:S(2)}) collective-permute-start(bf16[2,64,128]{2,1,0:T(8,128)(2,1)S(1)} %get-tuple-element.122), channel_id=1, source_target_pairs={{0,15},{1,0},{2,1},{3,2},{4,3},{5,4},{6,5},{7,6},{8,7},{9,8},{10,9... | collective-permute-start | bytes 98312 | tf_op jit(solution)/shard_map/while/body/eval_jaxpr/ppermute | solution.py:12
  195.1 10.8 %collective-permute-start.1 = (bf16[2,64,128]{2,1,0:T(8,128)(2,1)S(1)}, bf16[2,64,128]{2,1,0:T(8,128)(2,1)S(1)}, u32[]{:S(2)}, u32[]{:S(2)}) collective-permute-start(bf16[2,64,128]{2,1,0:T(8,128)(2,1)S(1)} %get-tuple-element.123), channel_id=1, source_target_pairs={{0,1},{1,2},{2,3},{3,4},{4,5},{5,6},{6,7},{7,8},{8,9},{9,10},{10,1... | collective-permute-start | bytes 98312 | tf_op jit(solution)/shard_map/while/body/eval_jaxpr/ppermute | solution.py:12
  197.0 8.9 %collective-permute-start.2 = (bf16[2,64,128]{2,1,0:T(8,128)(2,1)S(1)}, bf16[2,64,128]{2,1,0:T(8,128)(2,1)S(1)}, u32[]{:S(2)}, u32[]{:S(2)}) collective-permute-start(bf16[2,64,128]{2,1,0:T(8,128)(2,1)S(1)} %get-tuple-element.124), channel_id=1, source_target_pairs={{0,496},{16,0},{32,16},{48,32},{64,48},{80,64},{96,80},{112,96},{1... | collective-permute-start | bytes 98312 | tf_op jit(solution)/shard_map/while/body/eval_jaxpr/ppermute | solution.py:12
  200.5 8.3 %collective-permute-start.3 = (bf16[2,64,128]{2,1,0:T(8,128)(2,1)S(1)}, bf16[2,64,128]{2,1,0:T(8,128)(2,1)S(1)}, u32[]{:S(2)}, u32[]{:S(2)}) collective-permute-start(bf16[2,64,128]{2,1,0:T(8,128)(2,1)S(1)} %get-tuple-element.125), channel_id=1, source_target_pairs={{0,16},{16,32},{32,48},{48,64},{64,80},{80,96},{96,112},{112,128},... | collective-permute-start | bytes 98312 | tf_op jit(solution)/shard_map/while/body/eval_jaxpr/ppermute | solution.py:12
  (10 other events, 15.4 us)
